TPU v7x, 128 devices: a whole 4x4x4 slice. The times are simulated.
128 devices in a mesh: freq: 4 (over y), rcv: 32 (over x, z, core).
Axes of the slice: x: 4, y: 4, z: 4, core: 2. Of those that a mesh axis runs over, the one named last changes fastest.
Arguments:
- up_time: bfloat16 [128, 256, 20480], P(('freq', 'rcv')), may hold values from -74 to 74
- down_blocks: bfloat16 [8, 160, 11, 2, 128, 128], P('freq', 'rcv'), may hold values from -0.09375 to 0.09375
- block_cols: int32 [8, 160, 11], P('freq', 'rcv'), may hold values from 0 to 159, as said below
- block_counts: int32 [8, 160], P('freq', 'rcv'), may hold values from 1 to 11, as said below
Outputs:
- solution: float32 [2, 8, 128, 20480], P(None, 'freq', None, 'rcv')
- normal_residual: float32 [2, 8, 128, 20480], P(None, 'freq', None, 'rcv')
Inputs may be any that keep to these rules, and one draw needn't show every extreme that they name: block_cols[f, r, s] is the column block of slot s of row block r at frequency f; it differs from r by at most 5. Row block r of frequency f stores blocks in its first block_counts[f, r] slots.
All inputs are finite; a program needn't handle non-finite values.
Results may differ from a plain program's by a relative error of at most 0.0062.
Values may be sent and summed in bfloat16 or wider, within the bound.
No kernel may reach another device: no remote copies, remote signals or barrier semaphores. Data moves between devices by JAX's collectives and lax.ppermute only.
A program may use at most 192 MiB of HBM per device.

v0:
```python
import math

import jax
import jax.numpy as jnp
from jax import lax
from jax.sharding import PartitionSpec as P

ITERS = 2


EPSILON = 1e-06


def with_halo(cells, sides, width):
    for axis, dim in sides:
        count = lax.axis_size(axis)
        ends = count - 1
        head = lax.slice_in_dim(cells, 0, width, axis=dim)
        tail = lax.slice_in_dim(cells, cells.shape[dim] - width, cells.shape[dim], axis=dim)
        cells = jnp.concatenate(
            [
                lax.ppermute(tail, axis, [(i, (i + 1) % count) for i in range(ends)]),
                cells,
                lax.ppermute(head, axis, [((i + 1) % count, i) for i in range(ends)]),
            ],
            axis=dim,
        )
    return cells


def from_behind(value, axis, steps):
    count = lax.axis_size(axis)
    first, last = (max(0, -steps), min(count, count - steps))
    return lax.ppermute(value, axis, [(source, source + steps) for source in range(first, last)])


def fourier_table(time_steps, freq_groups, local_freqs):
    shape = (time_steps, freq_groups, local_freqs)
    sample = lax.broadcasted_iota(jnp.int32, shape, 0)
    harmonic = (
        lax.broadcasted_iota(jnp.int32, shape, 1) * local_freqs
        + lax.broadcasted_iota(jnp.int32, shape, 2)
        + 1
    )
    phase_angle = 2.0 * math.pi / time_steps * (harmonic * sample % time_steps).astype(jnp.float32)
    scale_factor = 1.0 / math.sqrt(time_steps)
    return jnp.stack(
        [jnp.cos(phase_angle) * scale_factor, -jnp.sin(phase_angle) * scale_factor], axis=1
    ).astype(jnp.bfloat16)


def field_norm(field):
    squares = lax.psum(jnp.sum(field * field, axis=(0, 2, 3)), "rcv")
    return jnp.sqrt(squares + EPSILON)[None, :, None, None]


def gather_slots(extended, positions):
    return extended[:, :, positions]


def place_terms(running, contributions, positions):
    flat_terms = contributions.reshape(
        contributions.shape[0], contributions.shape[1], -1, contributions.shape[-1]
    )
    return running.at[:, :, positions.reshape(-1), :].add(flat_terms)


def body(up_time, down_blocks, block_cols, block_counts):
    freq_groups = lax.axis_size("freq")
    receiver_groups = lax.axis_size("rcv")
    shot_count, time_steps, receivers = up_time.shape
    local_freqs, local_blocks, slot_count, _, block_size, _ = down_blocks.shape
    local_rows = receivers // receiver_groups
    reach_blocks = (slot_count - 1) // 2
    rim_rows = reach_blocks * block_size
    span_blocks = local_blocks + 2 * reach_blocks
    fourier = fourier_table(time_steps, freq_groups, local_freqs)
    spectrum = jnp.einsum(
        "snr,ncgf->cfsgr", up_time, fourier, preferred_element_type=jnp.float32
    ).astype(jnp.bfloat16)
    spectrum = spectrum.reshape(
        2, local_freqs, shot_count, freq_groups * receiver_groups, local_rows
    )
    received = lax.all_to_all(spectrum, ("freq", "rcv"), split_axis=3, concat_axis=2, tiled=True)
    right_side = received.reshape(2, local_freqs, -1, local_rows).astype(jnp.float32)
    sources = right_side.shape[2]
    position = lax.axis_index("rcv")
    active = lax.broadcasted_iota(jnp.int32, block_cols.shape, 2) < block_counts[:, :, None]
    columns = block_cols - position * local_blocks + reach_blocks
    pick_slots = jax.vmap(gather_slots, in_axes=(1, 0), out_axes=1)
    place_all = jax.vmap(place_terms, in_axes=(1, 1, 0), out_axes=1)
    zero_half = jnp.zeros((), jnp.bfloat16)

    def adjoint(field):
        rounded = field.astype(jnp.bfloat16).reshape(
            2, local_freqs, sources, local_blocks, block_size
        )
        initial = jnp.zeros((2, local_freqs, sources, span_blocks, block_size), jnp.float32)
        products = jnp.einsum(
            "cfvri,frseij->fcevrsj", rounded, down_blocks, preferred_element_type=jnp.float32
        )
        contributions = jnp.stack(
            [products[:, 0, 0] + products[:, 1, 1], products[:, 1, 0] - products[:, 0, 1]]
        )
        contributions = contributions * active[None, :, None, :, :, None].astype(jnp.float32)
        spread = place_all(initial, contributions, columns)
        spread = spread.reshape(2, local_freqs, sources, span_blocks * block_size)
        lower_rim = spread[..., :rim_rows]
        middle = spread[..., rim_rows : rim_rows + local_rows]
        upper_rim = spread[..., rim_rows + local_rows :]
        from_above = from_behind(lower_rim, "rcv", -1)
        from_below = from_behind(upper_rim, "rcv", 1)
        middle = middle.at[..., :rim_rows].add(from_below)
        middle = middle.at[..., local_rows - rim_rows :].add(from_above)
        return field + middle

    beta_norm = field_norm(right_side)
    left_vector = right_side / beta_norm
    residual_right = adjoint(left_vector)
    alpha_norm = field_norm(residual_right)
    right_vector = residual_right / alpha_norm
    search_direction = right_vector
    solution = jnp.zeros_like(right_side)
    phibar = beta_norm
    rhobar = alpha_norm
    for iteration in range(ITERS):
        forward_rounded = right_vector.astype(jnp.bfloat16)
        extended = with_halo(forward_rounded, (("rcv", 3),), rim_rows)
        extended = extended.reshape(2, local_freqs, sources, span_blocks, block_size)
        picked = pick_slots(extended, columns)
        picked = jnp.where(active[None, :, None, :, :, None], picked, zero_half)
        forward_products = jnp.einsum(
            "cfvrsj,frseij->fcevri", picked, down_blocks, preferred_element_type=jnp.float32
        )
        real_part = forward_products[:, 0, 0] - forward_products[:, 1, 1]
        imaginary = forward_products[:, 0, 1] + forward_products[:, 1, 0]
        residual_left = (
            right_vector
            + jnp.stack([real_part, imaginary]).reshape(right_vector.shape)
            - alpha_norm * left_vector
        )
        beta_norm = field_norm(residual_left)
        left_vector = residual_left / beta_norm
        residual_right = adjoint(left_vector) - beta_norm * right_vector
        alpha_norm = field_norm(residual_right)
        right_vector = residual_right / alpha_norm
        rho_value = jnp.sqrt(rhobar * rhobar + beta_norm * beta_norm)
        cosine = rhobar / rho_value
        sine_value = beta_norm / rho_value
        theta_value = sine_value * alpha_norm
        rhobar = -cosine * alpha_norm
        phi_value = cosine * phibar
        phibar = sine_value * phibar
        solution = solution + phi_value / rho_value * search_direction
        search_direction = right_vector - theta_value / rho_value * search_direction
    return (solution, phibar * alpha_norm * cosine * right_vector)


def solution(mesh):
    return jax.shard_map(
        body,
        mesh=mesh,
        in_specs=(
            P(("freq", "rcv"), None, None),
            P("freq", "rcv", None, None, None, None),
            P("freq", "rcv", None),
            P("freq", "rcv"),
        ),
        out_specs=(P(None, "freq", None, "rcv"), P(None, "freq", None, "rcv")),
        check_vma=False,
    )
```

profile of v0, /device:TPU:1, one launch (start us, length us, event | category | flops | bytes accessed | tf_op | source)
XLA Modules:
  0.0 859.8 jit_solution(10818839690562564004)
XLA Ops:
  8.2 11.5 %all-to-all-start = ((bf16[2,2,1,128,640]{4,1,0,2,3:T(2,128)(2,1)}), bf16[2,2,1,128,640]{4,1,0,2,3:T(2,128)(2,1)S(1)}, u32[]{:S(2)}, u32[]{:S(2)}) async-start(bf16[2,2,1,128,640]{4,1,0,2,3:T(2,128)(2,1)} %copy.48), calls=%async_computation | async-start | bytes 1310720 | tf_op jit(solution)/shard_map/all_to_all | solution.py:84
  20.0 14.7 %all-to-all-done = bf16[2,2,1,128,640]{4,1,0,2,3:T(2,128)(2,1)S(1)} async-done(((bf16[2,2,1,128,640]{4,1,0,2,3:T(2,128)(2,1)}), bf16[2,2,1,128,640]{4,1,0,2,3:T(2,128)(2,1)S(1)}, u32[]{:S(2)}, u32[]{:S(2)}) %all-to-all-start) | async-done | bytes 655392 | tf_op jit(solution)/shard_map/all_to_all | solution.py:84
  36.1 63.8 %psum.42 = f32[2]{0:T(128)S(1)} all-reduce(f32[2]{0:T(128)S(1)} %fusion.38), channel_id=1, replica_groups=mesh['freq'=4,'rcv'=32] {'rcv'}, use_global_device_ids=true, to_apply=%region_1.2 | all-reduce | flops 2 | bytes 16 | tf_op jit(solution)/shard_map/psum | solution.py:53
  99.9 14.7 %convolution_bitcast_fusion = f32[2,2,2,128,5,11,128]{6,3,2,5,1,4,0:T(8,128)} fusion(bf16[2,5,11,2,128,128]{5,4,3,2,1,0:T(8,128)(2,1)} %param.29, f32[2]{0:T(128)S(1)} %add_sqrt_fusion.7, bf16[2,2,128,5,128]{2,4,3,1,0:T(8,128)(2,1)S(1)} %bitcast.164), kind=kOutput, calls=%fused_computation.7 | convolution fusion | flops 1846476800 | bytes 36700168 | tf_op jit(solution)/shard_map/cfvri,frseij->fcevrsj/dot_general | solution.py:99
  114.6 10.3 %fusion.6 = f32[1,2,128,5,11,128]{5,2,4,3,1,0:T(8,128)} fusion(f32[2,2,2,128,5,11,128]{6,3,2,5,1,4,0:T(8,128)} %convolution_bitcast_fusion), kind=kLoop, calls=%fused_computation.23 | loop fusion | flops 1802240 | bytes 21626880 | tf_op jit(solution)/shard_map/sub | solution.py:103
  124.9 10.3 %fusion.8 = f32[1,2,128,5,11,128]{5,2,4,3,1,0:T(8,128)} fusion(f32[2,2,2,128,5,11,128]{6,3,2,5,1,4,0:T(8,128)} %convolution_bitcast_fusion), kind=kLoop, calls=%fused_computation.26 | loop fusion | flops 1802240 | bytes 21626880 | tf_op jit(solution)/shard_map/add | solution.py:103
  135.2 13.3 %maximum_multiply_fusion = f32[2,2,128,5,11,128]{5,2,4,3,1,0:T(8,128)} fusion(f32[1,2,128,5,11,128]{5,2,4,3,1,0:T(8,128)} %fusion.6, f32[1,2,128,5,11,128]{5,2,4,3,1,0:T(8,128)} %fusion.8, f32[2,5,11]{2,1,0:T(8,128)S(1)} %get-tuple-element.157), kind=kLoop, calls=%fused_computation.8 | loop fusion | flops 7208960 | bytes 28836280 | tf_op jit(solution)/shard_map/mul | solution.py:105
  148.5 12.9 %copy.54 = f32[2,55,2,128,128]{4,3,2,1,0:T(8,128)} copy(f32[2,55,2,128,128]{4,3,1,0,2:T(8,128)} %bitcast.162) | data formatting | bytes 28835840 | tf_op jit(solution)/shard_map/vmap()/reshape | solution.py:62
  163.8 33.6 %scatter_fusion = f32[2,2,128,15,128]{4,2,3,1,0:T(8,128)} fusion(f32[2,2,128,15,128]{4,2,3,1,0:T(8,128)} %broadcast.403.clone, s32[110]{0:T(128)S(1)} %reshape.646, f32[110,2,128,128]{3,2,1,0:T(8,128)} %bitcast.159), kind=kCustom, calls=%fused_computation.2 | custom fusion | flops 3604480 | bytes 43254640 | tf_op jit(solution)/shard_map/vmap()/scatter-add | solution.py:65
  209.2 12.0 %collective-permute-done = f32[2,2,128,640]{2,3,1,0:T(8,128)S(1)} collective-permute-done((f32[2,2,128,640]{2,3,1,0:T(8,128)S(1)}, f32[2,2,128,640]{2,3,1,0:T(8,128)S(1)}, u32[]{:S(2)}, u32[]{:S(2)}) %collective-permute-start) | collective-permute-done | bytes 1310752 | tf_op jit(solution)/shard_map/ppermute | solution.py:34
  227.5 56.9 %psum.43 = f32[2]{0:T(128)S(1)} all-reduce(f32[2]{0:T(128)S(1)} %get-tuple-element.140), channel_id=1, replica_groups=mesh['freq'=4,'rcv'=32] {'rcv'}, use_global_device_ids=true, to_apply=%region_4.5 | all-reduce | flops 2 | bytes 16 | tf_op jit(solution)/shard_map/psum | solution.py:53
  305.7 7.8 gather_fusion
  313.4 9.0 %fusion.18 = f32[2,2,2,128,5,128]{3,5,2,1,4,0:T(8,128)} fusion(bf16[2,5,11,2,128,128]{5,4,3,2,1,0:T(8,128)(2,1)} %bitcast.172, pred[2,5,11]{2,1,0:T(8,128)(4,1)S(1)} %get-tuple-element.156, bf16[2,5,11,2,128,128]{5,4,3,2,1,0:T(8,128)(2,1)} %param.29), kind=kOutput, calls=%fused_computation.41 | convolution fusion | flops 1849098240 | bytes 17039470 | tf_op jit(solution)/shard_map/cfvrsj,frseij->fcevri/dot_general | solution.py:132
  324.9 59.0 %psum.44 = f32[2]{0:T(128)S(1)} all-reduce(f32[2]{0:T(128)S(1)} %get-tuple-element.138), channel_id=1, replica_groups=mesh['freq'=4,'rcv'=32] {'rcv'}, use_global_device_ids=true, to_apply=%region_6.7 | all-reduce | flops 2 | bytes 16 | tf_op jit(solution)/shard_map/psum | solution.py:53
  384.1 14.6 %convolution_bitcast_fusion.2 = f32[2,2,2,128,5,11,128]{6,3,5,4,0,2,1:T(8,128)} fusion(bf16[2,2,128,5,128,1,1]{2,4,5,3,1,6,0:T(8,128)(2,1)S(1)} %bitcast.179, bf16[2,5,11,2,128,128]{5,4,3,2,1,0:T(8,128)(2,1)} %param.29), kind=kOutput, calls=%fused_computation.12 | convolution fusion | flops 1845493760 | bytes 36700160 | tf_op jit(solution)/shard_map/cfvri,frseij->fcevrsj/dot_general | solution.py:99
  398.7 16.5 %fusion.5 = (f32[1,2,128,5,11,128]{5,2,4,3,1,0:T(8,128)}, f32[1,2,128,5,11,128]{5,2,4,3,1,0:T(8,128)}) fusion(f32[2,2,2,128,5,11,128]{6,3,5,4,0,2,1:T(8,128)} %convolution_bitcast_fusion.2), kind=kLoop, calls=%fused_computation.21 | loop fusion | flops 3604480 | bytes 43253760 | tf_op jit(solution)/shard_map/add | solution.py:103
  415.2 13.3 %maximum_multiply_fusion.1 = f32[2,2,128,5,11,128]{5,2,4,3,1,0:T(8,128)} fusion(f32[1,2,128,5,11,128]{5,2,4,3,1,0:T(8,128)} %get-tuple-element.145, f32[1,2,128,5,11,128]{5,2,4,3,1,0:T(8,128)} %get-tuple-element.144, f32[2,5,11]{2,1,0:T(8,128)S(1)} %get-tuple-element.157), kind=kLoop, calls=%fused_computation.9 | loop fusion | flops 7208960 | bytes 28836280 | tf_op jit(solution)/shard_map/mul | solution.py:105
  428.6 12.9 %copy.62 = f32[2,55,2,128,128]{4,3,2,1,0:T(8,128)} copy(f32[2,55,2,128,128]{4,3,1,0,2:T(8,128)} %bitcast.163) | data formatting | bytes 28835840 | tf_op jit(solution)/shard_map/vmap()/reshape | solution.py:62
  443.8 33.6 %scatter_fusion.1 = f32[2,2,128,15,128]{4,2,3,1,0:T(8,128)} fusion(f32[2,2,128,15,128]{4,2,3,1,0:T(8,128)} %broadcast.403.clone.1, s32[110]{0:T(128)S(1)} %reshape.646, f32[110,2,128,128]{3,2,1,0:T(8,128)} %bitcast.160), kind=kCustom, calls=%fused_computation.3 | custom fusion | flops 3604480 | bytes 43254640 | tf_op jit(solution)/shard_map/vmap()/scatter-add | solution.py:65
  491.8 9.8 %collective-permute-done.4 = f32[2,2,128,640]{2,3,1,0:T(8,128)S(1)} collective-permute-done((f32[2,2,128,640]{2,3,1,0:T(8,128)S(1)}, f32[2,2,128,640]{2,3,1,0:T(8,128)S(1)}, u32[]{:S(2)}, u32[]{:S(2)}) %collective-permute-start.4) | collective-permute-done | bytes 1310752 | tf_op jit(solution)/shard_map/ppermute | solution.py:34
  508.0 58.3 %psum.45 = f32[2]{0:T(128)S(1)} all-reduce(f32[2]{0:T(128)S(1)} %get-tuple-element.136), channel_id=1, replica_groups=mesh['freq'=4,'rcv'=32] {'rcv'}, use_global_device_ids=true, to_apply=%region_9.10 | all-reduce | flops 2 | bytes 16 | tf_op jit(solution)/shard_map/psum | solution.py:53
  569.3 5.5 collective-permute-start.7
  585.5 7.8 gather_fusion.1
  593.3 9.0 %fusion.23 = f32[2,2,2,128,5,128]{3,5,2,1,4,0:T(8,128)} fusion(bf16[2,5,11,2,128,128]{5,4,3,2,1,0:T(8,128)(2,1)} %bitcast.171, pred[2,5,11]{2,1,0:T(8,128)(4,1)S(1)} %get-tuple-element.156, bf16[2,5,11,2,128,128]{5,4,3,2,1,0:T(8,128)(2,1)} %param.29), kind=kOutput, calls=%fused_computation.42 | convolution fusion | flops 1849098240 | bytes 17039470 | tf_op jit(solution)/shard_map/cfvrsj,frseij->fcevri/dot_general | solution.py:132
  606.2 59.0 %psum.46 = f32[2]{0:T(128)S(1)} all-reduce(f32[2]{0:T(128)S(1)} %get-tuple-element.134), channel_id=1, replica_groups=mesh['freq'=4,'rcv'=32] {'rcv'}, use_global_device_ids=true, to_apply=%region_11.12 | all-reduce | flops 2 | bytes 16 | tf_op jit(solution)/shard_map/psum | solution.py:53
  666.7 14.6 %convolution_bitcast_fusion.1 = f32[2,2,2,128,5,11,128]{6,3,5,4,0,2,1:T(8,128)} fusion(bf16[2,2,128,5,128,1,1]{2,4,5,3,1,6,0:T(8,128)(2,1)S(1)} %bitcast.180, bf16[2,5,11,2,128,128]{5,4,3,2,1,0:T(8,128)(2,1)} %param.29), kind=kOutput, calls=%fused_computation.11 | convolution fusion | flops 1845493760 | bytes 36700160 | tf_op jit(solution)/shard_map/cfvri,frseij->fcevrsj/dot_general | solution.py:99
  681.3 16.5 %fusion.3 = (f32[1,2,128,5,11,128]{5,2,4,3,1,0:T(8,128)}, f32[1,2,128,5,11,128]{5,2,4,3,1,0:T(8,128)}) fusion(f32[2,2,2,128,5,11,128]{6,3,5,4,0,2,1:T(8,128)} %convolution_bitcast_fusion.1), kind=kLoop, calls=%fused_computation.17 | loop fusion | flops 3604480 | bytes 43253760 | tf_op jit(solution)/shard_map/add | solution.py:103
  697.8 13.3 %maximum_multiply_fusion.2 = f32[2,2,128,5,11,128]{5,2,4,3,1,0:T(8,128)} fusion(f32[1,2,128,5,11,128]{5,2,4,3,1,0:T(8,128)} %get-tuple-element.143, f32[1,2,128,5,11,128]{5,2,4,3,1,0:T(8,128)} %get-tuple-element.142, f32[2,5,11]{2,1,0:T(8,128)S(1)} %get-tuple-element.157), kind=kLoop, calls=%fused_computation.10 | loop fusion | flops 7208960 | bytes 28836280 | tf_op jit(solution)/shard_map/mul | solution.py:105
  711.1 12.9 %copy.69 = f32[2,55,2,128,128]{4,3,2,1,0:T(8,128)} copy(f32[2,55,2,128,128]{4,3,1,0,2:T(8,128)} %bitcast.161) | data formatting | bytes 28835840 | tf_op jit(solution)/shard_map/vmap()/reshape | solution.py:62
  726.4 33.6 %scatter_fusion.2 = f32[2,2,128,15,128]{4,2,3,1,0:T(8,128)} fusion(f32[2,2,128,15,128]{4,2,3,1,0:T(8,128)} %broadcast.403, s32[110]{0:T(128)S(1)} %reshape.646, f32[110,2,128,128]{3,2,1,0:T(8,128)} %bitcast.158), kind=kCustom, calls=%fused_computation.4 | custom fusion | flops 3604480 | bytes 43254640 | tf_op jit(solution)/shard_map/vmap()/scatter-add | solution.py:65
  774.4 9.8 %collective-permute-done.8 = f32[2,2,128,640]{2,3,1,0:T(8,128)S(1)} collective-permute-done((f32[2,2,128,640]{2,3,1,0:T(8,128)S(1)}, f32[2,2,128,640]{2,3,1,0:T(8,128)S(1)}, u32[]{:S(2)}, u32[]{:S(2)}) %collective-permute-start.8) | collective-permute-done | bytes 1310752 | tf_op jit(solution)/shard_map/ppermute | solution.py:34
  791.5 58.3 %psum.47 = f32[2]{0:T(128)S(1)} all-reduce(f32[2]{0:T(128)S(1)} %get-tuple-element.132), channel_id=1, replica_groups=mesh['freq'=4,'rcv'=32] {'rcv'}, use_global_device_ids=true, to_apply=%region_14.15 | all-reduce | flops 2 | bytes 16 | tf_op jit(solution)/shard_map/psum | solution.py:53
  (95 shorter events, 129.4 us)
Async XLA Ops:
  6.2 13.5 %copy-start.8 = (s32[2,5,11]{2,0,1:T(2,128)S(1)}, s32[2,5,11]{2,0,1:T(2,128)}, u32[]{:S(2)}) copy-start(s32[2,5,11]{2,0,1:T(2,128)} %param.30) | copy-start | bytes 1324
  6.3 13.6 %copy-start.11 = (s32[2,5]{1,0:T(2,128)S(1)}, s32[2,5]{1,0:T(2,128)}, u32[]{:S(2)}) copy-start(s32[2,5]{1,0:T(2,128)} %param.31) | copy-start | bytes 124
  8.2 26.4 %all-to-all-start = ((bf16[2,2,1,128,640]{4,1,0,2,3:T(2,128)(2,1)}), bf16[2,2,1,128,640]{4,1,0,2,3:T(2,128)(2,1)S(1)}, u32[]{:S(2)}, u32[]{:S(2)}) async-start(bf16[2,2,1,128,640]{4,1,0,2,3:T(2,128)(2,1)} %copy.48), calls=%async_computation | async-start | bytes 1310720 | tf_op jit(solution)/shard_map/all_to_all | solution.py:84
  35.8 189.8 %copy-start.5 = (bf16[2,2,1,128,640]{3,4,1,0,2:T(8,128)(2,1)}, bf16[2,2,1,128,640]{3,4,1,0,2:T(8,128)(2,1)S(1)}, u32[]{:S(2)}) copy-start(bf16[2,2,1,128,640]{3,4,1,0,2:T(8,128)(2,1)S(1)} %copy.49) | copy-start | bytes 1966084
  99.9 14.7 %copy-start.9 = (f32[2]{0:T(128)}, f32[2]{0:T(128)S(1)}, u32[]{:S(2)}) copy-start(f32[2]{0:T(128)S(1)} %psum.42) | copy-start | bytes 28
  204.7 16.5 %collective-permute-start = (f32[2,2,128,640]{2,3,1,0:T(8,128)S(1)}, f32[2,2,128,640]{2,3,1,0:T(8,128)S(1)}, u32[]{:S(2)}, u32[]{:S(2)}) collective-permute-start(f32[2,2,128,640]{2,3,1,0:T(8,128)S(1)} %get-tuple-element.150), channel_id=1, source_target_pairs={{0,1},{1,2},{2,3},{3,4},{4,5},{5,6},{6,7},{7,8},{8,9},{9,10},{10,1... | collective-permute-start | bytes 3932168 | tf_op jit(solution)/shard_map/ppermute | solution.py:34
  206.7 18.9 %collective-permute-start.1 = (f32[2,2,128,640]{2,3,1,0:T(8,128)S(1)}, f32[2,2,128,640]{2,3,1,0:T(8,128)S(1)}, u32[]{:S(2)}, u32[]{:S(2)}) collective-permute-start(f32[2,2,128,640]{2,3,1,0:T(8,128)S(1)} %get-tuple-element.151), channel_id=1, source_target_pairs={{1,0},{2,1},{3,2},{4,3},{5,4},{6,5},{7,6},{8,7},{9,8},{10,9},{11,1... | collective-permute-start | bytes 3932168 | tf_op jit(solution)/shard_map/ppermute | solution.py:34
  284.4 0.5 copy-start.12
  285.1 11.9 %collective-permute-start.2 = (bf16[2,2,128,640]{2,3,1,0:T(8,128)(2,1)S(1)}, bf16[2,2,128,640]{2,3,1,0:T(8,128)(2,1)S(1)}, u32[]{:S(2)}, u32[]{:S(2)}) collective-permute-start(bf16[2,2,128,640]{2,3,1,0:T(8,128)(2,1)S(1)} %fusion.60), channel_id=1, source_target_pairs={{0,1},{1,2},{2,3},{3,4},{4,5},{5,6},{6,7},{7,8},{8,9},{9,10},{10,1... | collective-permute-start | bytes 1966088 | tf_op jit(solution)/shard_map/ppermute | solution.py:22
  289.5 11.9 %collective-permute-start.3 = (bf16[2,2,128,640]{2,3,1,0:T(8,128)(2,1)S(1)}, bf16[2,2,128,640]{2,3,1,0:T(8,128)(2,1)S(1)}, u32[]{:S(2)}, u32[]{:S(2)}) collective-permute-start(bf16[2,2,128,640]{2,3,1,0:T(8,128)(2,1)S(1)} %fusion.60), channel_id=1, source_target_pairs={{1,0},{2,1},{3,2},{4,3},{5,4},{6,5},{7,6},{8,7},{9,8},{10,9},{11,1... | collective-permute-start | bytes 1966088 | tf_op jit(solution)/shard_map/ppermute | solution.py:24
  322.4 1.9 copy-start.6
  324.9 73.8 %copy-start.2 = (f32[2,2,128,640]{2,3,1,0:T(8,128)}, f32[2,2,128,640]{2,3,1,0:T(8,128)S(1)}, u32[]{:S(2)}) copy-start(f32[2,2,128,640]{2,3,1,0:T(8,128)S(1)} %get-tuple-element.139) | copy-start | bytes 3932164
  482.9 23.2 %copy-start.3 = (f32[2,2,128,640]{2,3,1,0:T(8,128)S(1)}, f32[2,2,128,640]{2,3,1,0:T(8,128)}, u32[]{:S(2)}) copy-start(f32[2,2,128,640]{2,3,1,0:T(8,128)} %copy-done.2) | copy-start | bytes 3932164
  484.9 16.7 %collective-permute-start.4 = (f32[2,2,128,640]{2,3,1,0:T(8,128)S(1)}, f32[2,2,128,640]{2,3,1,0:T(8,128)S(1)}, u32[]{:S(2)}, u32[]{:S(2)}) collective-permute-start(f32[2,2,128,640]{2,3,1,0:T(8,128)S(1)} %get-tuple-element.148), channel_id=1, source_target_pairs={{0,1},{1,2},{2,3},{3,4},{4,5},{5,6},{6,7},{7,8},{8,9},{9,10},{10,1... | collective-permute-start | bytes 3932168 | tf_op jit(solution)/shard_map/ppermute | solution.py:34
  487.1 18.9 %collective-permute-start.5 = (f32[2,2,128,640]{2,3,1,0:T(8,128)S(1)}, f32[2,2,128,640]{2,3,1,0:T(8,128)S(1)}, u32[]{:S(2)}, u32[]{:S(2)}) collective-permute-start(f32[2,2,128,640]{2,3,1,0:T(8,128)S(1)} %get-tuple-element.149), channel_id=1, source_target_pairs={{1,0},{2,1},{3,2},{4,3},{5,4},{6,5},{7,6},{8,7},{9,8},{10,9},{11,1... | collective-permute-start | bytes 3932168 | tf_op jit(solution)/shard_map/ppermute | solution.py:34
  508.0 74.6 %copy-start = (f32[2,2,128,640]{2,3,1,0:T(8,128)}, f32[2,2,128,640]{2,3,1,0:T(8,128)S(1)}, u32[]{:S(2)}) copy-start(f32[2,2,128,640]{2,3,1,0:T(8,128)S(1)} %get-tuple-element.137) | copy-start | bytes 3932164
  566.5 10.3 %collective-permute-start.6 = (bf16[2,2,128,640]{2,3,1,0:T(8,128)(2,1)S(1)}, bf16[2,2,128,640]{2,3,1,0:T(8,128)(2,1)S(1)}, u32[]{:S(2)}, u32[]{:S(2)}) collective-permute-start(bf16[2,2,128,640]{2,3,1,0:T(8,128)(2,1)S(1)} %fusion.61), channel_id=1, source_target_pairs={{0,1},{1,2},{2,3},{3,4},{4,5},{5,6},{6,7},{7,8},{8,9},{9,10},{10,1... | collective-permute-start | bytes 1966088 | tf_op jit(solution)/shard_map/ppermute | solution.py:22
  569.3 11.9 %collective-permute-start.7 = (bf16[2,2,128,640]{2,3,1,0:T(8,128)(2,1)S(1)}, bf16[2,2,128,640]{2,3,1,0:T(8,128)(2,1)S(1)}, u32[]{:S(2)}, u32[]{:S(2)}) collective-permute-start(bf16[2,2,128,640]{2,3,1,0:T(8,128)(2,1)S(1)} %fusion.61), channel_id=1, source_target_pairs={{1,0},{2,1},{3,2},{4,3},{5,4},{6,5},{7,6},{8,7},{9,8},{10,9},{11,1... | collective-permute-start | bytes 1966088 | tf_op jit(solution)/shard_map/ppermute | solution.py:24
  602.2 2.1 copy-start.1
  602.2 2.5 copy-start.4
  765.4 23.2 %copy-start.7 = (f32[2,2,128,640]{2,3,1,0:T(8,128)S(1)}, f32[2,2,128,640]{2,3,1,0:T(8,128)}, u32[]{:S(2)}) copy-start(f32[2,2,128,640]{2,3,1,0:T(8,128)} %get-tuple-element.135) | copy-start | bytes 3932164
  767.4 16.7 %collective-permute-start.8 = (f32[2,2,128,640]{2,3,1,0:T(8,128)S(1)}, f32[2,2,128,640]{2,3,1,0:T(8,128)S(1)}, u32[]{:S(2)}, u32[]{:S(2)}) collective-permute-start(f32[2,2,128,640]{2,3,1,0:T(8,128)S(1)} %get-tuple-element.146), channel_id=1, source_target_pairs={{0,1},{1,2},{2,3},{3,4},{4,5},{5,6},{6,7},{7,8},{8,9},{9,10},{10,1... | collective-permute-start | bytes 3932168 | tf_op jit(solution)/shard_map/ppermute | solution.py:34
  769.7 80.2 %copy-start.10 = (f32[2]{0:T(128)S(1)}, f32[2]{0:T(128)}, u32[]{:S(2)}) copy-start(f32[2]{0:T(128)} %copy-done.9) | copy-start | bytes 28
  769.7 80.2 %copy-start.13 = (f32[2]{0:T(128)S(1)}, f32[2]{0:T(128)}, u32[]{:S(2)}) copy-start(f32[2]{0:T(128)} %copy-done.12) | copy-start | bytes 28
  769.7 18.9 %collective-permute-start.9 = (f32[2,2,128,640]{2,3,1,0:T(8,128)S(1)}, f32[2,2,128,640]{2,3,1,0:T(8,128)S(1)}, u32[]{:S(2)}, u32[]{:S(2)}) collective-permute-start(f32[2,2,128,640]{2,3,1,0:T(8,128)S(1)} %get-tuple-element.147), channel_id=1, source_target_pairs={{1,0},{2,1},{3,2},{4,3},{5,4},{6,5},{7,6},{8,7},{9,8},{10,9},{11,1... | collective-permute-start | bytes 3932168 | tf_op jit(solution)/shard_map/ppermute | solution.py:34
where the time goes:
time: 869 us; the launch traced here: 860 us
  blocking collectives  355 us (41%)
  other arithmetic  217 us (25%)
  local copies, waits for them, and re-layouts  99.4 us (11%)
  waiting for transfers between devices  72.4 us (8%)
  matrix products  67.2 us (8%)
  starting transfers between devices  47.6 us (5%)
    psum x6, blocking collectives, field_norm(): squares = lax.psum(jnp.sum(field * field, axis=(0, 2, 3)), 'rcv')  355 us
    scatter-add x4, other arithmetic, place_terms(): return running.at[:, :, positions.reshape(-1), :].add(flat_terms)  101 us
    ppermute x6, waiting for transfers between devices, from_behind(): lax.ppermute(value, axis, [(source, source + steps) for source in range(f...  44.9 us
    dot_general x3, matrix products, adjoint(): jnp.einsum('cfvri,frseij->fcevrsj', rounded, down_blocks, preferred_eleme...  43.9 us
    add x3, other arithmetic, adjoint(): products[:, 0, 0] + products[:, 1, 1]  43.3 us
    mul x3, other arithmetic, adjoint(): contributions * active[None, :, None, :, :, None].astype(jnp.float32)  40 us
    reshape x3, local copies, waits for them, and re-layouts, place_terms(): contributions.reshape(contributions.shape[0], contributions.shape[1], -1,...  38.7 us
    ppermute x6, starting transfers between devices, from_behind(): lax.ppermute(value, axis, [(source, source + steps) for source in range(f...  18.2 us
  transfers between devices with their start and end apart: 11, of which 11 were waited for; matrix products, arithmetic and copies ran while one was open for 0% of the time, Pallas kernels for 0%

commit v1 on v0

--- a/solution.py
+++ b/solution.py
@@ -3,6 +3,8 @@
 import jax
 import jax.numpy as jnp
 from jax import lax
+from jax.experimental import pallas as pl
+from jax.experimental.pallas import tpu as pltpu
 from jax.sharding import PartitionSpec as P
 
 ITERS = 2
@@ -49,20 +51,115 @@
     ).astype(jnp.bfloat16)
 
 
+def rcv_sum(partial):
+    count = lax.axis_size("rcv")
+    spread = jnp.broadcast_to(partial[None], (count,) + partial.shape)
+    gathered = lax.all_to_all(spread, "rcv", 0, 0, tiled=False)
+    return jnp.sum(gathered, axis=0)
+
+
 def field_norm(field):
-    squares = lax.psum(jnp.sum(field * field, axis=(0, 2, 3)), "rcv")
+    squares = rcv_sum(jnp.sum(field * field, axis=(0, 2, 3)))
     return jnp.sqrt(squares + EPSILON)[None, :, None, None]
 
 
-def gather_slots(extended, positions):
-    return extended[:, :, positions]
-
-
-def place_terms(running, contributions, positions):
-    flat_terms = contributions.reshape(
-        contributions.shape[0], contributions.shape[1], -1, contributions.shape[-1]
-    )
-    return running.at[:, :, positions.reshape(-1), :].add(flat_terms)
+def _forward_kernel(cols_ref, counts_ref, x_ref, a_ref, o_ref):
+    freq = pl.program_id(0)
+    row = pl.program_id(1)
+    rows = pl.num_programs(1)
+    slots, _, block, _ = a_ref.shape
+    sources = o_ref.shape[1]
+    index = freq * rows + row
+    count = counts_ref[index]
+    o_ref[...] = jnp.zeros(o_ref.shape, o_ref.dtype)
+    contract = (((1,), (1,)), ((), ()))
+    for slot in range(slots):
+
+        @pl.when(slot < count)
+        def _():
+            start = pl.multiple_of(cols_ref[index * slots + slot] * block, block)
+            picked = x_ref[:, :, pl.ds(start, block)].reshape(2 * sources, block)
+            by_real = lax.dot_general(
+                picked, a_ref[slot, 0], contract, preferred_element_type=jnp.float32
+            )
+            by_imag = lax.dot_general(
+                picked, a_ref[slot, 1], contract, preferred_element_type=jnp.float32
+            )
+            o_ref[0] += by_real[:sources] - by_imag[sources:]
+            o_ref[1] += by_imag[:sources] + by_real[sources:]
+
+
+def _adjoint_kernel(cols_ref, counts_ref, u_ref, a_ref, o_ref):
+    freq = pl.program_id(0)
+    row = pl.program_id(1)
+    rows = pl.num_programs(1)
+    slots, _, block, _ = a_ref.shape
+    sources = u_ref.shape[1]
+    index = freq * rows + row
+    count = counts_ref[index]
+
+    @pl.when(row == 0)
+    def _():
+        o_ref[...] = jnp.zeros(o_ref.shape, o_ref.dtype)
+
+    field = u_ref[...].reshape(2 * sources, block)
+    for slot in range(slots):
+
+        @pl.when(slot < count)
+        def _():
+            start = pl.multiple_of(cols_ref[index * slots + slot] * block, block)
+            by_real = jnp.dot(field, a_ref[slot, 0], preferred_element_type=jnp.float32)
+            by_imag = jnp.dot(field, a_ref[slot, 1], preferred_element_type=jnp.float32)
+            o_ref[0, :, pl.ds(start, block)] += by_real[:sources] + by_imag[sources:]
+            o_ref[1, :, pl.ds(start, block)] += by_real[sources:] - by_imag[:sources]
+
+
+def apply_forward(extended, down_blocks, cols, counts):
+    local_freqs, local_blocks, slot_count, _, block_size, _ = down_blocks.shape
+    _, _, sources, span = extended.shape
+    grid_spec = pltpu.PrefetchScalarGridSpec(
+        num_scalar_prefetch=2,
+        grid=(local_freqs, local_blocks),
+        in_specs=[
+            pl.BlockSpec((2, None, sources, span), lambda f, r, c, n: (0, f, 0, 0)),
+            pl.BlockSpec(
+                (None, None, slot_count, 2, block_size, block_size),
+                lambda f, r, c, n: (f, r, 0, 0, 0, 0),
+            ),
+        ],
+        out_specs=pl.BlockSpec((2, None, sources, block_size), lambda f, r, c, n: (0, f, 0, r)),
+    )
+    return pl.pallas_call(
+        _forward_kernel,
+        grid_spec=grid_spec,
+        out_shape=jax.ShapeDtypeStruct(
+            (2, local_freqs, sources, local_blocks * block_size), jnp.float32
+        ),
+        compiler_params=pltpu.CompilerParams(dimension_semantics=("arbitrary", "arbitrary")),
+    )(cols, counts, extended, down_blocks)
+
+
+def apply_adjoint(rounded, down_blocks, cols, counts, span):
+    local_freqs, local_blocks, slot_count, _, block_size, _ = down_blocks.shape
+    sources = rounded.shape[2]
+    grid_spec = pltpu.PrefetchScalarGridSpec(
+        num_scalar_prefetch=2,
+        grid=(local_freqs, local_blocks),
+        in_specs=[
+            pl.BlockSpec((2, None, sources, block_size), lambda f, r, c, n: (0, f, 0, r)),
+            pl.BlockSpec(
+                (None, None, slot_count, 2, block_size, block_size),
+                lambda f, r, c, n: (f, r, 0, 0, 0, 0),
+            ),
+        ],
+        out_specs=pl.BlockSpec((2, None, sources, span), lambda f, r, c, n: (0, f, 0, 0)),
+    )
+    return pl.pallas_call(
+        _adjoint_kernel,
+        grid_spec=grid_spec,
+        out_shape=jax.ShapeDtypeStruct((2, local_freqs, sources, span), jnp.float32),
+        compiler_params=pltpu.CompilerParams(dimension_semantics=("arbitrary", "arbitrary")),
+    )(cols, counts, rounded, down_blocks)
 
 
 def body(up_time, down_blocks, block_cols, block_counts):
@@ -83,28 +180,15 @@
     )
     received = lax.all_to_all(spectrum, ("freq", "rcv"), split_axis=3, concat_axis=2, tiled=True)
     right_side = received.reshape(2, local_freqs, -1, local_rows).astype(jnp.float32)
-    sources = right_side.shape[2]
     position = lax.axis_index("rcv")
-    active = lax.broadcasted_iota(jnp.int32, block_cols.shape, 2) < block_counts[:, :, None]
-    columns = block_cols - position * local_blocks + reach_blocks
-    pick_slots = jax.vmap(gather_slots, in_axes=(1, 0), out_axes=1)
-    place_all = jax.vmap(place_terms, in_axes=(1, 1, 0), out_axes=1)
-    zero_half = jnp.zeros((), jnp.bfloat16)
+    columns = jnp.clip(
+        block_cols - position * local_blocks + reach_blocks, 0, span_blocks - 1
+    ).reshape(-1)
+    counts = jnp.clip(block_counts, 0, slot_count).reshape(-1)
 
     def adjoint(field):
-        rounded = field.astype(jnp.bfloat16).reshape(
-            2, local_freqs, sources, local_blocks, block_size
-        )
-        initial = jnp.zeros((2, local_freqs, sources, span_blocks, block_size), jnp.float32)
-        products = jnp.einsum(
-            "cfvri,frseij->fcevrsj", rounded, down_blocks, preferred_element_type=jnp.float32
-        )
-        contributions = jnp.stack(
-            [products[:, 0, 0] + products[:, 1, 1], products[:, 1, 0] - products[:, 0, 1]]
-        )
-        contributions = contributions * active[None, :, None, :, :, None].astype(jnp.float32)
-        spread = place_all(initial, contributions, columns)
-        spread = spread.reshape(2, local_freqs, sources, span_blocks * block_size)
+        rounded = field.astype(jnp.bfloat16)
+        spread = apply_adjoint(rounded, down_blocks, columns, counts, span_blocks * block_size)
         lower_rim = spread[..., :rim_rows]
         middle = spread[..., rim_rows : rim_rows + local_rows]
         upper_rim = spread[..., rim_rows + local_rows :]
@@ -113,6 +197,10 @@
         middle = middle.at[..., :rim_rows].add(from_below)
         middle = middle.at[..., local_rows - rim_rows :].add(from_above)
         return field + middle
+
+    def forward(field):
+        extended = with_halo(field.astype(jnp.bfloat16), (("rcv", 3),), rim_rows)
+        return field + apply_forward(extended, down_blocks, columns, counts)
 
     beta_norm = field_norm(right_side)
     left_vector = right_side / beta_norm
@@ -124,21 +212,7 @@
     phibar = beta_norm
     rhobar = alpha_norm
     for iteration in range(ITERS):
-        forward_rounded = right_vector.astype(jnp.bfloat16)
-        extended = with_halo(forward_rounded, (("rcv", 3),), rim_rows)
-        extended = extended.reshape(2, local_freqs, sources, span_blocks, block_size)
-        picked = pick_slots(extended, columns)
-        picked = jnp.where(active[None, :, None, :, :, None], picked, zero_half)
-        forward_products = jnp.einsum(
-            "cfvrsj,frseij->fcevri", picked, down_blocks, preferred_element_type=jnp.float32
-        )
-        real_part = forward_products[:, 0, 0] - forward_products[:, 1, 1]
-        imaginary = forward_products[:, 0, 1] + forward_products[:, 1, 0]
-        residual_left = (
-            right_vector
-            + jnp.stack([real_part, imaginary]).reshape(right_vector.shape)
-            - alpha_norm * left_vector
-        )
+        residual_left = forward(right_vector) - alpha_norm * left_vector
         beta_norm = field_norm(residual_left)
         left_vector = residual_left / beta_norm
         residual_right = adjoint(left_vector) - beta_norm * right_vector

time: 869 us -> 328 us (0.38)
  blocking collectives: 355 us -> 85.9 us
  other arithmetic: 217 us -> 23.9 us
  local copies, waits for them, and re-layouts: 99.4 us -> 9.71 us
  Pallas kernels: 0 us -> 73.9 us
  matrix products: 67.2 us -> 5.45 us
  waiting for transfers between devices: 72.4 us -> 84.9 us
    psum x6 -> x0, blocking collectives: 355 us -> none  [field_norm(): squares = lax.psum(jnp.sum(field * field, axis=(0, 2, 3)), 'rcv')]
    scatter-add x4 -> x0, other arithmetic: 101 us -> none  [place_terms(): return running.at[:, :, positions.reshape(-1), :].add(flat_terms)]
    all_to_all x0 -> x5, blocking collectives: none -> 85.9 us  [rcv_sum(): gathered = lax.all_to_all(spread, 'rcv', 0, 0, tiled=False)]
    pallas_call x0 -> x5, Pallas kernels: none -> 73.9 us  [the longest x3 43.5 us: apply_adjoint(): pl.pallas_call(_adjoint_kernel, grid_spec=grid_spec, out_shape=jax.ShapeD...]
    dot_general x5 -> x0, matrix products: 61.8 us -> none  [the longest x3 43.9 us: adjoint(): jnp.einsum('cfvri,frseij->fcevrsj', rounded, down_blocks, preferred_eleme...]
    add x5 -> x0, other arithmetic: 44.7 us -> none  [the longest x3 43.3 us: adjoint(): products[:, 0, 0] + products[:, 1, 1]]
    reshape x6 -> x2, local copies, waits for them, and re-layouts: 44.5 us -> 1.24 us  [the longest x1 0.62 us: body(): counts = jnp.clip(block_counts, 0, slot_count).reshape(-1)]
    mul x3 -> x0, other arithmetic: 40 us -> none  [adjoint(): contributions * active[None, :, None, :, :, None].astype(jnp.float32)]
  transfers between devices with their start and end apart: 11 -> 12, of which waited for: 11 -> 12; matrix products, arithmetic and copies ran while one was open for 0% -> 0% of each run, Pallas kernels for 0% -> 0%
where the time goes in v1:
time: 328 us; the launch traced here: 325 us
  blocking collectives  85.9 us (26%)
  waiting for transfers between devices  84.9 us (26%)
  Pallas kernels  73.9 us (23%)
  starting transfers between devices  40.8 us (12%)
  other arithmetic  23.9 us (7%)
  local copies, waits for them, and re-layouts  9.71 us (3%)
  matrix products  5.45 us (2%)
    all_to_all x5, blocking collectives, rcv_sum(): gathered = lax.all_to_all(spread, 'rcv', 0, 0, tiled=False)  85.9 us
    ppermute x6, waiting for transfers between devices, from_behind(): lax.ppermute(value, axis, [(source, source + steps) for source in range(f...  49.3 us
    pallas_call x3, Pallas kernels, apply_adjoint(): pl.pallas_call(_adjoint_kernel, grid_spec=grid_spec, out_shape=jax.ShapeD...  43.5 us
    pallas_call x2, Pallas kernels, apply_forward(): pl.pallas_call(_forward_kernel, grid_spec=grid_spec, out_shape=jax.ShapeD...  30.4 us
    all_to_all x1, waiting for transfers between devices, body(): lax.all_to_all(spectrum, ('freq', 'rcv'), split_axis=3, concat_axis=2, ti...  14.8 us
    ppermute x6, starting transfers between devices, from_behind(): lax.ppermute(value, axis, [(source, source + steps) for source in range(f...  13.2 us
    ppermute x2, waiting for transfers between devices, with_halo(): lax.ppermute(head, axis, [((i + 1) % count, i) for i in range(ends)])  12.5 us
    reduce_sum x6, other arithmetic, field_norm(): squares = rcv_sum(jnp.sum(field * field, axis=(0, 2, 3)))  12.4 us
  transfers between devices with their start and end apart: 12, of which 12 were waited for; matrix products, arithmetic and copies ran while one was open for 0% of the time, Pallas kernels for 0%

profile of v1, /device:TPU:1, one launch (start us, length us, event | category | flops | bytes accessed | tf_op | source)
XLA Modules:
  0.0 325.4 jit_solution(11585495343630055695)
XLA Ops:
  0.8 5.5 %fusion = bf16[2,2,1,4,20480]{4,3,1,0,2:T(4,128)(2,1)S(1)} fusion(bf16[1,256,20480]{2,1,0:T(8,128)(2,1)} %param.28, bf16[256,1,4,2]{0,2,3,1:T(4,128)(2,1)S(1)} %get-tuple-element.149, bf16[256,1,4,2]{0,2,3,1:T(4,128)(2,1)S(1)} %get-tuple-element.148), kind=kOutput, calls=%fused_computation.1 | convolution fusion | flops 168116224 | bytes 11149312 | tf_op jit(solution)/shard_map/snr,ncgf->cfsgr/dot_general | solution.py:175
  8.3 11.5 %all-to-all-start = ((bf16[2,2,1,128,640]{4,1,0,2,3:T(2,128)(2,1)}), bf16[2,2,1,128,640]{4,1,0,2,3:T(2,128)(2,1)S(1)}, u32[]{:S(2)}, u32[]{:S(2)}) async-start(bf16[2,2,1,128,640]{4,1,0,2,3:T(2,128)(2,1)} %copy.14), calls=%async_computation | async-start | bytes 1310720 | tf_op jit(solution)/shard_map/all_to_all | solution.py:181
  19.8 14.8 %all-to-all-done = bf16[2,2,1,128,640]{4,1,0,2,3:T(2,128)(2,1)S(1)} async-done(((bf16[2,2,1,128,640]{4,1,0,2,3:T(2,128)(2,1)}), bf16[2,2,1,128,640]{4,1,0,2,3:T(2,128)(2,1)S(1)}, u32[]{:S(2)}, u32[]{:S(2)}) %all-to-all-start) | async-done | bytes 655392 | tf_op jit(solution)/shard_map/all_to_all | solution.py:181
  35.5 4.8 %all-to-all-start.1 = ((f32[32,1,2]{2,1,0:T(1,128)}), f32[32,1,2]{2,1,0:T(1,128)S(1)}, u32[]{:S(2)}, u32[]{:S(2)}) async-start(f32[32,1,2]{2,1,0:T(1,128)} %broadcast_in_dim.12), calls=%async_computation.1 | async-start | bytes 32768 | tf_op jit(solution)/shard_map/all_to_all | solution.py:57
  41.6 5.7 %all-to-all-done.1 = f32[32,1,2]{2,1,0:T(1,128)S(1)} async-done(((f32[32,1,2]{2,1,0:T(1,128)}), f32[32,1,2]{2,1,0:T(1,128)S(1)}, u32[]{:S(2)}, u32[]{:S(2)}) %all-to-all-start.1) | async-done | bytes 288 | tf_op jit(solution)/shard_map/all_to_all | solution.py:57
  48.4 14.5 %shard_map.89 = f32[2,2,128,1920]{3,2,1,0:T(8,128)} custom-call(s32[110]{0:T(128)} %reshape.464.cols_ref, s32[10]{0:T(128)} %reshape.465.counts_ref, bf16[2,2,128,640]{3,2,1,0:T(8,128)(2,1)} %fusion.22.u_ref, bf16[2,5,11,2,128,128]{5,4,3,2,1,0:T(8,128)(2,1)} %a_ref.9), custom_call_target="tpu_custom_call" | custom-call | tf_op jit(solution)/shard_map/pallas_call | solution.py:157
  66.7 2.5 collective-permute-start.1
  69.2 12.0 %collective-permute-done = f32[2,2,128,640]{3,2,1,0:T(8,128)S(1)} collective-permute-done((f32[2,2,128,640]{3,2,1,0:T(8,128)S(1)}, f32[2,2,128,640]{3,2,1,0:T(8,128)S(1)}, u32[]{:S(2)}, u32[]{:S(2)}) %collective-permute-start) | collective-permute-done | bytes 1310752 | tf_op jit(solution)/shard_map/ppermute | solution.py:36
  81.3 4.4 %collective-permute-done.1 = f32[2,2,128,640]{3,2,1,0:T(8,128)S(1)} collective-permute-done((f32[2,2,128,640]{3,2,1,0:T(8,128)S(1)}, f32[2,2,128,640]{3,2,1,0:T(8,128)S(1)}, u32[]{:S(2)}, u32[]{:S(2)}) %collective-permute-start.1) | collective-permute-done | bytes 1310752 | tf_op jit(solution)/shard_map/ppermute | solution.py:36
  87.6 17.5 %all_to_all.45 = f32[32,1,2]{2,1,0:T(1,128)S(1)} all-to-all(f32[32,1,2]{2,1,0:T(1,128)S(1)} %broadcast_in_dim.13), channel_id=1, replica_groups=mesh['freq'=4,'rcv'=32] {'rcv'}, dimensions={0} | all-to-all | bytes 512 | tf_op jit(solution)/shard_map/all_to_all | solution.py:57
  105.3 2.6 collective-permute-start.3
  107.9 3.0 collective-permute-start.2
  110.9 6.3 %collective-permute-done.3 = bf16[2,2,128,640]{3,2,1,0:T(8,128)(2,1)S(1)} collective-permute-done((bf16[2,2,128,640]{3,2,1,0:T(8,128)(2,1)S(1)}, bf16[2,2,128,640]{3,2,1,0:T(8,128)(2,1)S(1)}, u32[]{:S(2)}, u32[]{:S(2)}) %collective-permute-start.3) | collective-permute-done | bytes 655392 | tf_op jit(solution)/shard_map/ppermute | solution.py:26
  119.9 15.2 %shard_map.90 = f32[2,2,128,640]{3,2,1,0:T(8,128)} custom-call(s32[110]{0:T(128)} %reshape.464.cols_ref, s32[10]{0:T(128)} %reshape.465.counts_ref, bf16[2,2,128,1920]{3,2,1,0:T(8,128)(2,1)} %pad_maximum_fusion.x_ref, bf16[2,5,11,2,128,128]{5,4,3,2,1,0:T(8,128)(2,1)} %a_ref.9), custom_call_target="tpu_custom_call" | custom-call | tf_op jit(solution)/shard_map/pallas_call | solution.py:132
  136.9 16.7 %all_to_all.46 = f32[32,1,2]{2,1,0:T(1,128)S(1)} all-to-all(f32[32,1,2]{2,1,0:T(1,128)S(1)} %broadcast_in_dim.14), channel_id=1, replica_groups=mesh['freq'=4,'rcv'=32] {'rcv'}, dimensions={0} | all-to-all | bytes 512 | tf_op jit(solution)/shard_map/all_to_all | solution.py:57
  154.7 14.5 %shard_map.91 = f32[2,2,128,1920]{3,2,1,0:T(8,128)} custom-call(s32[110]{0:T(128)} %reshape.464.cols_ref, s32[10]{0:T(128)} %reshape.465.counts_ref, bf16[2,2,128,640]{3,2,1,0:T(8,128)(2,1)} %fusion.23.u_ref, bf16[2,5,11,2,128,128]{5,4,3,2,1,0:T(8,128)(2,1)} %a_ref.9), custom_call_target="tpu_custom_call" | custom-call | tf_op jit(solution)/shard_map/pallas_call | solution.py:157
  173.0 2.5 collective-permute-start.5
  175.5 12.0 %collective-permute-done.4 = f32[2,2,128,640]{3,2,1,0:T(8,128)S(1)} collective-permute-done((f32[2,2,128,640]{3,2,1,0:T(8,128)S(1)}, f32[2,2,128,640]{3,2,1,0:T(8,128)S(1)}, u32[]{:S(2)}, u32[]{:S(2)}) %collective-permute-start.4) | collective-permute-done | bytes 1310752 | tf_op jit(solution)/shard_map/ppermute | solution.py:36
  187.5 4.4 %collective-permute-done.5 = f32[2,2,128,640]{3,2,1,0:T(8,128)S(1)} collective-permute-done((f32[2,2,128,640]{3,2,1,0:T(8,128)S(1)}, f32[2,2,128,640]{3,2,1,0:T(8,128)S(1)}, u32[]{:S(2)}, u32[]{:S(2)}) %collective-permute-start.5) | collective-permute-done | bytes 1310752 | tf_op jit(solution)/shard_map/ppermute | solution.py:36
  194.3 17.5 %all_to_all.47 = f32[32,1,2]{2,1,0:T(1,128)S(1)} all-to-all(f32[32,1,2]{2,1,0:T(1,128)S(1)} %broadcast_in_dim.15), channel_id=1, replica_groups=mesh['freq'=4,'rcv'=32] {'rcv'}, dimensions={0} | all-to-all | bytes 512 | tf_op jit(solution)/shard_map/all_to_all | solution.py:57
  212.0 2.6 collective-permute-start.7
  214.6 3.2 collective-permute-start.6
  217.8 6.1 %collective-permute-done.7 = bf16[2,2,128,640]{3,2,1,0:T(8,128)(2,1)S(1)} collective-permute-done((bf16[2,2,128,640]{3,2,1,0:T(8,128)(2,1)S(1)}, bf16[2,2,128,640]{3,2,1,0:T(8,128)(2,1)S(1)}, u32[]{:S(2)}, u32[]{:S(2)}) %collective-permute-start.7) | collective-permute-done | bytes 655392 | tf_op jit(solution)/shard_map/ppermute | solution.py:26
  226.8 15.2 %shard_map.92 = f32[2,2,128,640]{3,2,1,0:T(8,128)} custom-call(s32[110]{0:T(128)} %reshape.464.cols_ref, s32[10]{0:T(128)} %reshape.465.counts_ref, bf16[2,2,128,1920]{3,2,1,0:T(8,128)(2,1)} %pad_maximum_fusion.1.x_ref, bf16[2,5,11,2,128,128]{5,4,3,2,1,0:T(8,128)(2,1)} %a_ref.9), custom_call_target="tpu_custom_call" | custom-call | tf_op jit(solution)/shard_map/pallas_call | solution.py:132
  242.0 3.1 multiply_reduce_fusion.1
  245.1 16.7 %all_to_all.48 = f32[32,1,2]{2,1,0:T(1,128)S(1)} all-to-all(f32[32,1,2]{2,1,0:T(1,128)S(1)} %broadcast_in_dim.16), channel_id=1, replica_groups=mesh['freq'=4,'rcv'=32] {'rcv'}, dimensions={0} | all-to-all | bytes 512 | tf_op jit(solution)/shard_map/all_to_all | solution.py:57
  264.2 14.5 %shard_map.93 = f32[2,2,128,1920]{3,2,1,0:T(8,128)} custom-call(s32[110]{0:T(128)} %reshape.464.cols_ref, s32[10]{0:T(128)} %reshape.465.counts_ref, bf16[2,2,128,640]{3,2,1,0:T(8,128)(2,1)} %fusion.11.u_ref, bf16[2,5,11,2,128,128]{5,4,3,2,1,0:T(8,128)(2,1)} %a_ref.9), custom_call_target="tpu_custom_call" | custom-call | tf_op jit(solution)/shard_map/pallas_call | solution.py:157
  285.1 12.0 %collective-permute-done.8 = f32[2,2,128,640]{3,2,1,0:T(8,128)S(1)} collective-permute-done((f32[2,2,128,640]{3,2,1,0:T(8,128)S(1)}, f32[2,2,128,640]{3,2,1,0:T(8,128)S(1)}, u32[]{:S(2)}, u32[]{:S(2)}) %collective-permute-start.8) | collective-permute-done | bytes 1310752 | tf_op jit(solution)/shard_map/ppermute | solution.py:36
  297.2 4.4 %collective-permute-done.9 = f32[2,2,128,640]{3,2,1,0:T(8,128)S(1)} collective-permute-done((f32[2,2,128,640]{3,2,1,0:T(8,128)S(1)}, f32[2,2,128,640]{3,2,1,0:T(8,128)S(1)}, u32[]{:S(2)}, u32[]{:S(2)}) %collective-permute-start.9) | collective-permute-done | bytes 1310752 | tf_op jit(solution)/shard_map/ppermute | solution.py:36
  301.6 2.9 multiply_reduce_fusion
  304.5 17.5 %all_to_all.49 = f32[32,1,2]{2,1,0:T(1,128)S(1)} all-to-all(f32[32,1,2]{2,1,0:T(1,128)S(1)} %broadcast_in_dim.17), channel_id=1, replica_groups=mesh['freq'=4,'rcv'=32] {'rcv'}, dimensions={0} | all-to-all | bytes 512 | tf_op jit(solution)/shard_map/all_to_all | solution.py:57
  322.1 3.3 %divide_multiply_fusion = (f32[2,2,128,640]{3,2,1,0:T(8,128)}, f32[2,2,128,640]{3,2,1,0:T(8,128)}) fusion(f32[2,2,128,640]{3,2,1,0:T(8,128)} %get-tuple-element.129, f32[2]{0:T(128)S(1)} %get-tuple-element.144, f32[2]{0:T(128)S(1)} %get-tuple-element.122, f32[2]{0:T(128)S(1)} %get-tuple-element.147, f32[2,2,128,640]{3,2,1,0:T(8,128)S(1)} %get-tuple-element.133, ...), kind=kLoop, calls=%fused_computation.19 | loop fusion | flops 2949120 | bytes 6553656 | tf_op jit(solution)/shard_map/mul | solution.py:230
  (56 shorter events, 35.1 us)
Async XLA Ops:
  6.7 13.0 %copy-start.2 = (s32[2,5,11]{2,0,1:T(2,128)S(1)}, s32[2,5,11]{2,0,1:T(2,128)}, u32[]{:S(2)}) copy-start(s32[2,5,11]{2,0,1:T(2,128)} %param.30) | copy-start | bytes 1324
  8.3 32.0 %copy-start.3 = (s32[2,5]{1,0:T(2,128)S(1)}, s32[2,5]{1,0:T(2,128)}, u32[]{:S(2)}) copy-start(s32[2,5]{1,0:T(2,128)} %param.31) | copy-start | bytes 124
  8.3 26.4 %all-to-all-start = ((bf16[2,2,1,128,640]{4,1,0,2,3:T(2,128)(2,1)}), bf16[2,2,1,128,640]{4,1,0,2,3:T(2,128)(2,1)S(1)}, u32[]{:S(2)}, u32[]{:S(2)}) async-start(bf16[2,2,1,128,640]{4,1,0,2,3:T(2,128)(2,1)} %copy.14), calls=%async_computation | async-start | bytes 1310720 | tf_op jit(solution)/shard_map/all_to_all | solution.py:181
  35.5 11.8 %all-to-all-start.1 = ((f32[32,1,2]{2,1,0:T(1,128)}), f32[32,1,2]{2,1,0:T(1,128)S(1)}, u32[]{:S(2)}, u32[]{:S(2)}) async-start(f32[32,1,2]{2,1,0:T(1,128)} %broadcast_in_dim.12), calls=%async_computation.1 | async-start | bytes 32768 | tf_op jit(solution)/shard_map/all_to_all | solution.py:57
  64.8 16.5 %collective-permute-start = (f32[2,2,128,640]{3,2,1,0:T(8,128)S(1)}, f32[2,2,128,640]{3,2,1,0:T(8,128)S(1)}, u32[]{:S(2)}, u32[]{:S(2)}) collective-permute-start(f32[2,2,128,640]{3,2,1,0:T(8,128)S(1)} %get-tuple-element.142), channel_id=1, source_target_pairs={{0,1},{1,2},{2,3},{3,4},{4,5},{5,6},{6,7},{7,8},{8,9},{9,10},{10,1... | collective-permute-start | bytes 3932168 | tf_op jit(solution)/shard_map/ppermute | solution.py:36
  66.7 18.9 %collective-permute-start.1 = (f32[2,2,128,640]{3,2,1,0:T(8,128)S(1)}, f32[2,2,128,640]{3,2,1,0:T(8,128)S(1)}, u32[]{:S(2)}, u32[]{:S(2)}) collective-permute-start(f32[2,2,128,640]{3,2,1,0:T(8,128)S(1)} %get-tuple-element.143), channel_id=1, source_target_pairs={{1,0},{2,1},{3,2},{4,3},{5,4},{6,5},{7,6},{8,7},{9,8},{10,9},{11,1... | collective-permute-start | bytes 3932168 | tf_op jit(solution)/shard_map/ppermute | solution.py:36
  105.3 11.9 %collective-permute-start.3 = (bf16[2,2,128,640]{3,2,1,0:T(8,128)(2,1)S(1)}, bf16[2,2,128,640]{3,2,1,0:T(8,128)(2,1)S(1)}, u32[]{:S(2)}, u32[]{:S(2)}) collective-permute-start(bf16[2,2,128,640]{3,2,1,0:T(8,128)(2,1)S(1)} %fusion.24), channel_id=1, source_target_pairs={{1,0},{2,1},{3,2},{4,3},{5,4},{6,5},{7,6},{8,7},{9,8},{10,9},{11,1... | collective-permute-start | bytes 1966088 | tf_op jit(solution)/shard_map/ppermute | solution.py:26
  107.9 10.5 %collective-permute-start.2 = (bf16[2,2,128,640]{3,2,1,0:T(8,128)(2,1)S(1)}, bf16[2,2,128,640]{3,2,1,0:T(8,128)(2,1)S(1)}, u32[]{:S(2)}, u32[]{:S(2)}) collective-permute-start(bf16[2,2,128,640]{3,2,1,0:T(8,128)(2,1)S(1)} %fusion.24), channel_id=1, source_target_pairs={{0,1},{1,2},{2,3},{3,4},{4,5},{5,6},{6,7},{7,8},{8,9},{9,10},{10,1... | collective-permute-start | bytes 1966088 | tf_op jit(solution)/shard_map/ppermute | solution.py:24
  136.9 32.3 %copy-start = (f32[2,2,128,640]{3,2,1,0:T(8,128)}, f32[2,2,128,640]{3,2,1,0:T(8,128)S(1)}, u32[]{:S(2)}) copy-start(f32[2,2,128,640]{3,2,1,0:T(8,128)S(1)} %get-tuple-element.135) | copy-start | bytes 3932164
  171.1 16.5 %collective-permute-start.4 = (f32[2,2,128,640]{3,2,1,0:T(8,128)S(1)}, f32[2,2,128,640]{3,2,1,0:T(8,128)S(1)}, u32[]{:S(2)}, u32[]{:S(2)}) collective-permute-start(f32[2,2,128,640]{3,2,1,0:T(8,128)S(1)} %get-tuple-element.140), channel_id=1, source_target_pairs={{0,1},{1,2},{2,3},{3,4},{4,5},{5,6},{6,7},{7,8},{8,9},{9,10},{10,1... | collective-permute-start | bytes 3932168 | tf_op jit(solution)/shard_map/ppermute | solution.py:36
  173.0 18.9 %collective-permute-start.5 = (f32[2,2,128,640]{3,2,1,0:T(8,128)S(1)}, f32[2,2,128,640]{3,2,1,0:T(8,128)S(1)}, u32[]{:S(2)}, u32[]{:S(2)}) collective-permute-start(f32[2,2,128,640]{3,2,1,0:T(8,128)S(1)} %get-tuple-element.141), channel_id=1, source_target_pairs={{1,0},{2,1},{3,2},{4,3},{5,4},{6,5},{7,6},{8,7},{9,8},{10,9},{11,1... | collective-permute-start | bytes 3932168 | tf_op jit(solution)/shard_map/ppermute | solution.py:36
  212.0 11.9 %collective-permute-start.7 = (bf16[2,2,128,640]{3,2,1,0:T(8,128)(2,1)S(1)}, bf16[2,2,128,640]{3,2,1,0:T(8,128)(2,1)S(1)}, u32[]{:S(2)}, u32[]{:S(2)}) collective-permute-start(bf16[2,2,128,640]{3,2,1,0:T(8,128)(2,1)S(1)} %fusion.25), channel_id=1, source_target_pairs={{1,0},{2,1},{3,2},{4,3},{5,4},{6,5},{7,6},{8,7},{9,8},{10,9},{11,1... | collective-permute-start | bytes 1966088 | tf_op jit(solution)/shard_map/ppermute | solution.py:26
  214.6 10.7 %collective-permute-start.6 = (bf16[2,2,128,640]{3,2,1,0:T(8,128)(2,1)S(1)}, bf16[2,2,128,640]{3,2,1,0:T(8,128)(2,1)S(1)}, u32[]{:S(2)}, u32[]{:S(2)}) collective-permute-start(bf16[2,2,128,640]{3,2,1,0:T(8,128)(2,1)S(1)} %fusion.25), channel_id=1, source_target_pairs={{0,1},{1,2},{2,3},{3,4},{4,5},{5,6},{6,7},{7,8},{8,9},{9,10},{10,1... | collective-permute-start | bytes 1966088 | tf_op jit(solution)/shard_map/ppermute | solution.py:24
  278.7 22.9 %copy-start.1 = (f32[2,2,128,640]{3,2,1,0:T(8,128)S(1)}, f32[2,2,128,640]{3,2,1,0:T(8,128)}, u32[]{:S(2)}) copy-start(f32[2,2,128,640]{3,2,1,0:T(8,128)} %get-tuple-element.131) | copy-start | bytes 3932164
  280.7 16.5 %collective-permute-start.8 = (f32[2,2,128,640]{3,2,1,0:T(8,128)S(1)}, f32[2,2,128,640]{3,2,1,0:T(8,128)S(1)}, u32[]{:S(2)}, u32[]{:S(2)}) collective-permute-start(f32[2,2,128,640]{3,2,1,0:T(8,128)S(1)} %get-tuple-element.138), channel_id=1, source_target_pairs={{0,1},{1,2},{2,3},{3,4},{4,5},{5,6},{6,7},{7,8},{8,9},{9,10},{10,1... | collective-permute-start | bytes 3932168 | tf_op jit(solution)/shard_map/ppermute | solution.py:36
  282.6 18.9 %collective-permute-start.9 = (f32[2,2,128,640]{3,2,1,0:T(8,128)S(1)}, f32[2,2,128,640]{3,2,1,0:T(8,128)S(1)}, u32[]{:S(2)}, u32[]{:S(2)}) collective-permute-start(f32[2,2,128,640]{3,2,1,0:T(8,128)S(1)} %get-tuple-element.139), channel_id=1, source_target_pairs={{1,0},{2,1},{3,2},{4,3},{5,4},{6,5},{7,6},{8,7},{9,8},{10,9},{11,1... | collective-permute-start | bytes 3932168 | tf_op jit(solution)/shard_map/ppermute | solution.py:36

commit v2 on v1

--- a/solution.py
+++ b/solution.py
@@ -63,37 +63,35 @@
     return jnp.sqrt(squares + EPSILON)[None, :, None, None]
 
 
-def _forward_kernel(cols_ref, counts_ref, x_ref, a_ref, o_ref):
+def _forward_kernel(cols_ref, counts_ref, x_ref, a_ref, o_ref, picked_ref):
     freq = pl.program_id(0)
     row = pl.program_id(1)
     rows = pl.num_programs(1)
-    slots, _, block, _ = a_ref.shape
+    _, block, width = a_ref.shape
+    slots = width // block
     sources = o_ref.shape[1]
     index = freq * rows + row
     count = counts_ref[index]
-    o_ref[...] = jnp.zeros(o_ref.shape, o_ref.dtype)
+    for slot in range(slots):
+        start = pl.multiple_of(cols_ref[index * slots + slot] * block, block)
+        taken = x_ref[:, :, pl.ds(start, block)]
+        picked_ref[:, :, slot * block : (slot + 1) * block] = jnp.where(
+            slot < count, taken, jnp.zeros_like(taken)
+        )
+    picked = picked_ref[...].reshape(2 * sources, width)
     contract = (((1,), (1,)), ((), ()))
-    for slot in range(slots):
-
-        @pl.when(slot < count)
-        def _():
-            start = pl.multiple_of(cols_ref[index * slots + slot] * block, block)
-            picked = x_ref[:, :, pl.ds(start, block)].reshape(2 * sources, block)
-            by_real = lax.dot_general(
-                picked, a_ref[slot, 0], contract, preferred_element_type=jnp.float32
-            )
-            by_imag = lax.dot_general(
-                picked, a_ref[slot, 1], contract, preferred_element_type=jnp.float32
-            )
-            o_ref[0] += by_real[:sources] - by_imag[sources:]
-            o_ref[1] += by_imag[:sources] + by_real[sources:]
+    by_real = lax.dot_general(picked, a_ref[0], contract, preferred_element_type=jnp.float32)
+    by_imag = lax.dot_general(picked, a_ref[1], contract, preferred_element_type=jnp.float32)
+    o_ref[0] = by_real[:sources] - by_imag[sources:]
+    o_ref[1] = by_imag[:sources] + by_real[sources:]
 
 
 def _adjoint_kernel(cols_ref, counts_ref, u_ref, a_ref, o_ref):
     freq = pl.program_id(0)
     row = pl.program_id(1)
     rows = pl.num_programs(1)
-    slots, _, block, _ = a_ref.shape
+    _, block, width = a_ref.shape
+    slots = width // block
     sources = u_ref.shape[1]
     index = freq * rows + row
     count = counts_ref[index]
@@ -103,31 +101,32 @@
         o_ref[...] = jnp.zeros(o_ref.shape, o_ref.dtype)
 
     field = u_ref[...].reshape(2 * sources, block)
+    by_real = jnp.dot(field, a_ref[0], preferred_element_type=jnp.float32)
+    by_imag = jnp.dot(field, a_ref[1], preferred_element_type=jnp.float32)
+    real_part = by_real[:sources] + by_imag[sources:]
+    imaginary = by_real[sources:] - by_imag[:sources]
     for slot in range(slots):
 
         @pl.when(slot < count)
         def _():
             start = pl.multiple_of(cols_ref[index * slots + slot] * block, block)
-            by_real = jnp.dot(field, a_ref[slot, 0], preferred_element_type=jnp.float32)
-            by_imag = jnp.dot(field, a_ref[slot, 1], preferred_element_type=jnp.float32)
-            o_ref[0, :, pl.ds(start, block)] += by_real[:sources] + by_imag[sources:]
-            o_ref[1, :, pl.ds(start, block)] += by_real[sources:] - by_imag[:sources]
-
-
-def apply_forward(extended, down_blocks, cols, counts):
-    local_freqs, local_blocks, slot_count, _, block_size, _ = down_blocks.shape
+            lanes = slice(slot * block, (slot + 1) * block)
+            o_ref[0, :, pl.ds(start, block)] += real_part[:, lanes]
+            o_ref[1, :, pl.ds(start, block)] += imaginary[:, lanes]
+
+
+def apply_forward(extended, stacked, cols, counts):
+    local_freqs, local_blocks, _, block_size, width = stacked.shape
     _, _, sources, span = extended.shape
     grid_spec = pltpu.PrefetchScalarGridSpec(
         num_scalar_prefetch=2,
         grid=(local_freqs, local_blocks),
         in_specs=[
             pl.BlockSpec((2, None, sources, span), lambda f, r, c, n: (0, f, 0, 0)),
-            pl.BlockSpec(
-                (None, None, slot_count, 2, block_size, block_size),
-                lambda f, r, c, n: (f, r, 0, 0, 0, 0),
-            ),
+            pl.BlockSpec((None, None, 2, block_size, width), lambda f, r, c, n: (f, r, 0, 0, 0)),
         ],
         out_specs=pl.BlockSpec((2, None, sources, block_size), lambda f, r, c, n: (0, f, 0, r)),
+        scratch_shapes=[pltpu.VMEM((2, sources, width), jnp.bfloat16)],
     )
     return pl.pallas_call(
         _forward_kernel,
@@ -136,21 +135,18 @@
             (2, local_freqs, sources, local_blocks * block_size), jnp.float32
         ),
         compiler_params=pltpu.CompilerParams(dimension_semantics=("arbitrary", "arbitrary")),
-    )(cols, counts, extended, down_blocks)
-
-
-def apply_adjoint(rounded, down_blocks, cols, counts, span):
-    local_freqs, local_blocks, slot_count, _, block_size, _ = down_blocks.shape
+    )(cols, counts, extended, stacked)
+
+
+def apply_adjoint(rounded, stacked, cols, counts, span):
+    local_freqs, local_blocks, _, block_size, width = stacked.shape
     sources = rounded.shape[2]
     grid_spec = pltpu.PrefetchScalarGridSpec(
         num_scalar_prefetch=2,
         grid=(local_freqs, local_blocks),
         in_specs=[
             pl.BlockSpec((2, None, sources, block_size), lambda f, r, c, n: (0, f, 0, r)),
-            pl.BlockSpec(
-                (None, None, slot_count, 2, block_size, block_size),
-                lambda f, r, c, n: (f, r, 0, 0, 0, 0),
-            ),
+            pl.BlockSpec((None, None, 2, block_size, width), lambda f, r, c, n: (f, r, 0, 0, 0)),
         ],
         out_specs=pl.BlockSpec((2, None, sources, span), lambda f, r, c, n: (0, f, 0, 0)),
     )
@@ -159,7 +155,7 @@
         grid_spec=grid_spec,
         out_shape=jax.ShapeDtypeStruct((2, local_freqs, sources, span), jnp.float32),
         compiler_params=pltpu.CompilerParams(dimension_semantics=("arbitrary", "arbitrary")),
-    )(cols, counts, rounded, down_blocks)
+    )(cols, counts, rounded, stacked)
 
 
 def body(up_time, down_blocks, block_cols, block_counts):
@@ -185,10 +181,13 @@
         block_cols - position * local_blocks + reach_blocks, 0, span_blocks - 1
     ).reshape(-1)
     counts = jnp.clip(block_counts, 0, slot_count).reshape(-1)
+    stacked = jnp.transpose(down_blocks, (0, 1, 3, 4, 2, 5)).reshape(
+        local_freqs, local_blocks, 2, block_size, slot_count * block_size
+    )
 
     def adjoint(field):
         rounded = field.astype(jnp.bfloat16)
-        spread = apply_adjoint(rounded, down_blocks, columns, counts, span_blocks * block_size)
+        spread = apply_adjoint(rounded, stacked, columns, counts, span_blocks * block_size)
         lower_rim = spread[..., :rim_rows]
         middle = spread[..., rim_rows : rim_rows + local_rows]
         upper_rim = spread[..., rim_rows + local_rows :]
@@ -200,7 +199,7 @@
 
     def forward(field):
         extended = with_halo(field.astype(jnp.bfloat16), (("rcv", 3),), rim_rows)
-        return field + apply_forward(extended, down_blocks, columns, counts)
+        return field + apply_forward(extended, stacked, columns, counts)
 
     beta_norm = field_norm(right_side)
     left_vector = right_side / beta_norm

time: 328 us -> 320 us (0.976)
  local copies, waits for them, and re-layouts: 9.71 us -> 29.9 us
  Pallas kernels: 73.9 us -> 60.8 us
  blocking collectives: 85.9 us -> 73.6 us
  waiting for transfers between devices: 84.9 us -> 80.1 us
    all_to_all x5, blocking collectives: 85.9 us -> 73.6 us  [rcv_sum(): gathered = lax.all_to_all(spread, 'rcv', 0, 0, tiled=False)]
    reshape x0 -> x1, local copies, waits for them, and re-layouts: none -> 10.1 us  [body(): jnp.transpose(down_blocks, (0, 1, 3, 4, 2, 5))]
    unnamed x8 -> x9, local copies, waits for them, and re-layouts: 0.02 us -> 9.97 us
    pallas_call x2, Pallas kernels: 30.4 us -> 22.7 us  [apply_forward(): pl.pallas_call(_forward_kernel, grid_spec=grid_spec, out_shape=jax.ShapeD...]
    all_to_all x1, waiting for transfers between devices: 5.74 us -> 0.01 us  [rcv_sum(): gathered = lax.all_to_all(spread, 'rcv', 0, 0, tiled=False)]
    pallas_call x3, Pallas kernels: 43.5 us -> 38 us  [apply_adjoint(): pl.pallas_call(_adjoint_kernel, grid_spec=grid_spec, out_shape=jax.ShapeD...]
  transfers between devices with their start and end apart: 12 -> 12, of which waited for: 12 -> 11; matrix products, arithmetic and copies ran while one was open for 0% -> 7% of each run, Pallas kernels for 0% -> 0%
where the time goes in v2:
time: 320 us; the launch traced here: 318 us
  waiting for transfers between devices  80.1 us (25%)
  blocking collectives  73.6 us (23%)
  Pallas kernels  60.8 us (19%)
  starting transfers between devices  42.9 us (13%)
  local copies, waits for them, and re-layouts  29.9 us (9%)
  other arithmetic  24.1 us (8%)
  matrix products  5.47 us (2%)
    all_to_all x5, blocking collectives, rcv_sum(): gathered = lax.all_to_all(spread, 'rcv', 0, 0, tiled=False)  73.6 us
    ppermute x6, waiting for transfers between devices, from_behind(): lax.ppermute(value, axis, [(source, source + steps) for source in range(f...  51 us
    pallas_call x3, Pallas kernels, apply_adjoint(): pl.pallas_call(_adjoint_kernel, grid_spec=grid_spec, out_shape=jax.ShapeD...  38 us
    pallas_call x2, Pallas kernels, apply_forward(): pl.pallas_call(_forward_kernel, grid_spec=grid_spec, out_shape=jax.ShapeD...  22.7 us
    ppermute x6, starting transfers between devices, from_behind(): lax.ppermute(value, axis, [(source, source + steps) for source in range(f...  15.5 us
    all_to_all x1, waiting for transfers between devices, body(): lax.all_to_all(spectrum, ('freq', 'rcv'), split_axis=3, concat_axis=2, ti...  14.1 us
    ppermute x2, waiting for transfers between devices, with_halo(): lax.ppermute(head, axis, [((i + 1) % count, i) for i in range(ends)])  12.7 us
    reduce_sum x6, other arithmetic, field_norm(): squares = rcv_sum(jnp.sum(field * field, axis=(0, 2, 3)))  12.4 us
  transfers between devices with their start and end apart: 12, of which 11 were waited for; matrix products, arithmetic and copies ran while one was open for 7% of the time, Pallas kernels for 0%

profile of v2, /device:TPU:1, one launch (start us, length us, event | category | flops | bytes accessed | tf_op | source)
XLA Modules:
  0.0 317.8 jit_solution(15713522032884632326)
XLA Ops:
  0.8 5.5 %fusion = bf16[2,2,1,4,20480]{4,3,1,0,2:T(4,128)(2,1)S(1)} fusion(bf16[1,256,20480]{2,1,0:T(8,128)(2,1)} %param.28, bf16[256,1,4,2]{0,2,3,1:T(4,128)(2,1)S(1)} %get-tuple-element.149, bf16[256,1,4,2]{0,2,3,1:T(4,128)(2,1)S(1)} %get-tuple-element.148), kind=kOutput, calls=%fused_computation.1 | convolution fusion | flops 168116224 | bytes 11149312 | tf_op jit(solution)/shard_map/snr,ncgf->cfsgr/dot_general | solution.py:171
  8.3 11.5 %all-to-all-start = ((bf16[2,2,1,128,640]{4,1,0,2,3:T(2,128)(2,1)}), bf16[2,2,1,128,640]{4,1,0,2,3:T(2,128)(2,1)S(1)}, u32[]{:S(2)}, u32[]{:S(2)}) async-start(bf16[2,2,1,128,640]{4,1,0,2,3:T(2,128)(2,1)} %copy.33), calls=%async_computation | async-start | bytes 1310720 | tf_op jit(solution)/shard_map/all_to_all | solution.py:177
  20.5 14.1 %all-to-all-done = bf16[2,2,1,128,640]{4,1,0,2,3:T(2,128)(2,1)S(1)} async-done(((bf16[2,2,1,128,640]{4,1,0,2,3:T(2,128)(2,1)}), bf16[2,2,1,128,640]{4,1,0,2,3:T(2,128)(2,1)S(1)}, u32[]{:S(2)}, u32[]{:S(2)}) %all-to-all-start) | async-done | bytes 655392 | tf_op jit(solution)/shard_map/all_to_all | solution.py:177
  35.5 4.8 %all-to-all-start.1 = ((f32[32,1,2]{2,1,0:T(1,128)}), f32[32,1,2]{2,1,0:T(1,128)S(1)}, u32[]{:S(2)}, u32[]{:S(2)}) async-start(f32[32,1,2]{2,1,0:T(1,128)} %broadcast_in_dim.12), calls=%async_computation.1 | async-start | bytes 32768 | tf_op jit(solution)/shard_map/all_to_all | solution.py:57
  41.0 9.9 %copy.37 = bf16[2,5,11,2,128,128]{4,5,2,3,1,0:T(8,128)(2,1)} copy(bf16[2,5,11,2,128,128]{5,4,3,2,1,0:T(8,128)(2,1)} %param.29) | data formatting | bytes 14417920 | tf_op args[1]
  50.9 10.1 %copy.38.a_ref = bf16[2,5,2,128,1408]{4,3,2,1,0:T(8,128)(2,1)} copy(bf16[2,5,2,128,1408]{3,4,2,1,0:T(8,128)(2,1)} %bitcast.28) | data formatting | bytes 14417920 | tf_op jit(solution)/shard_map/reshape | solution.py:184
  62.2 12.7 %shard_map.89 = f32[2,2,128,1920]{3,2,1,0:T(8,128)} custom-call(s32[110]{0:T(128)} %reshape.467.cols_ref, s32[10]{0:T(128)} %reshape.468.counts_ref, bf16[2,2,128,640]{3,2,1,0:T(8,128)(2,1)} %fusion.22.u_ref, bf16[2,5,2,128,1408]{4,3,2,1,0:T(8,128)(2,1)} %copy.38.a_ref), custom_call_target="tpu_custom_call" | custom-call | tf_op jit(solution)/shard_map/pallas_call | solution.py:153
  76.8 3.8 %collective-permute-start = (f32[2,2,128,640]{3,2,1,0:T(8,128)S(1)}, f32[2,2,128,640]{3,2,1,0:T(8,128)S(1)}, u32[]{:S(2)}, u32[]{:S(2)}) collective-permute-start(f32[2,2,128,640]{3,2,1,0:T(8,128)S(1)} %get-tuple-element.142), channel_id=1, source_target_pairs={{0,1},{1,2},{2,3},{3,4},{4,5},{5,6},{6,7},{7,8},{8,9},{9,10},{10,1... | collective-permute-start | bytes 3932168 | tf_op jit(solution)/shard_map/ppermute | solution.py:36
  82.5 12.6 %collective-permute-done = f32[2,2,128,640]{3,2,1,0:T(8,128)S(1)} collective-permute-done((f32[2,2,128,640]{3,2,1,0:T(8,128)S(1)}, f32[2,2,128,640]{3,2,1,0:T(8,128)S(1)}, u32[]{:S(2)}, u32[]{:S(2)}) %collective-permute-start) | collective-permute-done | bytes 1310752 | tf_op jit(solution)/shard_map/ppermute | solution.py:36
  95.1 4.4 %collective-permute-done.1 = f32[2,2,128,640]{3,2,1,0:T(8,128)S(1)} collective-permute-done((f32[2,2,128,640]{3,2,1,0:T(8,128)S(1)}, f32[2,2,128,640]{3,2,1,0:T(8,128)S(1)}, u32[]{:S(2)}, u32[]{:S(2)}) %collective-permute-start.1) | collective-permute-done | bytes 1310752 | tf_op jit(solution)/shard_map/ppermute | solution.py:36
  101.4 15.4 %all_to_all.45 = f32[32,1,2]{2,1,0:T(1,128)S(1)} all-to-all(f32[32,1,2]{2,1,0:T(1,128)S(1)} %broadcast_in_dim.13), channel_id=1, replica_groups=mesh['freq'=4,'rcv'=32] {'rcv'}, dimensions={0} | all-to-all | bytes 512 | tf_op jit(solution)/shard_map/all_to_all | solution.py:57
  119.6 3.0 collective-permute-start.2
  122.6 6.3 %collective-permute-done.3 = bf16[2,2,128,640]{3,2,1,0:T(8,128)(2,1)S(1)} collective-permute-done((bf16[2,2,128,640]{3,2,1,0:T(8,128)(2,1)S(1)}, bf16[2,2,128,640]{3,2,1,0:T(8,128)(2,1)S(1)}, u32[]{:S(2)}, u32[]{:S(2)}) %collective-permute-start.3) | collective-permute-done | bytes 655392 | tf_op jit(solution)/shard_map/ppermute | solution.py:26
  131.7 11.4 %shard_map.90 = f32[2,2,128,640]{3,2,1,0:T(8,128)} custom-call(s32[110]{0:T(128)} %reshape.467.cols_ref, s32[10]{0:T(128)} %reshape.468.counts_ref, bf16[2,2,128,1920]{3,2,1,0:T(8,128)(2,1)} %pad_maximum_fusion.x_ref, bf16[2,5,2,128,1408]{4,3,2,1,0:T(8,128)(2,1)} %copy.38.a_ref), custom_call_target="tpu_custom_call" | custom-call | tf_op jit(solution)/shard_map/pallas_call | solution.py:131
  144.9 14.5 %all_to_all.46 = f32[32,1,2]{2,1,0:T(1,128)S(1)} all-to-all(f32[32,1,2]{2,1,0:T(1,128)S(1)} %broadcast_in_dim.14), channel_id=1, replica_groups=mesh['freq'=4,'rcv'=32] {'rcv'}, dimensions={0} | all-to-all | bytes 512 | tf_op jit(solution)/shard_map/all_to_all | solution.py:57
  160.4 12.7 %shard_map.91 = f32[2,2,128,1920]{3,2,1,0:T(8,128)} custom-call(s32[110]{0:T(128)} %reshape.467.cols_ref, s32[10]{0:T(128)} %reshape.468.counts_ref, bf16[2,2,128,640]{3,2,1,0:T(8,128)(2,1)} %fusion.23.u_ref, bf16[2,5,2,128,1408]{4,3,2,1,0:T(8,128)(2,1)} %copy.38.a_ref), custom_call_target="tpu_custom_call" | custom-call | tf_op jit(solution)/shard_map/pallas_call | solution.py:153
  175.0 3.0 collective-permute-start.4
  179.9 12.6 %collective-permute-done.4 = f32[2,2,128,640]{3,2,1,0:T(8,128)S(1)} collective-permute-done((f32[2,2,128,640]{3,2,1,0:T(8,128)S(1)}, f32[2,2,128,640]{3,2,1,0:T(8,128)S(1)}, u32[]{:S(2)}, u32[]{:S(2)}) %collective-permute-start.4) | collective-permute-done | bytes 1310752 | tf_op jit(solution)/shard_map/ppermute | solution.py:36
  192.5 4.4 %collective-permute-done.5 = f32[2,2,128,640]{3,2,1,0:T(8,128)S(1)} collective-permute-done((f32[2,2,128,640]{3,2,1,0:T(8,128)S(1)}, f32[2,2,128,640]{3,2,1,0:T(8,128)S(1)}, u32[]{:S(2)}, u32[]{:S(2)}) %collective-permute-start.5) | collective-permute-done | bytes 1310752 | tf_op jit(solution)/shard_map/ppermute | solution.py:36
  199.3 14.6 %all_to_all.47 = f32[32,1,2]{2,1,0:T(1,128)S(1)} all-to-all(f32[32,1,2]{2,1,0:T(1,128)S(1)} %broadcast_in_dim.15), channel_id=1, replica_groups=mesh['freq'=4,'rcv'=32] {'rcv'}, dimensions={0} | all-to-all | bytes 512 | tf_op jit(solution)/shard_map/all_to_all | solution.py:57
  216.8 3.0 collective-permute-start.6
  219.8 6.3 %collective-permute-done.7 = bf16[2,2,128,640]{3,2,1,0:T(8,128)(2,1)S(1)} collective-permute-done((bf16[2,2,128,640]{3,2,1,0:T(8,128)(2,1)S(1)}, bf16[2,2,128,640]{3,2,1,0:T(8,128)(2,1)S(1)}, u32[]{:S(2)}, u32[]{:S(2)}) %collective-permute-start.7) | collective-permute-done | bytes 655392 | tf_op jit(solution)/shard_map/ppermute | solution.py:26
  228.8 11.4 %shard_map.92 = f32[2,2,128,640]{3,2,1,0:T(8,128)} custom-call(s32[110]{0:T(128)} %reshape.467.cols_ref, s32[10]{0:T(128)} %reshape.468.counts_ref, bf16[2,2,128,1920]{3,2,1,0:T(8,128)(2,1)} %pad_maximum_fusion.1.x_ref, bf16[2,5,2,128,1408]{4,3,2,1,0:T(8,128)(2,1)} %copy.38.a_ref), custom_call_target="tpu_custom_call" | custom-call | tf_op jit(solution)/shard_map/pallas_call | solution.py:131
  240.2 3.1 multiply_reduce_fusion.1
  243.4 14.5 %all_to_all.48 = f32[32,1,2]{2,1,0:T(1,128)S(1)} all-to-all(f32[32,1,2]{2,1,0:T(1,128)S(1)} %broadcast_in_dim.16), channel_id=1, replica_groups=mesh['freq'=4,'rcv'=32] {'rcv'}, dimensions={0} | all-to-all | bytes 512 | tf_op jit(solution)/shard_map/all_to_all | solution.py:57
  260.2 12.7 %shard_map.93 = f32[2,2,128,1920]{3,2,1,0:T(8,128)} custom-call(s32[110]{0:T(128)} %reshape.467.cols_ref, s32[10]{0:T(128)} %reshape.468.counts_ref, bf16[2,2,128,640]{3,2,1,0:T(8,128)(2,1)} %fusion.11.u_ref, bf16[2,5,2,128,1408]{4,3,2,1,0:T(8,128)(2,1)} %copy.38.a_ref), custom_call_target="tpu_custom_call" | custom-call | tf_op jit(solution)/shard_map/pallas_call | solution.py:153
  274.9 3.0 collective-permute-start.8
  279.8 12.6 %collective-permute-done.8 = f32[2,2,128,640]{3,2,1,0:T(8,128)S(1)} collective-permute-done((f32[2,2,128,640]{3,2,1,0:T(8,128)S(1)}, f32[2,2,128,640]{3,2,1,0:T(8,128)S(1)}, u32[]{:S(2)}, u32[]{:S(2)}) %collective-permute-start.8) | collective-permute-done | bytes 1310752 | tf_op jit(solution)/shard_map/ppermute | solution.py:36
  292.4 4.4 %collective-permute-done.9 = f32[2,2,128,640]{3,2,1,0:T(8,128)S(1)} collective-permute-done((f32[2,2,128,640]{3,2,1,0:T(8,128)S(1)}, f32[2,2,128,640]{3,2,1,0:T(8,128)S(1)}, u32[]{:S(2)}, u32[]{:S(2)}) %collective-permute-start.9) | collective-permute-done | bytes 1310752 | tf_op jit(solution)/shard_map/ppermute | solution.py:36
  296.8 2.9 multiply_reduce_fusion
  299.8 14.6 %all_to_all.49 = f32[32,1,2]{2,1,0:T(1,128)S(1)} all-to-all(f32[32,1,2]{2,1,0:T(1,128)S(1)} %broadcast_in_dim.17), channel_id=1, replica_groups=mesh['freq'=4,'rcv'=32] {'rcv'}, dimensions={0} | all-to-all | bytes 512 | tf_op jit(solution)/shard_map/all_to_all | solution.py:57
  314.5 3.3 %divide_multiply_fusion = (f32[2,2,128,640]{3,2,1,0:T(8,128)}, f32[2,2,128,640]{3,2,1,0:T(8,128)}) fusion(f32[2,2,128,640]{3,2,1,0:T(8,128)} %get-tuple-element.129, f32[2]{0:T(128)S(1)} %get-tuple-element.144, f32[2]{0:T(128)S(1)} %get-tuple-element.122, f32[2]{0:T(128)S(1)} %get-tuple-element.147, f32[2,2,128,640]{3,2,1,0:T(8,128)S(1)} %get-tuple-element.133, ...), kind=kLoop, calls=%fused_computation.19 | loop fusion | flops 2949120 | bytes 6553656 | tf_op jit(solution)/shard_map/mul | solution.py:229
  (58 shorter events, 37.9 us)
Async XLA Ops:
  6.8 13.0 %copy-start.3 = (s32[2,5]{1,0:T(2,128)S(1)}, s32[2,5]{1,0:T(2,128)}, u32[]{:S(2)}) copy-start(s32[2,5]{1,0:T(2,128)} %param.31) | copy-start | bytes 124
  6.8 13.7 %copy-start.2 = (s32[2,5,11]{2,0,1:T(2,128)S(1)}, s32[2,5,11]{2,0,1:T(2,128)}, u32[]{:S(2)}) copy-start(s32[2,5,11]{2,0,1:T(2,128)} %param.30) | copy-start | bytes 1324
  8.3 26.4 %all-to-all-start = ((bf16[2,2,1,128,640]{4,1,0,2,3:T(2,128)(2,1)}), bf16[2,2,1,128,640]{4,1,0,2,3:T(2,128)(2,1)S(1)}, u32[]{:S(2)}, u32[]{:S(2)}) async-start(bf16[2,2,1,128,640]{4,1,0,2,3:T(2,128)(2,1)} %copy.33), calls=%async_computation | async-start | bytes 1310720 | tf_op jit(solution)/shard_map/all_to_all | solution.py:177
  35.5 25.5 %all-to-all-start.1 = ((f32[32,1,2]{2,1,0:T(1,128)}), f32[32,1,2]{2,1,0:T(1,128)S(1)}, u32[]{:S(2)}, u32[]{:S(2)}) async-start(f32[32,1,2]{2,1,0:T(1,128)} %broadcast_in_dim.12), calls=%async_computation.1 | async-start | bytes 32768 | tf_op jit(solution)/shard_map/all_to_all | solution.py:57
  76.8 18.3 %collective-permute-start = (f32[2,2,128,640]{3,2,1,0:T(8,128)S(1)}, f32[2,2,128,640]{3,2,1,0:T(8,128)S(1)}, u32[]{:S(2)}, u32[]{:S(2)}) collective-permute-start(f32[2,2,128,640]{3,2,1,0:T(8,128)S(1)} %get-tuple-element.142), channel_id=1, source_target_pairs={{0,1},{1,2},{2,3},{3,4},{4,5},{5,6},{6,7},{7,8},{8,9},{9,10},{10,1... | collective-permute-start | bytes 3932168 | tf_op jit(solution)/shard_map/ppermute | solution.py:36
  80.6 18.9 %collective-permute-start.1 = (f32[2,2,128,640]{3,2,1,0:T(8,128)S(1)}, f32[2,2,128,640]{3,2,1,0:T(8,128)S(1)}, u32[]{:S(2)}, u32[]{:S(2)}) collective-permute-start(f32[2,2,128,640]{3,2,1,0:T(8,128)S(1)} %get-tuple-element.143), channel_id=1, source_target_pairs={{1,0},{2,1},{3,2},{4,3},{5,4},{6,5},{7,6},{8,7},{9,8},{10,9},{11,1... | collective-permute-start | bytes 3932168 | tf_op jit(solution)/shard_map/ppermute | solution.py:36
  117.0 11.9 %collective-permute-start.3 = (bf16[2,2,128,640]{3,2,1,0:T(8,128)(2,1)S(1)}, bf16[2,2,128,640]{3,2,1,0:T(8,128)(2,1)S(1)}, u32[]{:S(2)}, u32[]{:S(2)}) collective-permute-start(bf16[2,2,128,640]{3,2,1,0:T(8,128)(2,1)S(1)} %fusion.24), channel_id=1, source_target_pairs={{1,0},{2,1},{3,2},{4,3},{5,4},{6,5},{7,6},{8,7},{9,8},{10,9},{11,1... | collective-permute-start | bytes 1966088 | tf_op jit(solution)/shard_map/ppermute | solution.py:26
  119.6 10.5 %collective-permute-start.2 = (bf16[2,2,128,640]{3,2,1,0:T(8,128)(2,1)S(1)}, bf16[2,2,128,640]{3,2,1,0:T(8,128)(2,1)S(1)}, u32[]{:S(2)}, u32[]{:S(2)}) collective-permute-start(bf16[2,2,128,640]{3,2,1,0:T(8,128)(2,1)S(1)} %fusion.24), channel_id=1, source_target_pairs={{0,1},{1,2},{2,3},{3,4},{4,5},{5,6},{6,7},{7,8},{8,9},{9,10},{10,1... | collective-permute-start | bytes 1966088 | tf_op jit(solution)/shard_map/ppermute | solution.py:24
  144.9 28.2 %copy-start = (f32[2,2,128,640]{3,2,1,0:T(8,128)}, f32[2,2,128,640]{3,2,1,0:T(8,128)S(1)}, u32[]{:S(2)}) copy-start(f32[2,2,128,640]{3,2,1,0:T(8,128)S(1)} %get-tuple-element.135) | copy-start | bytes 3932164
  175.0 17.5 %collective-permute-start.4 = (f32[2,2,128,640]{3,2,1,0:T(8,128)S(1)}, f32[2,2,128,640]{3,2,1,0:T(8,128)S(1)}, u32[]{:S(2)}, u32[]{:S(2)}) collective-permute-start(f32[2,2,128,640]{3,2,1,0:T(8,128)S(1)} %get-tuple-element.140), channel_id=1, source_target_pairs={{0,1},{1,2},{2,3},{3,4},{4,5},{5,6},{6,7},{7,8},{8,9},{9,10},{10,1... | collective-permute-start | bytes 3932168 | tf_op jit(solution)/shard_map/ppermute | solution.py:36
  178.0 18.9 %collective-permute-start.5 = (f32[2,2,128,640]{3,2,1,0:T(8,128)S(1)}, f32[2,2,128,640]{3,2,1,0:T(8,128)S(1)}, u32[]{:S(2)}, u32[]{:S(2)}) collective-permute-start(f32[2,2,128,640]{3,2,1,0:T(8,128)S(1)} %get-tuple-element.141), channel_id=1, source_target_pairs={{1,0},{2,1},{3,2},{4,3},{5,4},{6,5},{7,6},{8,7},{9,8},{10,9},{11,1... | collective-permute-start | bytes 3932168 | tf_op jit(solution)/shard_map/ppermute | solution.py:36
  214.2 11.9 %collective-permute-start.7 = (bf16[2,2,128,640]{3,2,1,0:T(8,128)(2,1)S(1)}, bf16[2,2,128,640]{3,2,1,0:T(8,128)(2,1)S(1)}, u32[]{:S(2)}, u32[]{:S(2)}) collective-permute-start(bf16[2,2,128,640]{3,2,1,0:T(8,128)(2,1)S(1)} %fusion.25), channel_id=1, source_target_pairs={{1,0},{2,1},{3,2},{4,3},{5,4},{6,5},{7,6},{8,7},{9,8},{10,9},{11,1... | collective-permute-start | bytes 1966088 | tf_op jit(solution)/shard_map/ppermute | solution.py:26
  216.8 10.5 %collective-permute-start.6 = (bf16[2,2,128,640]{3,2,1,0:T(8,128)(2,1)S(1)}, bf16[2,2,128,640]{3,2,1,0:T(8,128)(2,1)S(1)}, u32[]{:S(2)}, u32[]{:S(2)}) collective-permute-start(bf16[2,2,128,640]{3,2,1,0:T(8,128)(2,1)S(1)} %fusion.25), channel_id=1, source_target_pairs={{0,1},{1,2},{2,3},{3,4},{4,5},{5,6},{6,7},{7,8},{8,9},{9,10},{10,1... | collective-permute-start | bytes 1966088 | tf_op jit(solution)/shard_map/ppermute | solution.py:24
  272.9 23.9 %copy-start.1 = (f32[2,2,128,640]{3,2,1,0:T(8,128)S(1)}, f32[2,2,128,640]{3,2,1,0:T(8,128)}, u32[]{:S(2)}) copy-start(f32[2,2,128,640]{3,2,1,0:T(8,128)} %get-tuple-element.131) | copy-start | bytes 3932164
  274.9 17.5 %collective-permute-start.8 = (f32[2,2,128,640]{3,2,1,0:T(8,128)S(1)}, f32[2,2,128,640]{3,2,1,0:T(8,128)S(1)}, u32[]{:S(2)}, u32[]{:S(2)}) collective-permute-start(f32[2,2,128,640]{3,2,1,0:T(8,128)S(1)} %get-tuple-element.138), channel_id=1, source_target_pairs={{0,1},{1,2},{2,3},{3,4},{4,5},{5,6},{6,7},{7,8},{8,9},{9,10},{10,1... | collective-permute-start | bytes 3932168 | tf_op jit(solution)/shard_map/ppermute | solution.py:36
  277.9 18.9 %collective-permute-start.9 = (f32[2,2,128,640]{3,2,1,0:T(8,128)S(1)}, f32[2,2,128,640]{3,2,1,0:T(8,128)S(1)}, u32[]{:S(2)}, u32[]{:S(2)}) collective-permute-start(f32[2,2,128,640]{3,2,1,0:T(8,128)S(1)} %get-tuple-element.139), channel_id=1, source_target_pairs={{1,0},{2,1},{3,2},{4,3},{5,4},{6,5},{7,6},{8,7},{9,8},{10,9},{11,1... | collective-permute-start | bytes 3932168 | tf_op jit(solution)/shard_map/ppermute | solution.py:36

commit v3 on v2

--- a/solution.py
+++ b/solution.py
@@ -63,36 +63,68 @@
     return jnp.sqrt(squares + EPSILON)[None, :, None, None]
 
 
-def _forward_kernel(cols_ref, counts_ref, x_ref, a_ref, o_ref, picked_ref):
+def _stack_kernel(a_ref, m_ref):
+    slots, _, block, _ = a_ref.shape
+    for slot in range(slots):
+        real_part = a_ref[slot, 0]
+        imaginary = a_ref[slot, 1]
+        left = slice(2 * slot * block, (2 * slot + 1) * block)
+        right = slice((2 * slot + 1) * block, (2 * slot + 2) * block)
+        m_ref[:block, left] = real_part
+        m_ref[:block, right] = -imaginary
+        m_ref[block:, left] = imaginary
+        m_ref[block:, right] = real_part
+
+
+def stack_blocks(down_blocks):
+    local_freqs, local_blocks, slot_count, _, block_size, _ = down_blocks.shape
+    width = 2 * slot_count * block_size
+    return pl.pallas_call(
+        _stack_kernel,
+        grid=(local_freqs, local_blocks),
+        in_specs=[
+            pl.BlockSpec(
+                (None, None, slot_count, 2, block_size, block_size),
+                lambda f, r: (f, r, 0, 0, 0, 0),
+            )
+        ],
+        out_specs=pl.BlockSpec((None, None, 2 * block_size, width), lambda f, r: (f, r, 0, 0)),
+        out_shape=jax.ShapeDtypeStruct(
+            (local_freqs, local_blocks, 2 * block_size, width), jnp.bfloat16
+        ),
+    )(down_blocks)
+
+
+def _forward_kernel(cols_ref, counts_ref, x_ref, m_ref, o_ref, picked_ref):
     freq = pl.program_id(0)
     row = pl.program_id(1)
     rows = pl.num_programs(1)
-    _, block, width = a_ref.shape
-    slots = width // block
-    sources = o_ref.shape[1]
+    depth, width = m_ref.shape
+    block = depth // 2
+    slots = width // depth
     index = freq * rows + row
     count = counts_ref[index]
     for slot in range(slots):
         start = pl.multiple_of(cols_ref[index * slots + slot] * block, block)
-        taken = x_ref[:, :, pl.ds(start, block)]
-        picked_ref[:, :, slot * block : (slot + 1) * block] = jnp.where(
-            slot < count, taken, jnp.zeros_like(taken)
-        )
-    picked = picked_ref[...].reshape(2 * sources, width)
+        for part in range(2):
+            taken = x_ref[part, :, pl.ds(start, block)]
+            lanes = slice((2 * slot + part) * block, (2 * slot + part + 1) * block)
+            picked_ref[:, lanes] = jnp.where(slot < count, taken, jnp.zeros_like(taken))
     contract = (((1,), (1,)), ((), ()))
-    by_real = lax.dot_general(picked, a_ref[0], contract, preferred_element_type=jnp.float32)
-    by_imag = lax.dot_general(picked, a_ref[1], contract, preferred_element_type=jnp.float32)
-    o_ref[0] = by_real[:sources] - by_imag[sources:]
-    o_ref[1] = by_imag[:sources] + by_real[sources:]
-
-
-def _adjoint_kernel(cols_ref, counts_ref, u_ref, a_ref, o_ref):
+    product = lax.dot_general(
+        picked_ref[...], m_ref[...], contract, preferred_element_type=jnp.float32
+    )
+    o_ref[0] = product[:, :block]
+    o_ref[1] = product[:, block:]
+
+
+def _adjoint_kernel(cols_ref, counts_ref, u_ref, m_ref, o_ref):
     freq = pl.program_id(0)
     row = pl.program_id(1)
     rows = pl.num_programs(1)
-    _, block, width = a_ref.shape
-    slots = width // block
-    sources = u_ref.shape[1]
+    depth, width = m_ref.shape
+    block = depth // 2
+    slots = width // depth
     index = freq * rows + row
     count = counts_ref[index]
 
@@ -100,33 +132,31 @@
     def _():
         o_ref[...] = jnp.zeros(o_ref.shape, o_ref.dtype)
 
-    field = u_ref[...].reshape(2 * sources, block)
-    by_real = jnp.dot(field, a_ref[0], preferred_element_type=jnp.float32)
-    by_imag = jnp.dot(field, a_ref[1], preferred_element_type=jnp.float32)
-    real_part = by_real[:sources] + by_imag[sources:]
-    imaginary = by_real[sources:] - by_imag[:sources]
+    field = jnp.concatenate([u_ref[0], u_ref[1]], axis=1)
+    product = jnp.dot(field, m_ref[...], preferred_element_type=jnp.float32)
     for slot in range(slots):
 
         @pl.when(slot < count)
         def _():
             start = pl.multiple_of(cols_ref[index * slots + slot] * block, block)
-            lanes = slice(slot * block, (slot + 1) * block)
-            o_ref[0, :, pl.ds(start, block)] += real_part[:, lanes]
-            o_ref[1, :, pl.ds(start, block)] += imaginary[:, lanes]
+            for part in range(2):
+                lanes = slice((2 * slot + part) * block, (2 * slot + part + 1) * block)
+                o_ref[part, :, pl.ds(start, block)] += product[:, lanes]
 
 
 def apply_forward(extended, stacked, cols, counts):
-    local_freqs, local_blocks, _, block_size, width = stacked.shape
+    local_freqs, local_blocks, depth, width = stacked.shape
+    block_size = depth // 2
     _, _, sources, span = extended.shape
     grid_spec = pltpu.PrefetchScalarGridSpec(
         num_scalar_prefetch=2,
         grid=(local_freqs, local_blocks),
         in_specs=[
             pl.BlockSpec((2, None, sources, span), lambda f, r, c, n: (0, f, 0, 0)),
-            pl.BlockSpec((None, None, 2, block_size, width), lambda f, r, c, n: (f, r, 0, 0, 0)),
+            pl.BlockSpec((None, None, depth, width), lambda f, r, c, n: (f, r, 0, 0)),
         ],
         out_specs=pl.BlockSpec((2, None, sources, block_size), lambda f, r, c, n: (0, f, 0, r)),
-        scratch_shapes=[pltpu.VMEM((2, sources, width), jnp.bfloat16)],
+        scratch_shapes=[pltpu.VMEM((sources, width), jnp.bfloat16)],
     )
     return pl.pallas_call(
         _forward_kernel,
@@ -139,14 +169,15 @@
 
 
 def apply_adjoint(rounded, stacked, cols, counts, span):
-    local_freqs, local_blocks, _, block_size, width = stacked.shape
+    local_freqs, local_blocks, depth, width = stacked.shape
+    block_size = depth // 2
     sources = rounded.shape[2]
     grid_spec = pltpu.PrefetchScalarGridSpec(
         num_scalar_prefetch=2,
         grid=(local_freqs, local_blocks),
         in_specs=[
             pl.BlockSpec((2, None, sources, block_size), lambda f, r, c, n: (0, f, 0, r)),
-            pl.BlockSpec((None, None, 2, block_size, width), lambda f, r, c, n: (f, r, 0, 0, 0)),
+            pl.BlockSpec((None, None, depth, width), lambda f, r, c, n: (f, r, 0, 0)),
         ],
         out_specs=pl.BlockSpec((2, None, sources, span), lambda f, r, c, n: (0, f, 0, 0)),
     )
@@ -181,9 +212,7 @@
         block_cols - position * local_blocks + reach_blocks, 0, span_blocks - 1
     ).reshape(-1)
     counts = jnp.clip(block_counts, 0, slot_count).reshape(-1)
-    stacked = jnp.transpose(down_blocks, (0, 1, 3, 4, 2, 5)).reshape(
-        local_freqs, local_blocks, 2, block_size, slot_count * block_size
-    )
+    stacked = stack_blocks(down_blocks)
 
     def adjoint(field):
         rounded = field.astype(jnp.bfloat16)

time: 320 us -> 316 us (0.988)
  local copies, waits for them, and re-layouts: 29.9 us -> 9.76 us
  Pallas kernels: 60.8 us -> 76.2 us
    pallas_call x0 -> x1, Pallas kernels: none -> 10.7 us  [stack_blocks(): pl.pallas_call(_stack_kernel, grid=(local_freqs, local_blocks), in_specs=...]
    reshape x1 -> x0, local copies, waits for them, and re-layouts: 10.1 us -> none  [body(): jnp.transpose(down_blocks, (0, 1, 3, 4, 2, 5))]
    unnamed x9 -> x8, local copies, waits for them, and re-layouts: 9.97 us -> 0.02 us
    pallas_call x2, Pallas kernels: 22.7 us -> 26.9 us  [apply_forward(): pl.pallas_call(_forward_kernel, grid_spec=grid_spec, out_shape=jax.ShapeD...]
  transfers between devices with their start and end apart: 12 -> 12, of which waited for: 11 -> 11; matrix products, arithmetic and copies ran while one was open for 7% -> 0% of each run, Pallas kernels for 0% -> 3%
where the time goes in v3:
time: 316 us; the launch traced here: 314 us
  waiting for transfers between devices  80.6 us (26%)
  Pallas kernels  76.2 us (24%)
  blocking collectives  73.8 us (23%)
  starting transfers between devices  43.1 us (14%)
  other arithmetic  23.9 us (8%)
  local copies, waits for them, and re-layouts  9.76 us (3%)
  matrix products  5.45 us (2%)
    all_to_all x5, blocking collectives, rcv_sum(): gathered = lax.all_to_all(spread, 'rcv', 0, 0, tiled=False)  73.8 us
    ppermute x6, waiting for transfers between devices, from_behind(): lax.ppermute(value, axis, [(source, source + steps) for source in range(f...  51 us
    pallas_call x3, Pallas kernels, apply_adjoint(): pl.pallas_call(_adjoint_kernel, grid_spec=grid_spec, out_shape=jax.ShapeD...  38.6 us
    pallas_call x2, Pallas kernels, apply_forward(): pl.pallas_call(_forward_kernel, grid_spec=grid_spec, out_shape=jax.ShapeD...  26.9 us
    ppermute x6, starting transfers between devices, from_behind(): lax.ppermute(value, axis, [(source, source + steps) for source in range(f...  15.6 us
    all_to_all x1, waiting for transfers between devices, body(): lax.all_to_all(spectrum, ('freq', 'rcv'), split_axis=3, concat_axis=2, ti...  14.8 us
    ppermute x2, waiting for transfers between devices, with_halo(): lax.ppermute(head, axis, [((i + 1) % count, i) for i in range(ends)])  12.5 us
    reduce_sum x6, other arithmetic, field_norm(): squares = rcv_sum(jnp.sum(field * field, axis=(0, 2, 3)))  12.4 us
  transfers between devices with their start and end apart: 12, of which 11 were waited for; matrix products, arithmetic and copies ran while one was open for 0% of the time, Pallas kernels for 3%

profile of v3, /device:TPU:1, one launch (start us, length us, event | category | flops | bytes accessed | tf_op | source)
XLA Modules:
  0.0 313.8 jit_solution(2040818321656015238)
XLA Ops:
  0.8 5.5 %fusion = bf16[2,2,1,4,20480]{4,3,1,0,2:T(4,128)(2,1)S(1)} fusion(bf16[1,256,20480]{2,1,0:T(8,128)(2,1)} %param.28, bf16[256,1,4,2]{0,2,3,1:T(4,128)(2,1)S(1)} %get-tuple-element.149, bf16[256,1,4,2]{0,2,3,1:T(4,128)(2,1)S(1)} %get-tuple-element.148), kind=kOutput, calls=%fused_computation.1 | convolution fusion | flops 168116224 | bytes 11149312 | tf_op jit(solution)/shard_map/snr,ncgf->cfsgr/dot_general | solution.py:202
  8.3 11.5 %all-to-all-start = ((bf16[2,2,1,128,640]{4,1,0,2,3:T(2,128)(2,1)}), bf16[2,2,1,128,640]{4,1,0,2,3:T(2,128)(2,1)S(1)}, u32[]{:S(2)}, u32[]{:S(2)}) async-start(bf16[2,2,1,128,640]{4,1,0,2,3:T(2,128)(2,1)} %copy.14), calls=%async_computation | async-start | bytes 1310720 | tf_op jit(solution)/shard_map/all_to_all | solution.py:208
  19.8 14.8 %all-to-all-done = bf16[2,2,1,128,640]{4,1,0,2,3:T(2,128)(2,1)S(1)} async-done(((bf16[2,2,1,128,640]{4,1,0,2,3:T(2,128)(2,1)}), bf16[2,2,1,128,640]{4,1,0,2,3:T(2,128)(2,1)S(1)}, u32[]{:S(2)}, u32[]{:S(2)}) %all-to-all-start) | async-done | bytes 655392 | tf_op jit(solution)/shard_map/all_to_all | solution.py:208
  35.5 4.8 %all-to-all-start.1 = ((f32[32,1,2]{2,1,0:T(1,128)}), f32[32,1,2]{2,1,0:T(1,128)S(1)}, u32[]{:S(2)}, u32[]{:S(2)}) async-start(f32[32,1,2]{2,1,0:T(1,128)} %broadcast_in_dim.12), calls=%async_computation.1 | async-start | bytes 32768 | tf_op jit(solution)/shard_map/all_to_all | solution.py:57
  41.6 10.7 %shard_map.89.m_ref = bf16[2,5,256,2816]{3,2,1,0:T(8,128)(2,1)} custom-call(bf16[2,5,11,2,128,128]{5,4,3,2,1,0:T(8,128)(2,1)} %a_ref.1), custom_call_target="tpu_custom_call" | custom-call | tf_op jit(solution)/shard_map/pallas_call | solution.py:82
  53.4 12.9 %shard_map.90 = f32[2,2,128,1920]{3,2,1,0:T(8,128)} custom-call(s32[110]{0:T(128)} %reshape.464.cols_ref, s32[10]{0:T(128)} %reshape.465.counts_ref, bf16[2,2,128,640]{3,2,1,0:T(8,128)(2,1)} %fusion.22.u_ref, bf16[2,5,256,2816]{3,2,1,0:T(8,128)(2,1)} %shard_map.89.m_ref), custom_call_target="tpu_custom_call" | custom-call | tf_op jit(solution)/shard_map/pallas_call | solution.py:184
  68.2 3.8 %collective-permute-start = (f32[2,2,128,640]{3,2,1,0:T(8,128)S(1)}, f32[2,2,128,640]{3,2,1,0:T(8,128)S(1)}, u32[]{:S(2)}, u32[]{:S(2)}) collective-permute-start(f32[2,2,128,640]{3,2,1,0:T(8,128)S(1)} %get-tuple-element.142), channel_id=1, source_target_pairs={{0,1},{1,2},{2,3},{3,4},{4,5},{5,6},{6,7},{7,8},{8,9},{9,10},{10,1... | collective-permute-start | bytes 3932168 | tf_op jit(solution)/shard_map/ppermute | solution.py:36
  73.9 12.6 %collective-permute-done = f32[2,2,128,640]{3,2,1,0:T(8,128)S(1)} collective-permute-done((f32[2,2,128,640]{3,2,1,0:T(8,128)S(1)}, f32[2,2,128,640]{3,2,1,0:T(8,128)S(1)}, u32[]{:S(2)}, u32[]{:S(2)}) %collective-permute-start) | collective-permute-done | bytes 1310752 | tf_op jit(solution)/shard_map/ppermute | solution.py:36
  86.5 4.4 %collective-permute-done.1 = f32[2,2,128,640]{3,2,1,0:T(8,128)S(1)} collective-permute-done((f32[2,2,128,640]{3,2,1,0:T(8,128)S(1)}, f32[2,2,128,640]{3,2,1,0:T(8,128)S(1)}, u32[]{:S(2)}, u32[]{:S(2)}) %collective-permute-start.1) | collective-permute-done | bytes 1310752 | tf_op jit(solution)/shard_map/ppermute | solution.py:36
  92.9 15.5 %all_to_all.45 = f32[32,1,2]{2,1,0:T(1,128)S(1)} all-to-all(f32[32,1,2]{2,1,0:T(1,128)S(1)} %broadcast_in_dim.13), channel_id=1, replica_groups=mesh['freq'=4,'rcv'=32] {'rcv'}, dimensions={0} | all-to-all | bytes 512 | tf_op jit(solution)/shard_map/all_to_all | solution.py:57
  108.6 2.6 collective-permute-start.3
  111.1 3.0 collective-permute-start.2
  114.1 6.3 %collective-permute-done.3 = bf16[2,2,128,640]{3,2,1,0:T(8,128)(2,1)S(1)} collective-permute-done((bf16[2,2,128,640]{3,2,1,0:T(8,128)(2,1)S(1)}, bf16[2,2,128,640]{3,2,1,0:T(8,128)(2,1)S(1)}, u32[]{:S(2)}, u32[]{:S(2)}) %collective-permute-start.3) | collective-permute-done | bytes 655392 | tf_op jit(solution)/shard_map/ppermute | solution.py:26
  123.1 13.4 %shard_map.91 = f32[2,2,128,640]{3,2,1,0:T(8,128)} custom-call(s32[110]{0:T(128)} %reshape.464.cols_ref, s32[10]{0:T(128)} %reshape.465.counts_ref, bf16[2,2,128,1920]{3,2,1,0:T(8,128)(2,1)} %pad_maximum_fusion.x_ref, bf16[2,5,256,2816]{3,2,1,0:T(8,128)(2,1)} %shard_map.89.m_ref), custom_call_target="tpu_custom_call" | custom-call | tf_op jit(solution)/shard_map/pallas_call | solution.py:161
  138.4 14.5 %all_to_all.46 = f32[32,1,2]{2,1,0:T(1,128)S(1)} all-to-all(f32[32,1,2]{2,1,0:T(1,128)S(1)} %broadcast_in_dim.14), channel_id=1, replica_groups=mesh['freq'=4,'rcv'=32] {'rcv'}, dimensions={0} | all-to-all | bytes 512 | tf_op jit(solution)/shard_map/all_to_all | solution.py:57
  153.9 12.9 %shard_map.92 = f32[2,2,128,1920]{3,2,1,0:T(8,128)} custom-call(s32[110]{0:T(128)} %reshape.464.cols_ref, s32[10]{0:T(128)} %reshape.465.counts_ref, bf16[2,2,128,640]{3,2,1,0:T(8,128)(2,1)} %fusion.23.u_ref, bf16[2,5,256,2816]{3,2,1,0:T(8,128)(2,1)} %shard_map.89.m_ref), custom_call_target="tpu_custom_call" | custom-call | tf_op jit(solution)/shard_map/pallas_call | solution.py:184
  168.7 3.0 collective-permute-start.4
  173.6 12.6 %collective-permute-done.4 = f32[2,2,128,640]{3,2,1,0:T(8,128)S(1)} collective-permute-done((f32[2,2,128,640]{3,2,1,0:T(8,128)S(1)}, f32[2,2,128,640]{3,2,1,0:T(8,128)S(1)}, u32[]{:S(2)}, u32[]{:S(2)}) %collective-permute-start.4) | collective-permute-done | bytes 1310752 | tf_op jit(solution)/shard_map/ppermute | solution.py:36
  186.2 4.4 %collective-permute-done.5 = f32[2,2,128,640]{3,2,1,0:T(8,128)S(1)} collective-permute-done((f32[2,2,128,640]{3,2,1,0:T(8,128)S(1)}, f32[2,2,128,640]{3,2,1,0:T(8,128)S(1)}, u32[]{:S(2)}, u32[]{:S(2)}) %collective-permute-start.5) | collective-permute-done | bytes 1310752 | tf_op jit(solution)/shard_map/ppermute | solution.py:36
  193.0 14.7 %all_to_all.47 = f32[32,1,2]{2,1,0:T(1,128)S(1)} all-to-all(f32[32,1,2]{2,1,0:T(1,128)S(1)} %broadcast_in_dim.15), channel_id=1, replica_groups=mesh['freq'=4,'rcv'=32] {'rcv'}, dimensions={0} | all-to-all | bytes 512 | tf_op jit(solution)/shard_map/all_to_all | solution.py:57
  210.5 3.2 %collective-permute-start.6 = (bf16[2,2,128,640]{3,2,1,0:T(8,128)(2,1)S(1)}, bf16[2,2,128,640]{3,2,1,0:T(8,128)(2,1)S(1)}, u32[]{:S(2)}, u32[]{:S(2)}) collective-permute-start(bf16[2,2,128,640]{3,2,1,0:T(8,128)(2,1)S(1)} %fusion.25), channel_id=1, source_target_pairs={{0,1},{1,2},{2,3},{3,4},{4,5},{5,6},{6,7},{7,8},{8,9},{9,10},{10,1... | collective-permute-start | bytes 1966088 | tf_op jit(solution)/shard_map/ppermute | solution.py:24
  213.7 6.1 %collective-permute-done.7 = bf16[2,2,128,640]{3,2,1,0:T(8,128)(2,1)S(1)} collective-permute-done((bf16[2,2,128,640]{3,2,1,0:T(8,128)(2,1)S(1)}, bf16[2,2,128,640]{3,2,1,0:T(8,128)(2,1)S(1)}, u32[]{:S(2)}, u32[]{:S(2)}) %collective-permute-start.7) | collective-permute-done | bytes 655392 | tf_op jit(solution)/shard_map/ppermute | solution.py:26
  222.5 13.4 %shard_map.93 = f32[2,2,128,640]{3,2,1,0:T(8,128)} custom-call(s32[110]{0:T(128)} %reshape.464.cols_ref, s32[10]{0:T(128)} %reshape.465.counts_ref, bf16[2,2,128,1920]{3,2,1,0:T(8,128)(2,1)} %pad_maximum_fusion.1.x_ref, bf16[2,5,256,2816]{3,2,1,0:T(8,128)(2,1)} %shard_map.89.m_ref), custom_call_target="tpu_custom_call" | custom-call | tf_op jit(solution)/shard_map/pallas_call | solution.py:161
  236.0 3.1 multiply_reduce_fusion.1
  239.1 14.5 %all_to_all.48 = f32[32,1,2]{2,1,0:T(1,128)S(1)} all-to-all(f32[32,1,2]{2,1,0:T(1,128)S(1)} %broadcast_in_dim.16), channel_id=1, replica_groups=mesh['freq'=4,'rcv'=32] {'rcv'}, dimensions={0} | all-to-all | bytes 512 | tf_op jit(solution)/shard_map/all_to_all | solution.py:57
  255.9 12.9 %shard_map.94 = f32[2,2,128,1920]{3,2,1,0:T(8,128)} custom-call(s32[110]{0:T(128)} %reshape.464.cols_ref, s32[10]{0:T(128)} %reshape.465.counts_ref, bf16[2,2,128,640]{3,2,1,0:T(8,128)(2,1)} %fusion.11.u_ref, bf16[2,5,256,2816]{3,2,1,0:T(8,128)(2,1)} %shard_map.89.m_ref), custom_call_target="tpu_custom_call" | custom-call | tf_op jit(solution)/shard_map/pallas_call | solution.py:184
  270.8 3.0 collective-permute-start.8
  275.8 12.6 %collective-permute-done.8 = f32[2,2,128,640]{3,2,1,0:T(8,128)S(1)} collective-permute-done((f32[2,2,128,640]{3,2,1,0:T(8,128)S(1)}, f32[2,2,128,640]{3,2,1,0:T(8,128)S(1)}, u32[]{:S(2)}, u32[]{:S(2)}) %collective-permute-start.8) | collective-permute-done | bytes 1310752 | tf_op jit(solution)/shard_map/ppermute | solution.py:36
  288.4 4.4 %collective-permute-done.9 = f32[2,2,128,640]{3,2,1,0:T(8,128)S(1)} collective-permute-done((f32[2,2,128,640]{3,2,1,0:T(8,128)S(1)}, f32[2,2,128,640]{3,2,1,0:T(8,128)S(1)}, u32[]{:S(2)}, u32[]{:S(2)}) %collective-permute-start.9) | collective-permute-done | bytes 1310752 | tf_op jit(solution)/shard_map/ppermute | solution.py:36
  292.8 2.9 multiply_reduce_fusion
  295.7 14.7 %all_to_all.49 = f32[32,1,2]{2,1,0:T(1,128)S(1)} all-to-all(f32[32,1,2]{2,1,0:T(1,128)S(1)} %broadcast_in_dim.17), channel_id=1, replica_groups=mesh['freq'=4,'rcv'=32] {'rcv'}, dimensions={0} | all-to-all | bytes 512 | tf_op jit(solution)/shard_map/all_to_all | solution.py:57
  310.5 3.3 %divide_multiply_fusion = (f32[2,2,128,640]{3,2,1,0:T(8,128)}, f32[2,2,128,640]{3,2,1,0:T(8,128)}) fusion(f32[2,2,128,640]{3,2,1,0:T(8,128)} %get-tuple-element.129, f32[2]{0:T(128)S(1)} %get-tuple-element.144, f32[2]{0:T(128)S(1)} %get-tuple-element.122, f32[2]{0:T(128)S(1)} %get-tuple-element.147, f32[2,2,128,640]{3,2,1,0:T(8,128)S(1)} %get-tuple-element.133, ...), kind=kLoop, calls=%fused_computation.19 | loop fusion | flops 2949120 | bytes 6553656 | tf_op jit(solution)/shard_map/mul | solution.py:258
  (57 shorter events, 35.1 us)
Async XLA Ops:
  6.7 13.0 %copy-start.3 = (s32[2,5]{1,0:T(2,128)S(1)}, s32[2,5]{1,0:T(2,128)}, u32[]{:S(2)}) copy-start(s32[2,5]{1,0:T(2,128)} %param.31) | copy-start | bytes 124
  6.7 13.0 %copy-start.2 = (s32[2,5,11]{2,0,1:T(2,128)S(1)}, s32[2,5,11]{2,0,1:T(2,128)}, u32[]{:S(2)}) copy-start(s32[2,5,11]{2,0,1:T(2,128)} %param.30) | copy-start | bytes 1324
  8.3 26.4 %all-to-all-start = ((bf16[2,2,1,128,640]{4,1,0,2,3:T(2,128)(2,1)}), bf16[2,2,1,128,640]{4,1,0,2,3:T(2,128)(2,1)S(1)}, u32[]{:S(2)}, u32[]{:S(2)}) async-start(bf16[2,2,1,128,640]{4,1,0,2,3:T(2,128)(2,1)} %copy.14), calls=%async_computation | async-start | bytes 1310720 | tf_op jit(solution)/shard_map/all_to_all | solution.py:208
  35.5 16.8 %all-to-all-start.1 = ((f32[32,1,2]{2,1,0:T(1,128)}), f32[32,1,2]{2,1,0:T(1,128)S(1)}, u32[]{:S(2)}, u32[]{:S(2)}) async-start(f32[32,1,2]{2,1,0:T(1,128)} %broadcast_in_dim.12), calls=%async_computation.1 | async-start | bytes 32768 | tf_op jit(solution)/shard_map/all_to_all | solution.py:57
  68.2 18.4 %collective-permute-start = (f32[2,2,128,640]{3,2,1,0:T(8,128)S(1)}, f32[2,2,128,640]{3,2,1,0:T(8,128)S(1)}, u32[]{:S(2)}, u32[]{:S(2)}) collective-permute-start(f32[2,2,128,640]{3,2,1,0:T(8,128)S(1)} %get-tuple-element.142), channel_id=1, source_target_pairs={{0,1},{1,2},{2,3},{3,4},{4,5},{5,6},{6,7},{7,8},{8,9},{9,10},{10,1... | collective-permute-start | bytes 3932168 | tf_op jit(solution)/shard_map/ppermute | solution.py:36
  72.0 18.9 %collective-permute-start.1 = (f32[2,2,128,640]{3,2,1,0:T(8,128)S(1)}, f32[2,2,128,640]{3,2,1,0:T(8,128)S(1)}, u32[]{:S(2)}, u32[]{:S(2)}) collective-permute-start(f32[2,2,128,640]{3,2,1,0:T(8,128)S(1)} %get-tuple-element.143), channel_id=1, source_target_pairs={{1,0},{2,1},{3,2},{4,3},{5,4},{6,5},{7,6},{8,7},{9,8},{10,9},{11,1... | collective-permute-start | bytes 3932168 | tf_op jit(solution)/shard_map/ppermute | solution.py:36
  108.6 11.9 %collective-permute-start.3 = (bf16[2,2,128,640]{3,2,1,0:T(8,128)(2,1)S(1)}, bf16[2,2,128,640]{3,2,1,0:T(8,128)(2,1)S(1)}, u32[]{:S(2)}, u32[]{:S(2)}) collective-permute-start(bf16[2,2,128,640]{3,2,1,0:T(8,128)(2,1)S(1)} %fusion.24), channel_id=1, source_target_pairs={{1,0},{2,1},{3,2},{4,3},{5,4},{6,5},{7,6},{8,7},{9,8},{10,9},{11,1... | collective-permute-start | bytes 1966088 | tf_op jit(solution)/shard_map/ppermute | solution.py:26
  111.1 10.5 %collective-permute-start.2 = (bf16[2,2,128,640]{3,2,1,0:T(8,128)(2,1)S(1)}, bf16[2,2,128,640]{3,2,1,0:T(8,128)(2,1)S(1)}, u32[]{:S(2)}, u32[]{:S(2)}) collective-permute-start(bf16[2,2,128,640]{3,2,1,0:T(8,128)(2,1)S(1)} %fusion.24), channel_id=1, source_target_pairs={{0,1},{1,2},{2,3},{3,4},{4,5},{5,6},{6,7},{7,8},{8,9},{9,10},{10,1... | collective-permute-start | bytes 1966088 | tf_op jit(solution)/shard_map/ppermute | solution.py:24
  138.4 28.4 %copy-start = (f32[2,2,128,640]{3,2,1,0:T(8,128)}, f32[2,2,128,640]{3,2,1,0:T(8,128)S(1)}, u32[]{:S(2)}) copy-start(f32[2,2,128,640]{3,2,1,0:T(8,128)S(1)} %get-tuple-element.135) | copy-start | bytes 3932164
  168.7 17.5 %collective-permute-start.4 = (f32[2,2,128,640]{3,2,1,0:T(8,128)S(1)}, f32[2,2,128,640]{3,2,1,0:T(8,128)S(1)}, u32[]{:S(2)}, u32[]{:S(2)}) collective-permute-start(f32[2,2,128,640]{3,2,1,0:T(8,128)S(1)} %get-tuple-element.140), channel_id=1, source_target_pairs={{0,1},{1,2},{2,3},{3,4},{4,5},{5,6},{6,7},{7,8},{8,9},{9,10},{10,1... | collective-permute-start | bytes 3932168 | tf_op jit(solution)/shard_map/ppermute | solution.py:36
  171.7 18.9 %collective-permute-start.5 = (f32[2,2,128,640]{3,2,1,0:T(8,128)S(1)}, f32[2,2,128,640]{3,2,1,0:T(8,128)S(1)}, u32[]{:S(2)}, u32[]{:S(2)}) collective-permute-start(f32[2,2,128,640]{3,2,1,0:T(8,128)S(1)} %get-tuple-element.141), channel_id=1, source_target_pairs={{1,0},{2,1},{3,2},{4,3},{5,4},{6,5},{7,6},{8,7},{9,8},{10,9},{11,1... | collective-permute-start | bytes 3932168 | tf_op jit(solution)/shard_map/ppermute | solution.py:36
  208.0 11.9 %collective-permute-start.7 = (bf16[2,2,128,640]{3,2,1,0:T(8,128)(2,1)S(1)}, bf16[2,2,128,640]{3,2,1,0:T(8,128)(2,1)S(1)}, u32[]{:S(2)}, u32[]{:S(2)}) collective-permute-start(bf16[2,2,128,640]{3,2,1,0:T(8,128)(2,1)S(1)} %fusion.25), channel_id=1, source_target_pairs={{1,0},{2,1},{3,2},{4,3},{5,4},{6,5},{7,6},{8,7},{9,8},{10,9},{11,1... | collective-permute-start | bytes 1966088 | tf_op jit(solution)/shard_map/ppermute | solution.py:26
  210.5 10.5 %collective-permute-start.6 = (bf16[2,2,128,640]{3,2,1,0:T(8,128)(2,1)S(1)}, bf16[2,2,128,640]{3,2,1,0:T(8,128)(2,1)S(1)}, u32[]{:S(2)}, u32[]{:S(2)}) collective-permute-start(bf16[2,2,128,640]{3,2,1,0:T(8,128)(2,1)S(1)} %fusion.25), channel_id=1, source_target_pairs={{0,1},{1,2},{2,3},{3,4},{4,5},{5,6},{6,7},{7,8},{8,9},{9,10},{10,1... | collective-permute-start | bytes 1966088 | tf_op jit(solution)/shard_map/ppermute | solution.py:24
  268.8 24.0 %copy-start.1 = (f32[2,2,128,640]{3,2,1,0:T(8,128)S(1)}, f32[2,2,128,640]{3,2,1,0:T(8,128)}, u32[]{:S(2)}) copy-start(f32[2,2,128,640]{3,2,1,0:T(8,128)} %get-tuple-element.131) | copy-start | bytes 3932164
  270.8 17.5 %collective-permute-start.8 = (f32[2,2,128,640]{3,2,1,0:T(8,128)S(1)}, f32[2,2,128,640]{3,2,1,0:T(8,128)S(1)}, u32[]{:S(2)}, u32[]{:S(2)}) collective-permute-start(f32[2,2,128,640]{3,2,1,0:T(8,128)S(1)} %get-tuple-element.138), channel_id=1, source_target_pairs={{0,1},{1,2},{2,3},{3,4},{4,5},{5,6},{6,7},{7,8},{8,9},{9,10},{10,1... | collective-permute-start | bytes 3932168 | tf_op jit(solution)/shard_map/ppermute | solution.py:36
  273.8 18.9 %collective-permute-start.9 = (f32[2,2,128,640]{3,2,1,0:T(8,128)S(1)}, f32[2,2,128,640]{3,2,1,0:T(8,128)S(1)}, u32[]{:S(2)}, u32[]{:S(2)}) collective-permute-start(f32[2,2,128,640]{3,2,1,0:T(8,128)S(1)} %get-tuple-element.139), channel_id=1, source_target_pairs={{1,0},{2,1},{3,2},{4,3},{5,4},{6,5},{7,6},{8,7},{9,8},{10,9},{11,1... | collective-permute-start | bytes 3932168 | tf_op jit(solution)/shard_map/ppermute | solution.py:36

commit v4 on v3

--- a/solution.py
+++ b/solution.py
@@ -58,9 +58,8 @@
     return jnp.sum(gathered, axis=0)
 
 
-def field_norm(field):
-    squares = rcv_sum(jnp.sum(field * field, axis=(0, 2, 3)))
-    return jnp.sqrt(squares + EPSILON)[None, :, None, None]
+def squares(field):
+    return rcv_sum(jnp.sum(field * field, axis=(0, 2, 3)))[None, :, None, None]
 
 
 def _stack_kernel(a_ref, m_ref):
@@ -165,6 +164,11 @@
             (2, local_freqs, sources, local_blocks * block_size), jnp.float32
         ),
         compiler_params=pltpu.CompilerParams(dimension_semantics=("arbitrary", "arbitrary")),
+        cost_estimate=pl.CostEstimate(
+            flops=2 * local_freqs * local_blocks * sources * depth * width,
+            transcendentals=0,
+            bytes_accessed=stacked.size * 2 + extended.size * 2 + extended.size * 4,
+        ),
     )(cols, counts, extended, stacked)
 
 
@@ -186,6 +190,11 @@
         grid_spec=grid_spec,
         out_shape=jax.ShapeDtypeStruct((2, local_freqs, sources, span), jnp.float32),
         compiler_params=pltpu.CompilerParams(dimension_semantics=("arbitrary", "arbitrary")),
+        cost_estimate=pl.CostEstimate(
+            flops=2 * local_freqs * local_blocks * sources * depth * width,
+            transcendentals=0,
+            bytes_accessed=stacked.size * 2 + rounded.size * 2 + rounded.size * 12,
+        ),
     )(cols, counts, rounded, stacked)
 
 
@@ -230,21 +239,25 @@
         extended = with_halo(field.astype(jnp.bfloat16), (("rcv", 3),), rim_rows)
         return field + apply_forward(extended, stacked, columns, counts)
 
-    beta_norm = field_norm(right_side)
+    beta_norm = jnp.sqrt(squares(right_side) + EPSILON)
+    lifted = adjoint(right_side)
+    alpha_norm = jnp.sqrt(squares(lifted) / (beta_norm * beta_norm) + EPSILON)
     left_vector = right_side / beta_norm
-    residual_right = adjoint(left_vector)
-    alpha_norm = field_norm(residual_right)
-    right_vector = residual_right / alpha_norm
+    right_raw = lifted
+    right_scale = beta_norm * alpha_norm
+    right_vector = right_raw / right_scale
     search_direction = right_vector
     solution = jnp.zeros_like(right_side)
     phibar = beta_norm
     rhobar = alpha_norm
     for iteration in range(ITERS):
-        residual_left = forward(right_vector) - alpha_norm * left_vector
-        beta_norm = field_norm(residual_left)
+        residual_left = forward(right_raw) / right_scale - alpha_norm * left_vector
+        beta_norm = jnp.sqrt(squares(residual_left) + EPSILON)
         left_vector = residual_left / beta_norm
-        residual_right = adjoint(left_vector) - beta_norm * right_vector
-        alpha_norm = field_norm(residual_right)
+        residual_right = adjoint(residual_left) / beta_norm - beta_norm * right_vector
+        alpha_norm = jnp.sqrt(squares(residual_right) + EPSILON)
+        right_raw = residual_right
+        right_scale = alpha_norm
         right_vector = residual_right / alpha_norm
         rho_value = jnp.sqrt(rhobar * rhobar + beta_norm * beta_norm)
         cosine = rhobar / rho_value

time: 316 us -> 276 us (0.87)
  waiting for transfers between devices: 80.6 us -> 26.8 us
  blocking collectives: 73.8 us -> 82.2 us
  local copies, waits for them, and re-layouts: 9.76 us -> 13.6 us
    ppermute x6, waiting for transfers between devices: 51 us -> 17 us  [from_behind(): lax.ppermute(value, axis, [(source, source + steps) for source in range(f...]
    ppermute x2, waiting for transfers between devices: 12.5 us -> 0.01 us  [with_halo(): lax.ppermute(head, axis, [((i + 1) % count, i) for i in range(ends)])]
    all_to_all x1, waiting for transfers between devices: 14.8 us -> 2.85 us  [body(): lax.all_to_all(spectrum, ('freq', 'rcv'), split_axis=3, concat_axis=2, ti...]
    all_to_all x5, blocking collectives: 73.8 us -> 82.2 us  [rcv_sum(): gathered = lax.all_to_all(spread, 'rcv', 0, 0, tiled=False)]
    reduce_sum x6 -> x5, other arithmetic: 12.4 us -> 5.06 us  [squares(): return rcv_sum(jnp.sum(field * field, axis=(0, 2, 3)))[None, :, None, None]]
    all_to_all x1, waiting for transfers between devices: 0.01 us -> 6.96 us  [rcv_sum(): gathered = lax.all_to_all(spread, 'rcv', 0, 0, tiled=False)]
    convert_element_type x2, other arithmetic: 0.33 us -> 4.86 us  [forward(): extended = with_halo(field.astype(jnp.bfloat16), (('rcv', 3),), rim_rows)]
  transfers between devices with their start and end apart: 12 -> 12, of which waited for: 11 -> 4; matrix products, arithmetic and copies ran while one was open for 0% -> 1% of each run, Pallas kernels for 3% -> 4%
where the time goes in v4:
time: 276 us; the launch traced here: 274 us
  blocking collectives  82.2 us (30%)
  Pallas kernels  77.5 us (28%)
  starting transfers between devices  42.3 us (15%)
  waiting for transfers between devices  26.8 us (10%)
  other arithmetic  24.9 us (9%)
  local copies, waits for them, and re-layouts  13.6 us (5%)
  matrix products  5.45 us (2%)
    all_to_all x5, blocking collectives, rcv_sum(): gathered = lax.all_to_all(spread, 'rcv', 0, 0, tiled=False)  82.2 us
    pallas_call x3, Pallas kernels, apply_adjoint(): pl.pallas_call(_adjoint_kernel, grid_spec=grid_spec, out_shape=jax.ShapeD...  39.9 us
    pallas_call x2, Pallas kernels, apply_forward(): pl.pallas_call(_forward_kernel, grid_spec=grid_spec, out_shape=jax.ShapeD...  26.9 us
    ppermute x6, waiting for transfers between devices, from_behind(): lax.ppermute(value, axis, [(source, source + steps) for source in range(f...  17 us
    ppermute x6, starting transfers between devices, from_behind(): lax.ppermute(value, axis, [(source, source + steps) for source in range(f...  15.5 us
    all_to_all x1, starting transfers between devices, body(): lax.all_to_all(spectrum, ('freq', 'rcv'), split_axis=3, concat_axis=2, ti...  11.5 us
    pallas_call x1, Pallas kernels, stack_blocks(): pl.pallas_call(_stack_kernel, grid=(local_freqs, local_blocks), in_specs=...  10.7 us
    slice x3, local copies, waits for them, and re-layouts, adjoint(): upper_rim = spread[..., rim_rows + local_rows:]  8.81 us
  transfers between devices with their start and end apart: 12, of which 4 were waited for; matrix products, arithmetic and copies ran while one was open for 1% of the time, Pallas kernels for 4%

profile of v4, /device:TPU:1, one launch (start us, length us, event | category | flops | bytes accessed | tf_op | source)
XLA Modules:
  0.0 273.7 jit_solution(9472040916810318967)
XLA Ops:
  0.8 5.5 %fusion = bf16[2,2,1,4,20480]{4,3,1,0,2:T(4,128)(2,1)S(1)} fusion(bf16[1,256,20480]{2,1,0:T(8,128)(2,1)} %param.28, bf16[256,1,4,2]{0,2,3,1:T(4,128)(2,1)S(1)} %get-tuple-element.153, bf16[256,1,4,2]{0,2,3,1:T(4,128)(2,1)S(1)} %get-tuple-element.152), kind=kOutput, calls=%fused_computation.1 | convolution fusion | flops 168116224 | bytes 11149312 | tf_op jit(solution)/shard_map/snr,ncgf->cfsgr/dot_general | solution.py:211
  8.3 11.5 %all-to-all-start = ((bf16[2,2,1,128,640]{4,1,0,2,3:T(2,128)(2,1)}), bf16[2,2,1,128,640]{4,1,0,2,3:T(2,128)(2,1)S(1)}, u32[]{:S(2)}, u32[]{:S(2)}) async-start(bf16[2,2,1,128,640]{4,1,0,2,3:T(2,128)(2,1)} %copy.14), calls=%async_computation | async-start | bytes 1310720 | tf_op jit(solution)/shard_map/all_to_all | solution.py:217
  21.0 10.7 %shard_map.89.m_ref = bf16[2,5,256,2816]{3,2,1,0:T(8,128)(2,1)} custom-call(bf16[2,5,11,2,128,128]{5,4,3,2,1,0:T(8,128)(2,1)} %a_ref.1), custom_call_target="tpu_custom_call" | custom-call | tf_op jit(solution)/shard_map/pallas_call | solution.py:81
  31.8 2.9 %all-to-all-done = bf16[2,2,1,128,640]{4,1,0,2,3:T(2,128)(2,1)S(1)} async-done(((bf16[2,2,1,128,640]{4,1,0,2,3:T(2,128)(2,1)}), bf16[2,2,1,128,640]{4,1,0,2,3:T(2,128)(2,1)S(1)}, u32[]{:S(2)}, u32[]{:S(2)}) %all-to-all-start) | async-done | bytes 655392 | tf_op jit(solution)/shard_map/all_to_all | solution.py:217
  35.5 13.3 %shard_map.90 = f32[2,2,128,1920]{3,2,1,0:T(8,128)} custom-call(s32[110]{0:T(128)} %reshape.491.cols_ref, s32[10]{0:T(128)} %reshape.492.counts_ref, bf16[2,2,128,640]{3,2,1,0:T(8,128)(2,1)} %bitcast.24, bf16[2,5,256,2816]{3,2,1,0:T(8,128)(2,1)} %shard_map.89.m_ref), custom_call_target="tpu_custom_call" | custom-call | flops 1845493760 | bytes 19005440 | tf_op jit(solution)/shard_map/pallas_call | solution.py:188
  50.7 2.8 %collective-permute-start = (f32[2,2,128,640]{3,2,1,0:T(8,128)S(1)}, f32[2,2,128,640]{3,2,1,0:T(8,128)S(1)}, u32[]{:S(2)}, u32[]{:S(2)}) collective-permute-start(f32[2,2,128,640]{3,2,1,0:T(8,128)S(1)} %get-tuple-element.144), channel_id=1, source_target_pairs={{0,1},{1,2},{2,3},{3,4},{4,5},{5,6},{6,7},{7,8},{8,9},{9,10},{10,1... | collective-permute-start | bytes 3932168 | tf_op jit(solution)/shard_map/ppermute | solution.py:36
  55.5 12.6 %collective-permute-done = f32[2,2,128,640]{3,2,1,0:T(8,128)S(1)} collective-permute-done((f32[2,2,128,640]{3,2,1,0:T(8,128)S(1)}, f32[2,2,128,640]{3,2,1,0:T(8,128)S(1)}, u32[]{:S(2)}, u32[]{:S(2)}) %collective-permute-start) | collective-permute-done | bytes 1310752 | tf_op jit(solution)/shard_map/ppermute | solution.py:36
  68.1 4.4 %collective-permute-done.1 = f32[2,2,128,640]{3,2,1,0:T(8,128)S(1)} collective-permute-done((f32[2,2,128,640]{3,2,1,0:T(8,128)S(1)}, f32[2,2,128,640]{3,2,1,0:T(8,128)S(1)}, u32[]{:S(2)}, u32[]{:S(2)}) %collective-permute-start.1) | collective-permute-done | bytes 1310752 | tf_op jit(solution)/shard_map/ppermute | solution.py:36
  76.4 3.6 %collective-permute-start.2 = (bf16[2,2,128,640]{3,2,1,0:T(8,128)(2,1)S(1)}, bf16[2,2,128,640]{3,2,1,0:T(8,128)(2,1)}, u32[]{:S(2)}, u32[]{:S(2)}) collective-permute-start(bf16[2,2,128,640]{3,2,1,0:T(8,128)(2,1)S(1)} %get-tuple-element.138), channel_id=1, source_target_pairs={{0,1},{1,2},{2,3},{3,4},{4,5},{5,6},{6,7},{7,8},{8,9},{9,10},{10,1... | collective-permute-start | bytes 1966088 | tf_op jit(solution)/shard_map/ppermute | solution.py:24
  80.3 16.9 %all_to_all.45 = f32[32,1,2]{2,1,0:T(1,128)S(1)} all-to-all(f32[32,1,2]{2,1,0:T(1,128)S(1)} %broadcast_in_dim.12), channel_id=1, replica_groups=mesh['freq'=4,'rcv'=32] {'rcv'}, dimensions={0} | all-to-all | bytes 512 | tf_op jit(solution)/shard_map/all_to_all | solution.py:57
  97.9 4.1 %all-to-all-start.2 = ((f32[32,1,2]{2,1,0:T(1,128)}), f32[32,1,2]{2,1,0:T(1,128)S(1)}, u32[]{:S(2)}, u32[]{:S(2)}) async-start(f32[32,1,2]{2,1,0:T(1,128)} %broadcast_in_dim.13), calls=%async_computation.2 | async-start | bytes 32768 | tf_op jit(solution)/shard_map/all_to_all | solution.py:57
  102.1 7.0 %all-to-all-done.2 = f32[32,1,2]{2,1,0:T(1,128)S(1)} async-done(((f32[32,1,2]{2,1,0:T(1,128)}), f32[32,1,2]{2,1,0:T(1,128)S(1)}, u32[]{:S(2)}, u32[]{:S(2)}) %all-to-all-start.2) | async-done | bytes 288 | tf_op jit(solution)/shard_map/all_to_all | solution.py:57
  109.1 2.5 pad_maximum_fusion.x_ref
  111.7 13.4 %shard_map.91 = f32[2,2,128,640]{3,2,1,0:T(8,128)} custom-call(s32[110]{0:T(128)} %reshape.491.cols_ref, s32[10]{0:T(128)} %reshape.492.counts_ref, bf16[2,2,128,1920]{3,2,1,0:T(8,128)(2,1)} %pad_maximum_fusion.x_ref, bf16[2,5,256,2816]{3,2,1,0:T(8,128)(2,1)} %shard_map.89.m_ref), custom_call_target="tpu_custom_call" | custom-call | flops 1845493760 | bytes 20316160 | tf_op jit(solution)/shard_map/pallas_call | solution.py:160
  127.6 13.3 %shard_map.92 = f32[2,2,128,1920]{3,2,1,0:T(8,128)} custom-call(s32[110]{0:T(128)} %reshape.491.cols_ref, s32[10]{0:T(128)} %reshape.492.counts_ref, bf16[2,2,128,640]{3,2,1,0:T(8,128)(2,1)} %get-tuple-element.134.u_ref, bf16[2,5,256,2816]{3,2,1,0:T(8,128)(2,1)} %shard_map.89.m_ref), custom_call_target="tpu_custom_call" | custom-call | flops 1845493760 | bytes 19005440 | tf_op jit(solution)/shard_map/pallas_call | solution.py:188
  140.9 3.4 %fusion.34 = (f32[2,2,128,640]{3,2,1,0:T(8,128)}, f32[2,2,128,640]{3,2,1,0:T(8,128)}) fusion(f32[2,2,128,1920]{3,2,1,0:T(8,128)} %shard_map.92), kind=kLoop, calls=%fused_computation.71 | loop fusion | bytes 5242880 | tf_op jit(solution)/shard_map/slice | solution.py:231
  146.8 2.9 %collective-permute-start.5 = (f32[2,2,128,640]{3,2,1,0:T(8,128)}, f32[2,2,128,640]{3,2,1,0:T(8,128)}, u32[]{:S(2)}, u32[]{:S(2)}) collective-permute-start(f32[2,2,128,640]{3,2,1,0:T(8,128)} %get-tuple-element.143), channel_id=1, source_target_pairs={{1,0},{2,1},{3,2},{4,3},{5,4},{6,5},{7,6},{8,7},{9,8},{10,9},{11,1... | collective-permute-start | bytes 3932168 | tf_op jit(solution)/shard_map/ppermute | solution.py:36
  150.0 18.4 %all_to_all.46 = f32[32,1,2]{2,1,0:T(1,128)S(1)} all-to-all(f32[32,1,2]{2,1,0:T(1,128)S(1)} %broadcast_in_dim.14), channel_id=1, replica_groups=mesh['freq'=4,'rcv'=32] {'rcv'}, dimensions={0} | all-to-all | bytes 512 | tf_op jit(solution)/shard_map/all_to_all | solution.py:57
  168.4 2.9 %fusion.28 = (bf16[2,2,128,640]{3,2,1,0:T(8,128)(2,1)S(1)}, f32[2,2,128,640]{3,2,1,0:T(8,128)S(1)}) fusion(f32[2,2,128,640]{3,2,1,0:T(8,128)S(1)} %get-tuple-element.139, f32[2]{0:T(128)S(1)} %get-tuple-element.136, f32[2]{0:T(128)S(1)} %add_sqrt_fusion.5, f32[2,2,128,640]{3,2,1,0:T(8,128)} %copy-done, f32[2,2,128,640]{3,2,1,0:T(8,128)} %collective-permute-done.5, ...), kind=kLoop, calls=%fused_computation.67 | loop fusion | flops 2621440 | bytes 8519696 | tf_op jit(solution)/shard_map/convert_element_type | solution.py:239
  171.3 2.6 collective-permute-start.7
  173.9 3.1 %collective-permute-start.6 = (bf16[2,2,128,640]{3,2,1,0:T(8,128)(2,1)S(1)}, bf16[2,2,128,640]{3,2,1,0:T(8,128)(2,1)}, u32[]{:S(2)}, u32[]{:S(2)}) collective-permute-start(bf16[2,2,128,640]{3,2,1,0:T(8,128)(2,1)S(1)} %get-tuple-element.132), channel_id=1, source_target_pairs={{0,1},{1,2},{2,3},{3,4},{4,5},{5,6},{6,7},{7,8},{8,9},{9,10},{10,1... | collective-permute-start | bytes 1966088 | tf_op jit(solution)/shard_map/ppermute | solution.py:24
  177.2 14.6 %all_to_all.47 = f32[32,1,2]{2,1,0:T(1,128)S(1)} all-to-all(f32[32,1,2]{2,1,0:T(1,128)S(1)} %broadcast_in_dim.15), channel_id=1, replica_groups=mesh['freq'=4,'rcv'=32] {'rcv'}, dimensions={0} | all-to-all | bytes 512 | tf_op jit(solution)/shard_map/all_to_all | solution.py:57
  191.9 2.7 %pad_maximum_fusion.1.x_ref = bf16[2,2,128,1920]{3,2,1,0:T(8,128)(2,1)} fusion(bf16[2,2,128,640]{3,2,1,0:T(8,128)(2,1)} %collective-permute-done.7, bf16[2,2,128,640]{3,2,1,0:T(8,128)(2,1)S(1)} %get-tuple-element.132, bf16[2,2,128,640]{3,2,1,0:T(8,128)(2,1)} %collective-permute-done.6), kind=kLoop, calls=%fused_computation.4 | loop fusion | flops 5898240 | bytes 3932160 | tf_op jit(solution)/shard_map/concatenate | solution.py:22
  194.6 13.4 %shard_map.93 = f32[2,2,128,640]{3,2,1,0:T(8,128)} custom-call(s32[110]{0:T(128)} %reshape.491.cols_ref, s32[10]{0:T(128)} %reshape.492.counts_ref, bf16[2,2,128,1920]{3,2,1,0:T(8,128)(2,1)} %pad_maximum_fusion.1.x_ref, bf16[2,5,256,2816]{3,2,1,0:T(8,128)(2,1)} %shard_map.89.m_ref), custom_call_target="tpu_custom_call" | custom-call | flops 1845493760 | bytes 20316160 | tf_op jit(solution)/shard_map/pallas_call | solution.py:160
  208.1 3.3 %fusion.27 = (bf16[2,2,128,640]{3,2,1,0:T(8,128)(2,1)}, f32[2,2,128,640]{3,2,1,0:T(8,128)}) fusion(f32[2,2,128,640]{3,2,1,0:T(8,128)} %copy-done, f32[2]{0:T(128)S(1)} %add_sqrt_fusion.5, f32[2]{0:T(128)S(1)} %add_sqrt_fusion.3, f32[2,2,128,640]{3,2,1,0:T(8,128)S(1)} %get-tuple-element.133, f32[2,2,128,640]{3,2,1,0:T(8,128)} %shard_map.93), kind=kLoop, calls=%fused_computation.66 | loop fusion | flops 1966080 | bytes 5898256 | tf_op jit(solution)/shard_map/convert_element_type | solution.py:227
  211.4 13.3 %shard_map.94 = f32[2,2,128,1920]{3,2,1,0:T(8,128)} custom-call(s32[110]{0:T(128)} %reshape.491.cols_ref, s32[10]{0:T(128)} %reshape.492.counts_ref, bf16[2,2,128,640]{3,2,1,0:T(8,128)(2,1)} %get-tuple-element.130.u_ref, bf16[2,5,256,2816]{3,2,1,0:T(8,128)(2,1)} %shard_map.89.m_ref), custom_call_target="tpu_custom_call" | custom-call | flops 1845493760 | bytes 19005440 | tf_op jit(solution)/shard_map/pallas_call | solution.py:188
  224.7 3.5 %fusion.33 = (f32[2,2,128,640]{3,2,1,0:T(8,128)}, f32[2,2,128,640]{3,2,1,0:T(8,128)}) fusion(f32[2,2,128,1920]{3,2,1,0:T(8,128)} %shard_map.94), kind=kLoop, calls=%fused_computation.70 | loop fusion | bytes 5242880 | tf_op jit(solution)/shard_map/slice | solution.py:231
  230.7 2.9 %collective-permute-start.9 = (f32[2,2,128,640]{3,2,1,0:T(8,128)}, f32[2,2,128,640]{3,2,1,0:T(8,128)}, u32[]{:S(2)}, u32[]{:S(2)}) collective-permute-start(f32[2,2,128,640]{3,2,1,0:T(8,128)} %get-tuple-element.141), channel_id=1, source_target_pairs={{1,0},{2,1},{3,2},{4,3},{5,4},{6,5},{7,6},{8,7},{9,8},{10,9},{11,1... | collective-permute-start | bytes 3932168 | tf_op jit(solution)/shard_map/ppermute | solution.py:36
  233.9 18.4 %all_to_all.48 = f32[32,1,2]{2,1,0:T(1,128)S(1)} all-to-all(f32[32,1,2]{2,1,0:T(1,128)S(1)} %broadcast_in_dim.16), channel_id=1, replica_groups=mesh['freq'=4,'rcv'=32] {'rcv'}, dimensions={0} | all-to-all | bytes 512 | tf_op jit(solution)/shard_map/all_to_all | solution.py:57
  252.4 4.0 %multiply_reduce_fusion = (f32[2]{0:T(128)S(1)}, f32[2,2,128,640]{3,2,1,0:T(8,128)}) fusion(f32[2,2,128,640]{3,2,1,0:T(8,128)S(1)} %get-tuple-element.133, f32[2]{0:T(128)S(1)} %add_sqrt_fusion.3, f32[2]{0:T(128)S(1)} %add_sqrt_fusion.2, f32[2,2,128,640]{3,2,1,0:T(8,128)} %get-tuple-element.131, f32[2,2,128,640]{3,2,1,0:T(8,128)} %collective-permute-done.9, ...), kind=kLoop, calls=%fused_computation.24 | loop fusion | flops 2949118 | bytes 7864344 | tf_op jit(solution)/shard_map/reduce_sum | solution.py:62
  256.4 14.0 %all_to_all.49 = f32[32,1,2]{2,1,0:T(1,128)S(1)} all-to-all(f32[32,1,2]{2,1,0:T(1,128)S(1)} %broadcast_in_dim.17), channel_id=1, replica_groups=mesh['freq'=4,'rcv'=32] {'rcv'}, dimensions={0} | all-to-all | bytes 512 | tf_op jit(solution)/shard_map/all_to_all | solution.py:57
  270.4 3.3 %divide_multiply_fusion = (f32[2,2,128,640]{3,2,1,0:T(8,128)}, f32[2,2,128,640]{3,2,1,0:T(8,128)}) fusion(f32[2,2,128,640]{3,2,1,0:T(8,128)} %get-tuple-element.129, f32[2]{0:T(128)S(1)} %get-tuple-element.147, f32[2]{0:T(128)S(1)} %get-tuple-element.122, f32[2]{0:T(128)S(1)} %get-tuple-element.150, f32[2,2,128,640]{3,2,1,0:T(8,128)S(1)} %get-tuple-element.133, ...), kind=kLoop, calls=%fused_computation.23 | loop fusion | flops 2949120 | bytes 6553656 | tf_op jit(solution)/shard_map/mul | solution.py:271
  (55 shorter events, 21.7 us)
Async XLA Ops:
  6.7 13.0 %copy-start.3 = (s32[2,5]{1,0:T(2,128)S(1)}, s32[2,5]{1,0:T(2,128)}, u32[]{:S(2)}) copy-start(s32[2,5]{1,0:T(2,128)} %param.31) | copy-start | bytes 124
  6.7 13.6 %copy-start.2 = (s32[2,5,11]{2,0,1:T(2,128)S(1)}, s32[2,5,11]{2,0,1:T(2,128)}, u32[]{:S(2)}) copy-start(s32[2,5,11]{2,0,1:T(2,128)} %param.30) | copy-start | bytes 1324
  8.3 26.4 %all-to-all-start = ((bf16[2,2,1,128,640]{4,1,0,2,3:T(2,128)(2,1)}), bf16[2,2,1,128,640]{4,1,0,2,3:T(2,128)(2,1)S(1)}, u32[]{:S(2)}, u32[]{:S(2)}) async-start(bf16[2,2,1,128,640]{4,1,0,2,3:T(2,128)(2,1)} %copy.14), calls=%async_computation | async-start | bytes 1310720 | tf_op jit(solution)/shard_map/all_to_all | solution.py:217
  50.7 17.4 %collective-permute-start = (f32[2,2,128,640]{3,2,1,0:T(8,128)S(1)}, f32[2,2,128,640]{3,2,1,0:T(8,128)S(1)}, u32[]{:S(2)}, u32[]{:S(2)}) collective-permute-start(f32[2,2,128,640]{3,2,1,0:T(8,128)S(1)} %get-tuple-element.144), channel_id=1, source_target_pairs={{0,1},{1,2},{2,3},{3,4},{4,5},{5,6},{6,7},{7,8},{8,9},{9,10},{10,1... | collective-permute-start | bytes 3932168 | tf_op jit(solution)/shard_map/ppermute | solution.py:36
  53.6 18.9 %collective-permute-start.1 = (f32[2,2,128,640]{3,2,1,0:T(8,128)S(1)}, f32[2,2,128,640]{3,2,1,0:T(8,128)S(1)}, u32[]{:S(2)}, u32[]{:S(2)}) collective-permute-start(f32[2,2,128,640]{3,2,1,0:T(8,128)S(1)} %get-tuple-element.145), channel_id=1, source_target_pairs={{1,0},{2,1},{3,2},{4,3},{5,4},{6,5},{7,6},{8,7},{9,8},{10,9},{11,1... | collective-permute-start | bytes 3932168 | tf_op jit(solution)/shard_map/ppermute | solution.py:36
  74.5 34.6 %collective-permute-start.3 = (bf16[2,2,128,640]{3,2,1,0:T(8,128)(2,1)S(1)}, bf16[2,2,128,640]{3,2,1,0:T(8,128)(2,1)S(1)}, u32[]{:S(2)}, u32[]{:S(2)}) collective-permute-start(bf16[2,2,128,640]{3,2,1,0:T(8,128)(2,1)S(1)} %get-tuple-element.138), channel_id=1, source_target_pairs={{1,0},{2,1},{3,2},{4,3},{5,4},{6,5},{7,6},{8,7},{9,8},{10,9},{11,1... | collective-permute-start | bytes 1966088 | tf_op jit(solution)/shard_map/ppermute | solution.py:26
  76.4 32.7 %collective-permute-start.2 = (bf16[2,2,128,640]{3,2,1,0:T(8,128)(2,1)S(1)}, bf16[2,2,128,640]{3,2,1,0:T(8,128)(2,1)}, u32[]{:S(2)}, u32[]{:S(2)}) collective-permute-start(bf16[2,2,128,640]{3,2,1,0:T(8,128)(2,1)S(1)} %get-tuple-element.138), channel_id=1, source_target_pairs={{0,1},{1,2},{2,3},{3,4},{4,5},{5,6},{6,7},{7,8},{8,9},{9,10},{10,1... | collective-permute-start | bytes 1966088 | tf_op jit(solution)/shard_map/ppermute | solution.py:24
  97.9 11.2 %all-to-all-start.2 = ((f32[32,1,2]{2,1,0:T(1,128)}), f32[32,1,2]{2,1,0:T(1,128)S(1)}, u32[]{:S(2)}, u32[]{:S(2)}) async-start(f32[32,1,2]{2,1,0:T(1,128)} %broadcast_in_dim.13), calls=%async_computation.2 | async-start | bytes 32768 | tf_op jit(solution)/shard_map/all_to_all | solution.py:57
  127.6 22.1 %copy-start = (f32[2,2,128,640]{3,2,1,0:T(8,128)}, f32[2,2,128,640]{3,2,1,0:T(8,128)S(1)}, u32[]{:S(2)}) copy-start(f32[2,2,128,640]{3,2,1,0:T(8,128)S(1)} %get-tuple-element.135) | copy-start | bytes 3932164
  144.3 24.1 %collective-permute-start.4 = (f32[2,2,128,640]{3,2,1,0:T(8,128)}, f32[2,2,128,640]{3,2,1,0:T(8,128)}, u32[]{:S(2)}, u32[]{:S(2)}) collective-permute-start(f32[2,2,128,640]{3,2,1,0:T(8,128)} %get-tuple-element.142), channel_id=1, source_target_pairs={{0,1},{1,2},{2,3},{3,4},{4,5},{5,6},{6,7},{7,8},{8,9},{9,10},{10,1... | collective-permute-start | bytes 3932168 | tf_op jit(solution)/shard_map/ppermute | solution.py:36
  146.8 21.6 %collective-permute-start.5 = (f32[2,2,128,640]{3,2,1,0:T(8,128)}, f32[2,2,128,640]{3,2,1,0:T(8,128)}, u32[]{:S(2)}, u32[]{:S(2)}) collective-permute-start(f32[2,2,128,640]{3,2,1,0:T(8,128)} %get-tuple-element.143), channel_id=1, source_target_pairs={{1,0},{2,1},{3,2},{4,3},{5,4},{6,5},{7,6},{8,7},{9,8},{10,9},{11,1... | collective-permute-start | bytes 3932168 | tf_op jit(solution)/shard_map/ppermute | solution.py:36
  171.3 20.6 %collective-permute-start.7 = (bf16[2,2,128,640]{3,2,1,0:T(8,128)(2,1)S(1)}, bf16[2,2,128,640]{3,2,1,0:T(8,128)(2,1)}, u32[]{:S(2)}, u32[]{:S(2)}) collective-permute-start(bf16[2,2,128,640]{3,2,1,0:T(8,128)(2,1)S(1)} %get-tuple-element.132), channel_id=1, source_target_pairs={{1,0},{2,1},{3,2},{4,3},{5,4},{6,5},{7,6},{8,7},{9,8},{10,9},{11,1... | collective-permute-start | bytes 1966088 | tf_op jit(solution)/shard_map/ppermute | solution.py:26
  173.9 18.0 %collective-permute-start.6 = (bf16[2,2,128,640]{3,2,1,0:T(8,128)(2,1)S(1)}, bf16[2,2,128,640]{3,2,1,0:T(8,128)(2,1)}, u32[]{:S(2)}, u32[]{:S(2)}) collective-permute-start(bf16[2,2,128,640]{3,2,1,0:T(8,128)(2,1)S(1)} %get-tuple-element.132), channel_id=1, source_target_pairs={{0,1},{1,2},{2,3},{3,4},{4,5},{5,6},{6,7},{7,8},{8,9},{9,10},{10,1... | collective-permute-start | bytes 1966088 | tf_op jit(solution)/shard_map/ppermute | solution.py:24
  224.7 8.9 %copy-start.1 = (f32[2,2,128,640]{3,2,1,0:T(8,128)S(1)}, f32[2,2,128,640]{3,2,1,0:T(8,128)}, u32[]{:S(2)}) copy-start(f32[2,2,128,640]{3,2,1,0:T(8,128)} %get-tuple-element.131) | copy-start | bytes 3932164
  228.2 24.1 %collective-permute-start.8 = (f32[2,2,128,640]{3,2,1,0:T(8,128)}, f32[2,2,128,640]{3,2,1,0:T(8,128)}, u32[]{:S(2)}, u32[]{:S(2)}) collective-permute-start(f32[2,2,128,640]{3,2,1,0:T(8,128)} %get-tuple-element.140), channel_id=1, source_target_pairs={{0,1},{1,2},{2,3},{3,4},{4,5},{5,6},{6,7},{7,8},{8,9},{9,10},{10,1... | collective-permute-start | bytes 3932168 | tf_op jit(solution)/shard_map/ppermute | solution.py:36
  230.7 21.6 %collective-permute-start.9 = (f32[2,2,128,640]{3,2,1,0:T(8,128)}, f32[2,2,128,640]{3,2,1,0:T(8,128)}, u32[]{:S(2)}, u32[]{:S(2)}) collective-permute-start(f32[2,2,128,640]{3,2,1,0:T(8,128)} %get-tuple-element.141), channel_id=1, source_target_pairs={{1,0},{2,1},{3,2},{4,3},{5,4},{6,5},{7,6},{8,7},{9,8},{10,9},{11,1... | collective-permute-start | bytes 3932168 | tf_op jit(solution)/shard_map/ppermute | solution.py:36

commit v5 on v4

--- a/solution.py
+++ b/solution.py
@@ -143,6 +143,88 @@
                 o_ref[part, :, pl.ds(start, block)] += product[:, lanes]
 
 
+def _both_kernel(
+    cols_ref, counts_ref, coef_ref, x_ref, q_ref, u_ref, m_ref, p_ref, o_ref, picked_ref
+):
+    freq = pl.program_id(0)
+    row = pl.program_id(1)
+    rows = pl.num_programs(1)
+    depth, width = m_ref.shape
+    block = depth // 2
+    slots = width // depth
+    index = freq * rows + row
+    count = counts_ref[index]
+
+    @pl.when(row == 0)
+    def _():
+        o_ref[...] = jnp.zeros(o_ref.shape, o_ref.dtype)
+
+    for slot in range(slots):
+        start = pl.multiple_of(cols_ref[index * slots + slot] * block, block)
+        for part in range(2):
+            taken = x_ref[part, :, pl.ds(start, block)]
+            lanes = slice((2 * slot + part) * block, (2 * slot + part + 1) * block)
+            picked_ref[:, lanes] = jnp.where(slot < count, taken, jnp.zeros_like(taken))
+    contract = (((1,), (1,)), ((), ()))
+    product = lax.dot_general(
+        picked_ref[...], m_ref[...], contract, preferred_element_type=jnp.float32
+    )
+    scale = coef_ref[2 * freq]
+    shift = coef_ref[2 * freq + 1]
+    for part in range(2):
+        lanes = slice(part * block, (part + 1) * block)
+        p_ref[part] = (q_ref[part] + product[:, lanes]) / scale - shift * u_ref[part]
+    field = jnp.concatenate(
+        [p_ref[0].astype(jnp.bfloat16), p_ref[1].astype(jnp.bfloat16)], axis=1
+    )
+    spread = jnp.dot(field, m_ref[...], preferred_element_type=jnp.float32)
+    for slot in range(slots):
+
+        @pl.when(slot < count)
+        def _():
+            start = pl.multiple_of(cols_ref[index * slots + slot] * block, block)
+            for part in range(2):
+                lanes = slice((2 * slot + part) * block, (2 * slot + part + 1) * block)
+                o_ref[part, :, pl.ds(start, block)] += spread[:, lanes]
+
+
+def apply_both(extended, raw, left, coefs, stacked, cols, counts):
+    local_freqs, local_blocks, depth, width = stacked.shape
+    block_size = depth // 2
+    _, _, sources, span = extended.shape
+    own = pl.BlockSpec((2, None, sources, block_size), lambda f, r, c, n: (0, f, 0, r))
+    grid_spec = pltpu.PrefetchScalarGridSpec(
+        num_scalar_prefetch=2,
+        grid=(local_freqs, local_blocks),
+        in_specs=[
+            pl.BlockSpec(memory_space=pltpu.SMEM),
+            pl.BlockSpec((2, None, sources, span), lambda f, r, c, n: (0, f, 0, 0)),
+            own,
+            own,
+            pl.BlockSpec((None, None, depth, width), lambda f, r, c, n: (f, r, 0, 0)),
+        ],
+        out_specs=[
+            own,
+            pl.BlockSpec((2, None, sources, span), lambda f, r, c, n: (0, f, 0, 0)),
+        ],
+        scratch_shapes=[pltpu.VMEM((sources, width), jnp.bfloat16)],
+    )
+    return pl.pallas_call(
+        _both_kernel,
+        grid_spec=grid_spec,
+        out_shape=[
+            jax.ShapeDtypeStruct(raw.shape, jnp.float32),
+            jax.ShapeDtypeStruct((2, local_freqs, sources, span), jnp.float32),
+        ],
+        compiler_params=pltpu.CompilerParams(dimension_semantics=("arbitrary", "arbitrary")),
+        cost_estimate=pl.CostEstimate(
+            flops=4 * local_freqs * local_blocks * sources * depth * width,
+            transcendentals=0,
+            bytes_accessed=stacked.size * 2 + extended.size * 2 + raw.size * 40,
+        ),
+    )(cols, counts, coefs, extended, raw, left, stacked)
+
+
 def apply_forward(extended, stacked, cols, counts):
     local_freqs, local_blocks, depth, width = stacked.shape
     block_size = depth // 2
@@ -223,9 +305,7 @@
     counts = jnp.clip(block_counts, 0, slot_count).reshape(-1)
     stacked = stack_blocks(down_blocks)
 
-    def adjoint(field):
-        rounded = field.astype(jnp.bfloat16)
-        spread = apply_adjoint(rounded, stacked, columns, counts, span_blocks * block_size)
+    def exchange(spread):
         lower_rim = spread[..., :rim_rows]
         middle = spread[..., rim_rows : rim_rows + local_rows]
         upper_rim = spread[..., rim_rows + local_rows :]
@@ -233,7 +313,20 @@
         from_below = from_behind(upper_rim, "rcv", 1)
         middle = middle.at[..., :rim_rows].add(from_below)
         middle = middle.at[..., local_rows - rim_rows :].add(from_above)
-        return field + middle
+        return middle
+
+    def adjoint(field):
+        rounded = field.astype(jnp.bfloat16)
+        spread = apply_adjoint(rounded, stacked, columns, counts, span_blocks * block_size)
+        return field + exchange(spread)
+
+    def forward_adjoint(raw, scale, left, shift):
+        extended = with_halo(raw.astype(jnp.bfloat16), (("rcv", 3),), rim_rows)
+        coefs = jnp.stack(
+            [jnp.broadcast_to(scale, shift.shape).reshape(-1), shift.reshape(-1)], axis=1
+        ).reshape(-1)
+        residual, spread = apply_both(extended, raw, left, coefs, stacked, columns, counts)
+        return residual, residual + exchange(spread)
 
     def forward(field):
         extended = with_halo(field.astype(jnp.bfloat16), (("rcv", 3),), rim_rows)
@@ -251,10 +344,10 @@
     phibar = beta_norm
     rhobar = alpha_norm
     for iteration in range(ITERS):
-        residual_left = forward(right_raw) / right_scale - alpha_norm * left_vector
+        residual_left, lifted = forward_adjoint(right_raw, right_scale, left_vector, alpha_norm)
         beta_norm = jnp.sqrt(squares(residual_left) + EPSILON)
         left_vector = residual_left / beta_norm
-        residual_right = adjoint(residual_left) / beta_norm - beta_norm * right_vector
+        residual_right = lifted / beta_norm - beta_norm * right_vector
         alpha_norm = jnp.sqrt(squares(residual_right) + EPSILON)
         right_raw = residual_right
         right_scale = alpha_norm

time: 276 us -> 248 us (0.90)
  waiting for transfers between devices: 26.8 us -> 2.77 us
  blocking collectives: 82.2 us -> 99.2 us
  Pallas kernels: 77.5 us -> 62.1 us
  starting transfers between devices: 42.3 us -> 38.4 us
  other arithmetic: 24.9 us -> 21.7 us
    pallas_call x3 -> x1, Pallas kernels: 39.9 us -> 13.2 us  [apply_adjoint(): pl.pallas_call(_adjoint_kernel, grid_spec=grid_spec, out_shape=jax.ShapeD...]
    ppermute x6, waiting for transfers between devices: 17 us -> 0.02 us  [from_behind(): lax.ppermute(value, axis, [(source, source + steps) for source in range(f...]
    all_to_all x5 -> x6, blocking collectives: 82.2 us -> 99.2 us  [rcv_sum(): gathered = lax.all_to_all(spread, 'rcv', 0, 0, tiled=False)]
    pallas_call x2, Pallas kernels: 26.9 us -> 38.1 us  [apply_both(): pl.pallas_call(_both_kernel, grid_spec=grid_spec, out_shape=[jax.ShapeDty...]
    all_to_all x1 -> x0, waiting for transfers between devices: 6.96 us -> none  [rcv_sum(): gathered = lax.all_to_all(spread, 'rcv', 0, 0, tiled=False)]
    all_to_all x1 -> x0, starting transfers between devices: 4.14 us -> none  [rcv_sum(): gathered = lax.all_to_all(spread, 'rcv', 0, 0, tiled=False)]
    convert_element_type x4 -> x2, other arithmetic: 10.7 us -> 7.51 us  [forward_adjoint(): extended = with_halo(raw.astype(jnp.bfloat16), (('rcv', 3),), rim_rows)]
  transfers between devices with their start and end apart: 12 -> 11, of which waited for: 4 -> 1; matrix products, arithmetic and copies ran while one was open for 1% -> 2% of each run, Pallas kernels for 4% -> 4%
where the time goes in v5:
time: 248 us; the launch traced here: 246 us
  blocking collectives  99.2 us (40%)
  Pallas kernels  62.1 us (25%)
  starting transfers between devices  38.4 us (15%)
  other arithmetic  21.7 us (9%)
  local copies, waits for them, and re-layouts  15.8 us (6%)
  matrix products  5.45 us (2%)
  waiting for transfers between devices  2.77 us (1%)
    all_to_all x6, blocking collectives, rcv_sum(): gathered = lax.all_to_all(spread, 'rcv', 0, 0, tiled=False)  99.2 us
    pallas_call x2, Pallas kernels, apply_both(): pl.pallas_call(_both_kernel, grid_spec=grid_spec, out_shape=[jax.ShapeDty...  38.1 us
    ppermute x6, starting transfers between devices, from_behind(): lax.ppermute(value, axis, [(source, source + steps) for source in range(f...  15.7 us
    pallas_call x1, Pallas kernels, apply_adjoint(): pl.pallas_call(_adjoint_kernel, grid_spec=grid_spec, out_shape=jax.ShapeD...  13.2 us
    all_to_all x1, starting transfers between devices, body(): lax.all_to_all(spectrum, ('freq', 'rcv'), split_axis=3, concat_axis=2, ti...  11.5 us
    pallas_call x1, Pallas kernels, stack_blocks(): pl.pallas_call(_stack_kernel, grid=(local_freqs, local_blocks), in_specs=...  10.7 us
    slice x3, local copies, waits for them, and re-layouts, exchange(): upper_rim = spread[..., rim_rows + local_rows:]  8.93 us
    convert_element_type x2, other arithmetic, forward_adjoint(): extended = with_halo(raw.astype(jnp.bfloat16), (('rcv', 3),), rim_rows)  7.51 us
  transfers between devices with their start and end apart: 11, of which 1 were waited for; matrix products, arithmetic and copies ran while one was open for 2% of the time, Pallas kernels for 4%

profile of v5, /device:TPU:1, one launch (start us, length us, event | category | flops | bytes accessed | tf_op | source)
XLA Modules:
  0.0 246.3 jit_solution(11349673777890701801)
XLA Ops:
  0.8 5.5 %fusion = bf16[2,2,1,4,20480]{4,3,1,0,2:T(4,128)(2,1)S(1)} fusion(bf16[1,256,20480]{2,1,0:T(8,128)(2,1)} %param.28, bf16[256,1,4,2]{0,2,3,1:T(4,128)(2,1)S(1)} %get-tuple-element.161, bf16[256,1,4,2]{0,2,3,1:T(4,128)(2,1)S(1)} %get-tuple-element.160), kind=kOutput, calls=%fused_computation.1 | convolution fusion | flops 168116224 | bytes 11149312 | tf_op jit(solution)/shard_map/snr,ncgf->cfsgr/dot_general | solution.py:293
  6.8 1.5 copy.22
  8.3 11.5 %all-to-all-start = ((bf16[2,2,1,128,640]{4,1,0,2,3:T(2,128)(2,1)}), bf16[2,2,1,128,640]{4,1,0,2,3:T(2,128)(2,1)S(1)}, u32[]{:S(2)}, u32[]{:S(2)}) async-start(bf16[2,2,1,128,640]{4,1,0,2,3:T(2,128)(2,1)} %copy.22), calls=%async_computation | async-start | bytes 1310720 | tf_op jit(solution)/shard_map/all_to_all | solution.py:299
  21.1 10.7 %shard_map.89.m_ref = bf16[2,5,256,2816]{3,2,1,0:T(8,128)(2,1)} custom-call(bf16[2,5,11,2,128,128]{5,4,3,2,1,0:T(8,128)(2,1)} %a_ref.1), custom_call_target="tpu_custom_call" | custom-call | tf_op jit(solution)/shard_map/pallas_call | solution.py:81
  31.9 2.7 %all-to-all-done = bf16[2,2,1,128,640]{4,1,0,2,3:T(2,128)(2,1)S(1)} async-done(((bf16[2,2,1,128,640]{4,1,0,2,3:T(2,128)(2,1)}), bf16[2,2,1,128,640]{4,1,0,2,3:T(2,128)(2,1)S(1)}, u32[]{:S(2)}, u32[]{:S(2)}) %all-to-all-start) | async-done | bytes 655392 | tf_op jit(solution)/shard_map/all_to_all | solution.py:299
  35.5 13.2 %shard_map.90 = f32[2,2,128,1920]{3,2,1,0:T(8,128)} custom-call(s32[110]{0:T(128)} %reshape.548.cols_ref, s32[10]{0:T(128)} %reshape.549.counts_ref, bf16[2,2,128,640]{3,2,1,0:T(8,128)(2,1)} %bitcast.40, bf16[2,5,256,2816]{3,2,1,0:T(8,128)(2,1)} %shard_map.89.m_ref), custom_call_target="tpu_custom_call" | custom-call | flops 1845493760 | bytes 19005440 | tf_op jit(solution)/shard_map/pallas_call | solution.py:270
  48.7 1.9 fusion.21
  50.6 3.0 %collective-permute-start = (f32[2,2,128,640]{3,2,1,0:T(8,128)S(1)}, f32[2,2,128,640]{3,2,1,0:T(8,128)}, u32[]{:S(2)}, u32[]{:S(2)}) collective-permute-start(f32[2,2,128,640]{3,2,1,0:T(8,128)S(1)} %get-tuple-element.148), channel_id=1, source_target_pairs={{0,1},{1,2},{2,3},{3,4},{4,5},{5,6},{6,7},{7,8},{8,9},{9,10},{10,1... | collective-permute-start | bytes 3932168 | tf_op jit(solution)/shard_map/ppermute | solution.py:36
  53.6 2.5 %collective-permute-start.1 = (f32[2,2,128,640]{3,2,1,0:T(8,128)S(1)}, f32[2,2,128,640]{3,2,1,0:T(8,128)}, u32[]{:S(2)}, u32[]{:S(2)}) collective-permute-start(f32[2,2,128,640]{3,2,1,0:T(8,128)S(1)} %get-tuple-element.149), channel_id=1, source_target_pairs={{1,0},{2,1},{3,2},{4,3},{5,4},{6,5},{7,6},{8,7},{9,8},{10,9},{11,1... | collective-permute-start | bytes 3932168 | tf_op jit(solution)/shard_map/ppermute | solution.py:36
  56.4 18.7 %all_to_all.45 = f32[32,1,2]{2,1,0:T(1,128)S(1)} all-to-all(f32[32,1,2]{2,1,0:T(1,128)S(1)} %broadcast_in_dim.13), channel_id=1, replica_groups=mesh['freq'=4,'rcv'=32] {'rcv'}, dimensions={0} | all-to-all | bytes 512 | tf_op jit(solution)/shard_map/all_to_all | solution.py:57
  75.2 3.5 %fusion.18 = (bf16[2,2,128,640]{3,2,1,0:T(8,128)(2,1)S(1)}, f32[2,2,128,640]{3,2,1,0:T(8,128)S(1)}, f32[2,2,128,640]{3,2,1,0:T(8,128)}) fusion(f32[2,2,128,640]{3,2,1,0:T(8,128)} %collective-permute-done.1, f32[2,2,128,640]{3,2,1,0:T(8,128)} %collective-permute-done, f32[2,2,128,1920]{3,2,1,0:T(8,128)} %shard_map.90, ...), kind=kLoop, calls=%fused_computation.64 | loop fusion | flops 1966080 | bytes 7864328 | tf_op jit(solution)/shard_map/convert_element_type | solution.py:324
  78.7 2.6 %collective-permute-start.3 = (bf16[2,2,128,640]{3,2,1,0:T(8,128)(2,1)S(1)}, bf16[2,2,128,640]{3,2,1,0:T(8,128)(2,1)S(1)}, u32[]{:S(2)}, u32[]{:S(2)}) collective-permute-start(bf16[2,2,128,640]{3,2,1,0:T(8,128)(2,1)S(1)} %get-tuple-element.142), channel_id=1, source_target_pairs={{1,0},{2,1},{3,2},{4,3},{5,4},{6,5},{7,6},{8,7},{9,8},{10,9},{11,1... | collective-permute-start | bytes 1966088 | tf_op jit(solution)/shard_map/ppermute | solution.py:26
  81.3 3.1 %collective-permute-start.2 = (bf16[2,2,128,640]{3,2,1,0:T(8,128)(2,1)S(1)}, bf16[2,2,128,640]{3,2,1,0:T(8,128)(2,1)S(1)}, u32[]{:S(2)}, u32[]{:S(2)}) collective-permute-start(bf16[2,2,128,640]{3,2,1,0:T(8,128)(2,1)S(1)} %get-tuple-element.142), channel_id=1, source_target_pairs={{0,1},{1,2},{2,3},{3,4},{4,5},{5,6},{6,7},{7,8},{8,9},{9,10},{10,1... | collective-permute-start | bytes 1966088 | tf_op jit(solution)/shard_map/ppermute | solution.py:24
  84.6 14.4 %all_to_all.46 = f32[32,1,2]{2,1,0:T(1,128)S(1)} all-to-all(f32[32,1,2]{2,1,0:T(1,128)S(1)} %broadcast_in_dim.12), channel_id=1, replica_groups=mesh['freq'=4,'rcv'=32] {'rcv'}, dimensions={0} | all-to-all | bytes 512 | tf_op jit(solution)/shard_map/all_to_all | solution.py:57
  101.4 19.1 %shard_map.91 = (f32[2,2,128,640]{3,2,1,0:T(8,128)}, f32[2,2,128,1920]{3,2,1,0:T(8,128)}) custom-call(s32[110]{0:T(128)} %reshape.548.cols_ref, s32[10]{0:T(128)} %reshape.549.counts_ref, f32[4]{0:T(128)} %reshape.550.coef_ref, bf16[2,2,128,1920]{3,2,1,0:T(8,128)(2,1)} %pad_maximum_fusion.x_ref, f32[2,2,128,640]{3,2,1,0:T(8,128)} %copy-done, ...), custom_call_target="tpu_custom_call" | custom-call | flops 3690987520 | bytes 29491200 | tf_op jit(solution)/shard_map/pallas_call | solution.py:212
  120.4 3.5 %fusion.20 = (f32[2,2,128,640]{3,2,1,0:T(8,128)}, f32[2,2,128,640]{3,2,1,0:T(8,128)}) fusion(f32[2,2,128,1920]{3,2,1,0:T(8,128)} %get-tuple-element.127), kind=kLoop, calls=%fused_computation.66 | loop fusion | bytes 5242880 | tf_op jit(solution)/shard_map/slice | solution.py:311
  123.9 2.8 %collective-permute-start.4 = (f32[2,2,128,640]{3,2,1,0:T(8,128)}, f32[2,2,128,640]{3,2,1,0:T(8,128)S(1)}, u32[]{:S(2)}, u32[]{:S(2)}) collective-permute-start(f32[2,2,128,640]{3,2,1,0:T(8,128)} %get-tuple-element.146), channel_id=1, source_target_pairs={{0,1},{1,2},{2,3},{3,4},{4,5},{5,6},{6,7},{7,8},{8,9},{9,10},{10,1... | collective-permute-start | bytes 3932168 | tf_op jit(solution)/shard_map/ppermute | solution.py:36
  126.7 1.9 collective-permute-start.5
  129.0 19.3 %all_to_all.47 = f32[32,1,2]{2,1,0:T(1,128)S(1)} all-to-all(f32[32,1,2]{2,1,0:T(1,128)S(1)} %broadcast_in_dim.14), channel_id=1, replica_groups=mesh['freq'=4,'rcv'=32] {'rcv'}, dimensions={0} | all-to-all | bytes 512 | tf_op jit(solution)/shard_map/all_to_all | solution.py:57
  149.4 4.0 %fusion.17 = (bf16[2,2,128,640]{3,2,1,0:T(8,128)(2,1)S(1)}, f32[2,2,128,640]{3,2,1,0:T(8,128)S(1)}, f32[2,2,128,640]{3,2,1,0:T(8,128)}) fusion(f32[2,2,128,640]{3,2,1,0:T(8,128)S(1)} %copy-done.1, f32[2]{0:T(128)S(1)} %get-tuple-element.140, f32[2]{0:T(128)S(1)} %get-tuple-element.162, f32[2,2,128,640]{3,2,1,0:T(8,128)} %get-tuple-element.126, ...), kind=kLoop, calls=%fused_computation.63 | loop fusion | flops 2949120 | bytes 9830416 | tf_op jit(solution)/shard_map/convert_element_type | solution.py:324
  153.4 2.6 %collective-permute-start.7 = (bf16[2,2,128,640]{3,2,1,0:T(8,128)(2,1)S(1)}, bf16[2,2,128,640]{3,2,1,0:T(8,128)(2,1)}, u32[]{:S(2)}, u32[]{:S(2)}) collective-permute-start(bf16[2,2,128,640]{3,2,1,0:T(8,128)(2,1)S(1)} %get-tuple-element.138), channel_id=1, source_target_pairs={{1,0},{2,1},{3,2},{4,3},{5,4},{6,5},{7,6},{8,7},{9,8},{10,9},{11,1... | collective-permute-start | bytes 1966088 | tf_op jit(solution)/shard_map/ppermute | solution.py:26
  155.9 3.1 %collective-permute-start.6 = (bf16[2,2,128,640]{3,2,1,0:T(8,128)(2,1)S(1)}, bf16[2,2,128,640]{3,2,1,0:T(8,128)(2,1)}, u32[]{:S(2)}, u32[]{:S(2)}) collective-permute-start(bf16[2,2,128,640]{3,2,1,0:T(8,128)(2,1)S(1)} %get-tuple-element.138), channel_id=1, source_target_pairs={{0,1},{1,2},{2,3},{3,4},{4,5},{5,6},{6,7},{7,8},{8,9},{9,10},{10,1... | collective-permute-start | bytes 1966088 | tf_op jit(solution)/shard_map/ppermute | solution.py:24
  159.3 14.4 %all_to_all.48 = f32[32,1,2]{2,1,0:T(1,128)S(1)} all-to-all(f32[32,1,2]{2,1,0:T(1,128)S(1)} %broadcast_in_dim.15), channel_id=1, replica_groups=mesh['freq'=4,'rcv'=32] {'rcv'}, dimensions={0} | all-to-all | bytes 512 | tf_op jit(solution)/shard_map/all_to_all | solution.py:57
  174.5 2.8 %pad_maximum_fusion.1.x_ref = bf16[2,2,128,1920]{3,2,1,0:T(8,128)(2,1)} fusion(bf16[2,2,128,640]{3,2,1,0:T(8,128)(2,1)} %collective-permute-done.7, bf16[2,2,128,640]{3,2,1,0:T(8,128)(2,1)S(1)} %get-tuple-element.138, bf16[2,2,128,640]{3,2,1,0:T(8,128)(2,1)} %collective-permute-done.6), kind=kLoop, calls=%fused_computation.4 | loop fusion | flops 5898240 | bytes 3932160 | tf_op jit(solution)/shard_map/concatenate | solution.py:22
  177.3 19.1 %shard_map.92 = (f32[2,2,128,640]{3,2,1,0:T(8,128)}, f32[2,2,128,1920]{3,2,1,0:T(8,128)}) custom-call(s32[110]{0:T(128)} %reshape.548.cols_ref, s32[10]{0:T(128)} %reshape.549.counts_ref, f32[4]{0:T(128)} %reshape.551.coef_ref, bf16[2,2,128,1920]{3,2,1,0:T(8,128)(2,1)} %pad_maximum_fusion.1.x_ref, f32[2,2,128,640]{3,2,1,0:T(8,128)} %copy-done.2, ...), custom_call_target="tpu_custom_call" | custom-call | flops 3690987520 | bytes 29491200 | tf_op jit(solution)/shard_map/pallas_call | solution.py:212
  196.3 3.5 %fusion.19 = (f32[2,2,128,640]{3,2,1,0:T(8,128)}, f32[2,2,128,640]{3,2,1,0:T(8,128)}) fusion(f32[2,2,128,1920]{3,2,1,0:T(8,128)} %get-tuple-element.129), kind=kLoop, calls=%fused_computation.65 | loop fusion | bytes 5242880 | tf_op jit(solution)/shard_map/slice | solution.py:311
  199.9 2.8 %collective-permute-start.8 = (f32[2,2,128,640]{3,2,1,0:T(8,128)}, f32[2,2,128,640]{3,2,1,0:T(8,128)}, u32[]{:S(2)}, u32[]{:S(2)}) collective-permute-start(f32[2,2,128,640]{3,2,1,0:T(8,128)} %get-tuple-element.144), channel_id=1, source_target_pairs={{0,1},{1,2},{2,3},{3,4},{4,5},{5,6},{6,7},{7,8},{8,9},{9,10},{10,1... | collective-permute-start | bytes 3932168 | tf_op jit(solution)/shard_map/ppermute | solution.py:36
  202.7 2.7 %collective-permute-start.9 = (f32[2,2,128,640]{3,2,1,0:T(8,128)}, f32[2,2,128,640]{3,2,1,0:T(8,128)}, u32[]{:S(2)}, u32[]{:S(2)}) collective-permute-start(f32[2,2,128,640]{3,2,1,0:T(8,128)} %get-tuple-element.145), channel_id=1, source_target_pairs={{1,0},{2,1},{3,2},{4,3},{5,4},{6,5},{7,6},{8,7},{9,8},{10,9},{11,1... | collective-permute-start | bytes 3932168 | tf_op jit(solution)/shard_map/ppermute | solution.py:36
  205.7 18.4 %all_to_all.49 = f32[32,1,2]{2,1,0:T(1,128)S(1)} all-to-all(f32[32,1,2]{2,1,0:T(1,128)S(1)} %broadcast_in_dim.16), channel_id=1, replica_groups=mesh['freq'=4,'rcv'=32] {'rcv'}, dimensions={0} | all-to-all | bytes 512 | tf_op jit(solution)/shard_map/all_to_all | solution.py:57
  224.2 4.0 %multiply_reduce_fusion = (f32[2]{0:T(128)S(1)}, f32[2,2,128,640]{3,2,1,0:T(8,128)}) fusion(f32[2,2,128,640]{3,2,1,0:T(8,128)S(1)} %copy-done.3, f32[2]{0:T(128)S(1)} %get-tuple-element.159, f32[2]{0:T(128)S(1)} %add_sqrt_fusion.2, f32[2,2,128,640]{3,2,1,0:T(8,128)} %get-tuple-element.128, f32[2,2,128,640]{3,2,1,0:T(8,128)} %collective-permute-done.9, ...), kind=kLoop, calls=%fused_computation.12 | loop fusion | flops 2949118 | bytes 7864344 | tf_op jit(solution)/shard_map/reduce_sum | solution.py:62
  228.2 14.0 %all_to_all.50 = f32[32,1,2]{2,1,0:T(1,128)S(1)} all-to-all(f32[32,1,2]{2,1,0:T(1,128)S(1)} %broadcast_in_dim.17), channel_id=1, replica_groups=mesh['freq'=4,'rcv'=32] {'rcv'}, dimensions={0} | all-to-all | bytes 512 | tf_op jit(solution)/shard_map/all_to_all | solution.py:57
  242.3 2.6 %divide_multiply_fusion = f32[2,2,128,640]{3,2,1,0:T(8,128)} fusion(f32[2,2,128,640]{3,2,1,0:T(8,128)} %get-tuple-element.137, f32[2]{0:T(128)S(1)} %get-tuple-element.154, f32[2]{0:T(128)S(1)} %get-tuple-element.130), kind=kLoop, calls=%fused_computation.11 | loop fusion | flops 655360 | bytes 2621456 | tf_op jit(solution)/shard_map/mul | solution.py:364
  (69 shorter events, 10.3 us)
Async XLA Ops:
  6.7 13.0 %copy-start.8 = (s32[2,5]{1,0:T(2,128)S(1)}, s32[2,5]{1,0:T(2,128)}, u32[]{:S(2)}) copy-start(s32[2,5]{1,0:T(2,128)} %param.31) | copy-start | bytes 124
  6.7 13.7 %copy-start.7 = (s32[2,5,11]{2,0,1:T(2,128)S(1)}, s32[2,5,11]{2,0,1:T(2,128)}, u32[]{:S(2)}) copy-start(s32[2,5,11]{2,0,1:T(2,128)} %param.30) | copy-start | bytes 1324
  8.3 26.4 %all-to-all-start = ((bf16[2,2,1,128,640]{4,1,0,2,3:T(2,128)(2,1)}), bf16[2,2,1,128,640]{4,1,0,2,3:T(2,128)(2,1)S(1)}, u32[]{:S(2)}, u32[]{:S(2)}) async-start(bf16[2,2,1,128,640]{4,1,0,2,3:T(2,128)(2,1)} %copy.22), calls=%async_computation | async-start | bytes 1310720 | tf_op jit(solution)/shard_map/all_to_all | solution.py:299
  50.6 24.6 %collective-permute-start = (f32[2,2,128,640]{3,2,1,0:T(8,128)S(1)}, f32[2,2,128,640]{3,2,1,0:T(8,128)}, u32[]{:S(2)}, u32[]{:S(2)}) collective-permute-start(f32[2,2,128,640]{3,2,1,0:T(8,128)S(1)} %get-tuple-element.148), channel_id=1, source_target_pairs={{0,1},{1,2},{2,3},{3,4},{4,5},{5,6},{6,7},{7,8},{8,9},{9,10},{10,1... | collective-permute-start | bytes 3932168 | tf_op jit(solution)/shard_map/ppermute | solution.py:36
  53.6 21.6 %collective-permute-start.1 = (f32[2,2,128,640]{3,2,1,0:T(8,128)S(1)}, f32[2,2,128,640]{3,2,1,0:T(8,128)}, u32[]{:S(2)}, u32[]{:S(2)}) collective-permute-start(f32[2,2,128,640]{3,2,1,0:T(8,128)S(1)} %get-tuple-element.149), channel_id=1, source_target_pairs={{1,0},{2,1},{3,2},{4,3},{5,4},{6,5},{7,6},{8,7},{9,8},{10,9},{11,1... | collective-permute-start | bytes 3932168 | tf_op jit(solution)/shard_map/ppermute | solution.py:36
  78.7 22.6 %copy-start = (f32[2,2,128,640]{3,2,1,0:T(8,128)}, f32[2,2,128,640]{3,2,1,0:T(8,128)S(1)}, u32[]{:S(2)}) copy-start(f32[2,2,128,640]{3,2,1,0:T(8,128)S(1)} %get-tuple-element.143.q_ref) | copy-start | bytes 3932164
  78.7 21.1 %collective-permute-start.3 = (bf16[2,2,128,640]{3,2,1,0:T(8,128)(2,1)S(1)}, bf16[2,2,128,640]{3,2,1,0:T(8,128)(2,1)S(1)}, u32[]{:S(2)}, u32[]{:S(2)}) collective-permute-start(bf16[2,2,128,640]{3,2,1,0:T(8,128)(2,1)S(1)} %get-tuple-element.142), channel_id=1, source_target_pairs={{1,0},{2,1},{3,2},{4,3},{5,4},{6,5},{7,6},{8,7},{9,8},{10,9},{11,1... | collective-permute-start | bytes 1966088 | tf_op jit(solution)/shard_map/ppermute | solution.py:26
  81.3 18.6 %collective-permute-start.2 = (bf16[2,2,128,640]{3,2,1,0:T(8,128)(2,1)S(1)}, bf16[2,2,128,640]{3,2,1,0:T(8,128)(2,1)S(1)}, u32[]{:S(2)}, u32[]{:S(2)}) collective-permute-start(bf16[2,2,128,640]{3,2,1,0:T(8,128)(2,1)S(1)} %get-tuple-element.142), channel_id=1, source_target_pairs={{0,1},{1,2},{2,3},{3,4},{4,5},{5,6},{6,7},{7,8},{8,9},{9,10},{10,1... | collective-permute-start | bytes 1966088 | tf_op jit(solution)/shard_map/ppermute | solution.py:24
  120.4 8.2 %copy-start.4 = (f32[2,2,128,640]{3,2,1,0:T(8,128)S(1)}, f32[2,2,128,640]{3,2,1,0:T(8,128)}, u32[]{:S(2)}) copy-start(f32[2,2,128,640]{3,2,1,0:T(8,128)} %get-tuple-element.126) | copy-start | bytes 3932164
  123.9 25.4 %copy-start.1 = (f32[2,2,128,640]{3,2,1,0:T(8,128)S(1)}, f32[2,2,128,640]{3,2,1,0:T(8,128)}, u32[]{:S(2)}) copy-start(f32[2,2,128,640]{3,2,1,0:T(8,128)} %copy-done) | copy-start | bytes 3932164
  123.9 24.3 %collective-permute-start.4 = (f32[2,2,128,640]{3,2,1,0:T(8,128)}, f32[2,2,128,640]{3,2,1,0:T(8,128)S(1)}, u32[]{:S(2)}, u32[]{:S(2)}) collective-permute-start(f32[2,2,128,640]{3,2,1,0:T(8,128)} %get-tuple-element.146), channel_id=1, source_target_pairs={{0,1},{1,2},{2,3},{3,4},{4,5},{5,6},{6,7},{7,8},{8,9},{9,10},{10,1... | collective-permute-start | bytes 3932168 | tf_op jit(solution)/shard_map/ppermute | solution.py:36
  126.7 21.6 %collective-permute-start.5 = (f32[2,2,128,640]{3,2,1,0:T(8,128)}, f32[2,2,128,640]{3,2,1,0:T(8,128)}, u32[]{:S(2)}, u32[]{:S(2)}) collective-permute-start(f32[2,2,128,640]{3,2,1,0:T(8,128)} %get-tuple-element.147), channel_id=1, source_target_pairs={{1,0},{2,1},{3,2},{4,3},{5,4},{6,5},{7,6},{8,7},{9,8},{10,9},{11,1... | collective-permute-start | bytes 3932168 | tf_op jit(solution)/shard_map/ppermute | solution.py:36
  148.3 1.1 copy-start.6
  153.4 23.9 %copy-start.2 = (f32[2,2,128,640]{3,2,1,0:T(8,128)}, f32[2,2,128,640]{3,2,1,0:T(8,128)S(1)}, u32[]{:S(2)}) copy-start(f32[2,2,128,640]{3,2,1,0:T(8,128)S(1)} %get-tuple-element.139.q_ref) | copy-start | bytes 3932164
  153.4 21.1 %collective-permute-start.7 = (bf16[2,2,128,640]{3,2,1,0:T(8,128)(2,1)S(1)}, bf16[2,2,128,640]{3,2,1,0:T(8,128)(2,1)}, u32[]{:S(2)}, u32[]{:S(2)}) collective-permute-start(bf16[2,2,128,640]{3,2,1,0:T(8,128)(2,1)S(1)} %get-tuple-element.138), channel_id=1, source_target_pairs={{1,0},{2,1},{3,2},{4,3},{5,4},{6,5},{7,6},{8,7},{9,8},{10,9},{11,1... | collective-permute-start | bytes 1966088 | tf_op jit(solution)/shard_map/ppermute | solution.py:26
  155.9 18.6 %collective-permute-start.6 = (bf16[2,2,128,640]{3,2,1,0:T(8,128)(2,1)S(1)}, bf16[2,2,128,640]{3,2,1,0:T(8,128)(2,1)}, u32[]{:S(2)}, u32[]{:S(2)}) collective-permute-start(bf16[2,2,128,640]{3,2,1,0:T(8,128)(2,1)S(1)} %get-tuple-element.138), channel_id=1, source_target_pairs={{0,1},{1,2},{2,3},{3,4},{4,5},{5,6},{6,7},{7,8},{8,9},{9,10},{10,1... | collective-permute-start | bytes 1966088 | tf_op jit(solution)/shard_map/ppermute | solution.py:24
  196.3 9.1 %copy-start.5 = (f32[2,2,128,640]{3,2,1,0:T(8,128)S(1)}, f32[2,2,128,640]{3,2,1,0:T(8,128)}, u32[]{:S(2)}) copy-start(f32[2,2,128,640]{3,2,1,0:T(8,128)} %get-tuple-element.128) | copy-start | bytes 3932164
  199.9 24.4 %copy-start.3 = (f32[2,2,128,640]{3,2,1,0:T(8,128)S(1)}, f32[2,2,128,640]{3,2,1,0:T(8,128)}, u32[]{:S(2)}) copy-start(f32[2,2,128,640]{3,2,1,0:T(8,128)} %copy-done.2) | copy-start | bytes 3932164
  199.9 24.3 %collective-permute-start.8 = (f32[2,2,128,640]{3,2,1,0:T(8,128)}, f32[2,2,128,640]{3,2,1,0:T(8,128)}, u32[]{:S(2)}, u32[]{:S(2)}) collective-permute-start(f32[2,2,128,640]{3,2,1,0:T(8,128)} %get-tuple-element.144), channel_id=1, source_target_pairs={{0,1},{1,2},{2,3},{3,4},{4,5},{5,6},{6,7},{7,8},{8,9},{9,10},{10,1... | collective-permute-start | bytes 3932168 | tf_op jit(solution)/shard_map/ppermute | solution.py:36
  202.7 21.5 %collective-permute-start.9 = (f32[2,2,128,640]{3,2,1,0:T(8,128)}, f32[2,2,128,640]{3,2,1,0:T(8,128)}, u32[]{:S(2)}, u32[]{:S(2)}) collective-permute-start(f32[2,2,128,640]{3,2,1,0:T(8,128)} %get-tuple-element.145), channel_id=1, source_target_pairs={{1,0},{2,1},{3,2},{4,3},{5,4},{6,5},{7,6},{8,7},{9,8},{10,9},{11,1... | collective-permute-start | bytes 3932168 | tf_op jit(solution)/shard_map/ppermute | solution.py:36

commit v6 on v5

--- a/solution.py
+++ b/solution.py
@@ -62,6 +62,14 @@
     return rcv_sum(jnp.sum(field * field, axis=(0, 2, 3)))[None, :, None, None]
 
 
+def both_squares(first, second):
+    partial = jnp.stack(
+        [jnp.sum(first * first, axis=(0, 2, 3)), jnp.sum(second * second, axis=(0, 2, 3))]
+    )
+    total = rcv_sum(partial)
+    return total[0][None, :, None, None], total[1][None, :, None, None]
+
+
 def _stack_kernel(a_ref, m_ref):
     slots, _, block, _ = a_ref.shape
     for slot in range(slots):
@@ -332,9 +340,10 @@
         extended = with_halo(field.astype(jnp.bfloat16), (("rcv", 3),), rim_rows)
         return field + apply_forward(extended, stacked, columns, counts)
 
-    beta_norm = jnp.sqrt(squares(right_side) + EPSILON)
     lifted = adjoint(right_side)
-    alpha_norm = jnp.sqrt(squares(lifted) / (beta_norm * beta_norm) + EPSILON)
+    right_squares, lifted_squares = both_squares(right_side, lifted)
+    beta_norm = jnp.sqrt(right_squares + EPSILON)
+    alpha_norm = jnp.sqrt(lifted_squares / (beta_norm * beta_norm) + EPSILON)
     left_vector = right_side / beta_norm
     right_raw = lifted
     right_scale = beta_norm * alpha_norm
@@ -344,24 +353,27 @@
     phibar = beta_norm
     rhobar = alpha_norm
     for iteration in range(ITERS):
+        last = iteration == ITERS - 1
         residual_left, lifted = forward_adjoint(right_raw, right_scale, left_vector, alpha_norm)
         beta_norm = jnp.sqrt(squares(residual_left) + EPSILON)
         left_vector = residual_left / beta_norm
         residual_right = lifted / beta_norm - beta_norm * right_vector
+        rho_value = jnp.sqrt(rhobar * rhobar + beta_norm * beta_norm)
+        cosine = rhobar / rho_value
+        sine_value = beta_norm / rho_value
+        phi_value = cosine * phibar
+        phibar = sine_value * phibar
+        solution = solution + phi_value / rho_value * search_direction
+        if last:
+            break
         alpha_norm = jnp.sqrt(squares(residual_right) + EPSILON)
         right_raw = residual_right
         right_scale = alpha_norm
         right_vector = residual_right / alpha_norm
-        rho_value = jnp.sqrt(rhobar * rhobar + beta_norm * beta_norm)
-        cosine = rhobar / rho_value
-        sine_value = beta_norm / rho_value
         theta_value = sine_value * alpha_norm
         rhobar = -cosine * alpha_norm
-        phi_value = cosine * phibar
-        phibar = sine_value * phibar
-        solution = solution + phi_value / rho_value * search_direction
         search_direction = right_vector - theta_value / rho_value * search_direction
-    return (solution, phibar * alpha_norm * cosine * right_vector)
+    return (solution, phibar * cosine * residual_right)
 
 
 def solution(mesh):

time: 248 us -> 236 us (0.952)
  blocking collectives: 99.2 us -> 34.2 us
  waiting for transfers between devices: 2.77 us -> 36.5 us
  starting transfers between devices: 38.4 us -> 59.4 us
  other arithmetic: 21.7 us -> 18.8 us
    all_to_all x6 -> x2, blocking collectives: 99.2 us -> 34.2 us  [rcv_sum(): gathered = lax.all_to_all(spread, 'rcv', 0, 0, tiled=False)]
    all_to_all x0 -> x2, starting transfers between devices: none -> 19.6 us  [rcv_sum(): gathered = lax.all_to_all(spread, 'rcv', 0, 0, tiled=False)]
    ppermute x6, waiting for transfers between devices: 0.02 us -> 17 us  [from_behind(): lax.ppermute(value, axis, [(source, source + steps) for source in range(f...]
    all_to_all x0 -> x2, waiting for transfers between devices: none -> 12.9 us  [rcv_sum(): gathered = lax.all_to_all(spread, 'rcv', 0, 0, tiled=False)]
    reduce_sum x6 -> x3, other arithmetic: 5.34 us -> 0.8 us  [squares(): return rcv_sum(jnp.sum(field * field, axis=(0, 2, 3)))[None, :, None, None]]
    ppermute x2, waiting for transfers between devices: 0.01 us -> 2.71 us  [with_halo(): lax.ppermute(head, axis, [((i + 1) % count, i) for i in range(ends)])]
  transfers between devices with their start and end apart: 11 -> 13, of which waited for: 1 -> 7; matrix products, arithmetic and copies ran while one was open for 2% -> 2% of each run, Pallas kernels for 4% -> 5%
where the time goes in v6:
time: 236 us; the launch traced here: 234 us
  Pallas kernels  61.5 us (26%)
  starting transfers between devices  59.4 us (25%)
  waiting for transfers between devices  36.5 us (15%)
  blocking collectives  34.2 us (14%)
  other arithmetic  18.8 us (8%)
  local copies, waits for them, and re-layouts  17 us (7%)
  matrix products  5.45 us (2%)
    pallas_call x2, Pallas kernels, apply_both(): pl.pallas_call(_both_kernel, grid_spec=grid_spec, out_shape=[jax.ShapeDty...  37.8 us
    all_to_all x2, blocking collectives, rcv_sum(): gathered = lax.all_to_all(spread, 'rcv', 0, 0, tiled=False)  34.2 us
    all_to_all x2, starting transfers between devices, rcv_sum(): gathered = lax.all_to_all(spread, 'rcv', 0, 0, tiled=False)  19.6 us
    ppermute x6, starting transfers between devices, from_behind(): lax.ppermute(value, axis, [(source, source + steps) for source in range(f...  17.2 us
    ppermute x6, waiting for transfers between devices, from_behind(): lax.ppermute(value, axis, [(source, source + steps) for source in range(f...  17 us
    pallas_call x1, Pallas kernels, apply_adjoint(): pl.pallas_call(_adjoint_kernel, grid_spec=grid_spec, out_shape=jax.ShapeD...  13 us
    all_to_all x2, waiting for transfers between devices, rcv_sum(): gathered = lax.all_to_all(spread, 'rcv', 0, 0, tiled=False)  12.9 us
    all_to_all x1, starting transfers between devices, body(): lax.all_to_all(spectrum, ('freq', 'rcv'), split_axis=3, concat_axis=2, ti...  11.5 us
  transfers between devices with their start and end apart: 13, of which 7 were waited for; matrix products, arithmetic and copies ran while one was open for 2% of the time, Pallas kernels for 5%

profile of v6, /device:TPU:1, one launch (start us, length us, event | category | flops | bytes accessed | tf_op | source)
XLA Modules:
  0.0 233.8 jit_solution(7187435235371263053)
XLA Ops:
  0.8 5.5 %fusion = bf16[2,2,1,4,20480]{4,3,1,0,2:T(4,128)(2,1)S(1)} fusion(bf16[1,256,20480]{2,1,0:T(8,128)(2,1)} %param.28, bf16[256,1,4,2]{0,2,3,1:T(4,128)(2,1)S(1)} %get-tuple-element.160, bf16[256,1,4,2]{0,2,3,1:T(4,128)(2,1)S(1)} %get-tuple-element.159), kind=kOutput, calls=%fused_computation.1 | convolution fusion | flops 168116224 | bytes 11149312 | tf_op jit(solution)/shard_map/snr,ncgf->cfsgr/dot_general | solution.py:301
  8.3 11.5 %all-to-all-start = ((bf16[2,2,1,128,640]{4,1,0,2,3:T(2,128)(2,1)}), bf16[2,2,1,128,640]{4,1,0,2,3:T(2,128)(2,1)S(1)}, u32[]{:S(2)}, u32[]{:S(2)}) async-start(bf16[2,2,1,128,640]{4,1,0,2,3:T(2,128)(2,1)} %copy.22), calls=%async_computation | async-start | bytes 1310720 | tf_op jit(solution)/shard_map/all_to_all | solution.py:307
  21.1 10.7 %shard_map.89.m_ref = bf16[2,5,256,2816]{3,2,1,0:T(8,128)(2,1)} custom-call(bf16[2,5,11,2,128,128]{5,4,3,2,1,0:T(8,128)(2,1)} %a_ref.1), custom_call_target="tpu_custom_call" | custom-call | tf_op jit(solution)/shard_map/pallas_call | solution.py:89
  31.8 2.8 %all-to-all-done = bf16[2,2,1,128,640]{4,1,0,2,3:T(2,128)(2,1)S(1)} async-done(((bf16[2,2,1,128,640]{4,1,0,2,3:T(2,128)(2,1)}), bf16[2,2,1,128,640]{4,1,0,2,3:T(2,128)(2,1)S(1)}, u32[]{:S(2)}, u32[]{:S(2)}) %all-to-all-start) | async-done | bytes 655392 | tf_op jit(solution)/shard_map/all_to_all | solution.py:307
  35.5 13.0 %shard_map.90 = f32[2,2,128,1920]{3,2,1,0:T(8,128)} custom-call(s32[110]{0:T(128)} %reshape.545.cols_ref, s32[10]{0:T(128)} %reshape.546.counts_ref, bf16[2,2,128,640]{3,2,1,0:T(8,128)(2,1)} %bitcast.53, bf16[2,5,256,2816]{3,2,1,0:T(8,128)(2,1)} %shard_map.89.m_ref), custom_call_target="tpu_custom_call" | custom-call | flops 1845493760 | bytes 19005440 | tf_op jit(solution)/shard_map/pallas_call | solution.py:278
  50.4 3.1 %collective-permute-start = (f32[2,2,128,640]{3,2,1,0:T(8,128)S(1)}, f32[2,2,128,640]{3,2,1,0:T(8,128)S(1)}, u32[]{:S(2)}, u32[]{:S(2)}) collective-permute-start(f32[2,2,128,640]{3,2,1,0:T(8,128)S(1)} %get-tuple-element.148), channel_id=1, source_target_pairs={{0,1},{1,2},{2,3},{3,4},{4,5},{5,6},{6,7},{7,8},{8,9},{9,10},{10,1... | collective-permute-start | bytes 3932168 | tf_op jit(solution)/shard_map/ppermute | solution.py:36
  53.6 1.9 collective-permute-start.1
  55.5 12.6 %collective-permute-done = f32[2,2,128,640]{3,2,1,0:T(8,128)S(1)} collective-permute-done((f32[2,2,128,640]{3,2,1,0:T(8,128)S(1)}, f32[2,2,128,640]{3,2,1,0:T(8,128)S(1)}, u32[]{:S(2)}, u32[]{:S(2)}) %collective-permute-start) | collective-permute-done | bytes 1310752 | tf_op jit(solution)/shard_map/ppermute | solution.py:36
  68.1 4.4 %collective-permute-done.1 = f32[2,2,128,640]{3,2,1,0:T(8,128)S(1)} collective-permute-done((f32[2,2,128,640]{3,2,1,0:T(8,128)S(1)}, f32[2,2,128,640]{3,2,1,0:T(8,128)S(1)}, u32[]{:S(2)}, u32[]{:S(2)}) %collective-permute-start.1) | collective-permute-done | bytes 1310752 | tf_op jit(solution)/shard_map/ppermute | solution.py:36
  72.5 2.0 fusion.18
  75.5 8.0 %all-to-all-start.1 = ((f32[32,2,2]{2,1,0:T(2,128)}), f32[32,2,2]{2,1,0:T(2,128)S(1)}, u32[]{:S(2)}, u32[]{:S(2)}) async-start(f32[32,2,2]{2,1,0:T(2,128)} %broadcast_in_dim.8), calls=%async_computation.1 | async-start | bytes 65536 | tf_op jit(solution)/shard_map/all_to_all | solution.py:57
  83.5 2.1 collective-permute-start.3
  85.7 3.4 %collective-permute-start.2 = (bf16[2,2,128,640]{3,2,1,0:T(8,128)(2,1)S(1)}, bf16[2,2,128,640]{3,2,1,0:T(8,128)(2,1)}, u32[]{:S(2)}, u32[]{:S(2)}) collective-permute-start(bf16[2,2,128,640]{3,2,1,0:T(8,128)(2,1)S(1)} %get-tuple-element.140), channel_id=1, source_target_pairs={{0,1},{1,2},{2,3},{3,4},{4,5},{5,6},{6,7},{7,8},{8,9},{9,10},{10,1... | collective-permute-start | bytes 1966088 | tf_op jit(solution)/shard_map/ppermute | solution.py:24
  92.8 2.7 %collective-permute-done.3 = bf16[2,2,128,640]{3,2,1,0:T(8,128)(2,1)S(1)} collective-permute-done((bf16[2,2,128,640]{3,2,1,0:T(8,128)(2,1)S(1)}, bf16[2,2,128,640]{3,2,1,0:T(8,128)(2,1)S(1)}, u32[]{:S(2)}, u32[]{:S(2)}) %collective-permute-start.3) | collective-permute-done | bytes 655392 | tf_op jit(solution)/shard_map/ppermute | solution.py:26
  96.6 2.6 %pad_maximum_fusion.x_ref = bf16[2,2,128,1920]{3,2,1,0:T(8,128)(2,1)} fusion(bf16[2,2,128,640]{3,2,1,0:T(8,128)(2,1)S(1)} %collective-permute-done.3, bf16[2,2,128,640]{3,2,1,0:T(8,128)(2,1)S(1)} %get-tuple-element.140, bf16[2,2,128,640]{3,2,1,0:T(8,128)(2,1)} %collective-permute-done.2), kind=kLoop, calls=%fused_computation.3 | loop fusion | flops 5898240 | bytes 3932160 | tf_op jit(solution)/shard_map/concatenate | solution.py:22
  99.2 18.9 %shard_map.91 = (f32[2,2,128,640]{3,2,1,0:T(8,128)}, f32[2,2,128,1920]{3,2,1,0:T(8,128)}) custom-call(s32[110]{0:T(128)} %reshape.545.cols_ref, s32[10]{0:T(128)} %reshape.546.counts_ref, f32[4]{0:T(128)} %reshape.547.coef_ref, bf16[2,2,128,1920]{3,2,1,0:T(8,128)(2,1)} %pad_maximum_fusion.x_ref, f32[2,2,128,640]{3,2,1,0:T(8,128)} %copy-done, ...), custom_call_target="tpu_custom_call" | custom-call | flops 3690987520 | bytes 29491200 | tf_op jit(solution)/shard_map/pallas_call | solution.py:220
  118.1 3.5 %fusion.20 = (f32[2,2,128,640]{3,2,1,0:T(8,128)}, f32[2,2,128,640]{3,2,1,0:T(8,128)}) fusion(f32[2,2,128,1920]{3,2,1,0:T(8,128)} %get-tuple-element.127), kind=kLoop, calls=%fused_computation.65 | loop fusion | bytes 5242880 | tf_op jit(solution)/shard_map/slice | solution.py:319
  121.6 4.7 %collective-permute-start.4 = (f32[2,2,128,640]{3,2,1,0:T(8,128)}, f32[2,2,128,640]{3,2,1,0:T(8,128)S(1)}, u32[]{:S(2)}, u32[]{:S(2)}) collective-permute-start(f32[2,2,128,640]{3,2,1,0:T(8,128)} %get-tuple-element.146), channel_id=1, source_target_pairs={{0,1},{1,2},{2,3},{3,4},{4,5},{5,6},{6,7},{7,8},{8,9},{9,10},{10,1... | collective-permute-start | bytes 3932168 | tf_op jit(solution)/shard_map/ppermute | solution.py:36
  126.3 1.9 collective-permute-start.5
  129.1 11.6 %all-to-all-start.2 = ((f32[32,1,2]{2,1,0:T(1,128)}), f32[32,1,2]{2,1,0:T(1,128)S(1)}, u32[]{:S(2)}, u32[]{:S(2)}) async-start(f32[32,1,2]{2,1,0:T(1,128)} %broadcast_in_dim.9), calls=%async_computation.2 | async-start | bytes 32768 | tf_op jit(solution)/shard_map/all_to_all | solution.py:57
  140.8 11.2 %all-to-all-done.2 = f32[32,1,2]{2,1,0:T(1,128)S(1)} async-done(((f32[32,1,2]{2,1,0:T(1,128)}), f32[32,1,2]{2,1,0:T(1,128)S(1)}, u32[]{:S(2)}, u32[]{:S(2)}) %all-to-all-start.2) | async-done | bytes 288 | tf_op jit(solution)/shard_map/all_to_all | solution.py:57
  153.1 4.0 %fusion.17 = (bf16[2,2,128,640]{3,2,1,0:T(8,128)(2,1)S(1)}, f32[2,2,128,640]{3,2,1,0:T(8,128)S(1)}, f32[2,2,128,640]{3,2,1,0:T(8,128)}) fusion(f32[2,2,128,640]{3,2,1,0:T(8,128)S(1)} %copy-done.1, f32[2]{0:T(128)S(1)} %get-tuple-element.138, f32[2]{0:T(128)S(1)} %add_sqrt_fusion.4, f32[2,2,128,640]{3,2,1,0:T(8,128)} %get-tuple-element.126, ...), kind=kLoop, calls=%fused_computation.62 | loop fusion | flops 2949120 | bytes 9830416 | tf_op jit(solution)/shard_map/convert_element_type | solution.py:332
  157.1 2.6 %collective-permute-start.7 = (bf16[2,2,128,640]{3,2,1,0:T(8,128)(2,1)S(1)}, bf16[2,2,128,640]{3,2,1,0:T(8,128)(2,1)}, u32[]{:S(2)}, u32[]{:S(2)}) collective-permute-start(bf16[2,2,128,640]{3,2,1,0:T(8,128)(2,1)S(1)} %get-tuple-element.136), channel_id=1, source_target_pairs={{1,0},{2,1},{3,2},{4,3},{5,4},{6,5},{7,6},{8,7},{9,8},{10,9},{11,1... | collective-permute-start | bytes 1966088 | tf_op jit(solution)/shard_map/ppermute | solution.py:26
  159.7 3.1 %collective-permute-start.6 = (bf16[2,2,128,640]{3,2,1,0:T(8,128)(2,1)S(1)}, bf16[2,2,128,640]{3,2,1,0:T(8,128)(2,1)}, u32[]{:S(2)}, u32[]{:S(2)}) collective-permute-start(bf16[2,2,128,640]{3,2,1,0:T(8,128)(2,1)S(1)} %get-tuple-element.136), channel_id=1, source_target_pairs={{0,1},{1,2},{2,3},{3,4},{4,5},{5,6},{6,7},{7,8},{8,9},{9,10},{10,1... | collective-permute-start | bytes 1966088 | tf_op jit(solution)/shard_map/ppermute | solution.py:24
  163.0 15.7 %all_to_all.32 = f32[32,1,2]{2,1,0:T(1,128)S(1)} all-to-all(f32[32,1,2]{2,1,0:T(1,128)S(1)} %broadcast_in_dim.10), channel_id=1, replica_groups=mesh['freq'=4,'rcv'=32] {'rcv'}, dimensions={0} | all-to-all | bytes 512 | tf_op jit(solution)/shard_map/all_to_all | solution.py:57
  179.5 2.8 %pad_maximum_fusion.1.x_ref = bf16[2,2,128,1920]{3,2,1,0:T(8,128)(2,1)} fusion(bf16[2,2,128,640]{3,2,1,0:T(8,128)(2,1)} %collective-permute-done.7, bf16[2,2,128,640]{3,2,1,0:T(8,128)(2,1)S(1)} %get-tuple-element.136, bf16[2,2,128,640]{3,2,1,0:T(8,128)(2,1)} %collective-permute-done.6), kind=kLoop, calls=%fused_computation.4 | loop fusion | flops 5898240 | bytes 3932160 | tf_op jit(solution)/shard_map/concatenate | solution.py:22
  182.3 18.9 %shard_map.92 = (f32[2,2,128,640]{3,2,1,0:T(8,128)}, f32[2,2,128,1920]{3,2,1,0:T(8,128)}) custom-call(s32[110]{0:T(128)} %reshape.545.cols_ref, s32[10]{0:T(128)} %reshape.546.counts_ref, f32[4]{0:T(128)} %reshape.548.coef_ref, bf16[2,2,128,1920]{3,2,1,0:T(8,128)(2,1)} %pad_maximum_fusion.1.x_ref, f32[2,2,128,640]{3,2,1,0:T(8,128)} %copy-done.2, ...), custom_call_target="tpu_custom_call" | custom-call | flops 3690987520 | bytes 29491200 | tf_op jit(solution)/shard_map/pallas_call | solution.py:220
  201.2 3.5 %fusion.19 = (f32[2,2,128,640]{3,2,1,0:T(8,128)}, f32[2,2,128,640]{3,2,1,0:T(8,128)}) fusion(f32[2,2,128,1920]{3,2,1,0:T(8,128)} %get-tuple-element.129), kind=kLoop, calls=%fused_computation.64 | loop fusion | bytes 5242880 | tf_op jit(solution)/shard_map/slice | solution.py:319
  204.7 3.0 %collective-permute-start.8 = (f32[2,2,128,640]{3,2,1,0:T(8,128)}, f32[2,2,128,640]{3,2,1,0:T(8,128)}, u32[]{:S(2)}, u32[]{:S(2)}) collective-permute-start(f32[2,2,128,640]{3,2,1,0:T(8,128)} %get-tuple-element.144), channel_id=1, source_target_pairs={{0,1},{1,2},{2,3},{3,4},{4,5},{5,6},{6,7},{7,8},{8,9},{9,10},{10,1... | collective-permute-start | bytes 3932168 | tf_op jit(solution)/shard_map/ppermute | solution.py:36
  207.7 2.5 %collective-permute-start.9 = (f32[2,2,128,640]{3,2,1,0:T(8,128)}, f32[2,2,128,640]{3,2,1,0:T(8,128)}, u32[]{:S(2)}, u32[]{:S(2)}) collective-permute-start(f32[2,2,128,640]{3,2,1,0:T(8,128)} %get-tuple-element.145), channel_id=1, source_target_pairs={{1,0},{2,1},{3,2},{4,3},{5,4},{6,5},{7,6},{8,7},{9,8},{10,9},{11,1... | collective-permute-start | bytes 3932168 | tf_op jit(solution)/shard_map/ppermute | solution.py:36
  210.5 18.5 %all_to_all.33 = f32[32,1,2]{2,1,0:T(1,128)S(1)} all-to-all(f32[32,1,2]{2,1,0:T(1,128)S(1)} %broadcast_in_dim.11), channel_id=1, replica_groups=mesh['freq'=4,'rcv'=32] {'rcv'}, dimensions={0} | all-to-all | bytes 512 | tf_op jit(solution)/shard_map/all_to_all | solution.py:57
  229.2 4.7 %subtract_multiply_fusion = (f32[2,2,128,640]{3,2,1,0:T(8,128)}, f32[2,2,128,640]{3,2,1,0:T(8,128)}) fusion(f32[2,2,128,640]{3,2,1,0:T(8,128)} %get-tuple-element.128, f32[2,2,128,640]{3,2,1,0:T(8,128)} %collective-permute-done.9, f32[2,2,128,640]{3,2,1,0:T(8,128)} %collective-permute-done.8, f32[2,2,128,1920]{3,2,1,0:T(8,128)} %get-tuple-element.129, ...), kind=kLoop, calls=%fused_computation.11 | loop fusion | flops 4587520 | bytes 10485816 | tf_op jit(solution)/shard_map/mul | solution.py:376
  (64 shorter events, 15.6 us)
Async XLA Ops:
  6.7 13.0 %copy-start.8 = (s32[2,5]{1,0:T(2,128)S(1)}, s32[2,5]{1,0:T(2,128)}, u32[]{:S(2)}) copy-start(s32[2,5]{1,0:T(2,128)} %param.31) | copy-start | bytes 124
  6.7 13.7 %copy-start.7 = (s32[2,5,11]{2,0,1:T(2,128)S(1)}, s32[2,5,11]{2,0,1:T(2,128)}, u32[]{:S(2)}) copy-start(s32[2,5,11]{2,0,1:T(2,128)} %param.30) | copy-start | bytes 1324
  8.3 26.4 %all-to-all-start = ((bf16[2,2,1,128,640]{4,1,0,2,3:T(2,128)(2,1)}), bf16[2,2,1,128,640]{4,1,0,2,3:T(2,128)(2,1)S(1)}, u32[]{:S(2)}, u32[]{:S(2)}) async-start(bf16[2,2,1,128,640]{4,1,0,2,3:T(2,128)(2,1)} %copy.22), calls=%async_computation | async-start | bytes 1310720 | tf_op jit(solution)/shard_map/all_to_all | solution.py:307
  50.4 17.7 %collective-permute-start = (f32[2,2,128,640]{3,2,1,0:T(8,128)S(1)}, f32[2,2,128,640]{3,2,1,0:T(8,128)S(1)}, u32[]{:S(2)}, u32[]{:S(2)}) collective-permute-start(f32[2,2,128,640]{3,2,1,0:T(8,128)S(1)} %get-tuple-element.148), channel_id=1, source_target_pairs={{0,1},{1,2},{2,3},{3,4},{4,5},{5,6},{6,7},{7,8},{8,9},{9,10},{10,1... | collective-permute-start | bytes 3932168 | tf_op jit(solution)/shard_map/ppermute | solution.py:36
  53.6 18.9 %collective-permute-start.1 = (f32[2,2,128,640]{3,2,1,0:T(8,128)S(1)}, f32[2,2,128,640]{3,2,1,0:T(8,128)S(1)}, u32[]{:S(2)}, u32[]{:S(2)}) collective-permute-start(f32[2,2,128,640]{3,2,1,0:T(8,128)S(1)} %get-tuple-element.149), channel_id=1, source_target_pairs={{1,0},{2,1},{3,2},{4,3},{5,4},{6,5},{7,6},{8,7},{9,8},{10,9},{11,1... | collective-permute-start | bytes 3932168 | tf_op jit(solution)/shard_map/ppermute | solution.py:36
  74.5 18.3 %copy-start = (f32[2,2,128,640]{3,2,1,0:T(8,128)}, f32[2,2,128,640]{3,2,1,0:T(8,128)S(1)}, u32[]{:S(2)}) copy-start(f32[2,2,128,640]{3,2,1,0:T(8,128)S(1)} %get-tuple-element.141.q_ref) | copy-start | bytes 3932164
  75.5 15.2 %all-to-all-start.1 = ((f32[32,2,2]{2,1,0:T(2,128)}), f32[32,2,2]{2,1,0:T(2,128)S(1)}, u32[]{:S(2)}, u32[]{:S(2)}) async-start(f32[32,2,2]{2,1,0:T(2,128)} %broadcast_in_dim.8), calls=%async_computation.1 | async-start | bytes 65536 | tf_op jit(solution)/shard_map/all_to_all | solution.py:57
  83.5 12.0 %collective-permute-start.3 = (bf16[2,2,128,640]{3,2,1,0:T(8,128)(2,1)S(1)}, bf16[2,2,128,640]{3,2,1,0:T(8,128)(2,1)S(1)}, u32[]{:S(2)}, u32[]{:S(2)}) collective-permute-start(bf16[2,2,128,640]{3,2,1,0:T(8,128)(2,1)S(1)} %get-tuple-element.140), channel_id=1, source_target_pairs={{1,0},{2,1},{3,2},{4,3},{5,4},{6,5},{7,6},{8,7},{9,8},{10,9},{11,1... | collective-permute-start | bytes 1966088 | tf_op jit(solution)/shard_map/ppermute | solution.py:26
  85.7 10.9 %collective-permute-start.2 = (bf16[2,2,128,640]{3,2,1,0:T(8,128)(2,1)S(1)}, bf16[2,2,128,640]{3,2,1,0:T(8,128)(2,1)}, u32[]{:S(2)}, u32[]{:S(2)}) collective-permute-start(bf16[2,2,128,640]{3,2,1,0:T(8,128)(2,1)S(1)} %get-tuple-element.140), channel_id=1, source_target_pairs={{0,1},{1,2},{2,3},{3,4},{4,5},{5,6},{6,7},{7,8},{8,9},{9,10},{10,1... | collective-permute-start | bytes 1966088 | tf_op jit(solution)/shard_map/ppermute | solution.py:24
  118.1 10.2 %copy-start.5 = (f32[2,2,128,640]{3,2,1,0:T(8,128)S(1)}, f32[2,2,128,640]{3,2,1,0:T(8,128)}, u32[]{:S(2)}) copy-start(f32[2,2,128,640]{3,2,1,0:T(8,128)} %get-tuple-element.126) | copy-start | bytes 3932164
  121.6 31.5 %copy-start.1 = (f32[2,2,128,640]{3,2,1,0:T(8,128)S(1)}, f32[2,2,128,640]{3,2,1,0:T(8,128)}, u32[]{:S(2)}) copy-start(f32[2,2,128,640]{3,2,1,0:T(8,128)} %copy-done) | copy-start | bytes 3932164
  121.6 30.5 %collective-permute-start.4 = (f32[2,2,128,640]{3,2,1,0:T(8,128)}, f32[2,2,128,640]{3,2,1,0:T(8,128)S(1)}, u32[]{:S(2)}, u32[]{:S(2)}) collective-permute-start(f32[2,2,128,640]{3,2,1,0:T(8,128)} %get-tuple-element.146), channel_id=1, source_target_pairs={{0,1},{1,2},{2,3},{3,4},{4,5},{5,6},{6,7},{7,8},{8,9},{9,10},{10,1... | collective-permute-start | bytes 3932168 | tf_op jit(solution)/shard_map/ppermute | solution.py:36
  126.3 25.8 %collective-permute-start.5 = (f32[2,2,128,640]{3,2,1,0:T(8,128)}, f32[2,2,128,640]{3,2,1,0:T(8,128)}, u32[]{:S(2)}, u32[]{:S(2)}) collective-permute-start(f32[2,2,128,640]{3,2,1,0:T(8,128)} %get-tuple-element.147), channel_id=1, source_target_pairs={{1,0},{2,1},{3,2},{4,3},{5,4},{6,5},{7,6},{8,7},{9,8},{10,9},{11,1... | collective-permute-start | bytes 3932168 | tf_op jit(solution)/shard_map/ppermute | solution.py:36
  129.1 22.9 %all-to-all-start.2 = ((f32[32,1,2]{2,1,0:T(1,128)}), f32[32,1,2]{2,1,0:T(1,128)S(1)}, u32[]{:S(2)}, u32[]{:S(2)}) async-start(f32[32,1,2]{2,1,0:T(1,128)} %broadcast_in_dim.9), calls=%async_computation.2 | async-start | bytes 32768 | tf_op jit(solution)/shard_map/all_to_all | solution.py:57
  152.1 1.1 copy-start.6
  157.1 25.2 %copy-start.2 = (f32[2,2,128,640]{3,2,1,0:T(8,128)}, f32[2,2,128,640]{3,2,1,0:T(8,128)S(1)}, u32[]{:S(2)}) copy-start(f32[2,2,128,640]{3,2,1,0:T(8,128)S(1)} %get-tuple-element.137.q_ref) | copy-start | bytes 3932164
  157.1 22.4 %collective-permute-start.7 = (bf16[2,2,128,640]{3,2,1,0:T(8,128)(2,1)S(1)}, bf16[2,2,128,640]{3,2,1,0:T(8,128)(2,1)}, u32[]{:S(2)}, u32[]{:S(2)}) collective-permute-start(bf16[2,2,128,640]{3,2,1,0:T(8,128)(2,1)S(1)} %get-tuple-element.136), channel_id=1, source_target_pairs={{1,0},{2,1},{3,2},{4,3},{5,4},{6,5},{7,6},{8,7},{9,8},{10,9},{11,1... | collective-permute-start | bytes 1966088 | tf_op jit(solution)/shard_map/ppermute | solution.py:26
  159.7 19.9 %collective-permute-start.6 = (bf16[2,2,128,640]{3,2,1,0:T(8,128)(2,1)S(1)}, bf16[2,2,128,640]{3,2,1,0:T(8,128)(2,1)}, u32[]{:S(2)}, u32[]{:S(2)}) collective-permute-start(bf16[2,2,128,640]{3,2,1,0:T(8,128)(2,1)S(1)} %get-tuple-element.136), channel_id=1, source_target_pairs={{0,1},{1,2},{2,3},{3,4},{4,5},{5,6},{6,7},{7,8},{8,9},{9,10},{10,1... | collective-permute-start | bytes 1966088 | tf_op jit(solution)/shard_map/ppermute | solution.py:24
  201.2 9.0 %copy-start.4 = (f32[2,2,128,640]{3,2,1,0:T(8,128)S(1)}, f32[2,2,128,640]{3,2,1,0:T(8,128)}, u32[]{:S(2)}) copy-start(f32[2,2,128,640]{3,2,1,0:T(8,128)} %get-tuple-element.128) | copy-start | bytes 3932164
  204.7 24.4 %copy-start.3 = (f32[2,2,128,640]{3,2,1,0:T(8,128)S(1)}, f32[2,2,128,640]{3,2,1,0:T(8,128)}, u32[]{:S(2)}) copy-start(f32[2,2,128,640]{3,2,1,0:T(8,128)} %copy-done.2) | copy-start | bytes 3932164
  204.7 24.4 %collective-permute-start.8 = (f32[2,2,128,640]{3,2,1,0:T(8,128)}, f32[2,2,128,640]{3,2,1,0:T(8,128)}, u32[]{:S(2)}, u32[]{:S(2)}) collective-permute-start(f32[2,2,128,640]{3,2,1,0:T(8,128)} %get-tuple-element.144), channel_id=1, source_target_pairs={{0,1},{1,2},{2,3},{3,4},{4,5},{5,6},{6,7},{7,8},{8,9},{9,10},{10,1... | collective-permute-start | bytes 3932168 | tf_op jit(solution)/shard_map/ppermute | solution.py:36
  207.7 21.5 %collective-permute-start.9 = (f32[2,2,128,640]{3,2,1,0:T(8,128)}, f32[2,2,128,640]{3,2,1,0:T(8,128)}, u32[]{:S(2)}, u32[]{:S(2)}) collective-permute-start(f32[2,2,128,640]{3,2,1,0:T(8,128)} %get-tuple-element.145), channel_id=1, source_target_pairs={{1,0},{2,1},{3,2},{4,3},{5,4},{6,5},{7,6},{8,7},{9,8},{10,9},{11,1... | collective-permute-start | bytes 3932168 | tf_op jit(solution)/shard_map/ppermute | solution.py:36

commit v7 on v6

--- a/solution.py
+++ b/solution.py
@@ -140,19 +140,19 @@
         o_ref[...] = jnp.zeros(o_ref.shape, o_ref.dtype)
 
     field = jnp.concatenate([u_ref[0], u_ref[1]], axis=1)
-    product = jnp.dot(field, m_ref[...], preferred_element_type=jnp.float32)
     for slot in range(slots):
 
         @pl.when(slot < count)
         def _():
             start = pl.multiple_of(cols_ref[index * slots + slot] * block, block)
+            weights = m_ref[:, slot * depth : (slot + 1) * depth]
+            product = jnp.dot(field, weights, preferred_element_type=jnp.float32)
             for part in range(2):
-                lanes = slice((2 * slot + part) * block, (2 * slot + part + 1) * block)
-                o_ref[part, :, pl.ds(start, block)] += product[:, lanes]
+                o_ref[part, :, pl.ds(start, block)] += product[:, part * block : (part + 1) * block]
 
 
 def _both_kernel(
-    cols_ref, counts_ref, coef_ref, x_ref, q_ref, u_ref, m_ref, p_ref, o_ref, picked_ref
+    cols_ref, counts_ref, coef_ref, x_ref, q_ref, u_ref, m_ref, p_ref, o_ref, acc_ref
 ):
     freq = pl.program_id(0)
     row = pl.program_id(1)
@@ -167,33 +167,38 @@
     def _():
         o_ref[...] = jnp.zeros(o_ref.shape, o_ref.dtype)
 
-    for slot in range(slots):
-        start = pl.multiple_of(cols_ref[index * slots + slot] * block, block)
-        for part in range(2):
-            taken = x_ref[part, :, pl.ds(start, block)]
-            lanes = slice((2 * slot + part) * block, (2 * slot + part + 1) * block)
-            picked_ref[:, lanes] = jnp.where(slot < count, taken, jnp.zeros_like(taken))
+    acc_ref[...] = jnp.zeros(acc_ref.shape, acc_ref.dtype)
     contract = (((1,), (1,)), ((), ()))
-    product = lax.dot_general(
-        picked_ref[...], m_ref[...], contract, preferred_element_type=jnp.float32
-    )
+    for slot in range(slots):
+
+        @pl.when(slot < count)
+        def _():
+            start = pl.multiple_of(cols_ref[index * slots + slot] * block, block)
+            picked = jnp.concatenate(
+                [x_ref[0, :, pl.ds(start, block)], x_ref[1, :, pl.ds(start, block)]], axis=1
+            )
+            weights = m_ref[:, slot * depth : (slot + 1) * depth]
+            acc_ref[...] += lax.dot_general(
+                picked, weights, contract, preferred_element_type=jnp.float32
+            )
+
     scale = coef_ref[2 * freq]
     shift = coef_ref[2 * freq + 1]
     for part in range(2):
         lanes = slice(part * block, (part + 1) * block)
-        p_ref[part] = (q_ref[part] + product[:, lanes]) / scale - shift * u_ref[part]
+        p_ref[part] = (q_ref[part] + acc_ref[:, lanes]) / scale - shift * u_ref[part]
     field = jnp.concatenate(
         [p_ref[0].astype(jnp.bfloat16), p_ref[1].astype(jnp.bfloat16)], axis=1
     )
-    spread = jnp.dot(field, m_ref[...], preferred_element_type=jnp.float32)
     for slot in range(slots):
 
         @pl.when(slot < count)
         def _():
             start = pl.multiple_of(cols_ref[index * slots + slot] * block, block)
+            weights = m_ref[:, slot * depth : (slot + 1) * depth]
+            product = jnp.dot(field, weights, preferred_element_type=jnp.float32)
             for part in range(2):
-                lanes = slice((2 * slot + part) * block, (2 * slot + part + 1) * block)
-                o_ref[part, :, pl.ds(start, block)] += spread[:, lanes]
+                o_ref[part, :, pl.ds(start, block)] += product[:, part * block : (part + 1) * block]
 
 
 def apply_both(extended, raw, left, coefs, stacked, cols, counts):
@@ -215,7 +220,7 @@
             own,
             pl.BlockSpec((2, None, sources, span), lambda f, r, c, n: (0, f, 0, 0)),
         ],
-        scratch_shapes=[pltpu.VMEM((sources, width), jnp.bfloat16)],
+        scratch_shapes=[pltpu.VMEM((sources, depth), jnp.float32)],
     )
     return pl.pallas_call(
         _both_kernel,

time: 236 us -> 265 us (1.12)
  the two profiles are of different devices: /device:TPU:1 before, /device:TPU:10 now
where the time goes in v7:
time: 265 us; the launch traced here: 264 us
  Pallas kernels  75.5 us (28%)
  starting transfers between devices  68.5 us (26%)
  blocking collectives  39.1 us (15%)
  waiting for transfers between devices  38.6 us (15%)
  other arithmetic  18.8 us (7%)
  local copies, waits for them, and re-layouts  17 us (6%)
  matrix products  5.45 us (2%)
    pallas_call x2, Pallas kernels, apply_both(): pl.pallas_call(_both_kernel, grid_spec=grid_spec, out_shape=[jax.ShapeDty...  48.9 us
    all_to_all x2, blocking collectives, rcv_sum(): gathered = lax.all_to_all(spread, 'rcv', 0, 0, tiled=False)  39.1 us
    ppermute x6, starting transfers between devices, from_behind(): lax.ppermute(value, axis, [(source, source + steps) for source in range(f...  24.4 us
    all_to_all x2, starting transfers between devices, rcv_sum(): gathered = lax.all_to_all(spread, 'rcv', 0, 0, tiled=False)  23.1 us
    pallas_call x1, Pallas kernels, apply_adjoint(): pl.pallas_call(_adjoint_kernel, grid_spec=grid_spec, out_shape=jax.ShapeD...  15.8 us
    ppermute x6, waiting for transfers between devices, from_behind(): lax.ppermute(value, axis, [(source, source + steps) for source in range(f...  15.1 us
    all_to_all x2, waiting for transfers between devices, rcv_sum(): gathered = lax.all_to_all(spread, 'rcv', 0, 0, tiled=False)  11.5 us
    pallas_call x1, Pallas kernels, stack_blocks(): pl.pallas_call(_stack_kernel, grid=(local_freqs, local_blocks), in_specs=...  10.7 us
  transfers between devices with their start and end apart: 13, of which 6 were waited for; matrix products, arithmetic and copies ran while one was open for 2% of the time, Pallas kernels for 4%

profile of v7, /device:TPU:10, one launch (start us, length us, event | category | flops | bytes accessed | tf_op | source)
XLA Modules:
  0.0 263.7 jit_solution(10135302380721549798)
XLA Ops:
  0.8 5.5 %fusion = bf16[2,2,1,4,20480]{4,3,1,0,2:T(4,128)(2,1)S(1)} fusion(bf16[1,256,20480]{2,1,0:T(8,128)(2,1)} %param.28, bf16[256,1,4,2]{0,2,3,1:T(4,128)(2,1)S(1)} %get-tuple-element.160, bf16[256,1,4,2]{0,2,3,1:T(4,128)(2,1)S(1)} %get-tuple-element.159), kind=kOutput, calls=%fused_computation.1 | convolution fusion | flops 168116224 | bytes 11149312 | tf_op jit(solution)/shard_map/snr,ncgf->cfsgr/dot_general | solution.py:306
  8.3 10.4 %all-to-all-start = ((bf16[2,2,1,128,640]{4,1,0,2,3:T(2,128)(2,1)}), bf16[2,2,1,128,640]{4,1,0,2,3:T(2,128)(2,1)S(1)}, u32[]{:S(2)}, u32[]{:S(2)}) async-start(bf16[2,2,1,128,640]{4,1,0,2,3:T(2,128)(2,1)} %copy.22), calls=%async_computation | async-start | bytes 1310720 | tf_op jit(solution)/shard_map/all_to_all | solution.py:312
  20.0 10.7 %shard_map.89.m_ref = bf16[2,5,256,2816]{3,2,1,0:T(8,128)(2,1)} custom-call(bf16[2,5,11,2,128,128]{5,4,3,2,1,0:T(8,128)(2,1)} %a_ref.1), custom_call_target="tpu_custom_call" | custom-call | tf_op jit(solution)/shard_map/pallas_call | solution.py:89
  33.5 15.8 %shard_map.90 = f32[2,2,128,1920]{3,2,1,0:T(8,128)} custom-call(s32[110]{0:T(128)} %reshape.545.cols_ref, s32[10]{0:T(128)} %reshape.546.counts_ref, bf16[2,2,128,640]{3,2,1,0:T(8,128)(2,1)} %bitcast.53, bf16[2,5,256,2816]{3,2,1,0:T(8,128)(2,1)} %shard_map.89.m_ref), custom_call_target="tpu_custom_call" | custom-call | flops 1845493760 | bytes 19005440 | tf_op jit(solution)/shard_map/pallas_call | solution.py:283
  49.4 1.9 fusion.21
  51.3 1.9 collective-permute-start
  53.2 5.8 %collective-permute-start.1 = (f32[2,2,128,640]{3,2,1,0:T(8,128)S(1)}, f32[2,2,128,640]{3,2,1,0:T(8,128)S(1)}, u32[]{:S(2)}, u32[]{:S(2)}) collective-permute-start(f32[2,2,128,640]{3,2,1,0:T(8,128)S(1)} %get-tuple-element.149), channel_id=1, source_target_pairs={{1,0},{2,1},{3,2},{4,3},{5,4},{6,5},{7,6},{8,7},{9,8},{10,9},{11,1... | collective-permute-start | bytes 3932168 | tf_op jit(solution)/shard_map/ppermute | solution.py:36
  59.0 13.3 %collective-permute-done = f32[2,2,128,640]{3,2,1,0:T(8,128)S(1)} collective-permute-done((f32[2,2,128,640]{3,2,1,0:T(8,128)S(1)}, f32[2,2,128,640]{3,2,1,0:T(8,128)S(1)}, u32[]{:S(2)}, u32[]{:S(2)}) %collective-permute-start) | collective-permute-done | bytes 1310752 | tf_op jit(solution)/shard_map/ppermute | solution.py:36
  74.1 2.0 fusion.18
  77.1 8.9 %all-to-all-start.1 = ((f32[32,2,2]{2,1,0:T(2,128)}), f32[32,2,2]{2,1,0:T(2,128)S(1)}, u32[]{:S(2)}, u32[]{:S(2)}) async-start(f32[32,2,2]{2,1,0:T(2,128)} %broadcast_in_dim.8), calls=%async_computation.1 | async-start | bytes 65536 | tf_op jit(solution)/shard_map/all_to_all | solution.py:57
  85.9 4.3 %collective-permute-start.3 = (bf16[2,2,128,640]{3,2,1,0:T(8,128)(2,1)S(1)}, bf16[2,2,128,640]{3,2,1,0:T(8,128)(2,1)S(1)}, u32[]{:S(2)}, u32[]{:S(2)}) collective-permute-start(bf16[2,2,128,640]{3,2,1,0:T(8,128)(2,1)S(1)} %get-tuple-element.140), channel_id=1, source_target_pairs={{1,0},{2,1},{3,2},{4,3},{5,4},{6,5},{7,6},{8,7},{9,8},{10,9},{11,1... | collective-permute-start | bytes 1966088 | tf_op jit(solution)/shard_map/ppermute | solution.py:26
  90.2 1.9 collective-permute-start.2
  94.2 4.1 %collective-permute-done.3 = bf16[2,2,128,640]{3,2,1,0:T(8,128)(2,1)S(1)} collective-permute-done((bf16[2,2,128,640]{3,2,1,0:T(8,128)(2,1)S(1)}, bf16[2,2,128,640]{3,2,1,0:T(8,128)(2,1)S(1)}, u32[]{:S(2)}, u32[]{:S(2)}) %collective-permute-start.3) | collective-permute-done | bytes 655392 | tf_op jit(solution)/shard_map/ppermute | solution.py:26
  98.3 6.0 %collective-permute-done.2 = bf16[2,2,128,640]{3,2,1,0:T(8,128)(2,1)} collective-permute-done((bf16[2,2,128,640]{3,2,1,0:T(8,128)(2,1)S(1)}, bf16[2,2,128,640]{3,2,1,0:T(8,128)(2,1)}, u32[]{:S(2)}, u32[]{:S(2)}) %collective-permute-start.2) | collective-permute-done | bytes 655392 | tf_op jit(solution)/shard_map/ppermute | solution.py:24
  104.4 2.6 pad_maximum_fusion.x_ref
  106.9 24.5 %shard_map.91 = (f32[2,2,128,640]{3,2,1,0:T(8,128)}, f32[2,2,128,1920]{3,2,1,0:T(8,128)}) custom-call(s32[110]{0:T(128)} %reshape.545.cols_ref, s32[10]{0:T(128)} %reshape.546.counts_ref, f32[4]{0:T(128)} %reshape.547.coef_ref, bf16[2,2,128,1920]{3,2,1,0:T(8,128)(2,1)} %pad_maximum_fusion.x_ref, f32[2,2,128,640]{3,2,1,0:T(8,128)} %copy-done, ...), custom_call_target="tpu_custom_call" | custom-call | flops 3690987520 | bytes 29491200 | tf_op jit(solution)/shard_map/pallas_call | solution.py:225
  131.4 3.5 %fusion.20 = (f32[2,2,128,640]{3,2,1,0:T(8,128)}, f32[2,2,128,640]{3,2,1,0:T(8,128)}) fusion(f32[2,2,128,1920]{3,2,1,0:T(8,128)} %get-tuple-element.127), kind=kLoop, calls=%fused_computation.65 | loop fusion | bytes 5242880 | tf_op jit(solution)/shard_map/slice | solution.py:324
  134.9 2.0 collective-permute-start.4
  137.0 5.8 %collective-permute-start.5 = (f32[2,2,128,640]{3,2,1,0:T(8,128)}, f32[2,2,128,640]{3,2,1,0:T(8,128)}, u32[]{:S(2)}, u32[]{:S(2)}) collective-permute-start(f32[2,2,128,640]{3,2,1,0:T(8,128)} %get-tuple-element.147), channel_id=1, source_target_pairs={{1,0},{2,1},{3,2},{4,3},{5,4},{6,5},{7,6},{8,7},{9,8},{10,9},{11,1... | collective-permute-start | bytes 3932168 | tf_op jit(solution)/shard_map/ppermute | solution.py:36
  143.6 14.2 %all-to-all-start.2 = ((f32[32,1,2]{2,1,0:T(1,128)}), f32[32,1,2]{2,1,0:T(1,128)S(1)}, u32[]{:S(2)}, u32[]{:S(2)}) async-start(f32[32,1,2]{2,1,0:T(1,128)} %broadcast_in_dim.9), calls=%async_computation.2 | async-start | bytes 32768 | tf_op jit(solution)/shard_map/all_to_all | solution.py:57
  157.9 11.5 %all-to-all-done.2 = f32[32,1,2]{2,1,0:T(1,128)S(1)} async-done(((f32[32,1,2]{2,1,0:T(1,128)}), f32[32,1,2]{2,1,0:T(1,128)S(1)}, u32[]{:S(2)}, u32[]{:S(2)}) %all-to-all-start.2) | async-done | bytes 288 | tf_op jit(solution)/shard_map/all_to_all | solution.py:57
  170.5 4.0 %fusion.17 = (bf16[2,2,128,640]{3,2,1,0:T(8,128)(2,1)S(1)}, f32[2,2,128,640]{3,2,1,0:T(8,128)S(1)}, f32[2,2,128,640]{3,2,1,0:T(8,128)}) fusion(f32[2,2,128,640]{3,2,1,0:T(8,128)S(1)} %copy-done.1, f32[2]{0:T(128)S(1)} %get-tuple-element.138, f32[2]{0:T(128)S(1)} %add_sqrt_fusion.4, f32[2,2,128,640]{3,2,1,0:T(8,128)} %get-tuple-element.126, ...), kind=kLoop, calls=%fused_computation.62 | loop fusion | flops 2949120 | bytes 9830416 | tf_op jit(solution)/shard_map/convert_element_type | solution.py:337
  174.5 1.9 collective-permute-start.7
  176.4 2.4 collective-permute-start.6
  179.1 14.5 %all_to_all.32 = f32[32,1,2]{2,1,0:T(1,128)S(1)} all-to-all(f32[32,1,2]{2,1,0:T(1,128)S(1)} %broadcast_in_dim.10), channel_id=1, replica_groups=mesh['freq'=4,'rcv'=32] {'rcv'}, dimensions={0} | all-to-all | bytes 512 | tf_op jit(solution)/shard_map/all_to_all | solution.py:57
  194.4 2.8 %pad_maximum_fusion.1.x_ref = bf16[2,2,128,1920]{3,2,1,0:T(8,128)(2,1)} fusion(bf16[2,2,128,640]{3,2,1,0:T(8,128)(2,1)} %collective-permute-done.7, bf16[2,2,128,640]{3,2,1,0:T(8,128)(2,1)S(1)} %get-tuple-element.136, bf16[2,2,128,640]{3,2,1,0:T(8,128)(2,1)} %collective-permute-done.6), kind=kLoop, calls=%fused_computation.4 | loop fusion | flops 5898240 | bytes 3932160 | tf_op jit(solution)/shard_map/concatenate | solution.py:22
  197.2 24.5 %shard_map.92 = (f32[2,2,128,640]{3,2,1,0:T(8,128)}, f32[2,2,128,1920]{3,2,1,0:T(8,128)}) custom-call(s32[110]{0:T(128)} %reshape.545.cols_ref, s32[10]{0:T(128)} %reshape.546.counts_ref, f32[4]{0:T(128)} %reshape.548.coef_ref, bf16[2,2,128,1920]{3,2,1,0:T(8,128)(2,1)} %pad_maximum_fusion.1.x_ref, f32[2,2,128,640]{3,2,1,0:T(8,128)} %copy-done.2, ...), custom_call_target="tpu_custom_call" | custom-call | flops 3690987520 | bytes 29491200 | tf_op jit(solution)/shard_map/pallas_call | solution.py:225
  221.6 3.5 %fusion.19 = (f32[2,2,128,640]{3,2,1,0:T(8,128)}, f32[2,2,128,640]{3,2,1,0:T(8,128)}) fusion(f32[2,2,128,1920]{3,2,1,0:T(8,128)} %get-tuple-element.129), kind=kLoop, calls=%fused_computation.64 | loop fusion | bytes 5242880 | tf_op jit(solution)/shard_map/slice | solution.py:324
  225.1 2.0 collective-permute-start.8
  227.2 6.9 %collective-permute-start.9 = (f32[2,2,128,640]{3,2,1,0:T(8,128)}, f32[2,2,128,640]{3,2,1,0:T(8,128)}, u32[]{:S(2)}, u32[]{:S(2)}) collective-permute-start(f32[2,2,128,640]{3,2,1,0:T(8,128)} %get-tuple-element.145), channel_id=1, source_target_pairs={{1,0},{2,1},{3,2},{4,3},{5,4},{6,5},{7,6},{8,7},{9,8},{10,9},{11,1... | collective-permute-start | bytes 3932168 | tf_op jit(solution)/shard_map/ppermute | solution.py:36
  234.4 24.6 %all_to_all.33 = f32[32,1,2]{2,1,0:T(1,128)S(1)} all-to-all(f32[32,1,2]{2,1,0:T(1,128)S(1)} %broadcast_in_dim.11), channel_id=1, replica_groups=mesh['freq'=4,'rcv'=32] {'rcv'}, dimensions={0} | all-to-all | bytes 512 | tf_op jit(solution)/shard_map/all_to_all | solution.py:57
  259.1 4.7 %subtract_multiply_fusion = (f32[2,2,128,640]{3,2,1,0:T(8,128)}, f32[2,2,128,640]{3,2,1,0:T(8,128)}) fusion(f32[2,2,128,640]{3,2,1,0:T(8,128)} %get-tuple-element.128, f32[2,2,128,640]{3,2,1,0:T(8,128)} %collective-permute-done.9, f32[2,2,128,640]{3,2,1,0:T(8,128)} %collective-permute-done.8, f32[2,2,128,1920]{3,2,1,0:T(8,128)} %get-tuple-element.129, ...), kind=kLoop, calls=%fused_computation.11 | loop fusion | flops 4587520 | bytes 10485816 | tf_op jit(solution)/shard_map/mul | solution.py:381
  (64 shorter events, 14.5 us)
Async XLA Ops:
  6.7 12.0 %copy-start.8 = (s32[2,5]{1,0:T(2,128)S(1)}, s32[2,5]{1,0:T(2,128)}, u32[]{:S(2)}) copy-start(s32[2,5]{1,0:T(2,128)} %param.31) | copy-start | bytes 124
  6.7 12.7 %copy-start.7 = (s32[2,5,11]{2,0,1:T(2,128)S(1)}, s32[2,5,11]{2,0,1:T(2,128)}, u32[]{:S(2)}) copy-start(s32[2,5,11]{2,0,1:T(2,128)} %param.30) | copy-start | bytes 1324
  8.3 24.3 %all-to-all-start = ((bf16[2,2,1,128,640]{4,1,0,2,3:T(2,128)(2,1)}), bf16[2,2,1,128,640]{4,1,0,2,3:T(2,128)(2,1)S(1)}, u32[]{:S(2)}, u32[]{:S(2)}) async-start(bf16[2,2,1,128,640]{4,1,0,2,3:T(2,128)(2,1)} %copy.22), calls=%async_computation | async-start | bytes 1310720 | tf_op jit(solution)/shard_map/all_to_all | solution.py:312
  51.3 21.0 %collective-permute-start = (f32[2,2,128,640]{3,2,1,0:T(8,128)S(1)}, f32[2,2,128,640]{3,2,1,0:T(8,128)S(1)}, u32[]{:S(2)}, u32[]{:S(2)}) collective-permute-start(f32[2,2,128,640]{3,2,1,0:T(8,128)S(1)} %get-tuple-element.148), channel_id=1, source_target_pairs={{0,1},{1,2},{2,3},{3,4},{4,5},{5,6},{6,7},{7,8},{8,9},{9,10},{10,1... | collective-permute-start | bytes 3932168 | tf_op jit(solution)/shard_map/ppermute | solution.py:36
  53.2 20.9 %collective-permute-start.1 = (f32[2,2,128,640]{3,2,1,0:T(8,128)S(1)}, f32[2,2,128,640]{3,2,1,0:T(8,128)S(1)}, u32[]{:S(2)}, u32[]{:S(2)}) collective-permute-start(f32[2,2,128,640]{3,2,1,0:T(8,128)S(1)} %get-tuple-element.149), channel_id=1, source_target_pairs={{1,0},{2,1},{3,2},{4,3},{5,4},{6,5},{7,6},{8,7},{9,8},{10,9},{11,1... | collective-permute-start | bytes 3932168 | tf_op jit(solution)/shard_map/ppermute | solution.py:36
  76.0 18.2 %copy-start = (f32[2,2,128,640]{3,2,1,0:T(8,128)}, f32[2,2,128,640]{3,2,1,0:T(8,128)S(1)}, u32[]{:S(2)}) copy-start(f32[2,2,128,640]{3,2,1,0:T(8,128)S(1)} %get-tuple-element.141.q_ref) | copy-start | bytes 3932164
  77.1 15.1 %all-to-all-start.1 = ((f32[32,2,2]{2,1,0:T(2,128)}), f32[32,2,2]{2,1,0:T(2,128)S(1)}, u32[]{:S(2)}, u32[]{:S(2)}) async-start(f32[32,2,2]{2,1,0:T(2,128)} %broadcast_in_dim.8), calls=%async_computation.1 | async-start | bytes 65536 | tf_op jit(solution)/shard_map/all_to_all | solution.py:57
  85.9 12.4 %collective-permute-start.3 = (bf16[2,2,128,640]{3,2,1,0:T(8,128)(2,1)S(1)}, bf16[2,2,128,640]{3,2,1,0:T(8,128)(2,1)S(1)}, u32[]{:S(2)}, u32[]{:S(2)}) collective-permute-start(bf16[2,2,128,640]{3,2,1,0:T(8,128)(2,1)S(1)} %get-tuple-element.140), channel_id=1, source_target_pairs={{1,0},{2,1},{3,2},{4,3},{5,4},{6,5},{7,6},{8,7},{9,8},{10,9},{11,1... | collective-permute-start | bytes 1966088 | tf_op jit(solution)/shard_map/ppermute | solution.py:26
  90.2 14.1 %collective-permute-start.2 = (bf16[2,2,128,640]{3,2,1,0:T(8,128)(2,1)S(1)}, bf16[2,2,128,640]{3,2,1,0:T(8,128)(2,1)}, u32[]{:S(2)}, u32[]{:S(2)}) collective-permute-start(bf16[2,2,128,640]{3,2,1,0:T(8,128)(2,1)S(1)} %get-tuple-element.140), channel_id=1, source_target_pairs={{0,1},{1,2},{2,3},{3,4},{4,5},{5,6},{6,7},{7,8},{8,9},{9,10},{10,1... | collective-permute-start | bytes 1966088 | tf_op jit(solution)/shard_map/ppermute | solution.py:24
  131.4 11.3 %copy-start.5 = (f32[2,2,128,640]{3,2,1,0:T(8,128)S(1)}, f32[2,2,128,640]{3,2,1,0:T(8,128)}, u32[]{:S(2)}) copy-start(f32[2,2,128,640]{3,2,1,0:T(8,128)} %get-tuple-element.126) | copy-start | bytes 3932164
  134.9 35.6 %copy-start.1 = (f32[2,2,128,640]{3,2,1,0:T(8,128)S(1)}, f32[2,2,128,640]{3,2,1,0:T(8,128)}, u32[]{:S(2)}) copy-start(f32[2,2,128,640]{3,2,1,0:T(8,128)} %copy-done) | copy-start | bytes 3932164
  134.9 34.5 %collective-permute-start.4 = (f32[2,2,128,640]{3,2,1,0:T(8,128)}, f32[2,2,128,640]{3,2,1,0:T(8,128)S(1)}, u32[]{:S(2)}, u32[]{:S(2)}) collective-permute-start(f32[2,2,128,640]{3,2,1,0:T(8,128)} %get-tuple-element.146), channel_id=1, source_target_pairs={{0,1},{1,2},{2,3},{3,4},{4,5},{5,6},{6,7},{7,8},{8,9},{9,10},{10,1... | collective-permute-start | bytes 3932168 | tf_op jit(solution)/shard_map/ppermute | solution.py:36
  137.0 32.5 %collective-permute-start.5 = (f32[2,2,128,640]{3,2,1,0:T(8,128)}, f32[2,2,128,640]{3,2,1,0:T(8,128)}, u32[]{:S(2)}, u32[]{:S(2)}) collective-permute-start(f32[2,2,128,640]{3,2,1,0:T(8,128)} %get-tuple-element.147), channel_id=1, source_target_pairs={{1,0},{2,1},{3,2},{4,3},{5,4},{6,5},{7,6},{8,7},{9,8},{10,9},{11,1... | collective-permute-start | bytes 3932168 | tf_op jit(solution)/shard_map/ppermute | solution.py:36
  143.6 25.8 %all-to-all-start.2 = ((f32[32,1,2]{2,1,0:T(1,128)}), f32[32,1,2]{2,1,0:T(1,128)S(1)}, u32[]{:S(2)}, u32[]{:S(2)}) async-start(f32[32,1,2]{2,1,0:T(1,128)} %broadcast_in_dim.9), calls=%async_computation.2 | async-start | bytes 32768 | tf_op jit(solution)/shard_map/all_to_all | solution.py:57
  169.4 1.1 copy-start.6
  174.5 22.6 %copy-start.2 = (f32[2,2,128,640]{3,2,1,0:T(8,128)}, f32[2,2,128,640]{3,2,1,0:T(8,128)S(1)}, u32[]{:S(2)}) copy-start(f32[2,2,128,640]{3,2,1,0:T(8,128)S(1)} %get-tuple-element.137.q_ref) | copy-start | bytes 3932164
  174.5 19.9 %collective-permute-start.7 = (bf16[2,2,128,640]{3,2,1,0:T(8,128)(2,1)S(1)}, bf16[2,2,128,640]{3,2,1,0:T(8,128)(2,1)}, u32[]{:S(2)}, u32[]{:S(2)}) collective-permute-start(bf16[2,2,128,640]{3,2,1,0:T(8,128)(2,1)S(1)} %get-tuple-element.136), channel_id=1, source_target_pairs={{1,0},{2,1},{3,2},{4,3},{5,4},{6,5},{7,6},{8,7},{9,8},{10,9},{11,1... | collective-permute-start | bytes 1966088 | tf_op jit(solution)/shard_map/ppermute | solution.py:26
  176.4 18.0 %collective-permute-start.6 = (bf16[2,2,128,640]{3,2,1,0:T(8,128)(2,1)S(1)}, bf16[2,2,128,640]{3,2,1,0:T(8,128)(2,1)}, u32[]{:S(2)}, u32[]{:S(2)}) collective-permute-start(bf16[2,2,128,640]{3,2,1,0:T(8,128)(2,1)S(1)} %get-tuple-element.136), channel_id=1, source_target_pairs={{0,1},{1,2},{2,3},{3,4},{4,5},{5,6},{6,7},{7,8},{8,9},{9,10},{10,1... | collective-permute-start | bytes 1966088 | tf_op jit(solution)/shard_map/ppermute | solution.py:24
  221.6 12.5 %copy-start.4 = (f32[2,2,128,640]{3,2,1,0:T(8,128)S(1)}, f32[2,2,128,640]{3,2,1,0:T(8,128)}, u32[]{:S(2)}) copy-start(f32[2,2,128,640]{3,2,1,0:T(8,128)} %get-tuple-element.128) | copy-start | bytes 3932164
  225.1 34.0 %copy-start.3 = (f32[2,2,128,640]{3,2,1,0:T(8,128)S(1)}, f32[2,2,128,640]{3,2,1,0:T(8,128)}, u32[]{:S(2)}) copy-start(f32[2,2,128,640]{3,2,1,0:T(8,128)} %copy-done.2) | copy-start | bytes 3932164
  225.1 33.9 %collective-permute-start.8 = (f32[2,2,128,640]{3,2,1,0:T(8,128)}, f32[2,2,128,640]{3,2,1,0:T(8,128)}, u32[]{:S(2)}, u32[]{:S(2)}) collective-permute-start(f32[2,2,128,640]{3,2,1,0:T(8,128)} %get-tuple-element.144), channel_id=1, source_target_pairs={{0,1},{1,2},{2,3},{3,4},{4,5},{5,6},{6,7},{7,8},{8,9},{9,10},{10,1... | collective-permute-start | bytes 3932168 | tf_op jit(solution)/shard_map/ppermute | solution.py:36
  227.2 31.9 %collective-permute-start.9 = (f32[2,2,128,640]{3,2,1,0:T(8,128)}, f32[2,2,128,640]{3,2,1,0:T(8,128)}, u32[]{:S(2)}, u32[]{:S(2)}) collective-permute-start(f32[2,2,128,640]{3,2,1,0:T(8,128)} %get-tuple-element.145), channel_id=1, source_target_pairs={{1,0},{2,1},{3,2},{4,3},{5,4},{6,5},{7,6},{8,7},{9,8},{10,9},{11,1... | collective-permute-start | bytes 3932168 | tf_op jit(solution)/shard_map/ppermute | solution.py:36

commit v8 on v6

--- a/solution.py
+++ b/solution.py
@@ -70,11 +70,13 @@
     return total[0][None, :, None, None], total[1][None, :, None, None]
 
 
-def _stack_kernel(a_ref, m_ref):
+def _stack_kernel(counts_ref, a_ref, m_ref):
     slots, _, block, _ = a_ref.shape
+    count = counts_ref[pl.program_id(0) * pl.num_programs(1) + pl.program_id(1)]
     for slot in range(slots):
-        real_part = a_ref[slot, 0]
-        imaginary = a_ref[slot, 1]
+        live = slot < count
+        real_part = jnp.where(live, a_ref[slot, 0], jnp.zeros_like(a_ref[slot, 0]))
+        imaginary = jnp.where(live, a_ref[slot, 1], jnp.zeros_like(a_ref[slot, 1]))
         left = slice(2 * slot * block, (2 * slot + 1) * block)
         right = slice((2 * slot + 1) * block, (2 * slot + 2) * block)
         m_ref[:block, left] = real_part
@@ -83,23 +85,29 @@
         m_ref[block:, right] = real_part
 
 
-def stack_blocks(down_blocks):
+def stack_blocks(down_blocks, counts):
     local_freqs, local_blocks, slot_count, _, block_size, _ = down_blocks.shape
     width = 2 * slot_count * block_size
-    return pl.pallas_call(
-        _stack_kernel,
+    grid_spec = pltpu.PrefetchScalarGridSpec(
+        num_scalar_prefetch=1,
         grid=(local_freqs, local_blocks),
         in_specs=[
             pl.BlockSpec(
                 (None, None, slot_count, 2, block_size, block_size),
-                lambda f, r: (f, r, 0, 0, 0, 0),
+                lambda f, r, n: (f, r, 0, 0, 0, 0),
             )
         ],
-        out_specs=pl.BlockSpec((None, None, 2 * block_size, width), lambda f, r: (f, r, 0, 0)),
+        out_specs=pl.BlockSpec(
+            (None, None, 2 * block_size, width), lambda f, r, n: (f, r, 0, 0)
+        ),
+    )
+    return pl.pallas_call(
+        _stack_kernel,
+        grid_spec=grid_spec,
         out_shape=jax.ShapeDtypeStruct(
             (local_freqs, local_blocks, 2 * block_size, width), jnp.bfloat16
         ),
-    )(down_blocks)
+    )(counts, down_blocks)
 
 
 def _forward_kernel(cols_ref, counts_ref, x_ref, m_ref, o_ref, picked_ref):
@@ -125,34 +133,57 @@
     o_ref[1] = product[:, block:]
 
 
-def _adjoint_kernel(cols_ref, counts_ref, u_ref, m_ref, o_ref):
+def _scatter(cols_ref, index, field, m_ref, acc_ref):
+    depth, width = m_ref.shape
+    block = depth // 2
+    slots = width // depth
+    spread = jnp.dot(field, m_ref[...], preferred_element_type=jnp.float32)
+    for slot in range(slots):
+        start = pl.multiple_of(cols_ref[index * slots + slot] * block, block)
+        for part in range(2):
+            lanes = slice((2 * slot + part) * block, (2 * slot + part + 1) * block)
+            acc_ref[part, :, pl.ds(start, block)] += spread[:, lanes]
+
+
+def _split(acc_ref, lower_ref, middle_ref, upper_ref):
+    rim = lower_ref.shape[-1]
+    own = middle_ref.shape[-1]
+    lower_ref[...] = acc_ref[:, :, :rim]
+    middle_ref[...] = acc_ref[:, :, rim : rim + own]
+    upper_ref[...] = acc_ref[:, :, rim + own :]
+
+
+def _adjoint_kernel(cols_ref, counts_ref, u_ref, m_ref, lower_ref, middle_ref, upper_ref, acc_ref):
     freq = pl.program_id(0)
     row = pl.program_id(1)
     rows = pl.num_programs(1)
-    depth, width = m_ref.shape
-    block = depth // 2
-    slots = width // depth
-    index = freq * rows + row
-    count = counts_ref[index]
 
     @pl.when(row == 0)
     def _():
-        o_ref[...] = jnp.zeros(o_ref.shape, o_ref.dtype)
+        acc_ref[...] = jnp.zeros(acc_ref.shape, acc_ref.dtype)
 
     field = jnp.concatenate([u_ref[0], u_ref[1]], axis=1)
-    product = jnp.dot(field, m_ref[...], preferred_element_type=jnp.float32)
-    for slot in range(slots):
-
-        @pl.when(slot < count)
-        def _():
-            start = pl.multiple_of(cols_ref[index * slots + slot] * block, block)
-            for part in range(2):
-                lanes = slice((2 * slot + part) * block, (2 * slot + part + 1) * block)
-                o_ref[part, :, pl.ds(start, block)] += product[:, lanes]
+    _scatter(cols_ref, freq * rows + row, field, m_ref, acc_ref)
+
+    @pl.when(row == rows - 1)
+    def _():
+        _split(acc_ref, lower_ref, middle_ref, upper_ref)
 
 
 def _both_kernel(
-    cols_ref, counts_ref, coef_ref, x_ref, q_ref, u_ref, m_ref, p_ref, o_ref, picked_ref
+    cols_ref,
+    counts_ref,
+    coef_ref,
+    x_ref,
+    q_ref,
+    u_ref,
+    m_ref,
+    p_ref,
+    lower_ref,
+    middle_ref,
+    upper_ref,
+    picked_ref,
+    acc_ref,
 ):
     freq = pl.program_id(0)
     row = pl.program_id(1)
@@ -161,18 +192,16 @@
     block = depth // 2
     slots = width // depth
     index = freq * rows + row
-    count = counts_ref[index]
 
     @pl.when(row == 0)
     def _():
-        o_ref[...] = jnp.zeros(o_ref.shape, o_ref.dtype)
+        acc_ref[...] = jnp.zeros(acc_ref.shape, acc_ref.dtype)
 
     for slot in range(slots):
         start = pl.multiple_of(cols_ref[index * slots + slot] * block, block)
         for part in range(2):
-            taken = x_ref[part, :, pl.ds(start, block)]
             lanes = slice((2 * slot + part) * block, (2 * slot + part + 1) * block)
-            picked_ref[:, lanes] = jnp.where(slot < count, taken, jnp.zeros_like(taken))
+            picked_ref[:, lanes] = x_ref[part, :, pl.ds(start, block)]
     contract = (((1,), (1,)), ((), ()))
     product = lax.dot_general(
         picked_ref[...], m_ref[...], contract, preferred_element_type=jnp.float32
@@ -185,21 +214,30 @@
     field = jnp.concatenate(
         [p_ref[0].astype(jnp.bfloat16), p_ref[1].astype(jnp.bfloat16)], axis=1
     )
-    spread = jnp.dot(field, m_ref[...], preferred_element_type=jnp.float32)
-    for slot in range(slots):
-
-        @pl.when(slot < count)
-        def _():
-            start = pl.multiple_of(cols_ref[index * slots + slot] * block, block)
-            for part in range(2):
-                lanes = slice((2 * slot + part) * block, (2 * slot + part + 1) * block)
-                o_ref[part, :, pl.ds(start, block)] += spread[:, lanes]
+    _scatter(cols_ref, index, field, m_ref, acc_ref)
+
+    @pl.when(row == rows - 1)
+    def _():
+        _split(acc_ref, lower_ref, middle_ref, upper_ref)
+
+
+def _part_specs(local_freqs, sources):
+    def part_spec(lanes):
+        return pl.BlockSpec((2, None, sources, lanes), lambda f, r, c, n: (0, f, 0, 0))
+
+    def part_shape(lanes):
+        return jax.ShapeDtypeStruct((2, local_freqs, sources, lanes), jnp.float32)
+
+    return part_spec, part_shape
 
 
 def apply_both(extended, raw, left, coefs, stacked, cols, counts):
     local_freqs, local_blocks, depth, width = stacked.shape
     block_size = depth // 2
     _, _, sources, span = extended.shape
+    own_rows = local_blocks * block_size
+    rim = (span - own_rows) // 2
+    part_spec, part_shape = _part_specs(local_freqs, sources)
     own = pl.BlockSpec((2, None, sources, block_size), lambda f, r, c, n: (0, f, 0, r))
     grid_spec = pltpu.PrefetchScalarGridSpec(
         num_scalar_prefetch=2,
@@ -211,18 +249,20 @@
             own,
             pl.BlockSpec((None, None, depth, width), lambda f, r, c, n: (f, r, 0, 0)),
         ],
-        out_specs=[
-            own,
-            pl.BlockSpec((2, None, sources, span), lambda f, r, c, n: (0, f, 0, 0)),
-        ],
-        scratch_shapes=[pltpu.VMEM((sources, width), jnp.bfloat16)],
+        out_specs=[own, part_spec(rim), part_spec(own_rows), part_spec(rim)],
+        scratch_shapes=[
+            pltpu.VMEM((sources, width), jnp.bfloat16),
+            pltpu.VMEM((2, sources, span), jnp.float32),
+        ],
     )
     return pl.pallas_call(
         _both_kernel,
         grid_spec=grid_spec,
         out_shape=[
             jax.ShapeDtypeStruct(raw.shape, jnp.float32),
-            jax.ShapeDtypeStruct((2, local_freqs, sources, span), jnp.float32),
+            part_shape(rim),
+            part_shape(own_rows),
+            part_shape(rim),
         ],
         compiler_params=pltpu.CompilerParams(dimension_semantics=("arbitrary", "arbitrary")),
         cost_estimate=pl.CostEstimate(
@@ -266,6 +306,9 @@
     local_freqs, local_blocks, depth, width = stacked.shape
     block_size = depth // 2
     sources = rounded.shape[2]
+    own = local_blocks * block_size
+    rim = (span - own) // 2
+    part_spec, part_shape = _part_specs(local_freqs, sources)
     grid_spec = pltpu.PrefetchScalarGridSpec(
         num_scalar_prefetch=2,
         grid=(local_freqs, local_blocks),
@@ -273,12 +316,13 @@
             pl.BlockSpec((2, None, sources, block_size), lambda f, r, c, n: (0, f, 0, r)),
             pl.BlockSpec((None, None, depth, width), lambda f, r, c, n: (f, r, 0, 0)),
         ],
-        out_specs=pl.BlockSpec((2, None, sources, span), lambda f, r, c, n: (0, f, 0, 0)),
+        out_specs=[part_spec(rim), part_spec(own), part_spec(rim)],
+        scratch_shapes=[pltpu.VMEM((2, sources, span), jnp.float32)],
     )
     return pl.pallas_call(
         _adjoint_kernel,
         grid_spec=grid_spec,
-        out_shape=jax.ShapeDtypeStruct((2, local_freqs, sources, span), jnp.float32),
+        out_shape=[part_shape(rim), part_shape(own), part_shape(rim)],
         compiler_params=pltpu.CompilerParams(dimension_semantics=("arbitrary", "arbitrary")),
         cost_estimate=pl.CostEstimate(
             flops=2 * local_freqs * local_blocks * sources * depth * width,
@@ -311,12 +355,9 @@
         block_cols - position * local_blocks + reach_blocks, 0, span_blocks - 1
     ).reshape(-1)
     counts = jnp.clip(block_counts, 0, slot_count).reshape(-1)
-    stacked = stack_blocks(down_blocks)
-
-    def exchange(spread):
-        lower_rim = spread[..., :rim_rows]
-        middle = spread[..., rim_rows : rim_rows + local_rows]
-        upper_rim = spread[..., rim_rows + local_rows :]
+    stacked = stack_blocks(down_blocks, counts)
+
+    def exchange(lower_rim, middle, upper_rim):
         from_above = from_behind(lower_rim, "rcv", -1)
         from_below = from_behind(upper_rim, "rcv", 1)
         middle = middle.at[..., :rim_rows].add(from_below)
@@ -325,16 +366,16 @@
 
     def adjoint(field):
         rounded = field.astype(jnp.bfloat16)
-        spread = apply_adjoint(rounded, stacked, columns, counts, span_blocks * block_size)
-        return field + exchange(spread)
+        parts = apply_adjoint(rounded, stacked, columns, counts, span_blocks * block_size)
+        return field + exchange(*parts)
 
     def forward_adjoint(raw, scale, left, shift):
         extended = with_halo(raw.astype(jnp.bfloat16), (("rcv", 3),), rim_rows)
         coefs = jnp.stack(
             [jnp.broadcast_to(scale, shift.shape).reshape(-1), shift.reshape(-1)], axis=1
         ).reshape(-1)
-        residual, spread = apply_both(extended, raw, left, coefs, stacked, columns, counts)
-        return residual, residual + exchange(spread)
+        residual, *parts = apply_both(extended, raw, left, coefs, stacked, columns, counts)
+        return residual, residual + exchange(*parts)
 
     def forward(field):
         extended = with_halo(field.astype(jnp.bfloat16), (("rcv", 3),), rim_rows)

time: 236 us -> 226 us (0.958)
  local copies, waits for them, and re-layouts: 17 us -> 8.01 us
  other arithmetic: 18.8 us -> 21.4 us
    slice x3 -> x0, local copies, waits for them, and re-layouts: 8.93 us -> none  [exchange(): upper_rim = spread[..., rim_rows + local_rows:]]
    reduce_sum x3, other arithmetic: 0.8 us -> 3.43 us  [squares(): return rcv_sum(jnp.sum(field * field, axis=(0, 2, 3)))[None, :, None, None]]
  transfers between devices with their start and end apart: 13 -> 13, of which waited for: 7 -> 7; matrix products, arithmetic and copies ran while one was open for 2% -> 4% of each run, Pallas kernels for 5% -> 5%
where the time goes in v8:
time: 226 us; the launch traced here: 225 us
  Pallas kernels  62.1 us (27%)
  starting transfers between devices  59.2 us (26%)
  waiting for transfers between devices  34.7 us (15%)
  blocking collectives  32.8 us (15%)
  other arithmetic  21.4 us (9%)
  local copies, waits for them, and re-layouts  8.01 us (4%)
  matrix products  5.45 us (2%)
    pallas_call x2, Pallas kernels, apply_both(): pl.pallas_call(_both_kernel, grid_spec=grid_spec, out_shape=[jax.ShapeDty...  37.6 us
    all_to_all x2, blocking collectives, rcv_sum(): gathered = lax.all_to_all(spread, 'rcv', 0, 0, tiled=False)  32.8 us
    all_to_all x2, starting transfers between devices, rcv_sum(): gathered = lax.all_to_all(spread, 'rcv', 0, 0, tiled=False)  19.6 us
    ppermute x6, waiting for transfers between devices, from_behind(): lax.ppermute(value, axis, [(source, source + steps) for source in range(f...  17.2 us
    ppermute x6, starting transfers between devices, from_behind(): lax.ppermute(value, axis, [(source, source + steps) for source in range(f...  17 us
    pallas_call x1, Pallas kernels, apply_adjoint(): pl.pallas_call(_adjoint_kernel, grid_spec=grid_spec, out_shape=[part_shap...  12.9 us
    all_to_all x2, waiting for transfers between devices, rcv_sum(): gathered = lax.all_to_all(spread, 'rcv', 0, 0, tiled=False)  11.8 us
    pallas_call x1, Pallas kernels, stack_blocks(): pl.pallas_call(_stack_kernel, grid_spec=grid_spec, out_shape=jax.ShapeDty...  11.6 us
  transfers between devices with their start and end apart: 13, of which 7 were waited for; matrix products, arithmetic and copies ran while one was open for 4% of the time, Pallas kernels for 5%

profile of v8, /device:TPU:1, one launch (start us, length us, event | category | flops | bytes accessed | tf_op | source)
XLA Modules:
  0.0 224.6 jit_solution(2542388997623401646)
XLA Ops:
  0.8 5.5 %fusion = bf16[2,2,1,4,20480]{4,3,1,0,2:T(4,128)(2,1)S(1)} fusion(bf16[1,256,20480]{2,1,0:T(8,128)(2,1)} %param.28, bf16[256,1,4,2]{0,2,3,1:T(4,128)(2,1)S(1)} %get-tuple-element.168, bf16[256,1,4,2]{0,2,3,1:T(4,128)(2,1)S(1)} %get-tuple-element.167), kind=kOutput, calls=%fused_computation.1 | convolution fusion | flops 168116224 | bytes 11149312 | tf_op jit(solution)/shard_map/snr,ncgf->cfsgr/dot_general | solution.py:345
  8.3 11.5 %all-to-all-start = ((bf16[2,2,1,128,640]{4,1,0,2,3:T(2,128)(2,1)}), bf16[2,2,1,128,640]{4,1,0,2,3:T(2,128)(2,1)S(1)}, u32[]{:S(2)}, u32[]{:S(2)}) async-start(bf16[2,2,1,128,640]{4,1,0,2,3:T(2,128)(2,1)} %copy.22), calls=%async_computation | async-start | bytes 1310720 | tf_op jit(solution)/shard_map/all_to_all | solution.py:351
  21.1 11.6 %shard_map.89.m_ref = bf16[2,5,256,2816]{3,2,1,0:T(8,128)(2,1)} custom-call(s32[10]{0:T(128)} %reshape.546.counts_ref, bf16[2,5,11,2,128,128]{5,4,3,2,1,0:T(8,128)(2,1)} %a_ref.1), custom_call_target="tpu_custom_call" | custom-call | tf_op jit(solution)/shard_map/pallas_call | solution.py:104
  32.7 1.9 all-to-all-done
  35.6 12.9 %shard_map.90 = (f32[2,2,128,640]{3,2,1,0:T(8,128)}, f32[2,2,128,640]{3,2,1,0:T(8,128)}, f32[2,2,128,640]{3,2,1,0:T(8,128)}) custom-call(s32[110]{0:T(128)} %reshape.545.cols_ref, s32[10]{0:T(128)} %reshape.546.counts_ref, bf16[2,2,128,640]{3,2,1,0:T(8,128)(2,1)} %bitcast.53, bf16[2,5,256,2816]{3,2,1,0:T(8,128)(2,1)} %shard_map.89.m_ref), custom_call_target="tpu_custom_call" | custom-call | flops 1845493760 | bytes 19005440 | tf_op jit(solution)/shard_map/pallas_call | solution.py:322
  48.4 3.0 %collective-permute-start = (f32[2,2,128,640]{3,2,1,0:T(8,128)}, f32[2,2,128,640]{3,2,1,0:T(8,128)S(1)}, u32[]{:S(2)}, u32[]{:S(2)}) collective-permute-start(f32[2,2,128,640]{3,2,1,0:T(8,128)} %get-tuple-element.134), channel_id=1, source_target_pairs={{0,1},{1,2},{2,3},{3,4},{4,5},{5,6},{6,7},{7,8},{8,9},{9,10},{10,1... | collective-permute-start | bytes 3932168 | tf_op jit(solution)/shard_map/ppermute | solution.py:36
  51.4 1.9 collective-permute-start.1
  53.4 12.9 %collective-permute-done = f32[2,2,128,640]{3,2,1,0:T(8,128)S(1)} collective-permute-done((f32[2,2,128,640]{3,2,1,0:T(8,128)}, f32[2,2,128,640]{3,2,1,0:T(8,128)S(1)}, u32[]{:S(2)}, u32[]{:S(2)}) %collective-permute-start) | collective-permute-done | bytes 1310752 | tf_op jit(solution)/shard_map/ppermute | solution.py:36
  66.3 4.3 %collective-permute-done.1 = f32[2,2,128,640]{3,2,1,0:T(8,128)S(1)} collective-permute-done((f32[2,2,128,640]{3,2,1,0:T(8,128)}, f32[2,2,128,640]{3,2,1,0:T(8,128)S(1)}, u32[]{:S(2)}, u32[]{:S(2)}) %collective-permute-start.1) | collective-permute-done | bytes 1310752 | tf_op jit(solution)/shard_map/ppermute | solution.py:36
  70.6 2.0 fusion.17
  73.6 8.0 %all-to-all-start.1 = ((f32[32,2,2]{2,1,0:T(2,128)}), f32[32,2,2]{2,1,0:T(2,128)S(1)}, u32[]{:S(2)}, u32[]{:S(2)}) async-start(f32[32,2,2]{2,1,0:T(2,128)} %broadcast_in_dim.8), calls=%async_computation.1 | async-start | bytes 65536 | tf_op jit(solution)/shard_map/all_to_all | solution.py:57
  81.6 2.1 collective-permute-start.3
  83.8 3.4 %collective-permute-start.2 = (bf16[2,2,128,640]{3,2,1,0:T(8,128)(2,1)S(1)}, bf16[2,2,128,640]{3,2,1,0:T(8,128)(2,1)}, u32[]{:S(2)}, u32[]{:S(2)}) collective-permute-start(bf16[2,2,128,640]{3,2,1,0:T(8,128)(2,1)S(1)} %get-tuple-element.154), channel_id=1, source_target_pairs={{0,1},{1,2},{2,3},{3,4},{4,5},{5,6},{6,7},{7,8},{8,9},{9,10},{10,1... | collective-permute-start | bytes 1966088 | tf_op jit(solution)/shard_map/ppermute | solution.py:24
  87.2 1.7 all-to-all-done.1
  90.9 2.7 %collective-permute-done.3 = bf16[2,2,128,640]{3,2,1,0:T(8,128)(2,1)S(1)} collective-permute-done((bf16[2,2,128,640]{3,2,1,0:T(8,128)(2,1)S(1)}, bf16[2,2,128,640]{3,2,1,0:T(8,128)(2,1)S(1)}, u32[]{:S(2)}, u32[]{:S(2)}) %collective-permute-start.3) | collective-permute-done | bytes 655392 | tf_op jit(solution)/shard_map/ppermute | solution.py:26
  94.7 2.5 %pad_maximum_fusion.x_ref = bf16[2,2,128,1920]{3,2,1,0:T(8,128)(2,1)} fusion(bf16[2,2,128,640]{3,2,1,0:T(8,128)(2,1)S(1)} %collective-permute-done.3, bf16[2,2,128,640]{3,2,1,0:T(8,128)(2,1)S(1)} %get-tuple-element.154, bf16[2,2,128,640]{3,2,1,0:T(8,128)(2,1)} %collective-permute-done.2), kind=kLoop, calls=%fused_computation.3 | loop fusion | flops 5898240 | bytes 3932160 | tf_op jit(solution)/shard_map/concatenate | solution.py:22
  97.2 18.8 %shard_map.91 = (f32[2,2,128,640]{3,2,1,0:T(8,128)}, f32[2,2,128,640]{3,2,1,0:T(8,128)}, f32[2,2,128,640]{3,2,1,0:T(8,128)}, f32[2,2,128,640]{3,2,1,0:T(8,128)}) custom-call(s32[110]{0:T(128)} %reshape.545.cols_ref, s32[10]{0:T(128)} %reshape.546.counts_ref, f32[4]{0:T(128)} %reshape.547.coef_ref, bf16[2,2,128,1920]{3,2,1,0:T(8,128)(2,1)} %pad_maximum_fusion.x_ref, ...), custom_call_target="tpu_custom_call" | custom-call | flops 3690987520 | bytes 29491200 | tf_op jit(solution)/shard_map/pallas_call | solution.py:258
  116.0 4.6 %collective-permute-start.4 = (f32[2,2,128,640]{3,2,1,0:T(8,128)}, f32[2,2,128,640]{3,2,1,0:T(8,128)S(1)}, u32[]{:S(2)}, u32[]{:S(2)}) collective-permute-start(f32[2,2,128,640]{3,2,1,0:T(8,128)} %get-tuple-element.138), channel_id=1, source_target_pairs={{0,1},{1,2},{2,3},{3,4},{4,5},{5,6},{6,7},{7,8},{8,9},{9,10},{10,1... | collective-permute-start | bytes 3932168 | tf_op jit(solution)/shard_map/ppermute | solution.py:36
  120.7 1.9 collective-permute-start.5
  122.6 1.6 multiply_reduce_fusion.2
  124.8 11.6 %all-to-all-start.2 = ((f32[32,1,2]{2,1,0:T(1,128)}), f32[32,1,2]{2,1,0:T(1,128)S(1)}, u32[]{:S(2)}, u32[]{:S(2)}) async-start(f32[32,1,2]{2,1,0:T(1,128)} %broadcast_in_dim.9), calls=%async_computation.2 | async-start | bytes 32768 | tf_op jit(solution)/shard_map/all_to_all | solution.py:57
  136.4 10.1 %all-to-all-done.2 = f32[32,1,2]{2,1,0:T(1,128)S(1)} async-done(((f32[32,1,2]{2,1,0:T(1,128)}), f32[32,1,2]{2,1,0:T(1,128)S(1)}, u32[]{:S(2)}, u32[]{:S(2)}) %all-to-all-start.2) | async-done | bytes 288 | tf_op jit(solution)/shard_map/all_to_all | solution.py:57
  147.6 4.0 %fusion.16 = (bf16[2,2,128,640]{3,2,1,0:T(8,128)(2,1)S(1)}, f32[2,2,128,640]{3,2,1,0:T(8,128)S(1)}, f32[2,2,128,640]{3,2,1,0:T(8,128)}) fusion(f32[2,2,128,640]{3,2,1,0:T(8,128)S(1)} %copy-done.1, f32[2]{0:T(128)S(1)} %get-tuple-element.152, f32[2]{0:T(128)S(1)} %add_sqrt_fusion.4, f32[2,2,128,640]{3,2,1,0:T(8,128)} %get-tuple-element.136, ...), kind=kLoop, calls=%fused_computation.60 | loop fusion | flops 2949120 | bytes 9830416 | tf_op jit(solution)/shard_map/convert_element_type | solution.py:373
  151.6 2.6 %collective-permute-start.7 = (bf16[2,2,128,640]{3,2,1,0:T(8,128)(2,1)S(1)}, bf16[2,2,128,640]{3,2,1,0:T(8,128)(2,1)}, u32[]{:S(2)}, u32[]{:S(2)}) collective-permute-start(bf16[2,2,128,640]{3,2,1,0:T(8,128)(2,1)S(1)} %get-tuple-element.150), channel_id=1, source_target_pairs={{1,0},{2,1},{3,2},{4,3},{5,4},{6,5},{7,6},{8,7},{9,8},{10,9},{11,1... | collective-permute-start | bytes 1966088 | tf_op jit(solution)/shard_map/ppermute | solution.py:26
  154.2 3.1 %collective-permute-start.6 = (bf16[2,2,128,640]{3,2,1,0:T(8,128)(2,1)S(1)}, bf16[2,2,128,640]{3,2,1,0:T(8,128)(2,1)}, u32[]{:S(2)}, u32[]{:S(2)}) collective-permute-start(bf16[2,2,128,640]{3,2,1,0:T(8,128)(2,1)S(1)} %get-tuple-element.150), channel_id=1, source_target_pairs={{0,1},{1,2},{2,3},{3,4},{4,5},{5,6},{6,7},{7,8},{8,9},{9,10},{10,1... | collective-permute-start | bytes 1966088 | tf_op jit(solution)/shard_map/ppermute | solution.py:24
  157.5 15.6 %all_to_all.32 = f32[32,1,2]{2,1,0:T(1,128)S(1)} all-to-all(f32[32,1,2]{2,1,0:T(1,128)S(1)} %broadcast_in_dim.10), channel_id=1, replica_groups=mesh['freq'=4,'rcv'=32] {'rcv'}, dimensions={0} | all-to-all | bytes 512 | tf_op jit(solution)/shard_map/all_to_all | solution.py:57
  173.9 2.7 %pad_maximum_fusion.1.x_ref = bf16[2,2,128,1920]{3,2,1,0:T(8,128)(2,1)} fusion(bf16[2,2,128,640]{3,2,1,0:T(8,128)(2,1)} %collective-permute-done.7, bf16[2,2,128,640]{3,2,1,0:T(8,128)(2,1)S(1)} %get-tuple-element.150, bf16[2,2,128,640]{3,2,1,0:T(8,128)(2,1)} %collective-permute-done.6), kind=kLoop, calls=%fused_computation.4 | loop fusion | flops 5898240 | bytes 3932160 | tf_op jit(solution)/shard_map/concatenate | solution.py:22
  176.6 18.8 %shard_map.92 = (f32[2,2,128,640]{3,2,1,0:T(8,128)}, f32[2,2,128,640]{3,2,1,0:T(8,128)}, f32[2,2,128,640]{3,2,1,0:T(8,128)}, f32[2,2,128,640]{3,2,1,0:T(8,128)}) custom-call(s32[110]{0:T(128)} %reshape.545.cols_ref, s32[10]{0:T(128)} %reshape.546.counts_ref, f32[4]{0:T(128)} %reshape.548.coef_ref, bf16[2,2,128,1920]{3,2,1,0:T(8,128)(2,1)} %pad_maximum_fusion.1.x_ref, ...), custom_call_target="tpu_custom_call" | custom-call | flops 3690987520 | bytes 29491200 | tf_op jit(solution)/shard_map/pallas_call | solution.py:258
  195.4 2.9 %collective-permute-start.8 = (f32[2,2,128,640]{3,2,1,0:T(8,128)}, f32[2,2,128,640]{3,2,1,0:T(8,128)}, u32[]{:S(2)}, u32[]{:S(2)}) collective-permute-start(f32[2,2,128,640]{3,2,1,0:T(8,128)} %get-tuple-element.142), channel_id=1, source_target_pairs={{0,1},{1,2},{2,3},{3,4},{4,5},{5,6},{6,7},{7,8},{8,9},{9,10},{10,1... | collective-permute-start | bytes 3932168 | tf_op jit(solution)/shard_map/ppermute | solution.py:36
  198.3 2.6 %collective-permute-start.9 = (f32[2,2,128,640]{3,2,1,0:T(8,128)}, f32[2,2,128,640]{3,2,1,0:T(8,128)}, u32[]{:S(2)}, u32[]{:S(2)}) collective-permute-start(f32[2,2,128,640]{3,2,1,0:T(8,128)} %get-tuple-element.143), channel_id=1, source_target_pairs={{1,0},{2,1},{3,2},{4,3},{5,4},{6,5},{7,6},{8,7},{9,8},{10,9},{11,1... | collective-permute-start | bytes 3932168 | tf_op jit(solution)/shard_map/ppermute | solution.py:36
  202.5 17.2 %all_to_all.33 = f32[32,1,2]{2,1,0:T(1,128)S(1)} all-to-all(f32[32,1,2]{2,1,0:T(1,128)S(1)} %broadcast_in_dim.11), channel_id=1, replica_groups=mesh['freq'=4,'rcv'=32] {'rcv'}, dimensions={0} | all-to-all | bytes 512 | tf_op jit(solution)/shard_map/all_to_all | solution.py:57
  219.9 4.7 %subtract_multiply_fusion = (f32[2,2,128,640]{3,2,1,0:T(8,128)}, f32[2,2,128,640]{3,2,1,0:T(8,128)}) fusion(f32[2,2,128,640]{3,2,1,0:T(8,128)} %get-tuple-element.140, f32[2,2,128,640]{3,2,1,0:T(8,128)} %collective-permute-done.9, f32[2,2,128,640]{3,2,1,0:T(8,128)} %get-tuple-element.141, f32[2,2,128,640]{3,2,1,0:T(8,128)} %collective-permute-done.8, ...), kind=kLoop, calls=%fused_computation.9 | loop fusion | flops 4587520 | bytes 10485816 | tf_op jit(solution)/shard_map/mul | solution.py:417
  (57 shorter events, 13.0 us)
Async XLA Ops:
  6.7 13.0 %copy-start.6 = (s32[2,5]{1,0:T(2,128)S(1)}, s32[2,5]{1,0:T(2,128)}, u32[]{:S(2)}) copy-start(s32[2,5]{1,0:T(2,128)} %param.31) | copy-start | bytes 124
  6.7 13.6 %copy-start.5 = (s32[2,5,11]{2,0,1:T(2,128)S(1)}, s32[2,5,11]{2,0,1:T(2,128)}, u32[]{:S(2)}) copy-start(s32[2,5,11]{2,0,1:T(2,128)} %param.30) | copy-start | bytes 1324
  8.3 26.4 %all-to-all-start = ((bf16[2,2,1,128,640]{4,1,0,2,3:T(2,128)(2,1)}), bf16[2,2,1,128,640]{4,1,0,2,3:T(2,128)(2,1)S(1)}, u32[]{:S(2)}, u32[]{:S(2)}) async-start(bf16[2,2,1,128,640]{4,1,0,2,3:T(2,128)(2,1)} %copy.22), calls=%async_computation | async-start | bytes 1310720 | tf_op jit(solution)/shard_map/all_to_all | solution.py:351
  48.4 17.9 %collective-permute-start = (f32[2,2,128,640]{3,2,1,0:T(8,128)}, f32[2,2,128,640]{3,2,1,0:T(8,128)S(1)}, u32[]{:S(2)}, u32[]{:S(2)}) collective-permute-start(f32[2,2,128,640]{3,2,1,0:T(8,128)} %get-tuple-element.134), channel_id=1, source_target_pairs={{0,1},{1,2},{2,3},{3,4},{4,5},{5,6},{6,7},{7,8},{8,9},{9,10},{10,1... | collective-permute-start | bytes 3932168 | tf_op jit(solution)/shard_map/ppermute | solution.py:36
  51.4 19.1 %collective-permute-start.1 = (f32[2,2,128,640]{3,2,1,0:T(8,128)}, f32[2,2,128,640]{3,2,1,0:T(8,128)S(1)}, u32[]{:S(2)}, u32[]{:S(2)}) collective-permute-start(f32[2,2,128,640]{3,2,1,0:T(8,128)} %get-tuple-element.135), channel_id=1, source_target_pairs={{1,0},{2,1},{3,2},{4,3},{5,4},{6,5},{7,6},{8,7},{9,8},{10,9},{11,1... | collective-permute-start | bytes 3932168 | tf_op jit(solution)/shard_map/ppermute | solution.py:36
  72.5 18.3 %copy-start = (f32[2,2,128,640]{3,2,1,0:T(8,128)}, f32[2,2,128,640]{3,2,1,0:T(8,128)S(1)}, u32[]{:S(2)}) copy-start(f32[2,2,128,640]{3,2,1,0:T(8,128)S(1)} %get-tuple-element.155.q_ref) | copy-start | bytes 3932164
  73.6 15.3 %all-to-all-start.1 = ((f32[32,2,2]{2,1,0:T(2,128)}), f32[32,2,2]{2,1,0:T(2,128)S(1)}, u32[]{:S(2)}, u32[]{:S(2)}) async-start(f32[32,2,2]{2,1,0:T(2,128)} %broadcast_in_dim.8), calls=%async_computation.1 | async-start | bytes 65536 | tf_op jit(solution)/shard_map/all_to_all | solution.py:57
  81.6 12.0 %collective-permute-start.3 = (bf16[2,2,128,640]{3,2,1,0:T(8,128)(2,1)S(1)}, bf16[2,2,128,640]{3,2,1,0:T(8,128)(2,1)S(1)}, u32[]{:S(2)}, u32[]{:S(2)}) collective-permute-start(bf16[2,2,128,640]{3,2,1,0:T(8,128)(2,1)S(1)} %get-tuple-element.154), channel_id=1, source_target_pairs={{1,0},{2,1},{3,2},{4,3},{5,4},{6,5},{7,6},{8,7},{9,8},{10,9},{11,1... | collective-permute-start | bytes 1966088 | tf_op jit(solution)/shard_map/ppermute | solution.py:26
  83.8 10.9 %collective-permute-start.2 = (bf16[2,2,128,640]{3,2,1,0:T(8,128)(2,1)S(1)}, bf16[2,2,128,640]{3,2,1,0:T(8,128)(2,1)}, u32[]{:S(2)}, u32[]{:S(2)}) collective-permute-start(bf16[2,2,128,640]{3,2,1,0:T(8,128)(2,1)S(1)} %get-tuple-element.154), channel_id=1, source_target_pairs={{0,1},{1,2},{2,3},{3,4},{4,5},{5,6},{6,7},{7,8},{8,9},{9,10},{10,1... | collective-permute-start | bytes 1966088 | tf_op jit(solution)/shard_map/ppermute | solution.py:24
  116.0 31.6 %copy-start.1 = (f32[2,2,128,640]{3,2,1,0:T(8,128)S(1)}, f32[2,2,128,640]{3,2,1,0:T(8,128)}, u32[]{:S(2)}) copy-start(f32[2,2,128,640]{3,2,1,0:T(8,128)} %copy-done) | copy-start | bytes 3932164
  116.0 30.5 %collective-permute-start.4 = (f32[2,2,128,640]{3,2,1,0:T(8,128)}, f32[2,2,128,640]{3,2,1,0:T(8,128)S(1)}, u32[]{:S(2)}, u32[]{:S(2)}) collective-permute-start(f32[2,2,128,640]{3,2,1,0:T(8,128)} %get-tuple-element.138), channel_id=1, source_target_pairs={{0,1},{1,2},{2,3},{3,4},{4,5},{5,6},{6,7},{7,8},{8,9},{9,10},{10,1... | collective-permute-start | bytes 3932168 | tf_op jit(solution)/shard_map/ppermute | solution.py:36
  120.7 25.9 %collective-permute-start.5 = (f32[2,2,128,640]{3,2,1,0:T(8,128)}, f32[2,2,128,640]{3,2,1,0:T(8,128)}, u32[]{:S(2)}, u32[]{:S(2)}) collective-permute-start(f32[2,2,128,640]{3,2,1,0:T(8,128)} %get-tuple-element.139), channel_id=1, source_target_pairs={{1,0},{2,1},{3,2},{4,3},{5,4},{6,5},{7,6},{8,7},{9,8},{10,9},{11,1... | collective-permute-start | bytes 3932168 | tf_op jit(solution)/shard_map/ppermute | solution.py:36
  124.8 21.7 %all-to-all-start.2 = ((f32[32,1,2]{2,1,0:T(1,128)}), f32[32,1,2]{2,1,0:T(1,128)S(1)}, u32[]{:S(2)}, u32[]{:S(2)}) async-start(f32[32,1,2]{2,1,0:T(1,128)} %broadcast_in_dim.9), calls=%async_computation.2 | async-start | bytes 32768 | tf_op jit(solution)/shard_map/all_to_all | solution.py:57
  146.6 1.1 copy-start.4
  151.6 25.0 %copy-start.2 = (f32[2,2,128,640]{3,2,1,0:T(8,128)}, f32[2,2,128,640]{3,2,1,0:T(8,128)S(1)}, u32[]{:S(2)}) copy-start(f32[2,2,128,640]{3,2,1,0:T(8,128)S(1)} %get-tuple-element.151.q_ref) | copy-start | bytes 3932164
  151.6 22.2 %collective-permute-start.7 = (bf16[2,2,128,640]{3,2,1,0:T(8,128)(2,1)S(1)}, bf16[2,2,128,640]{3,2,1,0:T(8,128)(2,1)}, u32[]{:S(2)}, u32[]{:S(2)}) collective-permute-start(bf16[2,2,128,640]{3,2,1,0:T(8,128)(2,1)S(1)} %get-tuple-element.150), channel_id=1, source_target_pairs={{1,0},{2,1},{3,2},{4,3},{5,4},{6,5},{7,6},{8,7},{9,8},{10,9},{11,1... | collective-permute-start | bytes 1966088 | tf_op jit(solution)/shard_map/ppermute | solution.py:26
  154.2 19.7 %collective-permute-start.6 = (bf16[2,2,128,640]{3,2,1,0:T(8,128)(2,1)S(1)}, bf16[2,2,128,640]{3,2,1,0:T(8,128)(2,1)}, u32[]{:S(2)}, u32[]{:S(2)}) collective-permute-start(bf16[2,2,128,640]{3,2,1,0:T(8,128)(2,1)S(1)} %get-tuple-element.150), channel_id=1, source_target_pairs={{0,1},{1,2},{2,3},{3,4},{4,5},{5,6},{6,7},{7,8},{8,9},{9,10},{10,1... | collective-permute-start | bytes 1966088 | tf_op jit(solution)/shard_map/ppermute | solution.py:24
  195.4 24.5 %copy-start.3 = (f32[2,2,128,640]{3,2,1,0:T(8,128)S(1)}, f32[2,2,128,640]{3,2,1,0:T(8,128)}, u32[]{:S(2)}) copy-start(f32[2,2,128,640]{3,2,1,0:T(8,128)} %copy-done.2) | copy-start | bytes 3932164
  195.4 24.5 %collective-permute-start.8 = (f32[2,2,128,640]{3,2,1,0:T(8,128)}, f32[2,2,128,640]{3,2,1,0:T(8,128)}, u32[]{:S(2)}, u32[]{:S(2)}) collective-permute-start(f32[2,2,128,640]{3,2,1,0:T(8,128)} %get-tuple-element.142), channel_id=1, source_target_pairs={{0,1},{1,2},{2,3},{3,4},{4,5},{5,6},{6,7},{7,8},{8,9},{9,10},{10,1... | collective-permute-start | bytes 3932168 | tf_op jit(solution)/shard_map/ppermute | solution.py:36
  198.3 21.6 %collective-permute-start.9 = (f32[2,2,128,640]{3,2,1,0:T(8,128)}, f32[2,2,128,640]{3,2,1,0:T(8,128)}, u32[]{:S(2)}, u32[]{:S(2)}) collective-permute-start(f32[2,2,128,640]{3,2,1,0:T(8,128)} %get-tuple-element.143), channel_id=1, source_target_pairs={{1,0},{2,1},{3,2},{4,3},{5,4},{6,5},{7,6},{8,7},{9,8},{10,9},{11,1... | collective-permute-start | bytes 3932168 | tf_op jit(solution)/shard_map/ppermute | solution.py:36

commit v9 on v8

--- a/solution.py
+++ b/solution.py
@@ -71,8 +71,12 @@
 
 
 def _stack_kernel(counts_ref, a_ref, m_ref):
+    count = counts_ref[pl.program_id(0) * pl.num_programs(1) + pl.program_id(1)]
+    _build(count, a_ref, m_ref)
+
+
+def _build(count, a_ref, m_ref):
     slots, _, block, _ = a_ref.shape
-    count = counts_ref[pl.program_id(0) * pl.num_programs(1) + pl.program_id(1)]
     for slot in range(slots):
         live = slot < count
         real_part = jnp.where(live, a_ref[slot, 0], jnp.zeros_like(a_ref[slot, 0]))
@@ -168,6 +172,66 @@
     @pl.when(row == rows - 1)
     def _():
         _split(acc_ref, lower_ref, middle_ref, upper_ref)
+
+
+def _first_kernel(
+    cols_ref, counts_ref, u_ref, a_ref, m_ref, lower_ref, middle_ref, upper_ref, acc_ref
+):
+    freq = pl.program_id(0)
+    row = pl.program_id(1)
+    rows = pl.num_programs(1)
+    index = freq * rows + row
+
+    @pl.when(row == 0)
+    def _():
+        acc_ref[...] = jnp.zeros(acc_ref.shape, acc_ref.dtype)
+
+    _build(counts_ref[index], a_ref, m_ref)
+    field = jnp.concatenate([u_ref[0], u_ref[1]], axis=1)
+    _scatter(cols_ref, index, field, m_ref, acc_ref)
+
+    @pl.when(row == rows - 1)
+    def _():
+        _split(acc_ref, lower_ref, middle_ref, upper_ref)
+
+
+def apply_first(rounded, down_blocks, cols, counts, span):
+    local_freqs, local_blocks, slot_count, _, block_size, _ = down_blocks.shape
+    depth = 2 * block_size
+    width = 2 * slot_count * block_size
+    sources = rounded.shape[2]
+    own = local_blocks * block_size
+    rim = (span - own) // 2
+    part_spec, part_shape = _part_specs(local_freqs, sources)
+    grid_spec = pltpu.PrefetchScalarGridSpec(
+        num_scalar_prefetch=2,
+        grid=(local_freqs, local_blocks),
+        in_specs=[
+            pl.BlockSpec((2, None, sources, block_size), lambda f, r, c, n: (0, f, 0, r)),
+            pl.BlockSpec(
+                (None, None, slot_count, 2, block_size, block_size),
+                lambda f, r, c, n: (f, r, 0, 0, 0, 0),
+            ),
+        ],
+        out_specs=[
+            pl.BlockSpec((None, None, depth, width), lambda f, r, c, n: (f, r, 0, 0)),
+            part_spec(rim),
+            part_spec(own),
+            part_spec(rim),
+        ],
+        scratch_shapes=[pltpu.VMEM((2, sources, span), jnp.float32)],
+    )
+    return pl.pallas_call(
+        _first_kernel,
+        grid_spec=grid_spec,
+        out_shape=[
+            jax.ShapeDtypeStruct((local_freqs, local_blocks, depth, width), jnp.bfloat16),
+            part_shape(rim),
+            part_shape(own),
+            part_shape(rim),
+        ],
+        compiler_params=pltpu.CompilerParams(dimension_semantics=("arbitrary", "arbitrary")),
+    )(cols, counts, rounded, down_blocks)
 
 
 def _both_kernel(
@@ -355,7 +419,6 @@
         block_cols - position * local_blocks + reach_blocks, 0, span_blocks - 1
     ).reshape(-1)
     counts = jnp.clip(block_counts, 0, slot_count).reshape(-1)
-    stacked = stack_blocks(down_blocks, counts)
 
     def exchange(lower_rim, middle, upper_rim):
         from_above = from_behind(lower_rim, "rcv", -1)
@@ -364,10 +427,12 @@
         middle = middle.at[..., local_rows - rim_rows :].add(from_above)
         return middle
 
-    def adjoint(field):
+    def first_adjoint(field):
         rounded = field.astype(jnp.bfloat16)
-        parts = apply_adjoint(rounded, stacked, columns, counts, span_blocks * block_size)
-        return field + exchange(*parts)
+        stacked, *parts = apply_first(
+            rounded, down_blocks, columns, counts, span_blocks * block_size
+        )
+        return stacked, field + exchange(*parts)
 
     def forward_adjoint(raw, scale, left, shift):
         extended = with_halo(raw.astype(jnp.bfloat16), (("rcv", 3),), rim_rows)
@@ -381,7 +446,7 @@
         extended = with_halo(field.astype(jnp.bfloat16), (("rcv", 3),), rim_rows)
         return field + apply_forward(extended, stacked, columns, counts)
 
-    lifted = adjoint(right_side)
+    stacked, lifted = first_adjoint(right_side)
     right_squares, lifted_squares = both_squares(right_side, lifted)
     beta_norm = jnp.sqrt(right_squares + EPSILON)
     alpha_norm = jnp.sqrt(lifted_squares / (beta_norm * beta_norm) + EPSILON)

time: 226 us -> 228 us (level)
  waiting for transfers between devices: 34.7 us -> 46.4 us
  Pallas kernels: 62.1 us -> 52.7 us
    all_to_all x1, waiting for transfers between devices: 1.93 us -> 13.6 us  [body(): lax.all_to_all(spectrum, ('freq', 'rcv'), split_axis=3, concat_axis=2, ti...]
    pallas_call x2 -> x1, Pallas kernels: 24.5 us -> 15.1 us  [apply_first(): pl.pallas_call(_first_kernel, grid_spec=grid_spec, out_shape=[jax.ShapeDt...]
  transfers between devices with their start and end apart: 13 -> 13, of which waited for: 7 -> 7; matrix products, arithmetic and copies ran while one was open for 4% -> 4% of each run, Pallas kernels for 5% -> 0%
where the time goes in v9:
time: 228 us; the launch traced here: 227 us
  starting transfers between devices  59.2 us (26%)
  Pallas kernels  52.7 us (23%)
  waiting for transfers between devices  46.4 us (20%)
  blocking collectives  32.8 us (14%)
  other arithmetic  21.4 us (9%)
  local copies, waits for them, and re-layouts  8.01 us (4%)
  matrix products  5.45 us (2%)
    pallas_call x2, Pallas kernels, apply_both(): pl.pallas_call(_both_kernel, grid_spec=grid_spec, out_shape=[jax.ShapeDty...  37.5 us
    all_to_all x2, blocking collectives, rcv_sum(): gathered = lax.all_to_all(spread, 'rcv', 0, 0, tiled=False)  32.8 us
    all_to_all x2, starting transfers between devices, rcv_sum(): gathered = lax.all_to_all(spread, 'rcv', 0, 0, tiled=False)  19.6 us
    ppermute x6, waiting for transfers between devices, from_behind(): lax.ppermute(value, axis, [(source, source + steps) for source in range(f...  17.2 us
    ppermute x6, starting transfers between devices, from_behind(): lax.ppermute(value, axis, [(source, source + steps) for source in range(f...  17 us
    pallas_call x1, Pallas kernels, apply_first(): pl.pallas_call(_first_kernel, grid_spec=grid_spec, out_shape=[jax.ShapeDt...  15.1 us
    all_to_all x1, waiting for transfers between devices, body(): lax.all_to_all(spectrum, ('freq', 'rcv'), split_axis=3, concat_axis=2, ti...  13.6 us
    all_to_all x2, waiting for transfers between devices, rcv_sum(): gathered = lax.all_to_all(spread, 'rcv', 0, 0, tiled=False)  11.8 us
  transfers between devices with their start and end apart: 13, of which 7 were waited for; matrix products, arithmetic and copies ran while one was open for 4% of the time, Pallas kernels for 0%

profile of v9, /device:TPU:1, one launch (start us, length us, event | category | flops | bytes accessed | tf_op | source)
XLA Modules:
  0.0 226.8 jit_solution(3213766947282378258)
XLA Ops:
  0.8 5.5 %fusion = bf16[2,2,1,4,20480]{4,3,1,0,2:T(4,128)(2,1)S(1)} fusion(bf16[1,256,20480]{2,1,0:T(8,128)(2,1)} %param.28, bf16[256,1,4,2]{0,2,3,1:T(4,128)(2,1)S(1)} %get-tuple-element.170, bf16[256,1,4,2]{0,2,3,1:T(4,128)(2,1)S(1)} %get-tuple-element.169), kind=kOutput, calls=%fused_computation.1 | convolution fusion | flops 168116224 | bytes 11149312 | tf_op jit(solution)/shard_map/snr,ncgf->cfsgr/dot_general | solution.py:409
  8.3 11.5 %all-to-all-start = ((bf16[2,2,1,128,640]{4,1,0,2,3:T(2,128)(2,1)}), bf16[2,2,1,128,640]{4,1,0,2,3:T(2,128)(2,1)S(1)}, u32[]{:S(2)}, u32[]{:S(2)}) async-start(bf16[2,2,1,128,640]{4,1,0,2,3:T(2,128)(2,1)} %copy.22), calls=%async_computation | async-start | bytes 1310720 | tf_op jit(solution)/shard_map/all_to_all | solution.py:415
  21.1 13.6 %all-to-all-done = bf16[2,2,1,128,640]{4,1,0,2,3:T(2,128)(2,1)S(1)} async-done(((bf16[2,2,1,128,640]{4,1,0,2,3:T(2,128)(2,1)}), bf16[2,2,1,128,640]{4,1,0,2,3:T(2,128)(2,1)S(1)}, u32[]{:S(2)}, u32[]{:S(2)}) %all-to-all-start) | async-done | bytes 655392 | tf_op jit(solution)/shard_map/all_to_all | solution.py:415
  35.6 15.1 %shard_map.89 = (bf16[2,5,256,2816]{3,2,1,0:T(8,128)(2,1)}, f32[2,2,128,640]{3,2,1,0:T(8,128)}, f32[2,2,128,640]{3,2,1,0:T(8,128)}, f32[2,2,128,640]{3,2,1,0:T(8,128)}) custom-call(s32[110]{0:T(128)} %reshape.545.cols_ref, s32[10]{0:T(128)} %reshape.546.counts_ref, bf16[2,2,128,640]{3,2,1,0:T(8,128)(2,1)} %bitcast.53, bf16[2,5,11,2,128,128]{5,4,3,2,1,0:T(8,128)(2,1)} %a_ref.1), custom_call_target="tpu_custom_call" | custom-call | tf_op jit(solution)/shard_map/pallas_call | solution.py:224
  50.7 3.0 %collective-permute-start = (f32[2,2,128,640]{3,2,1,0:T(8,128)}, f32[2,2,128,640]{3,2,1,0:T(8,128)S(1)}, u32[]{:S(2)}, u32[]{:S(2)}) collective-permute-start(f32[2,2,128,640]{3,2,1,0:T(8,128)} %get-tuple-element.135), channel_id=1, source_target_pairs={{0,1},{1,2},{2,3},{3,4},{4,5},{5,6},{6,7},{7,8},{8,9},{9,10},{10,1... | collective-permute-start | bytes 3932168 | tf_op jit(solution)/shard_map/ppermute | solution.py:36
  53.7 1.9 collective-permute-start.1
  55.6 12.9 %collective-permute-done = f32[2,2,128,640]{3,2,1,0:T(8,128)S(1)} collective-permute-done((f32[2,2,128,640]{3,2,1,0:T(8,128)}, f32[2,2,128,640]{3,2,1,0:T(8,128)S(1)}, u32[]{:S(2)}, u32[]{:S(2)}) %collective-permute-start) | collective-permute-done | bytes 1310752 | tf_op jit(solution)/shard_map/ppermute | solution.py:36
  68.6 4.3 %collective-permute-done.1 = f32[2,2,128,640]{3,2,1,0:T(8,128)S(1)} collective-permute-done((f32[2,2,128,640]{3,2,1,0:T(8,128)}, f32[2,2,128,640]{3,2,1,0:T(8,128)S(1)}, u32[]{:S(2)}, u32[]{:S(2)}) %collective-permute-start.1) | collective-permute-done | bytes 1310752 | tf_op jit(solution)/shard_map/ppermute | solution.py:36
  72.9 2.0 fusion.17
  75.9 8.0 %all-to-all-start.1 = ((f32[32,2,2]{2,1,0:T(2,128)}), f32[32,2,2]{2,1,0:T(2,128)S(1)}, u32[]{:S(2)}, u32[]{:S(2)}) async-start(f32[32,2,2]{2,1,0:T(2,128)} %broadcast_in_dim.8), calls=%async_computation.1 | async-start | bytes 65536 | tf_op jit(solution)/shard_map/all_to_all | solution.py:57
  83.9 2.1 collective-permute-start.3
  86.0 3.4 %collective-permute-start.2 = (bf16[2,2,128,640]{3,2,1,0:T(8,128)(2,1)S(1)}, bf16[2,2,128,640]{3,2,1,0:T(8,128)(2,1)}, u32[]{:S(2)}, u32[]{:S(2)}) collective-permute-start(bf16[2,2,128,640]{3,2,1,0:T(8,128)(2,1)S(1)} %get-tuple-element.156), channel_id=1, source_target_pairs={{0,1},{1,2},{2,3},{3,4},{4,5},{5,6},{6,7},{7,8},{8,9},{9,10},{10,1... | collective-permute-start | bytes 1966088 | tf_op jit(solution)/shard_map/ppermute | solution.py:24
  89.5 1.7 all-to-all-done.1
  93.2 2.7 %collective-permute-done.3 = bf16[2,2,128,640]{3,2,1,0:T(8,128)(2,1)S(1)} collective-permute-done((bf16[2,2,128,640]{3,2,1,0:T(8,128)(2,1)S(1)}, bf16[2,2,128,640]{3,2,1,0:T(8,128)(2,1)S(1)}, u32[]{:S(2)}, u32[]{:S(2)}) %collective-permute-start.3) | collective-permute-done | bytes 655392 | tf_op jit(solution)/shard_map/ppermute | solution.py:26
  97.0 2.5 %pad_maximum_fusion.x_ref = bf16[2,2,128,1920]{3,2,1,0:T(8,128)(2,1)} fusion(bf16[2,2,128,640]{3,2,1,0:T(8,128)(2,1)S(1)} %collective-permute-done.3, bf16[2,2,128,640]{3,2,1,0:T(8,128)(2,1)S(1)} %get-tuple-element.156, bf16[2,2,128,640]{3,2,1,0:T(8,128)(2,1)} %collective-permute-done.2), kind=kLoop, calls=%fused_computation.3 | loop fusion | flops 5898240 | bytes 3932160 | tf_op jit(solution)/shard_map/concatenate | solution.py:22
  99.5 18.8 %shard_map.90 = (f32[2,2,128,640]{3,2,1,0:T(8,128)}, f32[2,2,128,640]{3,2,1,0:T(8,128)}, f32[2,2,128,640]{3,2,1,0:T(8,128)}, f32[2,2,128,640]{3,2,1,0:T(8,128)}) custom-call(s32[110]{0:T(128)} %reshape.545.cols_ref, s32[10]{0:T(128)} %reshape.546.counts_ref, f32[4]{0:T(128)} %reshape.547.coef_ref, bf16[2,2,128,1920]{3,2,1,0:T(8,128)(2,1)} %pad_maximum_fusion.x_ref, ...), custom_call_target="tpu_custom_call" | custom-call | flops 3690987520 | bytes 29491200 | tf_op jit(solution)/shard_map/pallas_call | solution.py:322
  118.3 4.6 %collective-permute-start.4 = (f32[2,2,128,640]{3,2,1,0:T(8,128)}, f32[2,2,128,640]{3,2,1,0:T(8,128)S(1)}, u32[]{:S(2)}, u32[]{:S(2)}) collective-permute-start(f32[2,2,128,640]{3,2,1,0:T(8,128)} %get-tuple-element.140), channel_id=1, source_target_pairs={{0,1},{1,2},{2,3},{3,4},{4,5},{5,6},{6,7},{7,8},{8,9},{9,10},{10,1... | collective-permute-start | bytes 3932168 | tf_op jit(solution)/shard_map/ppermute | solution.py:36
  122.9 1.9 collective-permute-start.5
  124.8 1.6 multiply_reduce_fusion.2
  127.0 11.6 %all-to-all-start.2 = ((f32[32,1,2]{2,1,0:T(1,128)}), f32[32,1,2]{2,1,0:T(1,128)S(1)}, u32[]{:S(2)}, u32[]{:S(2)}) async-start(f32[32,1,2]{2,1,0:T(1,128)} %broadcast_in_dim.9), calls=%async_computation.2 | async-start | bytes 32768 | tf_op jit(solution)/shard_map/all_to_all | solution.py:57
  138.7 10.1 %all-to-all-done.2 = f32[32,1,2]{2,1,0:T(1,128)S(1)} async-done(((f32[32,1,2]{2,1,0:T(1,128)}), f32[32,1,2]{2,1,0:T(1,128)S(1)}, u32[]{:S(2)}, u32[]{:S(2)}) %all-to-all-start.2) | async-done | bytes 288 | tf_op jit(solution)/shard_map/all_to_all | solution.py:57
  149.9 4.0 %fusion.16 = (bf16[2,2,128,640]{3,2,1,0:T(8,128)(2,1)S(1)}, f32[2,2,128,640]{3,2,1,0:T(8,128)S(1)}, f32[2,2,128,640]{3,2,1,0:T(8,128)}) fusion(f32[2,2,128,640]{3,2,1,0:T(8,128)S(1)} %copy-done.1, f32[2]{0:T(128)S(1)} %get-tuple-element.154, f32[2]{0:T(128)S(1)} %add_sqrt_fusion.4, f32[2,2,128,640]{3,2,1,0:T(8,128)} %get-tuple-element.138, ...), kind=kLoop, calls=%fused_computation.60 | loop fusion | flops 2949120 | bytes 9830416 | tf_op jit(solution)/shard_map/convert_element_type | solution.py:438
  153.9 2.6 %collective-permute-start.7 = (bf16[2,2,128,640]{3,2,1,0:T(8,128)(2,1)S(1)}, bf16[2,2,128,640]{3,2,1,0:T(8,128)(2,1)}, u32[]{:S(2)}, u32[]{:S(2)}) collective-permute-start(bf16[2,2,128,640]{3,2,1,0:T(8,128)(2,1)S(1)} %get-tuple-element.152), channel_id=1, source_target_pairs={{1,0},{2,1},{3,2},{4,3},{5,4},{6,5},{7,6},{8,7},{9,8},{10,9},{11,1... | collective-permute-start | bytes 1966088 | tf_op jit(solution)/shard_map/ppermute | solution.py:26
  156.5 3.1 %collective-permute-start.6 = (bf16[2,2,128,640]{3,2,1,0:T(8,128)(2,1)S(1)}, bf16[2,2,128,640]{3,2,1,0:T(8,128)(2,1)}, u32[]{:S(2)}, u32[]{:S(2)}) collective-permute-start(bf16[2,2,128,640]{3,2,1,0:T(8,128)(2,1)S(1)} %get-tuple-element.152), channel_id=1, source_target_pairs={{0,1},{1,2},{2,3},{3,4},{4,5},{5,6},{6,7},{7,8},{8,9},{9,10},{10,1... | collective-permute-start | bytes 1966088 | tf_op jit(solution)/shard_map/ppermute | solution.py:24
  159.8 15.6 %all_to_all.32 = f32[32,1,2]{2,1,0:T(1,128)S(1)} all-to-all(f32[32,1,2]{2,1,0:T(1,128)S(1)} %broadcast_in_dim.10), channel_id=1, replica_groups=mesh['freq'=4,'rcv'=32] {'rcv'}, dimensions={0} | all-to-all | bytes 512 | tf_op jit(solution)/shard_map/all_to_all | solution.py:57
  176.1 2.7 %pad_maximum_fusion.1.x_ref = bf16[2,2,128,1920]{3,2,1,0:T(8,128)(2,1)} fusion(bf16[2,2,128,640]{3,2,1,0:T(8,128)(2,1)} %collective-permute-done.7, bf16[2,2,128,640]{3,2,1,0:T(8,128)(2,1)S(1)} %get-tuple-element.152, bf16[2,2,128,640]{3,2,1,0:T(8,128)(2,1)} %collective-permute-done.6), kind=kLoop, calls=%fused_computation.4 | loop fusion | flops 5898240 | bytes 3932160 | tf_op jit(solution)/shard_map/concatenate | solution.py:22
  178.9 18.8 %shard_map.91 = (f32[2,2,128,640]{3,2,1,0:T(8,128)}, f32[2,2,128,640]{3,2,1,0:T(8,128)}, f32[2,2,128,640]{3,2,1,0:T(8,128)}, f32[2,2,128,640]{3,2,1,0:T(8,128)}) custom-call(s32[110]{0:T(128)} %reshape.545.cols_ref, s32[10]{0:T(128)} %reshape.546.counts_ref, f32[4]{0:T(128)} %reshape.548.coef_ref, bf16[2,2,128,1920]{3,2,1,0:T(8,128)(2,1)} %pad_maximum_fusion.1.x_ref, ...), custom_call_target="tpu_custom_call" | custom-call | flops 3690987520 | bytes 29491200 | tf_op jit(solution)/shard_map/pallas_call | solution.py:322
  197.6 2.9 %collective-permute-start.8 = (f32[2,2,128,640]{3,2,1,0:T(8,128)}, f32[2,2,128,640]{3,2,1,0:T(8,128)}, u32[]{:S(2)}, u32[]{:S(2)}) collective-permute-start(f32[2,2,128,640]{3,2,1,0:T(8,128)} %get-tuple-element.144), channel_id=1, source_target_pairs={{0,1},{1,2},{2,3},{3,4},{4,5},{5,6},{6,7},{7,8},{8,9},{9,10},{10,1... | collective-permute-start | bytes 3932168 | tf_op jit(solution)/shard_map/ppermute | solution.py:36
  200.5 2.6 %collective-permute-start.9 = (f32[2,2,128,640]{3,2,1,0:T(8,128)}, f32[2,2,128,640]{3,2,1,0:T(8,128)}, u32[]{:S(2)}, u32[]{:S(2)}) collective-permute-start(f32[2,2,128,640]{3,2,1,0:T(8,128)} %get-tuple-element.145), channel_id=1, source_target_pairs={{1,0},{2,1},{3,2},{4,3},{5,4},{6,5},{7,6},{8,7},{9,8},{10,9},{11,1... | collective-permute-start | bytes 3932168 | tf_op jit(solution)/shard_map/ppermute | solution.py:36
  203.2 1.6 multiply_reduce_fusion
  204.8 17.3 %all_to_all.33 = f32[32,1,2]{2,1,0:T(1,128)S(1)} all-to-all(f32[32,1,2]{2,1,0:T(1,128)S(1)} %broadcast_in_dim.11), channel_id=1, replica_groups=mesh['freq'=4,'rcv'=32] {'rcv'}, dimensions={0} | all-to-all | bytes 512 | tf_op jit(solution)/shard_map/all_to_all | solution.py:57
  222.2 4.7 %subtract_multiply_fusion = (f32[2,2,128,640]{3,2,1,0:T(8,128)}, f32[2,2,128,640]{3,2,1,0:T(8,128)}) fusion(f32[2,2,128,640]{3,2,1,0:T(8,128)} %get-tuple-element.142, f32[2,2,128,640]{3,2,1,0:T(8,128)} %collective-permute-done.9, f32[2,2,128,640]{3,2,1,0:T(8,128)} %get-tuple-element.143, f32[2,2,128,640]{3,2,1,0:T(8,128)} %collective-permute-done.8, ...), kind=kLoop, calls=%fused_computation.9 | loop fusion | flops 4587520 | bytes 10485816 | tf_op jit(solution)/shard_map/mul | solution.py:482
  (56 shorter events, 11.4 us)
Async XLA Ops:
  6.7 13.0 %copy-start.6 = (s32[2,5]{1,0:T(2,128)S(1)}, s32[2,5]{1,0:T(2,128)}, u32[]{:S(2)}) copy-start(s32[2,5]{1,0:T(2,128)} %param.31) | copy-start | bytes 124
  6.7 13.6 %copy-start.5 = (s32[2,5,11]{2,0,1:T(2,128)S(1)}, s32[2,5,11]{2,0,1:T(2,128)}, u32[]{:S(2)}) copy-start(s32[2,5,11]{2,0,1:T(2,128)} %param.30) | copy-start | bytes 1324
  8.3 26.4 %all-to-all-start = ((bf16[2,2,1,128,640]{4,1,0,2,3:T(2,128)(2,1)}), bf16[2,2,1,128,640]{4,1,0,2,3:T(2,128)(2,1)S(1)}, u32[]{:S(2)}, u32[]{:S(2)}) async-start(bf16[2,2,1,128,640]{4,1,0,2,3:T(2,128)(2,1)} %copy.22), calls=%async_computation | async-start | bytes 1310720 | tf_op jit(solution)/shard_map/all_to_all | solution.py:415
  50.7 17.9 %collective-permute-start = (f32[2,2,128,640]{3,2,1,0:T(8,128)}, f32[2,2,128,640]{3,2,1,0:T(8,128)S(1)}, u32[]{:S(2)}, u32[]{:S(2)}) collective-permute-start(f32[2,2,128,640]{3,2,1,0:T(8,128)} %get-tuple-element.135), channel_id=1, source_target_pairs={{0,1},{1,2},{2,3},{3,4},{4,5},{5,6},{6,7},{7,8},{8,9},{9,10},{10,1... | collective-permute-start | bytes 3932168 | tf_op jit(solution)/shard_map/ppermute | solution.py:36
  53.7 19.1 %collective-permute-start.1 = (f32[2,2,128,640]{3,2,1,0:T(8,128)}, f32[2,2,128,640]{3,2,1,0:T(8,128)S(1)}, u32[]{:S(2)}, u32[]{:S(2)}) collective-permute-start(f32[2,2,128,640]{3,2,1,0:T(8,128)} %get-tuple-element.136), channel_id=1, source_target_pairs={{1,0},{2,1},{3,2},{4,3},{5,4},{6,5},{7,6},{8,7},{9,8},{10,9},{11,1... | collective-permute-start | bytes 3932168 | tf_op jit(solution)/shard_map/ppermute | solution.py:36
  74.8 18.3 %copy-start = (f32[2,2,128,640]{3,2,1,0:T(8,128)}, f32[2,2,128,640]{3,2,1,0:T(8,128)S(1)}, u32[]{:S(2)}) copy-start(f32[2,2,128,640]{3,2,1,0:T(8,128)S(1)} %get-tuple-element.157.q_ref) | copy-start | bytes 3932164
  75.9 15.3 %all-to-all-start.1 = ((f32[32,2,2]{2,1,0:T(2,128)}), f32[32,2,2]{2,1,0:T(2,128)S(1)}, u32[]{:S(2)}, u32[]{:S(2)}) async-start(f32[32,2,2]{2,1,0:T(2,128)} %broadcast_in_dim.8), calls=%async_computation.1 | async-start | bytes 65536 | tf_op jit(solution)/shard_map/all_to_all | solution.py:57
  83.9 12.0 %collective-permute-start.3 = (bf16[2,2,128,640]{3,2,1,0:T(8,128)(2,1)S(1)}, bf16[2,2,128,640]{3,2,1,0:T(8,128)(2,1)S(1)}, u32[]{:S(2)}, u32[]{:S(2)}) collective-permute-start(bf16[2,2,128,640]{3,2,1,0:T(8,128)(2,1)S(1)} %get-tuple-element.156), channel_id=1, source_target_pairs={{1,0},{2,1},{3,2},{4,3},{5,4},{6,5},{7,6},{8,7},{9,8},{10,9},{11,1... | collective-permute-start | bytes 1966088 | tf_op jit(solution)/shard_map/ppermute | solution.py:26
  86.0 10.9 %collective-permute-start.2 = (bf16[2,2,128,640]{3,2,1,0:T(8,128)(2,1)S(1)}, bf16[2,2,128,640]{3,2,1,0:T(8,128)(2,1)}, u32[]{:S(2)}, u32[]{:S(2)}) collective-permute-start(bf16[2,2,128,640]{3,2,1,0:T(8,128)(2,1)S(1)} %get-tuple-element.156), channel_id=1, source_target_pairs={{0,1},{1,2},{2,3},{3,4},{4,5},{5,6},{6,7},{7,8},{8,9},{9,10},{10,1... | collective-permute-start | bytes 1966088 | tf_op jit(solution)/shard_map/ppermute | solution.py:24
  118.3 31.6 %copy-start.1 = (f32[2,2,128,640]{3,2,1,0:T(8,128)S(1)}, f32[2,2,128,640]{3,2,1,0:T(8,128)}, u32[]{:S(2)}) copy-start(f32[2,2,128,640]{3,2,1,0:T(8,128)} %copy-done) | copy-start | bytes 3932164
  118.3 30.5 %collective-permute-start.4 = (f32[2,2,128,640]{3,2,1,0:T(8,128)}, f32[2,2,128,640]{3,2,1,0:T(8,128)S(1)}, u32[]{:S(2)}, u32[]{:S(2)}) collective-permute-start(f32[2,2,128,640]{3,2,1,0:T(8,128)} %get-tuple-element.140), channel_id=1, source_target_pairs={{0,1},{1,2},{2,3},{3,4},{4,5},{5,6},{6,7},{7,8},{8,9},{9,10},{10,1... | collective-permute-start | bytes 3932168 | tf_op jit(solution)/shard_map/ppermute | solution.py:36
  122.9 25.9 %collective-permute-start.5 = (f32[2,2,128,640]{3,2,1,0:T(8,128)}, f32[2,2,128,640]{3,2,1,0:T(8,128)}, u32[]{:S(2)}, u32[]{:S(2)}) collective-permute-start(f32[2,2,128,640]{3,2,1,0:T(8,128)} %get-tuple-element.141), channel_id=1, source_target_pairs={{1,0},{2,1},{3,2},{4,3},{5,4},{6,5},{7,6},{8,7},{9,8},{10,9},{11,1... | collective-permute-start | bytes 3932168 | tf_op jit(solution)/shard_map/ppermute | solution.py:36
  127.0 21.7 %all-to-all-start.2 = ((f32[32,1,2]{2,1,0:T(1,128)}), f32[32,1,2]{2,1,0:T(1,128)S(1)}, u32[]{:S(2)}, u32[]{:S(2)}) async-start(f32[32,1,2]{2,1,0:T(1,128)} %broadcast_in_dim.9), calls=%async_computation.2 | async-start | bytes 32768 | tf_op jit(solution)/shard_map/all_to_all | solution.py:57
  148.8 1.1 copy-start.4
  153.9 25.0 %copy-start.2 = (f32[2,2,128,640]{3,2,1,0:T(8,128)}, f32[2,2,128,640]{3,2,1,0:T(8,128)S(1)}, u32[]{:S(2)}) copy-start(f32[2,2,128,640]{3,2,1,0:T(8,128)S(1)} %get-tuple-element.153.q_ref) | copy-start | bytes 3932164
  153.9 22.2 %collective-permute-start.7 = (bf16[2,2,128,640]{3,2,1,0:T(8,128)(2,1)S(1)}, bf16[2,2,128,640]{3,2,1,0:T(8,128)(2,1)}, u32[]{:S(2)}, u32[]{:S(2)}) collective-permute-start(bf16[2,2,128,640]{3,2,1,0:T(8,128)(2,1)S(1)} %get-tuple-element.152), channel_id=1, source_target_pairs={{1,0},{2,1},{3,2},{4,3},{5,4},{6,5},{7,6},{8,7},{9,8},{10,9},{11,1... | collective-permute-start | bytes 1966088 | tf_op jit(solution)/shard_map/ppermute | solution.py:26
  156.5 19.7 %collective-permute-start.6 = (bf16[2,2,128,640]{3,2,1,0:T(8,128)(2,1)S(1)}, bf16[2,2,128,640]{3,2,1,0:T(8,128)(2,1)}, u32[]{:S(2)}, u32[]{:S(2)}) collective-permute-start(bf16[2,2,128,640]{3,2,1,0:T(8,128)(2,1)S(1)} %get-tuple-element.152), channel_id=1, source_target_pairs={{0,1},{1,2},{2,3},{3,4},{4,5},{5,6},{6,7},{7,8},{8,9},{9,10},{10,1... | collective-permute-start | bytes 1966088 | tf_op jit(solution)/shard_map/ppermute | solution.py:24
  197.6 24.5 %copy-start.3 = (f32[2,2,128,640]{3,2,1,0:T(8,128)S(1)}, f32[2,2,128,640]{3,2,1,0:T(8,128)}, u32[]{:S(2)}) copy-start(f32[2,2,128,640]{3,2,1,0:T(8,128)} %copy-done.2) | copy-start | bytes 3932164
  197.6 24.5 %collective-permute-start.8 = (f32[2,2,128,640]{3,2,1,0:T(8,128)}, f32[2,2,128,640]{3,2,1,0:T(8,128)}, u32[]{:S(2)}, u32[]{:S(2)}) collective-permute-start(f32[2,2,128,640]{3,2,1,0:T(8,128)} %get-tuple-element.144), channel_id=1, source_target_pairs={{0,1},{1,2},{2,3},{3,4},{4,5},{5,6},{6,7},{7,8},{8,9},{9,10},{10,1... | collective-permute-start | bytes 3932168 | tf_op jit(solution)/shard_map/ppermute | solution.py:36
  200.5 21.6 %collective-permute-start.9 = (f32[2,2,128,640]{3,2,1,0:T(8,128)}, f32[2,2,128,640]{3,2,1,0:T(8,128)}, u32[]{:S(2)}, u32[]{:S(2)}) collective-permute-start(f32[2,2,128,640]{3,2,1,0:T(8,128)} %get-tuple-element.145), channel_id=1, source_target_pairs={{1,0},{2,1},{3,2},{4,3},{5,4},{6,5},{7,6},{8,7},{9,8},{10,9},{11,1... | collective-permute-start | bytes 3932168 | tf_op jit(solution)/shard_map/ppermute | solution.py:36

commit v10 on v8

--- a/solution.py
+++ b/solution.py
@@ -174,7 +174,9 @@
     cols_ref,
     counts_ref,
     coef_ref,
-    x_ref,
+    below_ref,
+    own_ref,
+    above_ref,
     q_ref,
     u_ref,
     m_ref,
@@ -197,11 +199,24 @@
     def _():
         acc_ref[...] = jnp.zeros(acc_ref.shape, acc_ref.dtype)
 
+    rim_blocks = below_ref.shape[-1] // block
+    own_blocks = own_ref.shape[-1] // block
+    pieces = (
+        (below_ref, 0, rim_blocks),
+        (own_ref, rim_blocks, rim_blocks + own_blocks),
+        (above_ref, rim_blocks + own_blocks, 2 * rim_blocks + own_blocks),
+    )
     for slot in range(slots):
-        start = pl.multiple_of(cols_ref[index * slots + slot] * block, block)
-        for part in range(2):
-            lanes = slice((2 * slot + part) * block, (2 * slot + part + 1) * block)
-            picked_ref[:, lanes] = x_ref[part, :, pl.ds(start, block)]
+        column = cols_ref[index * slots + slot]
+        for source, first, end in pieces:
+
+            @pl.when((column >= first) & (column < end))
+            def _():
+                start = pl.multiple_of((column - first) * block, block)
+                for part in range(2):
+                    lanes = slice((2 * slot + part) * block, (2 * slot + part + 1) * block)
+                    picked_ref[:, lanes] = source[part, :, pl.ds(start, block)]
+
     contract = (((1,), (1,)), ((), ()))
     product = lax.dot_general(
         picked_ref[...], m_ref[...], contract, preferred_element_type=jnp.float32
@@ -231,12 +246,13 @@
     return part_spec, part_shape
 
 
-def apply_both(extended, raw, left, coefs, stacked, cols, counts):
+def apply_both(below, own_field, above, raw, left, coefs, stacked, cols, counts):
     local_freqs, local_blocks, depth, width = stacked.shape
     block_size = depth // 2
-    _, _, sources, span = extended.shape
+    sources = raw.shape[2]
     own_rows = local_blocks * block_size
-    rim = (span - own_rows) // 2
+    rim = below.shape[-1]
+    span = 2 * rim + own_rows
     part_spec, part_shape = _part_specs(local_freqs, sources)
     own = pl.BlockSpec((2, None, sources, block_size), lambda f, r, c, n: (0, f, 0, r))
     grid_spec = pltpu.PrefetchScalarGridSpec(
@@ -244,7 +260,9 @@
         grid=(local_freqs, local_blocks),
         in_specs=[
             pl.BlockSpec(memory_space=pltpu.SMEM),
-            pl.BlockSpec((2, None, sources, span), lambda f, r, c, n: (0, f, 0, 0)),
+            part_spec(rim),
+            part_spec(own_rows),
+            part_spec(rim),
             own,
             own,
             pl.BlockSpec((None, None, depth, width), lambda f, r, c, n: (f, r, 0, 0)),
@@ -268,9 +286,9 @@
         cost_estimate=pl.CostEstimate(
             flops=4 * local_freqs * local_blocks * sources * depth * width,
             transcendentals=0,
-            bytes_accessed=stacked.size * 2 + extended.size * 2 + raw.size * 40,
-        ),
-    )(cols, counts, coefs, extended, raw, left, stacked)
+            bytes_accessed=stacked.size * 2 + raw.size * 46,
+        ),
+    )(cols, counts, coefs, below, own_field, above, raw, left, stacked)
 
 
 def apply_forward(extended, stacked, cols, counts):
@@ -370,11 +388,15 @@
         return field + exchange(*parts)
 
     def forward_adjoint(raw, scale, left, shift):
-        extended = with_halo(raw.astype(jnp.bfloat16), (("rcv", 3),), rim_rows)
+        rounded = raw.astype(jnp.bfloat16)
+        below = from_behind(rounded[..., local_rows - rim_rows :], "rcv", 1)
+        above = from_behind(rounded[..., :rim_rows], "rcv", -1)
         coefs = jnp.stack(
             [jnp.broadcast_to(scale, shift.shape).reshape(-1), shift.reshape(-1)], axis=1
         ).reshape(-1)
-        residual, *parts = apply_both(extended, raw, left, coefs, stacked, columns, counts)
+        residual, *parts = apply_both(
+            below, rounded, above, raw, left, coefs, stacked, columns, counts
+        )
         return residual, residual + exchange(*parts)
 
     def forward(field):

time: 226 us -> 226 us (level)
  other arithmetic: 21.4 us -> 16.1 us
  Pallas kernels: 62.1 us -> 66.7 us
    ppermute x6 -> x10, starting transfers between devices: 17 us -> 28.2 us  [from_behind(): lax.ppermute(value, axis, [(source, source + steps) for source in range(f...]
    ppermute x4 -> x0, starting transfers between devices: 11.2 us -> none  [the longest x2 6.47 us: with_halo(): lax.ppermute(tail, axis, [(i, (i + 1) % count) for i in range(ends)])]
    concatenate x2 -> x0, other arithmetic: 5.29 us -> none  [with_halo(): jnp.concatenate([lax.ppermute(tail, axis, [(i, (i + 1) % count) for i in...]
    pallas_call x2, Pallas kernels: 37.6 us -> 42.2 us  [apply_both(): pl.pallas_call(_both_kernel, grid_spec=grid_spec, out_shape=[jax.ShapeDty...]
    ppermute x4 -> x0, waiting for transfers between devices: 3.81 us -> none  [the longest x2 2.73 us: with_halo(): lax.ppermute(head, axis, [((i + 1) % count, i) for i in range(ends)])]
    ppermute x6 -> x10, waiting for transfers between devices: 17.2 us -> 20.9 us  [from_behind(): lax.ppermute(value, axis, [(source, source + steps) for source in range(f...]
where the time goes in v10:
time: 226 us; the launch traced here: 224 us
  Pallas kernels  66.7 us (30%)
  starting transfers between devices  59.3 us (26%)
  waiting for transfers between devices  34.7 us (15%)
  blocking collectives  32.8 us (15%)
  other arithmetic  16.1 us (7%)
  local copies, waits for them, and re-layouts  8.3 us (4%)
  matrix products  5.45 us (2%)
    pallas_call x2, Pallas kernels, apply_both(): pl.pallas_call(_both_kernel, grid_spec=grid_spec, out_shape=[jax.ShapeDty...  42.2 us
    all_to_all x2, blocking collectives, rcv_sum(): gathered = lax.all_to_all(spread, 'rcv', 0, 0, tiled=False)  32.8 us
    ppermute x10, starting transfers between devices, from_behind(): lax.ppermute(value, axis, [(source, source + steps) for source in range(f...  28.2 us
    ppermute x10, waiting for transfers between devices, from_behind(): lax.ppermute(value, axis, [(source, source + steps) for source in range(f...  20.9 us
    all_to_all x2, starting transfers between devices, rcv_sum(): gathered = lax.all_to_all(spread, 'rcv', 0, 0, tiled=False)  19.6 us
    pallas_call x1, Pallas kernels, apply_adjoint(): pl.pallas_call(_adjoint_kernel, grid_spec=grid_spec, out_shape=[part_shap...  12.9 us
    all_to_all x2, waiting for transfers between devices, rcv_sum(): gathered = lax.all_to_all(spread, 'rcv', 0, 0, tiled=False)  11.8 us
    pallas_call x1, Pallas kernels, stack_blocks(): pl.pallas_call(_stack_kernel, grid_spec=grid_spec, out_shape=jax.ShapeDty...  11.6 us
  transfers between devices with their start and end apart: 13, of which 7 were waited for; matrix products, arithmetic and copies ran while one was open for 4% of the time, Pallas kernels for 5%

profile of v10, /device:TPU:1, one launch (start us, length us, event | category | flops | bytes accessed | tf_op | source)
XLA Modules:
  0.0 224.3 jit_solution(3592727142075454339)
XLA Ops:
  0.8 5.5 %fusion = bf16[2,2,1,4,20480]{4,3,1,0,2:T(4,128)(2,1)S(1)} fusion(bf16[1,256,20480]{2,1,0:T(8,128)(2,1)} %param.28, bf16[256,1,4,2]{0,2,3,1:T(4,128)(2,1)S(1)} %get-tuple-element.168, bf16[256,1,4,2]{0,2,3,1:T(4,128)(2,1)S(1)} %get-tuple-element.167), kind=kOutput, calls=%fused_computation.1 | convolution fusion | flops 168116224 | bytes 11149312 | tf_op jit(solution)/shard_map/snr,ncgf->cfsgr/dot_general | solution.py:363
  6.8 1.5 copy.22
  8.3 11.5 %all-to-all-start = ((bf16[2,2,1,128,640]{4,1,0,2,3:T(2,128)(2,1)}), bf16[2,2,1,128,640]{4,1,0,2,3:T(2,128)(2,1)S(1)}, u32[]{:S(2)}, u32[]{:S(2)}) async-start(bf16[2,2,1,128,640]{4,1,0,2,3:T(2,128)(2,1)} %copy.22), calls=%async_computation | async-start | bytes 1310720 | tf_op jit(solution)/shard_map/all_to_all | solution.py:369
  21.0 11.6 %shard_map.89.m_ref = bf16[2,5,256,2816]{3,2,1,0:T(8,128)(2,1)} custom-call(s32[10]{0:T(128)} %reshape.546.counts_ref, bf16[2,5,11,2,128,128]{5,4,3,2,1,0:T(8,128)(2,1)} %a_ref.1), custom_call_target="tpu_custom_call" | custom-call | tf_op jit(solution)/shard_map/pallas_call | solution.py:104
  32.6 2.0 all-to-all-done
  35.6 12.9 %shard_map.90 = (f32[2,2,128,640]{3,2,1,0:T(8,128)}, f32[2,2,128,640]{3,2,1,0:T(8,128)}, f32[2,2,128,640]{3,2,1,0:T(8,128)}) custom-call(s32[110]{0:T(128)} %reshape.545.cols_ref, s32[10]{0:T(128)} %reshape.546.counts_ref, bf16[2,2,128,640]{3,2,1,0:T(8,128)(2,1)} %bitcast.53, bf16[2,5,256,2816]{3,2,1,0:T(8,128)(2,1)} %shard_map.89.m_ref), custom_call_target="tpu_custom_call" | custom-call | flops 1845493760 | bytes 19005440 | tf_op jit(solution)/shard_map/pallas_call | solution.py:340
  48.5 3.0 %collective-permute-start = (f32[2,2,128,640]{3,2,1,0:T(8,128)}, f32[2,2,128,640]{3,2,1,0:T(8,128)S(1)}, u32[]{:S(2)}, u32[]{:S(2)}) collective-permute-start(f32[2,2,128,640]{3,2,1,0:T(8,128)} %get-tuple-element.134), channel_id=1, source_target_pairs={{0,1},{1,2},{2,3},{3,4},{4,5},{5,6},{6,7},{7,8},{8,9},{9,10},{10,1... | collective-permute-start | bytes 3932168 | tf_op jit(solution)/shard_map/ppermute | solution.py:36
  51.5 1.9 collective-permute-start.1
  53.4 12.9 %collective-permute-done = f32[2,2,128,640]{3,2,1,0:T(8,128)S(1)} collective-permute-done((f32[2,2,128,640]{3,2,1,0:T(8,128)}, f32[2,2,128,640]{3,2,1,0:T(8,128)S(1)}, u32[]{:S(2)}, u32[]{:S(2)}) %collective-permute-start) | collective-permute-done | bytes 1310752 | tf_op jit(solution)/shard_map/ppermute | solution.py:36
  66.3 4.3 %collective-permute-done.1 = f32[2,2,128,640]{3,2,1,0:T(8,128)S(1)} collective-permute-done((f32[2,2,128,640]{3,2,1,0:T(8,128)}, f32[2,2,128,640]{3,2,1,0:T(8,128)S(1)}, u32[]{:S(2)}, u32[]{:S(2)}) %collective-permute-start.1) | collective-permute-done | bytes 1310752 | tf_op jit(solution)/shard_map/ppermute | solution.py:36
  70.6 2.0 fusion.17
  73.8 8.0 %all-to-all-start.1 = ((f32[32,2,2]{2,1,0:T(2,128)}), f32[32,2,2]{2,1,0:T(2,128)S(1)}, u32[]{:S(2)}, u32[]{:S(2)}) async-start(f32[32,2,2]{2,1,0:T(2,128)} %broadcast_in_dim.8), calls=%async_computation.1 | async-start | bytes 65536 | tf_op jit(solution)/shard_map/all_to_all | solution.py:57
  81.8 2.1 collective-permute-start.3
  84.0 3.4 %collective-permute-start.2 = (bf16[2,2,128,640]{3,2,1,0:T(8,128)(2,1)S(1)}, bf16[2,2,128,640]{3,2,1,0:T(8,128)(2,1)}, u32[]{:S(2)}, u32[]{:S(2)}) collective-permute-start(bf16[2,2,128,640]{3,2,1,0:T(8,128)(2,1)S(1)} %get-tuple-element.154.own_ref), channel_id=1, source_target_pairs={{0,1},{1,2},{2,3},{3,4},{4,5},{5,6},{6,7},{7,8},{8,9},{9,10},{10,1... | collective-permute-start | bytes 1966088 | tf_op jit(solution)/shard_map/ppermute | solution.py:36
  87.4 1.7 all-to-all-done.1
  91.2 2.6 %collective-permute-done.3.above_ref = bf16[2,2,128,640]{3,2,1,0:T(8,128)(2,1)S(1)} collective-permute-done((bf16[2,2,128,640]{3,2,1,0:T(8,128)(2,1)S(1)}, bf16[2,2,128,640]{3,2,1,0:T(8,128)(2,1)S(1)}, u32[]{:S(2)}, u32[]{:S(2)}) %collective-permute-start.3) | collective-permute-done | bytes 655392 | tf_op jit(solution)/shard_map/ppermute | solution.py:36
  94.9 21.1 %shard_map.91 = (f32[2,2,128,640]{3,2,1,0:T(8,128)}, f32[2,2,128,640]{3,2,1,0:T(8,128)}, f32[2,2,128,640]{3,2,1,0:T(8,128)}, f32[2,2,128,640]{3,2,1,0:T(8,128)}) custom-call(s32[110]{0:T(128)} %reshape.545.cols_ref, s32[10]{0:T(128)} %reshape.546.counts_ref, f32[4]{0:T(128)} %reshape.547.coef_ref, bf16[2,2,128,640]{3,2,1,0:T(8,128)(2,1)} %collective-permute-done.2.below_ref, ...), custom_call_target="tpu_custom_call" | custom-call | flops 3690987520 | bytes 29491200 | tf_op jit(solution)/shard_map/pallas_call | solution.py:276
  116.0 4.6 %collective-permute-start.4 = (f32[2,2,128,640]{3,2,1,0:T(8,128)}, f32[2,2,128,640]{3,2,1,0:T(8,128)S(1)}, u32[]{:S(2)}, u32[]{:S(2)}) collective-permute-start(f32[2,2,128,640]{3,2,1,0:T(8,128)} %get-tuple-element.138), channel_id=1, source_target_pairs={{0,1},{1,2},{2,3},{3,4},{4,5},{5,6},{6,7},{7,8},{8,9},{9,10},{10,1... | collective-permute-start | bytes 3932168 | tf_op jit(solution)/shard_map/ppermute | solution.py:36
  120.7 1.9 collective-permute-start.5
  122.6 1.6 multiply_reduce_fusion.2
  124.8 11.6 %all-to-all-start.2 = ((f32[32,1,2]{2,1,0:T(1,128)}), f32[32,1,2]{2,1,0:T(1,128)S(1)}, u32[]{:S(2)}, u32[]{:S(2)}) async-start(f32[32,1,2]{2,1,0:T(1,128)} %broadcast_in_dim.9), calls=%async_computation.2 | async-start | bytes 32768 | tf_op jit(solution)/shard_map/all_to_all | solution.py:57
  136.4 10.1 %all-to-all-done.2 = f32[32,1,2]{2,1,0:T(1,128)S(1)} async-done(((f32[32,1,2]{2,1,0:T(1,128)}), f32[32,1,2]{2,1,0:T(1,128)S(1)}, u32[]{:S(2)}, u32[]{:S(2)}) %all-to-all-start.2) | async-done | bytes 288 | tf_op jit(solution)/shard_map/all_to_all | solution.py:57
  147.6 4.0 %fusion.16 = (bf16[2,2,128,640]{3,2,1,0:T(8,128)(2,1)S(1)}, f32[2,2,128,640]{3,2,1,0:T(8,128)S(1)}, f32[2,2,128,640]{3,2,1,0:T(8,128)}) fusion(f32[2,2,128,640]{3,2,1,0:T(8,128)S(1)} %copy-done.1, f32[2]{0:T(128)S(1)} %get-tuple-element.152, f32[2]{0:T(128)S(1)} %add_sqrt_fusion.4, f32[2,2,128,640]{3,2,1,0:T(8,128)} %get-tuple-element.136, ...), kind=kLoop, calls=%fused_computation.58 | loop fusion | flops 2949120 | bytes 9830416 | tf_op jit(solution)/shard_map/convert_element_type | solution.py:391
  151.6 2.6 %collective-permute-start.7 = (bf16[2,2,128,640]{3,2,1,0:T(8,128)(2,1)S(1)}, bf16[2,2,128,640]{3,2,1,0:T(8,128)(2,1)}, u32[]{:S(2)}, u32[]{:S(2)}) collective-permute-start(bf16[2,2,128,640]{3,2,1,0:T(8,128)(2,1)S(1)} %get-tuple-element.150.own_ref), channel_id=1, source_target_pairs={{1,0},{2,1},{3,2},{4,3},{5,4},{6,5},{7,6},{8,7},{9,8},{10,9},{11,1... | collective-permute-start | bytes 1966088 | tf_op jit(solution)/shard_map/ppermute | solution.py:36
  154.2 3.1 %collective-permute-start.6 = (bf16[2,2,128,640]{3,2,1,0:T(8,128)(2,1)S(1)}, bf16[2,2,128,640]{3,2,1,0:T(8,128)(2,1)}, u32[]{:S(2)}, u32[]{:S(2)}) collective-permute-start(bf16[2,2,128,640]{3,2,1,0:T(8,128)(2,1)S(1)} %get-tuple-element.150.own_ref), channel_id=1, source_target_pairs={{0,1},{1,2},{2,3},{3,4},{4,5},{5,6},{6,7},{7,8},{8,9},{9,10},{10,1... | collective-permute-start | bytes 1966088 | tf_op jit(solution)/shard_map/ppermute | solution.py:36
  157.5 15.6 %all_to_all.32 = f32[32,1,2]{2,1,0:T(1,128)S(1)} all-to-all(f32[32,1,2]{2,1,0:T(1,128)S(1)} %broadcast_in_dim.10), channel_id=1, replica_groups=mesh['freq'=4,'rcv'=32] {'rcv'}, dimensions={0} | all-to-all | bytes 512 | tf_op jit(solution)/shard_map/all_to_all | solution.py:57
  174.0 21.1 %shard_map.92 = (f32[2,2,128,640]{3,2,1,0:T(8,128)}, f32[2,2,128,640]{3,2,1,0:T(8,128)}, f32[2,2,128,640]{3,2,1,0:T(8,128)}, f32[2,2,128,640]{3,2,1,0:T(8,128)}) custom-call(s32[110]{0:T(128)} %reshape.545.cols_ref, s32[10]{0:T(128)} %reshape.546.counts_ref, f32[4]{0:T(128)} %reshape.548.coef_ref, bf16[2,2,128,640]{3,2,1,0:T(8,128)(2,1)} %collective-permute-done.6.below_ref, ...), custom_call_target="tpu_custom_call" | custom-call | flops 3690987520 | bytes 29491200 | tf_op jit(solution)/shard_map/pallas_call | solution.py:276
  195.1 2.9 %collective-permute-start.8 = (f32[2,2,128,640]{3,2,1,0:T(8,128)}, f32[2,2,128,640]{3,2,1,0:T(8,128)}, u32[]{:S(2)}, u32[]{:S(2)}) collective-permute-start(f32[2,2,128,640]{3,2,1,0:T(8,128)} %get-tuple-element.142), channel_id=1, source_target_pairs={{0,1},{1,2},{2,3},{3,4},{4,5},{5,6},{6,7},{7,8},{8,9},{9,10},{10,1... | collective-permute-start | bytes 3932168 | tf_op jit(solution)/shard_map/ppermute | solution.py:36
  198.0 2.6 %collective-permute-start.9 = (f32[2,2,128,640]{3,2,1,0:T(8,128)}, f32[2,2,128,640]{3,2,1,0:T(8,128)}, u32[]{:S(2)}, u32[]{:S(2)}) collective-permute-start(f32[2,2,128,640]{3,2,1,0:T(8,128)} %get-tuple-element.143), channel_id=1, source_target_pairs={{1,0},{2,1},{3,2},{4,3},{5,4},{6,5},{7,6},{8,7},{9,8},{10,9},{11,1... | collective-permute-start | bytes 3932168 | tf_op jit(solution)/shard_map/ppermute | solution.py:36
  200.6 1.6 multiply_reduce_fusion
  202.2 17.2 %all_to_all.33 = f32[32,1,2]{2,1,0:T(1,128)S(1)} all-to-all(f32[32,1,2]{2,1,0:T(1,128)S(1)} %broadcast_in_dim.11), channel_id=1, replica_groups=mesh['freq'=4,'rcv'=32] {'rcv'}, dimensions={0} | all-to-all | bytes 512 | tf_op jit(solution)/shard_map/all_to_all | solution.py:57
  219.6 4.7 %subtract_multiply_fusion = (f32[2,2,128,640]{3,2,1,0:T(8,128)}, f32[2,2,128,640]{3,2,1,0:T(8,128)}) fusion(f32[2,2,128,640]{3,2,1,0:T(8,128)} %get-tuple-element.140, f32[2,2,128,640]{3,2,1,0:T(8,128)} %collective-permute-done.9, f32[2,2,128,640]{3,2,1,0:T(8,128)} %get-tuple-element.141, f32[2,2,128,640]{3,2,1,0:T(8,128)} %collective-permute-done.8, ...), kind=kLoop, calls=%fused_computation.7 | loop fusion | flops 4587520 | bytes 10485816 | tf_op jit(solution)/shard_map/mul | solution.py:439
  (61 shorter events, 10.2 us)
Async XLA Ops:
  6.7 13.0 %copy-start.9 = (s32[2,5]{1,0:T(2,128)S(1)}, s32[2,5]{1,0:T(2,128)}, u32[]{:S(2)}) copy-start(s32[2,5]{1,0:T(2,128)} %param.31) | copy-start | bytes 124
  6.7 13.6 %copy-start.8 = (s32[2,5,11]{2,0,1:T(2,128)S(1)}, s32[2,5,11]{2,0,1:T(2,128)}, u32[]{:S(2)}) copy-start(s32[2,5,11]{2,0,1:T(2,128)} %param.30) | copy-start | bytes 1324
  8.3 26.4 %all-to-all-start = ((bf16[2,2,1,128,640]{4,1,0,2,3:T(2,128)(2,1)}), bf16[2,2,1,128,640]{4,1,0,2,3:T(2,128)(2,1)S(1)}, u32[]{:S(2)}, u32[]{:S(2)}) async-start(bf16[2,2,1,128,640]{4,1,0,2,3:T(2,128)(2,1)} %copy.22), calls=%async_computation | async-start | bytes 1310720 | tf_op jit(solution)/shard_map/all_to_all | solution.py:369
  48.5 17.9 %collective-permute-start = (f32[2,2,128,640]{3,2,1,0:T(8,128)}, f32[2,2,128,640]{3,2,1,0:T(8,128)S(1)}, u32[]{:S(2)}, u32[]{:S(2)}) collective-permute-start(f32[2,2,128,640]{3,2,1,0:T(8,128)} %get-tuple-element.134), channel_id=1, source_target_pairs={{0,1},{1,2},{2,3},{3,4},{4,5},{5,6},{6,7},{7,8},{8,9},{9,10},{10,1... | collective-permute-start | bytes 3932168 | tf_op jit(solution)/shard_map/ppermute | solution.py:36
  51.5 19.1 %collective-permute-start.1 = (f32[2,2,128,640]{3,2,1,0:T(8,128)}, f32[2,2,128,640]{3,2,1,0:T(8,128)S(1)}, u32[]{:S(2)}, u32[]{:S(2)}) collective-permute-start(f32[2,2,128,640]{3,2,1,0:T(8,128)} %get-tuple-element.135), channel_id=1, source_target_pairs={{1,0},{2,1},{3,2},{4,3},{5,4},{6,5},{7,6},{8,7},{9,8},{10,9},{11,1... | collective-permute-start | bytes 3932168 | tf_op jit(solution)/shard_map/ppermute | solution.py:36
  72.6 18.6 %copy-start = (f32[2,2,128,640]{3,2,1,0:T(8,128)}, f32[2,2,128,640]{3,2,1,0:T(8,128)S(1)}, u32[]{:S(2)}) copy-start(f32[2,2,128,640]{3,2,1,0:T(8,128)S(1)} %get-tuple-element.155.q_ref) | copy-start | bytes 3932164
  72.6 18.6 %copy-start.5 = (bf16[2,2,128,640]{3,2,1,0:T(8,128)(2,1)}, bf16[2,2,128,640]{3,2,1,0:T(8,128)(2,1)S(1)}, u32[]{:S(2)}) copy-start(bf16[2,2,128,640]{3,2,1,0:T(8,128)(2,1)S(1)} %get-tuple-element.154.own_ref) | copy-start | bytes 1966084
  73.8 15.3 %all-to-all-start.1 = ((f32[32,2,2]{2,1,0:T(2,128)}), f32[32,2,2]{2,1,0:T(2,128)S(1)}, u32[]{:S(2)}, u32[]{:S(2)}) async-start(f32[32,2,2]{2,1,0:T(2,128)} %broadcast_in_dim.8), calls=%async_computation.1 | async-start | bytes 65536 | tf_op jit(solution)/shard_map/all_to_all | solution.py:57
  81.8 12.0 %collective-permute-start.3 = (bf16[2,2,128,640]{3,2,1,0:T(8,128)(2,1)S(1)}, bf16[2,2,128,640]{3,2,1,0:T(8,128)(2,1)S(1)}, u32[]{:S(2)}, u32[]{:S(2)}) collective-permute-start(bf16[2,2,128,640]{3,2,1,0:T(8,128)(2,1)S(1)} %get-tuple-element.154.own_ref), channel_id=1, source_target_pairs={{1,0},{2,1},{3,2},{4,3},{5,4},{6,5},{7,6},{8,7},{9,8},{10,9},{11,1... | collective-permute-start | bytes 1966088 | tf_op jit(solution)/shard_map/ppermute | solution.py:36
  84.0 10.9 %collective-permute-start.2 = (bf16[2,2,128,640]{3,2,1,0:T(8,128)(2,1)S(1)}, bf16[2,2,128,640]{3,2,1,0:T(8,128)(2,1)}, u32[]{:S(2)}, u32[]{:S(2)}) collective-permute-start(bf16[2,2,128,640]{3,2,1,0:T(8,128)(2,1)S(1)} %get-tuple-element.154.own_ref), channel_id=1, source_target_pairs={{0,1},{1,2},{2,3},{3,4},{4,5},{5,6},{6,7},{7,8},{8,9},{9,10},{10,1... | collective-permute-start | bytes 1966088 | tf_op jit(solution)/shard_map/ppermute | solution.py:36
  93.9 1.1 copy-start.7
  116.0 31.6 %copy-start.1 = (f32[2,2,128,640]{3,2,1,0:T(8,128)S(1)}, f32[2,2,128,640]{3,2,1,0:T(8,128)}, u32[]{:S(2)}) copy-start(f32[2,2,128,640]{3,2,1,0:T(8,128)} %copy-done) | copy-start | bytes 3932164
  116.0 30.5 %collective-permute-start.4 = (f32[2,2,128,640]{3,2,1,0:T(8,128)}, f32[2,2,128,640]{3,2,1,0:T(8,128)S(1)}, u32[]{:S(2)}, u32[]{:S(2)}) collective-permute-start(f32[2,2,128,640]{3,2,1,0:T(8,128)} %get-tuple-element.138), channel_id=1, source_target_pairs={{0,1},{1,2},{2,3},{3,4},{4,5},{5,6},{6,7},{7,8},{8,9},{9,10},{10,1... | collective-permute-start | bytes 3932168 | tf_op jit(solution)/shard_map/ppermute | solution.py:36
  120.7 25.9 %collective-permute-start.5 = (f32[2,2,128,640]{3,2,1,0:T(8,128)}, f32[2,2,128,640]{3,2,1,0:T(8,128)}, u32[]{:S(2)}, u32[]{:S(2)}) collective-permute-start(f32[2,2,128,640]{3,2,1,0:T(8,128)} %get-tuple-element.139), channel_id=1, source_target_pairs={{1,0},{2,1},{3,2},{4,3},{5,4},{6,5},{7,6},{8,7},{9,8},{10,9},{11,1... | collective-permute-start | bytes 3932168 | tf_op jit(solution)/shard_map/ppermute | solution.py:36
  124.8 21.7 %all-to-all-start.2 = ((f32[32,1,2]{2,1,0:T(1,128)}), f32[32,1,2]{2,1,0:T(1,128)S(1)}, u32[]{:S(2)}, u32[]{:S(2)}) async-start(f32[32,1,2]{2,1,0:T(1,128)} %broadcast_in_dim.9), calls=%async_computation.2 | async-start | bytes 32768 | tf_op jit(solution)/shard_map/all_to_all | solution.py:57
  146.6 1.1 copy-start.6
  151.6 22.3 %copy-start.2 = (f32[2,2,128,640]{3,2,1,0:T(8,128)}, f32[2,2,128,640]{3,2,1,0:T(8,128)S(1)}, u32[]{:S(2)}) copy-start(f32[2,2,128,640]{3,2,1,0:T(8,128)S(1)} %get-tuple-element.151.q_ref) | copy-start | bytes 3932164
  151.6 22.3 %copy-start.4 = (bf16[2,2,128,640]{3,2,1,0:T(8,128)(2,1)}, bf16[2,2,128,640]{3,2,1,0:T(8,128)(2,1)S(1)}, u32[]{:S(2)}) copy-start(bf16[2,2,128,640]{3,2,1,0:T(8,128)(2,1)S(1)} %get-tuple-element.150.own_ref) | copy-start | bytes 1966084
  151.6 22.3 %collective-permute-start.7 = (bf16[2,2,128,640]{3,2,1,0:T(8,128)(2,1)S(1)}, bf16[2,2,128,640]{3,2,1,0:T(8,128)(2,1)}, u32[]{:S(2)}, u32[]{:S(2)}) collective-permute-start(bf16[2,2,128,640]{3,2,1,0:T(8,128)(2,1)S(1)} %get-tuple-element.150.own_ref), channel_id=1, source_target_pairs={{1,0},{2,1},{3,2},{4,3},{5,4},{6,5},{7,6},{8,7},{9,8},{10,9},{11,1... | collective-permute-start | bytes 1966088 | tf_op jit(solution)/shard_map/ppermute | solution.py:36
  154.2 19.8 %collective-permute-start.6 = (bf16[2,2,128,640]{3,2,1,0:T(8,128)(2,1)S(1)}, bf16[2,2,128,640]{3,2,1,0:T(8,128)(2,1)}, u32[]{:S(2)}, u32[]{:S(2)}) collective-permute-start(bf16[2,2,128,640]{3,2,1,0:T(8,128)(2,1)S(1)} %get-tuple-element.150.own_ref), channel_id=1, source_target_pairs={{0,1},{1,2},{2,3},{3,4},{4,5},{5,6},{6,7},{7,8},{8,9},{9,10},{10,1... | collective-permute-start | bytes 1966088 | tf_op jit(solution)/shard_map/ppermute | solution.py:36
  195.1 24.5 %copy-start.3 = (f32[2,2,128,640]{3,2,1,0:T(8,128)S(1)}, f32[2,2,128,640]{3,2,1,0:T(8,128)}, u32[]{:S(2)}) copy-start(f32[2,2,128,640]{3,2,1,0:T(8,128)} %copy-done.2) | copy-start | bytes 3932164
  195.1 24.5 %collective-permute-start.8 = (f32[2,2,128,640]{3,2,1,0:T(8,128)}, f32[2,2,128,640]{3,2,1,0:T(8,128)}, u32[]{:S(2)}, u32[]{:S(2)}) collective-permute-start(f32[2,2,128,640]{3,2,1,0:T(8,128)} %get-tuple-element.142), channel_id=1, source_target_pairs={{0,1},{1,2},{2,3},{3,4},{4,5},{5,6},{6,7},{7,8},{8,9},{9,10},{10,1... | collective-permute-start | bytes 3932168 | tf_op jit(solution)/shard_map/ppermute | solution.py:36
  198.0 21.6 %collective-permute-start.9 = (f32[2,2,128,640]{3,2,1,0:T(8,128)}, f32[2,2,128,640]{3,2,1,0:T(8,128)}, u32[]{:S(2)}, u32[]{:S(2)}) collective-permute-start(f32[2,2,128,640]{3,2,1,0:T(8,128)} %get-tuple-element.143), channel_id=1, source_target_pairs={{1,0},{2,1},{3,2},{4,3},{5,4},{6,5},{7,6},{8,7},{9,8},{10,9},{11,1... | collective-permute-start | bytes 3932168 | tf_op jit(solution)/shard_map/ppermute | solution.py:36

commit v11 on v8

--- a/solution.py
+++ b/solution.py
@@ -182,6 +182,7 @@
     lower_ref,
     middle_ref,
     upper_ref,
+    squares_ref,
     picked_ref,
     acc_ref,
 ):
@@ -196,6 +197,7 @@
     @pl.when(row == 0)
     def _():
         acc_ref[...] = jnp.zeros(acc_ref.shape, acc_ref.dtype)
+        squares_ref[...] = jnp.zeros(squares_ref.shape, squares_ref.dtype)
 
     for slot in range(slots):
         start = pl.multiple_of(cols_ref[index * slots + slot] * block, block)
@@ -211,6 +213,8 @@
     for part in range(2):
         lanes = slice(part * block, (part + 1) * block)
         p_ref[part] = (q_ref[part] + product[:, lanes]) / scale - shift * u_ref[part]
+    total = jnp.sum(p_ref[0] * p_ref[0] + p_ref[1] * p_ref[1], axis=(0, 1), keepdims=True)
+    squares_ref[...] += jnp.broadcast_to(total, squares_ref.shape)
     field = jnp.concatenate(
         [p_ref[0].astype(jnp.bfloat16), p_ref[1].astype(jnp.bfloat16)], axis=1
     )
@@ -249,7 +253,13 @@
             own,
             pl.BlockSpec((None, None, depth, width), lambda f, r, c, n: (f, r, 0, 0)),
         ],
-        out_specs=[own, part_spec(rim), part_spec(own_rows), part_spec(rim)],
+        out_specs=[
+            own,
+            part_spec(rim),
+            part_spec(own_rows),
+            part_spec(rim),
+            pl.BlockSpec((None, 8, 128), lambda f, r, c, n: (f, 0, 0)),
+        ],
         scratch_shapes=[
             pltpu.VMEM((sources, width), jnp.bfloat16),
             pltpu.VMEM((2, sources, span), jnp.float32),
@@ -263,6 +273,7 @@
             part_shape(rim),
             part_shape(own_rows),
             part_shape(rim),
+            jax.ShapeDtypeStruct((local_freqs, 8, 128), jnp.float32),
         ],
         compiler_params=pltpu.CompilerParams(dimension_semantics=("arbitrary", "arbitrary")),
         cost_estimate=pl.CostEstimate(
@@ -374,8 +385,11 @@
         coefs = jnp.stack(
             [jnp.broadcast_to(scale, shift.shape).reshape(-1), shift.reshape(-1)], axis=1
         ).reshape(-1)
-        residual, *parts = apply_both(extended, raw, left, coefs, stacked, columns, counts)
-        return residual, residual + exchange(*parts)
+        residual, lower, middle, upper, partial = apply_both(
+            extended, raw, left, coefs, stacked, columns, counts
+        )
+        total = rcv_sum(partial[:, 0, 0])[None, :, None, None]
+        return residual, residual + exchange(lower, middle, upper), total
 
     def forward(field):
         extended = with_halo(field.astype(jnp.bfloat16), (("rcv", 3),), rim_rows)
@@ -395,8 +409,10 @@
     rhobar = alpha_norm
     for iteration in range(ITERS):
         last = iteration == ITERS - 1
-        residual_left, lifted = forward_adjoint(right_raw, right_scale, left_vector, alpha_norm)
-        beta_norm = jnp.sqrt(squares(residual_left) + EPSILON)
+        residual_left, lifted, left_squares = forward_adjoint(
+            right_raw, right_scale, left_vector, alpha_norm
+        )
+        beta_norm = jnp.sqrt(left_squares + EPSILON)
         left_vector = residual_left / beta_norm
         residual_right = lifted / beta_norm - beta_norm * right_vector
         rho_value = jnp.sqrt(rhobar * rhobar + beta_norm * beta_norm)

time: 226 us -> 226 us (level)
  other arithmetic: 21.4 us -> 18.2 us
    reduce_sum x3 -> x1, other arithmetic: 3.43 us -> 0.27 us  [squares(): return rcv_sum(jnp.sum(field * field, axis=(0, 2, 3)))[None, :, None, None]]
  transfers between devices with their start and end apart: 13 -> 13, of which waited for: 7 -> 7; matrix products, arithmetic and copies ran while one was open for 4% -> 3% of each run, Pallas kernels for 5% -> 5%
where the time goes in v11:
time: 226 us; the launch traced here: 225 us
  Pallas kernels  62.4 us (28%)
  starting transfers between devices  59 us (26%)
  waiting for transfers between devices  35.6 us (16%)
  blocking collectives  33.6 us (15%)
  other arithmetic  18.2 us (8%)
  local copies, waits for them, and re-layouts  9.55 us (4%)
  matrix products  5.45 us (2%)
    pallas_call x2, Pallas kernels, apply_both(): pl.pallas_call(_both_kernel, grid_spec=grid_spec, out_shape=[jax.ShapeDty...  37.9 us
    all_to_all x2, blocking collectives, rcv_sum(): gathered = lax.all_to_all(spread, 'rcv', 0, 0, tiled=False)  33.6 us
    all_to_all x2, starting transfers between devices, rcv_sum(): gathered = lax.all_to_all(spread, 'rcv', 0, 0, tiled=False)  19.6 us
    ppermute x6, waiting for transfers between devices, from_behind(): lax.ppermute(value, axis, [(source, source + steps) for source in range(f...  17.2 us
    ppermute x6, starting transfers between devices, from_behind(): lax.ppermute(value, axis, [(source, source + steps) for source in range(f...  16.7 us
    pallas_call x1, Pallas kernels, apply_adjoint(): pl.pallas_call(_adjoint_kernel, grid_spec=grid_spec, out_shape=[part_shap...  12.9 us
    all_to_all x2, waiting for transfers between devices, rcv_sum(): gathered = lax.all_to_all(spread, 'rcv', 0, 0, tiled=False)  12.6 us
    pallas_call x1, Pallas kernels, stack_blocks(): pl.pallas_call(_stack_kernel, grid_spec=grid_spec, out_shape=jax.ShapeDty...  11.6 us
  transfers between devices with their start and end apart: 13, of which 7 were waited for; matrix products, arithmetic and copies ran while one was open for 3% of the time, Pallas kernels for 5%

profile of v11, /device:TPU:1, one launch (start us, length us, event | category | flops | bytes accessed | tf_op | source)
XLA Modules:
  0.0 224.6 jit_solution(9355757438013537372)
XLA Ops:
  0.8 5.5 %fusion = bf16[2,2,1,4,20480]{4,3,1,0,2:T(4,128)(2,1)S(1)} fusion(bf16[1,256,20480]{2,1,0:T(8,128)(2,1)} %param.28, bf16[256,1,4,2]{0,2,3,1:T(4,128)(2,1)S(1)} %get-tuple-element.172, bf16[256,1,4,2]{0,2,3,1:T(4,128)(2,1)S(1)} %get-tuple-element.171), kind=kOutput, calls=%fused_computation.1 | convolution fusion | flops 168116224 | bytes 11149312 | tf_op jit(solution)/shard_map/snr,ncgf->cfsgr/dot_general | solution.py:356
  6.8 1.5 copy.22
  8.3 11.5 %all-to-all-start = ((bf16[2,2,1,128,640]{4,1,0,2,3:T(2,128)(2,1)}), bf16[2,2,1,128,640]{4,1,0,2,3:T(2,128)(2,1)S(1)}, u32[]{:S(2)}, u32[]{:S(2)}) async-start(bf16[2,2,1,128,640]{4,1,0,2,3:T(2,128)(2,1)} %copy.22), calls=%async_computation | async-start | bytes 1310720 | tf_op jit(solution)/shard_map/all_to_all | solution.py:362
  21.0 11.6 %shard_map.89.m_ref = bf16[2,5,256,2816]{3,2,1,0:T(8,128)(2,1)} custom-call(s32[10]{0:T(128)} %reshape.550.counts_ref, bf16[2,5,11,2,128,128]{5,4,3,2,1,0:T(8,128)(2,1)} %a_ref.1), custom_call_target="tpu_custom_call" | custom-call | tf_op jit(solution)/shard_map/pallas_call | solution.py:104
  32.6 2.0 all-to-all-done
  35.6 12.9 %shard_map.90 = (f32[2,2,128,640]{3,2,1,0:T(8,128)}, f32[2,2,128,640]{3,2,1,0:T(8,128)}, f32[2,2,128,640]{3,2,1,0:T(8,128)}) custom-call(s32[110]{0:T(128)} %reshape.549.cols_ref, s32[10]{0:T(128)} %reshape.550.counts_ref, bf16[2,2,128,640]{3,2,1,0:T(8,128)(2,1)} %bitcast.53, bf16[2,5,256,2816]{3,2,1,0:T(8,128)(2,1)} %shard_map.89.m_ref), custom_call_target="tpu_custom_call" | custom-call | flops 1845493760 | bytes 19005440 | tf_op jit(solution)/shard_map/pallas_call | solution.py:333
  48.4 3.0 %collective-permute-start = (f32[2,2,128,640]{3,2,1,0:T(8,128)}, f32[2,2,128,640]{3,2,1,0:T(8,128)S(1)}, u32[]{:S(2)}, u32[]{:S(2)}) collective-permute-start(f32[2,2,128,640]{3,2,1,0:T(8,128)} %get-tuple-element.136), channel_id=1, source_target_pairs={{0,1},{1,2},{2,3},{3,4},{4,5},{5,6},{6,7},{7,8},{8,9},{9,10},{10,1... | collective-permute-start | bytes 3932168 | tf_op jit(solution)/shard_map/ppermute | solution.py:36
  51.4 1.9 collective-permute-start.1
  53.4 12.9 %collective-permute-done = f32[2,2,128,640]{3,2,1,0:T(8,128)S(1)} collective-permute-done((f32[2,2,128,640]{3,2,1,0:T(8,128)}, f32[2,2,128,640]{3,2,1,0:T(8,128)S(1)}, u32[]{:S(2)}, u32[]{:S(2)}) %collective-permute-start) | collective-permute-done | bytes 1310752 | tf_op jit(solution)/shard_map/ppermute | solution.py:36
  66.3 4.3 %collective-permute-done.1 = f32[2,2,128,640]{3,2,1,0:T(8,128)S(1)} collective-permute-done((f32[2,2,128,640]{3,2,1,0:T(8,128)}, f32[2,2,128,640]{3,2,1,0:T(8,128)S(1)}, u32[]{:S(2)}, u32[]{:S(2)}) %collective-permute-start.1) | collective-permute-done | bytes 1310752 | tf_op jit(solution)/shard_map/ppermute | solution.py:36
  70.6 2.0 fusion.17
  73.6 8.0 %all-to-all-start.1 = ((f32[32,2,2]{2,1,0:T(2,128)}), f32[32,2,2]{2,1,0:T(2,128)S(1)}, u32[]{:S(2)}, u32[]{:S(2)}) async-start(f32[32,2,2]{2,1,0:T(2,128)} %broadcast_in_dim.12), calls=%async_computation.1 | async-start | bytes 65536 | tf_op jit(solution)/shard_map/all_to_all | solution.py:57
  81.6 2.1 collective-permute-start.3
  83.8 3.4 %collective-permute-start.2 = (bf16[2,2,128,640]{3,2,1,0:T(8,128)(2,1)S(1)}, bf16[2,2,128,640]{3,2,1,0:T(8,128)(2,1)}, u32[]{:S(2)}, u32[]{:S(2)}) collective-permute-start(bf16[2,2,128,640]{3,2,1,0:T(8,128)(2,1)S(1)} %get-tuple-element.158), channel_id=1, source_target_pairs={{0,1},{1,2},{2,3},{3,4},{4,5},{5,6},{6,7},{7,8},{8,9},{9,10},{10,1... | collective-permute-start | bytes 1966088 | tf_op jit(solution)/shard_map/ppermute | solution.py:24
  87.2 1.7 all-to-all-done.1
  90.9 2.7 %collective-permute-done.3 = bf16[2,2,128,640]{3,2,1,0:T(8,128)(2,1)S(1)} collective-permute-done((bf16[2,2,128,640]{3,2,1,0:T(8,128)(2,1)S(1)}, bf16[2,2,128,640]{3,2,1,0:T(8,128)(2,1)S(1)}, u32[]{:S(2)}, u32[]{:S(2)}) %collective-permute-start.3) | collective-permute-done | bytes 655392 | tf_op jit(solution)/shard_map/ppermute | solution.py:26
  94.7 2.5 %pad_maximum_fusion.x_ref = bf16[2,2,128,1920]{3,2,1,0:T(8,128)(2,1)} fusion(bf16[2,2,128,640]{3,2,1,0:T(8,128)(2,1)S(1)} %collective-permute-done.3, bf16[2,2,128,640]{3,2,1,0:T(8,128)(2,1)S(1)} %get-tuple-element.158, bf16[2,2,128,640]{3,2,1,0:T(8,128)(2,1)} %collective-permute-done.2), kind=kLoop, calls=%fused_computation.3 | loop fusion | flops 5898240 | bytes 3932160 | tf_op jit(solution)/shard_map/concatenate | solution.py:22
  97.2 19.0 %shard_map.91 = (f32[2,2,128,640]{3,2,1,0:T(8,128)}, f32[2,2,128,640]{3,2,1,0:T(8,128)}, f32[2,2,128,640]{3,2,1,0:T(8,128)}, f32[2,2,128,640]{3,2,1,0:T(8,128)}, f32[2,8,128]{2,1,0:T(8,128)}) custom-call(s32[110]{0:T(128)} %reshape.549.cols_ref, s32[10]{0:T(128)} %reshape.550.counts_ref, f32[4]{0:T(128)} %reshape.551.coef_ref, ...), custom_call_target="tpu_custom_call" | custom-call | flops 3690987520 | bytes 29491200 | tf_op jit(solution)/shard_map/pallas_call | solution.py:268
  116.2 4.5 %collective-permute-start.4 = (f32[2,2,128,640]{3,2,1,0:T(8,128)}, f32[2,2,128,640]{3,2,1,0:T(8,128)S(1)}, u32[]{:S(2)}, u32[]{:S(2)}) collective-permute-start(f32[2,2,128,640]{3,2,1,0:T(8,128)} %get-tuple-element.141), channel_id=1, source_target_pairs={{0,1},{1,2},{2,3},{3,4},{4,5},{5,6},{6,7},{7,8},{8,9},{9,10},{10,1... | collective-permute-start | bytes 3932168 | tf_op jit(solution)/shard_map/ppermute | solution.py:36
  120.7 1.9 collective-permute-start.5
  124.0 11.6 %all-to-all-start.2 = ((f32[32,1,2]{2,1,0:T(1,128)}), f32[32,1,2]{2,1,0:T(1,128)S(1)}, u32[]{:S(2)}, u32[]{:S(2)}) async-start(f32[32,1,2]{2,1,0:T(1,128)} %broadcast_in_dim.14), calls=%async_computation.2 | async-start | bytes 32768 | tf_op jit(solution)/shard_map/all_to_all | solution.py:57
  135.7 10.9 %all-to-all-done.2 = f32[32,1,2]{2,1,0:T(1,128)S(1)} async-done(((f32[32,1,2]{2,1,0:T(1,128)}), f32[32,1,2]{2,1,0:T(1,128)S(1)}, u32[]{:S(2)}, u32[]{:S(2)}) %all-to-all-start.2) | async-done | bytes 288 | tf_op jit(solution)/shard_map/all_to_all | solution.py:57
  147.7 4.0 %fusion.16 = (bf16[2,2,128,640]{3,2,1,0:T(8,128)(2,1)S(1)}, f32[2,2,128,640]{3,2,1,0:T(8,128)S(1)}, f32[2,2,128,640]{3,2,1,0:T(8,128)}) fusion(f32[2,2,128,640]{3,2,1,0:T(8,128)S(1)} %copy-done.1, f32[2]{0:T(128)S(1)} %get-tuple-element.156, f32[2]{0:T(128)S(1)} %add_sqrt_fusion.4, f32[2,2,128,640]{3,2,1,0:T(8,128)} %get-tuple-element.139, ...), kind=kLoop, calls=%fused_computation.60 | loop fusion | flops 2949120 | bytes 9830416 | tf_op jit(solution)/shard_map/convert_element_type | solution.py:384
  151.7 2.6 %collective-permute-start.7 = (bf16[2,2,128,640]{3,2,1,0:T(8,128)(2,1)S(1)}, bf16[2,2,128,640]{3,2,1,0:T(8,128)(2,1)}, u32[]{:S(2)}, u32[]{:S(2)}) collective-permute-start(bf16[2,2,128,640]{3,2,1,0:T(8,128)(2,1)S(1)} %get-tuple-element.154), channel_id=1, source_target_pairs={{1,0},{2,1},{3,2},{4,3},{5,4},{6,5},{7,6},{8,7},{9,8},{10,9},{11,1... | collective-permute-start | bytes 1966088 | tf_op jit(solution)/shard_map/ppermute | solution.py:26
  154.2 3.1 %collective-permute-start.6 = (bf16[2,2,128,640]{3,2,1,0:T(8,128)(2,1)S(1)}, bf16[2,2,128,640]{3,2,1,0:T(8,128)(2,1)}, u32[]{:S(2)}, u32[]{:S(2)}) collective-permute-start(bf16[2,2,128,640]{3,2,1,0:T(8,128)(2,1)S(1)} %get-tuple-element.154), channel_id=1, source_target_pairs={{0,1},{1,2},{2,3},{3,4},{4,5},{5,6},{6,7},{7,8},{8,9},{9,10},{10,1... | collective-permute-start | bytes 1966088 | tf_op jit(solution)/shard_map/ppermute | solution.py:24
  157.6 15.6 %all_to_all.32 = f32[32,1,2]{2,1,0:T(1,128)S(1)} all-to-all(f32[32,1,2]{2,1,0:T(1,128)S(1)} %broadcast_in_dim.15), channel_id=1, replica_groups=mesh['freq'=4,'rcv'=32] {'rcv'}, dimensions={0} | all-to-all | bytes 512 | tf_op jit(solution)/shard_map/all_to_all | solution.py:57
  173.9 2.7 %pad_maximum_fusion.1.x_ref = bf16[2,2,128,1920]{3,2,1,0:T(8,128)(2,1)} fusion(bf16[2,2,128,640]{3,2,1,0:T(8,128)(2,1)} %collective-permute-done.7, bf16[2,2,128,640]{3,2,1,0:T(8,128)(2,1)S(1)} %get-tuple-element.154, bf16[2,2,128,640]{3,2,1,0:T(8,128)(2,1)} %collective-permute-done.6), kind=kLoop, calls=%fused_computation.4 | loop fusion | flops 5898240 | bytes 3932160 | tf_op jit(solution)/shard_map/concatenate | solution.py:22
  176.6 19.0 %shard_map.92 = (f32[2,2,128,640]{3,2,1,0:T(8,128)}, f32[2,2,128,640]{3,2,1,0:T(8,128)}, f32[2,2,128,640]{3,2,1,0:T(8,128)}, f32[2,2,128,640]{3,2,1,0:T(8,128)}, f32[2,8,128]{2,1,0:T(8,128)}) custom-call(s32[110]{0:T(128)} %reshape.549.cols_ref, s32[10]{0:T(128)} %reshape.550.counts_ref, f32[4]{0:T(128)} %reshape.552.coef_ref, ...), custom_call_target="tpu_custom_call" | custom-call | flops 3690987520 | bytes 29491200 | tf_op jit(solution)/shard_map/pallas_call | solution.py:268
  195.6 2.7 %collective-permute-start.8 = (f32[2,2,128,640]{3,2,1,0:T(8,128)}, f32[2,2,128,640]{3,2,1,0:T(8,128)}, u32[]{:S(2)}, u32[]{:S(2)}) collective-permute-start(f32[2,2,128,640]{3,2,1,0:T(8,128)} %get-tuple-element.146), channel_id=1, source_target_pairs={{0,1},{1,2},{2,3},{3,4},{4,5},{5,6},{6,7},{7,8},{8,9},{9,10},{10,1... | collective-permute-start | bytes 3932168 | tf_op jit(solution)/shard_map/ppermute | solution.py:36
  198.3 2.6 %collective-permute-start.9 = (f32[2,2,128,640]{3,2,1,0:T(8,128)}, f32[2,2,128,640]{3,2,1,0:T(8,128)}, u32[]{:S(2)}, u32[]{:S(2)}) collective-permute-start(f32[2,2,128,640]{3,2,1,0:T(8,128)} %get-tuple-element.147), channel_id=1, source_target_pairs={{1,0},{2,1},{3,2},{4,3},{5,4},{6,5},{7,6},{8,7},{9,8},{10,9},{11,1... | collective-permute-start | bytes 3932168 | tf_op jit(solution)/shard_map/ppermute | solution.py:36
  201.8 18.0 %all_to_all.33 = f32[32,1,2]{2,1,0:T(1,128)S(1)} all-to-all(f32[32,1,2]{2,1,0:T(1,128)S(1)} %broadcast_in_dim.34), channel_id=1, replica_groups=mesh['freq'=4,'rcv'=32] {'rcv'}, dimensions={0} | all-to-all | bytes 512 | tf_op jit(solution)/shard_map/all_to_all | solution.py:57
  220.0 4.7 %subtract_multiply_fusion = (f32[2,2,128,640]{3,2,1,0:T(8,128)}, f32[2,2,128,640]{3,2,1,0:T(8,128)}) fusion(f32[2,2,128,640]{3,2,1,0:T(8,128)} %get-tuple-element.144, f32[2,2,128,640]{3,2,1,0:T(8,128)} %collective-permute-done.9, f32[2,2,128,640]{3,2,1,0:T(8,128)} %get-tuple-element.145, f32[2,2,128,640]{3,2,1,0:T(8,128)} %collective-permute-done.8, ...), kind=kLoop, calls=%fused_computation.9 | loop fusion | flops 4587520 | bytes 10485816 | tf_op jit(solution)/shard_map/mul | solution.py:433
  (57 shorter events, 11.4 us)
Async XLA Ops:
  6.7 13.0 %copy-start.6 = (s32[2,5]{1,0:T(2,128)S(1)}, s32[2,5]{1,0:T(2,128)}, u32[]{:S(2)}) copy-start(s32[2,5]{1,0:T(2,128)} %param.31) | copy-start | bytes 124
  6.7 13.6 %copy-start.5 = (s32[2,5,11]{2,0,1:T(2,128)S(1)}, s32[2,5,11]{2,0,1:T(2,128)}, u32[]{:S(2)}) copy-start(s32[2,5,11]{2,0,1:T(2,128)} %param.30) | copy-start | bytes 1324
  8.3 26.4 %all-to-all-start = ((bf16[2,2,1,128,640]{4,1,0,2,3:T(2,128)(2,1)}), bf16[2,2,1,128,640]{4,1,0,2,3:T(2,128)(2,1)S(1)}, u32[]{:S(2)}, u32[]{:S(2)}) async-start(bf16[2,2,1,128,640]{4,1,0,2,3:T(2,128)(2,1)} %copy.22), calls=%async_computation | async-start | bytes 1310720 | tf_op jit(solution)/shard_map/all_to_all | solution.py:362
  48.4 17.9 %collective-permute-start = (f32[2,2,128,640]{3,2,1,0:T(8,128)}, f32[2,2,128,640]{3,2,1,0:T(8,128)S(1)}, u32[]{:S(2)}, u32[]{:S(2)}) collective-permute-start(f32[2,2,128,640]{3,2,1,0:T(8,128)} %get-tuple-element.136), channel_id=1, source_target_pairs={{0,1},{1,2},{2,3},{3,4},{4,5},{5,6},{6,7},{7,8},{8,9},{9,10},{10,1... | collective-permute-start | bytes 3932168 | tf_op jit(solution)/shard_map/ppermute | solution.py:36
  51.4 19.1 %collective-permute-start.1 = (f32[2,2,128,640]{3,2,1,0:T(8,128)}, f32[2,2,128,640]{3,2,1,0:T(8,128)S(1)}, u32[]{:S(2)}, u32[]{:S(2)}) collective-permute-start(f32[2,2,128,640]{3,2,1,0:T(8,128)} %get-tuple-element.137), channel_id=1, source_target_pairs={{1,0},{2,1},{3,2},{4,3},{5,4},{6,5},{7,6},{8,7},{9,8},{10,9},{11,1... | collective-permute-start | bytes 3932168 | tf_op jit(solution)/shard_map/ppermute | solution.py:36
  72.6 18.3 %copy-start = (f32[2,2,128,640]{3,2,1,0:T(8,128)}, f32[2,2,128,640]{3,2,1,0:T(8,128)S(1)}, u32[]{:S(2)}) copy-start(f32[2,2,128,640]{3,2,1,0:T(8,128)S(1)} %get-tuple-element.159.q_ref) | copy-start | bytes 3932164
  73.6 15.3 %all-to-all-start.1 = ((f32[32,2,2]{2,1,0:T(2,128)}), f32[32,2,2]{2,1,0:T(2,128)S(1)}, u32[]{:S(2)}, u32[]{:S(2)}) async-start(f32[32,2,2]{2,1,0:T(2,128)} %broadcast_in_dim.12), calls=%async_computation.1 | async-start | bytes 65536 | tf_op jit(solution)/shard_map/all_to_all | solution.py:57
  81.6 12.0 %collective-permute-start.3 = (bf16[2,2,128,640]{3,2,1,0:T(8,128)(2,1)S(1)}, bf16[2,2,128,640]{3,2,1,0:T(8,128)(2,1)S(1)}, u32[]{:S(2)}, u32[]{:S(2)}) collective-permute-start(bf16[2,2,128,640]{3,2,1,0:T(8,128)(2,1)S(1)} %get-tuple-element.158), channel_id=1, source_target_pairs={{1,0},{2,1},{3,2},{4,3},{5,4},{6,5},{7,6},{8,7},{9,8},{10,9},{11,1... | collective-permute-start | bytes 1966088 | tf_op jit(solution)/shard_map/ppermute | solution.py:26
  83.8 10.9 %collective-permute-start.2 = (bf16[2,2,128,640]{3,2,1,0:T(8,128)(2,1)S(1)}, bf16[2,2,128,640]{3,2,1,0:T(8,128)(2,1)}, u32[]{:S(2)}, u32[]{:S(2)}) collective-permute-start(bf16[2,2,128,640]{3,2,1,0:T(8,128)(2,1)S(1)} %get-tuple-element.158), channel_id=1, source_target_pairs={{0,1},{1,2},{2,3},{3,4},{4,5},{5,6},{6,7},{7,8},{8,9},{9,10},{10,1... | collective-permute-start | bytes 1966088 | tf_op jit(solution)/shard_map/ppermute | solution.py:24
  97.2 50.4 %copy-start.1 = (f32[2,2,128,640]{3,2,1,0:T(8,128)S(1)}, f32[2,2,128,640]{3,2,1,0:T(8,128)}, u32[]{:S(2)}) copy-start(f32[2,2,128,640]{3,2,1,0:T(8,128)} %copy-done) | copy-start | bytes 3932164
  116.2 30.4 %collective-permute-start.4 = (f32[2,2,128,640]{3,2,1,0:T(8,128)}, f32[2,2,128,640]{3,2,1,0:T(8,128)S(1)}, u32[]{:S(2)}, u32[]{:S(2)}) collective-permute-start(f32[2,2,128,640]{3,2,1,0:T(8,128)} %get-tuple-element.141), channel_id=1, source_target_pairs={{0,1},{1,2},{2,3},{3,4},{4,5},{5,6},{6,7},{7,8},{8,9},{9,10},{10,1... | collective-permute-start | bytes 3932168 | tf_op jit(solution)/shard_map/ppermute | solution.py:36
  120.7 25.9 %collective-permute-start.5 = (f32[2,2,128,640]{3,2,1,0:T(8,128)}, f32[2,2,128,640]{3,2,1,0:T(8,128)}, u32[]{:S(2)}, u32[]{:S(2)}) collective-permute-start(f32[2,2,128,640]{3,2,1,0:T(8,128)} %get-tuple-element.142), channel_id=1, source_target_pairs={{1,0},{2,1},{3,2},{4,3},{5,4},{6,5},{7,6},{8,7},{9,8},{10,9},{11,1... | collective-permute-start | bytes 3932168 | tf_op jit(solution)/shard_map/ppermute | solution.py:36
  124.0 22.5 %all-to-all-start.2 = ((f32[32,1,2]{2,1,0:T(1,128)}), f32[32,1,2]{2,1,0:T(1,128)S(1)}, u32[]{:S(2)}, u32[]{:S(2)}) async-start(f32[32,1,2]{2,1,0:T(1,128)} %broadcast_in_dim.14), calls=%async_computation.2 | async-start | bytes 32768 | tf_op jit(solution)/shard_map/all_to_all | solution.py:57
  146.6 1.1 copy-start.4
  151.7 25.0 %copy-start.2 = (f32[2,2,128,640]{3,2,1,0:T(8,128)}, f32[2,2,128,640]{3,2,1,0:T(8,128)S(1)}, u32[]{:S(2)}) copy-start(f32[2,2,128,640]{3,2,1,0:T(8,128)S(1)} %get-tuple-element.155.q_ref) | copy-start | bytes 3932164
  151.7 22.2 %collective-permute-start.7 = (bf16[2,2,128,640]{3,2,1,0:T(8,128)(2,1)S(1)}, bf16[2,2,128,640]{3,2,1,0:T(8,128)(2,1)}, u32[]{:S(2)}, u32[]{:S(2)}) collective-permute-start(bf16[2,2,128,640]{3,2,1,0:T(8,128)(2,1)S(1)} %get-tuple-element.154), channel_id=1, source_target_pairs={{1,0},{2,1},{3,2},{4,3},{5,4},{6,5},{7,6},{8,7},{9,8},{10,9},{11,1... | collective-permute-start | bytes 1966088 | tf_op jit(solution)/shard_map/ppermute | solution.py:26
  154.2 19.7 %collective-permute-start.6 = (bf16[2,2,128,640]{3,2,1,0:T(8,128)(2,1)S(1)}, bf16[2,2,128,640]{3,2,1,0:T(8,128)(2,1)}, u32[]{:S(2)}, u32[]{:S(2)}) collective-permute-start(bf16[2,2,128,640]{3,2,1,0:T(8,128)(2,1)S(1)} %get-tuple-element.154), channel_id=1, source_target_pairs={{0,1},{1,2},{2,3},{3,4},{4,5},{5,6},{6,7},{7,8},{8,9},{9,10},{10,1... | collective-permute-start | bytes 1966088 | tf_op jit(solution)/shard_map/ppermute | solution.py:24
  176.6 43.3 %copy-start.3 = (f32[2,2,128,640]{3,2,1,0:T(8,128)S(1)}, f32[2,2,128,640]{3,2,1,0:T(8,128)}, u32[]{:S(2)}) copy-start(f32[2,2,128,640]{3,2,1,0:T(8,128)} %copy-done.2) | copy-start | bytes 3932164
  195.6 24.3 %collective-permute-start.8 = (f32[2,2,128,640]{3,2,1,0:T(8,128)}, f32[2,2,128,640]{3,2,1,0:T(8,128)}, u32[]{:S(2)}, u32[]{:S(2)}) collective-permute-start(f32[2,2,128,640]{3,2,1,0:T(8,128)} %get-tuple-element.146), channel_id=1, source_target_pairs={{0,1},{1,2},{2,3},{3,4},{4,5},{5,6},{6,7},{7,8},{8,9},{9,10},{10,1... | collective-permute-start | bytes 3932168 | tf_op jit(solution)/shard_map/ppermute | solution.py:36
  198.3 21.6 %collective-permute-start.9 = (f32[2,2,128,640]{3,2,1,0:T(8,128)}, f32[2,2,128,640]{3,2,1,0:T(8,128)}, u32[]{:S(2)}, u32[]{:S(2)}) collective-permute-start(f32[2,2,128,640]{3,2,1,0:T(8,128)} %get-tuple-element.147), channel_id=1, source_target_pairs={{1,0},{2,1},{3,2},{4,3},{5,4},{6,5},{7,6},{8,7},{9,8},{10,9},{11,1... | collective-permute-start | bytes 3932168 | tf_op jit(solution)/shard_map/ppermute | solution.py:36

commit v12 on v11

--- a/solution.py
+++ b/solution.py
@@ -357,9 +357,10 @@
         "snr,ncgf->cfsgr", up_time, fourier, preferred_element_type=jnp.float32
     ).astype(jnp.bfloat16)
     spectrum = spectrum.reshape(
-        2, local_freqs, shot_count, freq_groups * receiver_groups, local_rows
-    )
-    received = lax.all_to_all(spectrum, ("freq", "rcv"), split_axis=3, concat_axis=2, tiled=True)
+        2, local_freqs, shot_count, freq_groups, receiver_groups, local_rows
+    )
+    by_freq = lax.all_to_all(spectrum, "freq", split_axis=3, concat_axis=2, tiled=True)
+    received = lax.all_to_all(by_freq, "rcv", split_axis=4, concat_axis=3, tiled=True)
     right_side = received.reshape(2, local_freqs, -1, local_rows).astype(jnp.float32)
     position = lax.axis_index("rcv")
     columns = jnp.clip(

time: 226 us -> 238 us (1.053)
  blocking collectives: 33.6 us -> 48.4 us
  waiting for transfers between devices: 35.6 us -> 33.2 us
    all_to_all x0 -> x1, blocking collectives: none -> 14.8 us  [body(): lax.all_to_all(spectrum, 'freq', split_axis=3, concat_axis=2, tiled=True)]
where the time goes in v12:
time: 238 us; the launch traced here: 236 us
  Pallas kernels  62.5 us (26%)
  starting transfers between devices  58.1 us (24%)
  blocking collectives  48.4 us (20%)
  waiting for transfers between devices  33.2 us (14%)
  other arithmetic  18.4 us (8%)
  local copies, waits for them, and re-layouts  9.44 us (4%)
  matrix products  5.45 us (2%)
    pallas_call x2, Pallas kernels, apply_both(): pl.pallas_call(_both_kernel, grid_spec=grid_spec, out_shape=[jax.ShapeDty...  37.9 us
    all_to_all x2, blocking collectives, rcv_sum(): gathered = lax.all_to_all(spread, 'rcv', 0, 0, tiled=False)  33.6 us
    all_to_all x2, starting transfers between devices, rcv_sum(): gathered = lax.all_to_all(spread, 'rcv', 0, 0, tiled=False)  20.1 us
    ppermute x6, starting transfers between devices, from_behind(): lax.ppermute(value, axis, [(source, source + steps) for source in range(f...  17.1 us
    ppermute x6, waiting for transfers between devices, from_behind(): lax.ppermute(value, axis, [(source, source + steps) for source in range(f...  16.7 us
    all_to_all x1, blocking collectives, body(): lax.all_to_all(spectrum, 'freq', split_axis=3, concat_axis=2, tiled=True)  14.8 us
    pallas_call x1, Pallas kernels, apply_adjoint(): pl.pallas_call(_adjoint_kernel, grid_spec=grid_spec, out_shape=[part_shap...  13 us
    all_to_all x2, waiting for transfers between devices, rcv_sum(): gathered = lax.all_to_all(spread, 'rcv', 0, 0, tiled=False)  12.6 us
  transfers between devices with their start and end apart: 13, of which 7 were waited for; matrix products, arithmetic and copies ran while one was open for 3% of the time, Pallas kernels for 5%

profile of v12, /device:TPU:1, one launch (start us, length us, event | category | flops | bytes accessed | tf_op | source)
XLA Modules:
  0.0 236.5 jit_solution(16347997675229736960)
XLA Ops:
  0.8 5.5 %fusion = bf16[2,2,1,4,20480]{4,3,1,0,2:T(4,128)(2,1)S(1)} fusion(bf16[1,256,20480]{2,1,0:T(8,128)(2,1)} %param.28, bf16[256,1,4,2]{0,2,3,1:T(4,128)(2,1)S(1)} %get-tuple-element.171, bf16[256,1,4,2]{0,2,3,1:T(4,128)(2,1)S(1)} %get-tuple-element.170), kind=kOutput, calls=%fused_computation.1 | convolution fusion | flops 168116224 | bytes 11149312 | tf_op jit(solution)/shard_map/snr,ncgf->cfsgr/dot_general | solution.py:356
  6.8 14.8 %all_to_all.44 = bf16[2,2,1,4,32,640]{5,4,1,0,2,3:T(8,128)(2,1)S(1)} all-to-all(bf16[2,2,1,4,32,640]{5,4,1,0,2,3:T(8,128)(2,1)S(1)} %copy.24), channel_id=1, replica_groups=mesh['freq'=4,'rcv'=32] {'freq'}, dimensions={3} | all-to-all | bytes 1310720 | tf_op jit(solution)/shard_map/all_to_all | solution.py:362
  21.6 1.3 copy.25
  23.0 9.7 %all-to-all-start.1 = ((bf16[2,2,4,1,32,640]{5,2,1,0,3,4:T(4,128)(2,1)}), bf16[2,2,4,1,32,640]{5,2,1,0,3,4:T(4,128)(2,1)S(1)}, u32[]{:S(2)}, u32[]{:S(2)}) async-start(bf16[2,2,4,1,32,640]{5,2,1,0,3,4:T(4,128)(2,1)} %copy.25), calls=%async_computation.1 | async-start | bytes 1310720 | tf_op jit(solution)/shard_map/all_to_all | solution.py:363
  34.0 11.6 %shard_map.89.m_ref = bf16[2,5,256,2816]{3,2,1,0:T(8,128)(2,1)} custom-call(s32[10]{0:T(128)} %reshape.557.counts_ref, bf16[2,5,11,2,128,128]{5,4,3,2,1,0:T(8,128)(2,1)} %a_ref.1), custom_call_target="tpu_custom_call" | custom-call | tf_op jit(solution)/shard_map/pallas_call | solution.py:104
  46.6 13.0 %shard_map.90 = (f32[2,2,128,640]{3,2,1,0:T(8,128)}, f32[2,2,128,640]{3,2,1,0:T(8,128)}, f32[2,2,128,640]{3,2,1,0:T(8,128)}) custom-call(s32[110]{0:T(128)} %reshape.556.cols_ref, s32[10]{0:T(128)} %reshape.557.counts_ref, bf16[2,2,128,640]{3,2,1,0:T(8,128)(2,1)} %bitcast.45, bf16[2,5,256,2816]{3,2,1,0:T(8,128)(2,1)} %shard_map.89.m_ref), custom_call_target="tpu_custom_call" | custom-call | flops 1845493760 | bytes 19005440 | tf_op jit(solution)/shard_map/pallas_call | solution.py:333
  59.7 3.5 %collective-permute-start = (f32[2,2,128,640]{3,2,1,0:T(8,128)}, f32[2,2,128,640]{3,2,1,0:T(8,128)S(1)}, u32[]{:S(2)}, u32[]{:S(2)}) collective-permute-start(f32[2,2,128,640]{3,2,1,0:T(8,128)} %get-tuple-element.136), channel_id=1, source_target_pairs={{0,1},{1,2},{2,3},{3,4},{4,5},{5,6},{6,7},{7,8},{8,9},{9,10},{10,1... | collective-permute-start | bytes 3932168 | tf_op jit(solution)/shard_map/ppermute | solution.py:36
  63.1 1.9 collective-permute-start.1
  65.5 12.4 %collective-permute-done = f32[2,2,128,640]{3,2,1,0:T(8,128)S(1)} collective-permute-done((f32[2,2,128,640]{3,2,1,0:T(8,128)}, f32[2,2,128,640]{3,2,1,0:T(8,128)S(1)}, u32[]{:S(2)}, u32[]{:S(2)}) %collective-permute-start) | collective-permute-done | bytes 1310752 | tf_op jit(solution)/shard_map/ppermute | solution.py:36
  78.0 4.3 %collective-permute-done.1 = f32[2,2,128,640]{3,2,1,0:T(8,128)S(1)} collective-permute-done((f32[2,2,128,640]{3,2,1,0:T(8,128)}, f32[2,2,128,640]{3,2,1,0:T(8,128)S(1)}, u32[]{:S(2)}, u32[]{:S(2)}) %collective-permute-start.1) | collective-permute-done | bytes 1310752 | tf_op jit(solution)/shard_map/ppermute | solution.py:36
  82.3 1.7 fusion.16
  85.0 8.5 %all-to-all-start.2 = ((f32[32,2,2]{2,1,0:T(2,128)}), f32[32,2,2]{2,1,0:T(2,128)S(1)}, u32[]{:S(2)}, u32[]{:S(2)}) async-start(f32[32,2,2]{2,1,0:T(2,128)} %broadcast_in_dim.12), calls=%async_computation.2 | async-start | bytes 65536 | tf_op jit(solution)/shard_map/all_to_all | solution.py:57
  93.5 2.1 collective-permute-start.3
  95.7 3.4 %collective-permute-start.2 = (bf16[2,2,128,640]{3,2,1,0:T(8,128)(2,1)S(1)}, bf16[2,2,128,640]{3,2,1,0:T(8,128)(2,1)}, u32[]{:S(2)}, u32[]{:S(2)}) collective-permute-start(bf16[2,2,128,640]{3,2,1,0:T(8,128)(2,1)S(1)} %get-tuple-element.158), channel_id=1, source_target_pairs={{0,1},{1,2},{2,3},{3,4},{4,5},{5,6},{6,7},{7,8},{8,9},{9,10},{10,1... | collective-permute-start | bytes 1966088 | tf_op jit(solution)/shard_map/ppermute | solution.py:24
  99.1 1.7 all-to-all-done.2
  102.8 2.7 %collective-permute-done.3 = bf16[2,2,128,640]{3,2,1,0:T(8,128)(2,1)S(1)} collective-permute-done((bf16[2,2,128,640]{3,2,1,0:T(8,128)(2,1)S(1)}, bf16[2,2,128,640]{3,2,1,0:T(8,128)(2,1)S(1)}, u32[]{:S(2)}, u32[]{:S(2)}) %collective-permute-start.3) | collective-permute-done | bytes 655392 | tf_op jit(solution)/shard_map/ppermute | solution.py:26
  106.6 2.5 %pad_maximum_fusion.x_ref = bf16[2,2,128,1920]{3,2,1,0:T(8,128)(2,1)} fusion(bf16[2,2,128,640]{3,2,1,0:T(8,128)(2,1)S(1)} %collective-permute-done.3, bf16[2,2,128,640]{3,2,1,0:T(8,128)(2,1)S(1)} %get-tuple-element.158, bf16[2,2,128,640]{3,2,1,0:T(8,128)(2,1)} %collective-permute-done.2), kind=kLoop, calls=%fused_computation.3 | loop fusion | flops 5898240 | bytes 3932160 | tf_op jit(solution)/shard_map/concatenate | solution.py:22
  109.2 18.9 %shard_map.91 = (f32[2,2,128,640]{3,2,1,0:T(8,128)}, f32[2,2,128,640]{3,2,1,0:T(8,128)}, f32[2,2,128,640]{3,2,1,0:T(8,128)}, f32[2,2,128,640]{3,2,1,0:T(8,128)}, f32[2,8,128]{2,1,0:T(8,128)}) custom-call(s32[110]{0:T(128)} %reshape.556.cols_ref, s32[10]{0:T(128)} %reshape.557.counts_ref, f32[4]{0:T(128)} %reshape.558.coef_ref, ...), custom_call_target="tpu_custom_call" | custom-call | flops 3690987520 | bytes 29491200 | tf_op jit(solution)/shard_map/pallas_call | solution.py:268
  128.1 4.5 %collective-permute-start.4 = (f32[2,2,128,640]{3,2,1,0:T(8,128)}, f32[2,2,128,640]{3,2,1,0:T(8,128)S(1)}, u32[]{:S(2)}, u32[]{:S(2)}) collective-permute-start(f32[2,2,128,640]{3,2,1,0:T(8,128)} %get-tuple-element.141), channel_id=1, source_target_pairs={{0,1},{1,2},{2,3},{3,4},{4,5},{5,6},{6,7},{7,8},{8,9},{9,10},{10,1... | collective-permute-start | bytes 3932168 | tf_op jit(solution)/shard_map/ppermute | solution.py:36
  132.6 1.9 collective-permute-start.5
  135.9 11.6 %all-to-all-start.3 = ((f32[32,1,2]{2,1,0:T(1,128)}), f32[32,1,2]{2,1,0:T(1,128)S(1)}, u32[]{:S(2)}, u32[]{:S(2)}) async-start(f32[32,1,2]{2,1,0:T(1,128)} %broadcast_in_dim.14), calls=%async_computation.3 | async-start | bytes 32768 | tf_op jit(solution)/shard_map/all_to_all | solution.py:57
  147.6 10.9 %all-to-all-done.3 = f32[32,1,2]{2,1,0:T(1,128)S(1)} async-done(((f32[32,1,2]{2,1,0:T(1,128)}), f32[32,1,2]{2,1,0:T(1,128)S(1)}, u32[]{:S(2)}, u32[]{:S(2)}) %all-to-all-start.3) | async-done | bytes 288 | tf_op jit(solution)/shard_map/all_to_all | solution.py:57
  159.6 4.0 %fusion.15 = (bf16[2,2,128,640]{3,2,1,0:T(8,128)(2,1)S(1)}, f32[2,2,128,640]{3,2,1,0:T(8,128)S(1)}, f32[2,2,128,640]{3,2,1,0:T(8,128)}) fusion(f32[2,2,128,640]{3,2,1,0:T(8,128)S(1)} %copy-done.1, f32[2]{0:T(128)S(1)} %get-tuple-element.156, f32[2]{0:T(128)S(1)} %add_sqrt_fusion.4, f32[2,2,128,640]{3,2,1,0:T(8,128)} %get-tuple-element.139, ...), kind=kLoop, calls=%fused_computation.58 | loop fusion | flops 2949120 | bytes 9830416 | tf_op jit(solution)/shard_map/convert_element_type | solution.py:385
  163.6 2.6 %collective-permute-start.7 = (bf16[2,2,128,640]{3,2,1,0:T(8,128)(2,1)S(1)}, bf16[2,2,128,640]{3,2,1,0:T(8,128)(2,1)}, u32[]{:S(2)}, u32[]{:S(2)}) collective-permute-start(bf16[2,2,128,640]{3,2,1,0:T(8,128)(2,1)S(1)} %get-tuple-element.154), channel_id=1, source_target_pairs={{1,0},{2,1},{3,2},{4,3},{5,4},{6,5},{7,6},{8,7},{9,8},{10,9},{11,1... | collective-permute-start | bytes 1966088 | tf_op jit(solution)/shard_map/ppermute | solution.py:26
  166.1 3.1 %collective-permute-start.6 = (bf16[2,2,128,640]{3,2,1,0:T(8,128)(2,1)S(1)}, bf16[2,2,128,640]{3,2,1,0:T(8,128)(2,1)}, u32[]{:S(2)}, u32[]{:S(2)}) collective-permute-start(bf16[2,2,128,640]{3,2,1,0:T(8,128)(2,1)S(1)} %get-tuple-element.154), channel_id=1, source_target_pairs={{0,1},{1,2},{2,3},{3,4},{4,5},{5,6},{6,7},{7,8},{8,9},{9,10},{10,1... | collective-permute-start | bytes 1966088 | tf_op jit(solution)/shard_map/ppermute | solution.py:24
  169.5 15.6 %all_to_all.45 = f32[32,1,2]{2,1,0:T(1,128)S(1)} all-to-all(f32[32,1,2]{2,1,0:T(1,128)S(1)} %broadcast_in_dim.15), channel_id=1, replica_groups=mesh['freq'=4,'rcv'=32] {'rcv'}, dimensions={0} | all-to-all | bytes 512 | tf_op jit(solution)/shard_map/all_to_all | solution.py:57
  185.8 2.7 %pad_maximum_fusion.1.x_ref = bf16[2,2,128,1920]{3,2,1,0:T(8,128)(2,1)} fusion(bf16[2,2,128,640]{3,2,1,0:T(8,128)(2,1)} %collective-permute-done.7, bf16[2,2,128,640]{3,2,1,0:T(8,128)(2,1)S(1)} %get-tuple-element.154, bf16[2,2,128,640]{3,2,1,0:T(8,128)(2,1)} %collective-permute-done.6), kind=kLoop, calls=%fused_computation.4 | loop fusion | flops 5898240 | bytes 3932160 | tf_op jit(solution)/shard_map/concatenate | solution.py:22
  188.5 18.9 %shard_map.92 = (f32[2,2,128,640]{3,2,1,0:T(8,128)}, f32[2,2,128,640]{3,2,1,0:T(8,128)}, f32[2,2,128,640]{3,2,1,0:T(8,128)}, f32[2,2,128,640]{3,2,1,0:T(8,128)}, f32[2,8,128]{2,1,0:T(8,128)}) custom-call(s32[110]{0:T(128)} %reshape.556.cols_ref, s32[10]{0:T(128)} %reshape.557.counts_ref, f32[4]{0:T(128)} %reshape.559.coef_ref, ...), custom_call_target="tpu_custom_call" | custom-call | flops 3690987520 | bytes 29491200 | tf_op jit(solution)/shard_map/pallas_call | solution.py:268
  207.5 2.7 %collective-permute-start.8 = (f32[2,2,128,640]{3,2,1,0:T(8,128)}, f32[2,2,128,640]{3,2,1,0:T(8,128)}, u32[]{:S(2)}, u32[]{:S(2)}) collective-permute-start(f32[2,2,128,640]{3,2,1,0:T(8,128)} %get-tuple-element.146), channel_id=1, source_target_pairs={{0,1},{1,2},{2,3},{3,4},{4,5},{5,6},{6,7},{7,8},{8,9},{9,10},{10,1... | collective-permute-start | bytes 3932168 | tf_op jit(solution)/shard_map/ppermute | solution.py:36
  210.2 2.6 %collective-permute-start.9 = (f32[2,2,128,640]{3,2,1,0:T(8,128)}, f32[2,2,128,640]{3,2,1,0:T(8,128)}, u32[]{:S(2)}, u32[]{:S(2)}) collective-permute-start(f32[2,2,128,640]{3,2,1,0:T(8,128)} %get-tuple-element.147), channel_id=1, source_target_pairs={{1,0},{2,1},{3,2},{4,3},{5,4},{6,5},{7,6},{8,7},{9,8},{10,9},{11,1... | collective-permute-start | bytes 3932168 | tf_op jit(solution)/shard_map/ppermute | solution.py:36
  213.7 18.0 %all_to_all.46 = f32[32,1,2]{2,1,0:T(1,128)S(1)} all-to-all(f32[32,1,2]{2,1,0:T(1,128)S(1)} %broadcast_in_dim.34), channel_id=1, replica_groups=mesh['freq'=4,'rcv'=32] {'rcv'}, dimensions={0} | all-to-all | bytes 512 | tf_op jit(solution)/shard_map/all_to_all | solution.py:57
  231.8 4.7 %subtract_multiply_fusion = (f32[2,2,128,640]{3,2,1,0:T(8,128)}, f32[2,2,128,640]{3,2,1,0:T(8,128)}) fusion(f32[2,2,128,640]{3,2,1,0:T(8,128)} %get-tuple-element.144, f32[2,2,128,640]{3,2,1,0:T(8,128)} %collective-permute-done.9, f32[2,2,128,640]{3,2,1,0:T(8,128)} %get-tuple-element.145, f32[2,2,128,640]{3,2,1,0:T(8,128)} %collective-permute-done.8, ...), kind=kLoop, calls=%fused_computation.7 | loop fusion | flops 4587520 | bytes 10485816 | tf_op jit(solution)/shard_map/mul | solution.py:434
  (62 shorter events, 12.0 us)
Async XLA Ops:
  21.6 11.1 %copy-start.7 = (s32[2,5]{1,0:T(2,128)S(1)}, s32[2,5]{1,0:T(2,128)}, u32[]{:S(2)}) copy-start(s32[2,5]{1,0:T(2,128)} %param.31) | copy-start | bytes 124
  21.6 11.7 %copy-start.6 = (s32[2,5,11]{2,0,1:T(2,128)S(1)}, s32[2,5,11]{2,0,1:T(2,128)}, u32[]{:S(2)}) copy-start(s32[2,5,11]{2,0,1:T(2,128)} %param.30) | copy-start | bytes 1324
  23.0 22.7 %all-to-all-start.1 = ((bf16[2,2,4,1,32,640]{5,2,1,0,3,4:T(4,128)(2,1)}), bf16[2,2,4,1,32,640]{5,2,1,0,3,4:T(4,128)(2,1)S(1)}, u32[]{:S(2)}, u32[]{:S(2)}) async-start(bf16[2,2,4,1,32,640]{5,2,1,0,3,4:T(4,128)(2,1)} %copy.25), calls=%async_computation.1 | async-start | bytes 1310720 | tf_op jit(solution)/shard_map/all_to_all | solution.py:363
  46.6 35.6 %copy-start.4 = (bf16[2,2,4,1,32,640]{5,4,2,1,0,3:T(8,128)(2,1)S(1)}, bf16[2,2,4,1,32,640]{5,4,2,1,0,3:T(8,128)(2,1)}, u32[]{:S(2)}) copy-start(bf16[2,2,4,1,32,640]{5,4,2,1,0,3:T(8,128)(2,1)} %copy.26) | copy-start | bytes 1966084
  59.7 18.3 %collective-permute-start = (f32[2,2,128,640]{3,2,1,0:T(8,128)}, f32[2,2,128,640]{3,2,1,0:T(8,128)S(1)}, u32[]{:S(2)}, u32[]{:S(2)}) collective-permute-start(f32[2,2,128,640]{3,2,1,0:T(8,128)} %get-tuple-element.136), channel_id=1, source_target_pairs={{0,1},{1,2},{2,3},{3,4},{4,5},{5,6},{6,7},{7,8},{8,9},{9,10},{10,1... | collective-permute-start | bytes 3932168 | tf_op jit(solution)/shard_map/ppermute | solution.py:36
  63.1 19.1 %collective-permute-start.1 = (f32[2,2,128,640]{3,2,1,0:T(8,128)}, f32[2,2,128,640]{3,2,1,0:T(8,128)S(1)}, u32[]{:S(2)}, u32[]{:S(2)}) collective-permute-start(f32[2,2,128,640]{3,2,1,0:T(8,128)} %get-tuple-element.137), channel_id=1, source_target_pairs={{1,0},{2,1},{3,2},{4,3},{5,4},{6,5},{7,6},{8,7},{9,8},{10,9},{11,1... | collective-permute-start | bytes 3932168 | tf_op jit(solution)/shard_map/ppermute | solution.py:36
  84.0 18.8 %copy-start = (f32[2,2,128,640]{3,2,1,0:T(8,128)}, f32[2,2,128,640]{3,2,1,0:T(8,128)S(1)}, u32[]{:S(2)}) copy-start(f32[2,2,128,640]{3,2,1,0:T(8,128)S(1)} %get-tuple-element.159.q_ref) | copy-start | bytes 3932164
  85.0 15.8 %all-to-all-start.2 = ((f32[32,2,2]{2,1,0:T(2,128)}), f32[32,2,2]{2,1,0:T(2,128)S(1)}, u32[]{:S(2)}, u32[]{:S(2)}) async-start(f32[32,2,2]{2,1,0:T(2,128)} %broadcast_in_dim.12), calls=%async_computation.2 | async-start | bytes 65536 | tf_op jit(solution)/shard_map/all_to_all | solution.py:57
  93.5 12.0 %collective-permute-start.3 = (bf16[2,2,128,640]{3,2,1,0:T(8,128)(2,1)S(1)}, bf16[2,2,128,640]{3,2,1,0:T(8,128)(2,1)S(1)}, u32[]{:S(2)}, u32[]{:S(2)}) collective-permute-start(bf16[2,2,128,640]{3,2,1,0:T(8,128)(2,1)S(1)} %get-tuple-element.158), channel_id=1, source_target_pairs={{1,0},{2,1},{3,2},{4,3},{5,4},{6,5},{7,6},{8,7},{9,8},{10,9},{11,1... | collective-permute-start | bytes 1966088 | tf_op jit(solution)/shard_map/ppermute | solution.py:26
  95.7 10.9 %collective-permute-start.2 = (bf16[2,2,128,640]{3,2,1,0:T(8,128)(2,1)S(1)}, bf16[2,2,128,640]{3,2,1,0:T(8,128)(2,1)}, u32[]{:S(2)}, u32[]{:S(2)}) collective-permute-start(bf16[2,2,128,640]{3,2,1,0:T(8,128)(2,1)S(1)} %get-tuple-element.158), channel_id=1, source_target_pairs={{0,1},{1,2},{2,3},{3,4},{4,5},{5,6},{6,7},{7,8},{8,9},{9,10},{10,1... | collective-permute-start | bytes 1966088 | tf_op jit(solution)/shard_map/ppermute | solution.py:24
  109.2 50.4 %copy-start.1 = (f32[2,2,128,640]{3,2,1,0:T(8,128)S(1)}, f32[2,2,128,640]{3,2,1,0:T(8,128)}, u32[]{:S(2)}) copy-start(f32[2,2,128,640]{3,2,1,0:T(8,128)} %copy-done) | copy-start | bytes 3932164
  128.1 30.4 %collective-permute-start.4 = (f32[2,2,128,640]{3,2,1,0:T(8,128)}, f32[2,2,128,640]{3,2,1,0:T(8,128)S(1)}, u32[]{:S(2)}, u32[]{:S(2)}) collective-permute-start(f32[2,2,128,640]{3,2,1,0:T(8,128)} %get-tuple-element.141), channel_id=1, source_target_pairs={{0,1},{1,2},{2,3},{3,4},{4,5},{5,6},{6,7},{7,8},{8,9},{9,10},{10,1... | collective-permute-start | bytes 3932168 | tf_op jit(solution)/shard_map/ppermute | solution.py:36
  132.6 25.9 %collective-permute-start.5 = (f32[2,2,128,640]{3,2,1,0:T(8,128)}, f32[2,2,128,640]{3,2,1,0:T(8,128)}, u32[]{:S(2)}, u32[]{:S(2)}) collective-permute-start(f32[2,2,128,640]{3,2,1,0:T(8,128)} %get-tuple-element.142), channel_id=1, source_target_pairs={{1,0},{2,1},{3,2},{4,3},{5,4},{6,5},{7,6},{8,7},{9,8},{10,9},{11,1... | collective-permute-start | bytes 3932168 | tf_op jit(solution)/shard_map/ppermute | solution.py:36
  135.9 22.5 %all-to-all-start.3 = ((f32[32,1,2]{2,1,0:T(1,128)}), f32[32,1,2]{2,1,0:T(1,128)S(1)}, u32[]{:S(2)}, u32[]{:S(2)}) async-start(f32[32,1,2]{2,1,0:T(1,128)} %broadcast_in_dim.14), calls=%async_computation.3 | async-start | bytes 32768 | tf_op jit(solution)/shard_map/all_to_all | solution.py:57
  158.5 1.1 copy-start.5
  163.6 25.0 %copy-start.2 = (f32[2,2,128,640]{3,2,1,0:T(8,128)}, f32[2,2,128,640]{3,2,1,0:T(8,128)S(1)}, u32[]{:S(2)}) copy-start(f32[2,2,128,640]{3,2,1,0:T(8,128)S(1)} %get-tuple-element.155.q_ref) | copy-start | bytes 3932164
  163.6 22.2 %collective-permute-start.7 = (bf16[2,2,128,640]{3,2,1,0:T(8,128)(2,1)S(1)}, bf16[2,2,128,640]{3,2,1,0:T(8,128)(2,1)}, u32[]{:S(2)}, u32[]{:S(2)}) collective-permute-start(bf16[2,2,128,640]{3,2,1,0:T(8,128)(2,1)S(1)} %get-tuple-element.154), channel_id=1, source_target_pairs={{1,0},{2,1},{3,2},{4,3},{5,4},{6,5},{7,6},{8,7},{9,8},{10,9},{11,1... | collective-permute-start | bytes 1966088 | tf_op jit(solution)/shard_map/ppermute | solution.py:26
  166.1 19.7 %collective-permute-start.6 = (bf16[2,2,128,640]{3,2,1,0:T(8,128)(2,1)S(1)}, bf16[2,2,128,640]{3,2,1,0:T(8,128)(2,1)}, u32[]{:S(2)}, u32[]{:S(2)}) collective-permute-start(bf16[2,2,128,640]{3,2,1,0:T(8,128)(2,1)S(1)} %get-tuple-element.154), channel_id=1, source_target_pairs={{0,1},{1,2},{2,3},{3,4},{4,5},{5,6},{6,7},{7,8},{8,9},{9,10},{10,1... | collective-permute-start | bytes 1966088 | tf_op jit(solution)/shard_map/ppermute | solution.py:24
  188.5 43.3 %copy-start.3 = (f32[2,2,128,640]{3,2,1,0:T(8,128)S(1)}, f32[2,2,128,640]{3,2,1,0:T(8,128)}, u32[]{:S(2)}) copy-start(f32[2,2,128,640]{3,2,1,0:T(8,128)} %copy-done.2) | copy-start | bytes 3932164
  207.5 24.3 %collective-permute-start.8 = (f32[2,2,128,640]{3,2,1,0:T(8,128)}, f32[2,2,128,640]{3,2,1,0:T(8,128)}, u32[]{:S(2)}, u32[]{:S(2)}) collective-permute-start(f32[2,2,128,640]{3,2,1,0:T(8,128)} %get-tuple-element.146), channel_id=1, source_target_pairs={{0,1},{1,2},{2,3},{3,4},{4,5},{5,6},{6,7},{7,8},{8,9},{9,10},{10,1... | collective-permute-start | bytes 3932168 | tf_op jit(solution)/shard_map/ppermute | solution.py:36
  210.2 21.6 %collective-permute-start.9 = (f32[2,2,128,640]{3,2,1,0:T(8,128)}, f32[2,2,128,640]{3,2,1,0:T(8,128)}, u32[]{:S(2)}, u32[]{:S(2)}) collective-permute-start(f32[2,2,128,640]{3,2,1,0:T(8,128)} %get-tuple-element.147), channel_id=1, source_target_pairs={{1,0},{2,1},{3,2},{4,3},{5,4},{6,5},{7,6},{8,7},{9,8},{10,9},{11,1... | collective-permute-start | bytes 3932168 | tf_op jit(solution)/shard_map/ppermute | solution.py:36

commit v13 on v11

--- a/solution.py
+++ b/solution.py
@@ -1,3 +1,4 @@
+import functools
 import math
 
 import jax
@@ -153,8 +154,10 @@
     upper_ref[...] = acc_ref[:, :, rim + own :]
 
 
-def _adjoint_kernel(cols_ref, counts_ref, u_ref, m_ref, lower_ref, middle_ref, upper_ref, acc_ref):
-    freq = pl.program_id(0)
+def _adjoint_kernel(
+    cols_ref, counts_ref, u_ref, m_ref, lower_ref, middle_ref, upper_ref, acc_ref, *, first
+):
+    freq = pl.program_id(0) + first
     row = pl.program_id(1)
     rows = pl.num_programs(1)
 
@@ -185,8 +188,10 @@
     squares_ref,
     picked_ref,
     acc_ref,
+    *,
+    first,
 ):
-    freq = pl.program_id(0)
+    freq = pl.program_id(0) + first
     row = pl.program_id(1)
     rows = pl.num_programs(1)
     depth, width = m_ref.shape
@@ -235,23 +240,25 @@
     return part_spec, part_shape
 
 
-def apply_both(extended, raw, left, coefs, stacked, cols, counts):
-    local_freqs, local_blocks, depth, width = stacked.shape
+def apply_both(extended, raw, left, coefs, stacked, cols, counts, first):
+    _, local_blocks, depth, width = stacked.shape
+    local_freqs = 1
     block_size = depth // 2
     _, _, sources, span = extended.shape
     own_rows = local_blocks * block_size
     rim = (span - own_rows) // 2
     part_spec, part_shape = _part_specs(local_freqs, sources)
     own = pl.BlockSpec((2, None, sources, block_size), lambda f, r, c, n: (0, f, 0, r))
+    taken = pl.BlockSpec((2, None, sources, block_size), lambda f, r, c, n: (0, f + first, 0, r))
     grid_spec = pltpu.PrefetchScalarGridSpec(
         num_scalar_prefetch=2,
         grid=(local_freqs, local_blocks),
         in_specs=[
             pl.BlockSpec(memory_space=pltpu.SMEM),
-            pl.BlockSpec((2, None, sources, span), lambda f, r, c, n: (0, f, 0, 0)),
-            own,
-            own,
-            pl.BlockSpec((None, None, depth, width), lambda f, r, c, n: (f, r, 0, 0)),
+            pl.BlockSpec((2, None, sources, span), lambda f, r, c, n: (0, f + first, 0, 0)),
+            taken,
+            taken,
+            pl.BlockSpec((None, None, depth, width), lambda f, r, c, n: (f + first, r, 0, 0)),
         ],
         out_specs=[
             own,
@@ -266,10 +273,10 @@
         ],
     )
     return pl.pallas_call(
-        _both_kernel,
+        functools.partial(_both_kernel, first=first),
         grid_spec=grid_spec,
         out_shape=[
-            jax.ShapeDtypeStruct(raw.shape, jnp.float32),
+            jax.ShapeDtypeStruct((2, local_freqs) + raw.shape[2:], jnp.float32),
             part_shape(rim),
             part_shape(own_rows),
             part_shape(rim),
@@ -277,9 +284,9 @@
         ],
         compiler_params=pltpu.CompilerParams(dimension_semantics=("arbitrary", "arbitrary")),
         cost_estimate=pl.CostEstimate(
-            flops=4 * local_freqs * local_blocks * sources * depth * width,
+            flops=4 * local_blocks * sources * depth * width,
             transcendentals=0,
-            bytes_accessed=stacked.size * 2 + extended.size * 2 + raw.size * 40,
+            bytes_accessed=(stacked.size + extended.size + raw.size * 20) // stacked.shape[0] * 2,
         ),
     )(cols, counts, coefs, extended, raw, left, stacked)
 
@@ -313,8 +320,9 @@
     )(cols, counts, extended, stacked)
 
 
-def apply_adjoint(rounded, stacked, cols, counts, span):
-    local_freqs, local_blocks, depth, width = stacked.shape
+def apply_adjoint(rounded, stacked, cols, counts, span, first):
+    _, local_blocks, depth, width = stacked.shape
+    local_freqs = 1
     block_size = depth // 2
     sources = rounded.shape[2]
     own = local_blocks * block_size
@@ -324,14 +332,16 @@
         num_scalar_prefetch=2,
         grid=(local_freqs, local_blocks),
         in_specs=[
-            pl.BlockSpec((2, None, sources, block_size), lambda f, r, c, n: (0, f, 0, r)),
-            pl.BlockSpec((None, None, depth, width), lambda f, r, c, n: (f, r, 0, 0)),
+            pl.BlockSpec(
+                (2, None, sources, block_size), lambda f, r, c, n: (0, f + first, 0, r)
+            ),
+            pl.BlockSpec((None, None, depth, width), lambda f, r, c, n: (f + first, r, 0, 0)),
         ],
         out_specs=[part_spec(rim), part_spec(own), part_spec(rim)],
         scratch_shapes=[pltpu.VMEM((2, sources, span), jnp.float32)],
     )
     return pl.pallas_call(
-        _adjoint_kernel,
+        functools.partial(_adjoint_kernel, first=first),
         grid_spec=grid_spec,
         out_shape=[part_shape(rim), part_shape(own), part_shape(rim)],
         compiler_params=pltpu.CompilerParams(dimension_semantics=("arbitrary", "arbitrary")),
@@ -377,19 +387,26 @@
 
     def adjoint(field):
         rounded = field.astype(jnp.bfloat16)
-        parts = apply_adjoint(rounded, stacked, columns, counts, span_blocks * block_size)
-        return field + exchange(*parts)
+        pieces = [
+            exchange(*apply_adjoint(rounded, stacked, columns, counts, span_blocks * block_size, f))
+            for f in range(local_freqs)
+        ]
+        return field + jnp.concatenate(pieces, axis=1)
 
     def forward_adjoint(raw, scale, left, shift):
         extended = with_halo(raw.astype(jnp.bfloat16), (("rcv", 3),), rim_rows)
         coefs = jnp.stack(
             [jnp.broadcast_to(scale, shift.shape).reshape(-1), shift.reshape(-1)], axis=1
         ).reshape(-1)
-        residual, lower, middle, upper, partial = apply_both(
-            extended, raw, left, coefs, stacked, columns, counts
-        )
-        total = rcv_sum(partial[:, 0, 0])[None, :, None, None]
-        return residual, residual + exchange(lower, middle, upper), total
+        results = [
+            apply_both(extended, raw, left, coefs, stacked, columns, counts, f)
+            for f in range(local_freqs)
+        ]
+        residual = jnp.concatenate([piece[0] for piece in results], axis=1)
+        spread = jnp.concatenate([exchange(*piece[1:4]) for piece in results], axis=1)
+        partial = jnp.concatenate([piece[4][:, 0, 0] for piece in results])
+        total = rcv_sum(partial)[None, :, None, None]
+        return residual, residual + spread, total
 
     def forward(field):
         extended = with_halo(field.astype(jnp.bfloat16), (("rcv", 3),), rim_rows)

time: 226 us -> 243 us (1.075)
  starting transfers between devices: 59 us -> 81 us
  blocking collectives: 33.6 us -> 12.6 us
  Pallas kernels: 62.4 us -> 70.7 us
  local copies, waits for them, and re-layouts: 9.55 us -> 16.8 us
    all_to_all x2 -> x1, blocking collectives: 33.6 us -> 12.6 us  [rcv_sum(): gathered = lax.all_to_all(spread, 'rcv', 0, 0, tiled=False)]
    ppermute x6 -> x12, starting transfers between devices: 16.7 us -> 30.4 us  [from_behind(): lax.ppermute(value, axis, [(source, source + steps) for source in range(f...]
    all_to_all x2 -> x3, starting transfers between devices: 19.6 us -> 28.3 us  [rcv_sum(): gathered = lax.all_to_all(spread, 'rcv', 0, 0, tiled=False)]
    pallas_call x3 -> x6, Pallas kernels: 50.8 us -> 59.1 us  [the longest x4 43.8 us: apply_both(): pl.pallas_call(functools.partial(_both_kernel, first=first), grid_spec=gr...]
    convert_element_type x2, other arithmetic: 5.97 us -> 1.9 us  [forward_adjoint(): extended = with_halo(raw.astype(jnp.bfloat16), (('rcv', 3),), rim_rows)]
    all_to_all x2 -> x3, waiting for transfers between devices: 12.6 us -> 9.04 us  [rcv_sum(): gathered = lax.all_to_all(spread, 'rcv', 0, 0, tiled=False)]
    add x0 -> x6, other arithmetic: none -> 3.45 us  [exchange(): middle = middle.at[..., local_rows - rim_rows:].add(from_above)]
    slice x2 -> x4, local copies, waits for them, and re-layouts: 1.59 us -> 4.8 us  [forward_adjoint(): partial = jnp.concatenate([piece[4][:, 0, 0] for piece in results])]
  transfers between devices with their start and end apart: 13 -> 20, of which waited for: 7 -> 10; matrix products, arithmetic and copies ran while one was open for 3% -> 6% of each run, Pallas kernels for 5% -> 17%
where the time goes in v13:
time: 243 us; the launch traced here: 241 us
  starting transfers between devices  81 us (33%)
  Pallas kernels  70.7 us (29%)
  waiting for transfers between devices  35.9 us (15%)
  other arithmetic  17.7 us (7%)
  local copies, waits for them, and re-layouts  16.8 us (7%)
  blocking collectives  12.6 us (5%)
  matrix products  5.45 us (2%)
    pallas_call x4, Pallas kernels, apply_both(): pl.pallas_call(functools.partial(_both_kernel, first=first), grid_spec=gr...  43.8 us
    ppermute x12, starting transfers between devices, from_behind(): lax.ppermute(value, axis, [(source, source + steps) for source in range(f...  30.4 us
    all_to_all x3, starting transfers between devices, rcv_sum(): gathered = lax.all_to_all(spread, 'rcv', 0, 0, tiled=False)  28.3 us
    ppermute x12, waiting for transfers between devices, from_behind(): lax.ppermute(value, axis, [(source, source + steps) for source in range(f...  18.7 us
    pallas_call x2, Pallas kernels, apply_adjoint(): pl.pallas_call(functools.partial(_adjoint_kernel, first=first), grid_spec...  15.3 us
    all_to_all x1, blocking collectives, rcv_sum(): gathered = lax.all_to_all(spread, 'rcv', 0, 0, tiled=False)  12.6 us
    pallas_call x1, Pallas kernels, stack_blocks(): pl.pallas_call(_stack_kernel, grid_spec=grid_spec, out_shape=jax.ShapeDty...  11.6 us
    all_to_all x1, starting transfers between devices, body(): lax.all_to_all(spectrum, ('freq', 'rcv'), split_axis=3, concat_axis=2, ti...  11.5 us
  transfers between devices with their start and end apart: 20, of which 10 were waited for; matrix products, arithmetic and copies ran while one was open for 6% of the time, Pallas kernels for 17%

profile of v13, /device:TPU:1, one launch (start us, length us, event | category | flops | bytes accessed | tf_op | source)
XLA Modules:
  0.0 241.2 jit_solution(7121507206266990209)
XLA Ops:
  0.8 5.5 %fusion = bf16[2,2,1,4,20480]{4,3,1,0,2:T(4,128)(2,1)S(1)} fusion(bf16[1,256,20480]{2,1,0:T(8,128)(2,1)} %param.52, bf16[256,1,4,2]{0,2,3,1:T(4,128)(2,1)S(1)} %get-tuple-element.318, bf16[256,1,4,2]{0,2,3,1:T(4,128)(2,1)S(1)} %get-tuple-element.317), kind=kOutput, calls=%fused_computation.1 | convolution fusion | flops 168116224 | bytes 11149312 | tf_op jit(solution)/shard_map/snr,ncgf->cfsgr/dot_general | solution.py:366
  8.3 11.5 %all-to-all-start = ((bf16[2,2,1,128,640]{4,1,0,2,3:T(2,128)(2,1)}), bf16[2,2,1,128,640]{4,1,0,2,3:T(2,128)(2,1)S(1)}, u32[]{:S(2)}, u32[]{:S(2)}) async-start(bf16[2,2,1,128,640]{4,1,0,2,3:T(2,128)(2,1)} %copy.22), calls=%async_computation | async-start | bytes 1310720 | tf_op jit(solution)/shard_map/all_to_all | solution.py:372
  21.1 11.6 %shard_map.119.m_ref = bf16[2,5,256,2816]{3,2,1,0:T(8,128)(2,1)} custom-call(s32[10]{0:T(128)} %reshape.768.counts_ref, bf16[2,5,11,2,128,128]{5,4,3,2,1,0:T(8,128)(2,1)} %a_ref.1), custom_call_target="tpu_custom_call" | custom-call | tf_op jit(solution)/shard_map/pallas_call | solution.py:105
  35.5 7.6 %shard_map.120 = (f32[2,1,128,640]{3,2,1,0:T(8,128)}, f32[2,1,128,640]{3,2,1,0:T(8,128)}, f32[2,1,128,640]{3,2,1,0:T(8,128)}) custom-call(s32[110]{0:T(128)} %reshape.767.cols_ref, s32[10]{0:T(128)} %reshape.768.counts_ref, bf16[2,2,128,640]{3,2,1,0:T(8,128)(2,1)} %bitcast.57, bf16[2,5,256,2816]{3,2,1,0:T(8,128)(2,1)} %shard_map.119.m_ref), custom_call_target="tpu_custom_call" | custom-call | flops 922746880 | bytes 19005440 | tf_op jit(solution)/shard_map/pallas_call | solution.py:343
  43.2 3.0 %collective-permute-start = (f32[2,1,128,640]{3,2,1,0:T(8,128)}, f32[2,1,128,640]{3,2,1,0:T(8,128)S(1)}, u32[]{:S(2)}, u32[]{:S(2)}) collective-permute-start(f32[2,1,128,640]{3,2,1,0:T(8,128)} %get-tuple-element.269), channel_id=1, source_target_pairs={{0,1},{1,2},{2,3},{3,4},{4,5},{5,6},{6,7},{7,8},{8,9},{9,10},{10,1... | collective-permute-start | bytes 1966088 | tf_op jit(solution)/shard_map/ppermute | solution.py:37
  46.2 2.1 collective-permute-start.1
  48.2 7.6 %shard_map.121 = (f32[2,1,128,640]{3,2,1,0:T(8,128)}, f32[2,1,128,640]{3,2,1,0:T(8,128)}, f32[2,1,128,640]{3,2,1,0:T(8,128)}) custom-call(s32[110]{0:T(128)} %reshape.767.cols_ref, s32[10]{0:T(128)} %reshape.768.counts_ref, bf16[2,2,128,640]{3,2,1,0:T(8,128)(2,1)} %bitcast.58, bf16[2,5,256,2816]{3,2,1,0:T(8,128)(2,1)} %shard_map.119.m_ref), custom_call_target="tpu_custom_call" | custom-call | flops 922746880 | bytes 19005440 | tf_op jit(solution)/shard_map/pallas_call | solution.py:343
  55.9 3.6 %collective-permute-start.2 = (f32[2,1,128,640]{3,2,1,0:T(8,128)}, f32[2,1,128,640]{3,2,1,0:T(8,128)S(1)}, u32[]{:S(2)}, u32[]{:S(2)}) collective-permute-start(f32[2,1,128,640]{3,2,1,0:T(8,128)} %get-tuple-element.272), channel_id=1, source_target_pairs={{0,1},{1,2},{2,3},{3,4},{4,5},{5,6},{6,7},{7,8},{8,9},{9,10},{10,1... | collective-permute-start | bytes 1966088 | tf_op jit(solution)/shard_map/ppermute | solution.py:37
  61.6 5.8 %collective-permute-done.2 = f32[2,1,128,640]{3,2,1,0:T(8,128)S(1)} collective-permute-done((f32[2,1,128,640]{3,2,1,0:T(8,128)}, f32[2,1,128,640]{3,2,1,0:T(8,128)S(1)}, u32[]{:S(2)}, u32[]{:S(2)}) %collective-permute-start.2) | collective-permute-done | bytes 655392 | tf_op jit(solution)/shard_map/ppermute | solution.py:37
  67.3 4.3 %collective-permute-done.3 = f32[2,1,128,640]{3,2,1,0:T(8,128)S(1)} collective-permute-done((f32[2,1,128,640]{3,2,1,0:T(8,128)}, f32[2,1,128,640]{3,2,1,0:T(8,128)S(1)}, u32[]{:S(2)}, u32[]{:S(2)}) %collective-permute-start.3) | collective-permute-done | bytes 655392 | tf_op jit(solution)/shard_map/ppermute | solution.py:37
  73.2 10.1 %all-to-all-start.1 = ((f32[32,2,2]{2,1,0:T(2,128)}), f32[32,2,2]{2,1,0:T(2,128)S(1)}, u32[]{:S(2)}, u32[]{:S(2)}) async-start(f32[32,2,2]{2,1,0:T(2,128)} %broadcast_in_dim.8), calls=%async_computation.1 | async-start | bytes 65536 | tf_op jit(solution)/shard_map/all_to_all | solution.py:58
  83.3 3.5 %collective-permute-start.4 = (bf16[2,2,128,640]{3,2,1,0:T(8,128)(2,1)S(1)}, bf16[2,2,128,640]{3,2,1,0:T(8,128)(2,1)S(1)}, u32[]{:S(2)}, u32[]{:S(2)}) collective-permute-start(bf16[2,2,128,640]{3,2,1,0:T(8,128)(2,1)S(1)} %get-tuple-element.304), channel_id=1, source_target_pairs={{0,1},{1,2},{2,3},{3,4},{4,5},{5,6},{6,7},{7,8},{8,9},{9,10},{10,1... | collective-permute-start | bytes 1966088 | tf_op jit(solution)/shard_map/ppermute | solution.py:25
  94.3 4.5 %collective-permute-done.5 = bf16[2,2,128,640]{3,2,1,0:T(8,128)(2,1)} collective-permute-done((bf16[2,2,128,640]{3,2,1,0:T(8,128)(2,1)S(1)}, bf16[2,2,128,640]{3,2,1,0:T(8,128)(2,1)}, u32[]{:S(2)}, u32[]{:S(2)}) %collective-permute-start.5) | collective-permute-done | bytes 655392 | tf_op jit(solution)/shard_map/ppermute | solution.py:27
  98.8 2.5 %pad_maximum_fusion.x_ref = bf16[2,2,128,1920]{3,2,1,0:T(8,128)(2,1)} fusion(bf16[2,2,128,640]{3,2,1,0:T(8,128)(2,1)} %collective-permute-done.5, bf16[2,2,128,640]{3,2,1,0:T(8,128)(2,1)S(1)} %get-tuple-element.304, bf16[2,2,128,640]{3,2,1,0:T(8,128)(2,1)S(1)} %collective-permute-done.4), kind=kLoop, calls=%fused_computation.3 | loop fusion | flops 5898240 | bytes 3932160 | tf_op jit(solution)/shard_map/concatenate | solution.py:23
  101.3 11.0 %shard_map.122 = (f32[2,1,128,640]{3,2,1,0:T(8,128)}, f32[2,1,128,640]{3,2,1,0:T(8,128)}, f32[2,1,128,640]{3,2,1,0:T(8,128)}, f32[2,1,128,640]{3,2,1,0:T(8,128)}, f32[1,8,128]{2,1,0:T(8,128)}) custom-call(s32[110]{0:T(128)} %reshape.767.cols_ref, s32[10]{0:T(128)} %reshape.768.counts_ref, f32[4]{0:T(128)} %reshape.769.coef_ref, ...), custom_call_target="tpu_custom_call" | custom-call | flops 1845493760 | bytes 14745600 | tf_op jit(solution)/shard_map/pallas_call | solution.py:275
  114.2 2.4 %collective-permute-start.7 = (f32[2,1,128,640]{3,2,1,0:T(8,128)}, f32[2,1,128,640]{3,2,1,0:T(8,128)S(1)}, u32[]{:S(2)}, u32[]{:S(2)}) collective-permute-start(f32[2,1,128,640]{3,2,1,0:T(8,128)} %get-tuple-element.280), channel_id=1, source_target_pairs={{1,0},{2,1},{3,2},{4,3},{5,4},{6,5},{7,6},{8,7},{9,8},{10,9},{11,1... | collective-permute-start | bytes 1966088 | tf_op jit(solution)/shard_map/ppermute | solution.py:37
  116.7 10.9 %shard_map.123 = (f32[2,1,128,640]{3,2,1,0:T(8,128)}, f32[2,1,128,640]{3,2,1,0:T(8,128)}, f32[2,1,128,640]{3,2,1,0:T(8,128)}, f32[2,1,128,640]{3,2,1,0:T(8,128)}, f32[1,8,128]{2,1,0:T(8,128)}) custom-call(s32[110]{0:T(128)} %reshape.767.cols_ref, s32[10]{0:T(128)} %reshape.768.counts_ref, f32[4]{0:T(128)} %reshape.769.coef_ref, ...), custom_call_target="tpu_custom_call" | custom-call | flops 1845493760 | bytes 14745600 | tf_op jit(solution)/shard_map/pallas_call | solution.py:275
  127.6 3.1 %collective-permute-start.8 = (f32[2,1,128,640]{3,2,1,0:T(8,128)}, f32[2,1,128,640]{3,2,1,0:T(8,128)}, u32[]{:S(2)}, u32[]{:S(2)}) collective-permute-start(f32[2,1,128,640]{3,2,1,0:T(8,128)} %get-tuple-element.282), channel_id=1, source_target_pairs={{0,1},{1,2},{2,3},{3,4},{4,5},{5,6},{6,7},{7,8},{8,9},{9,10},{10,1... | collective-permute-start | bytes 1966088 | tf_op jit(solution)/shard_map/ppermute | solution.py:37
  138.4 11.3 %all-to-all-start.2 = ((f32[32,1,2]{2,1,0:T(1,128)}), f32[32,1,2]{2,1,0:T(1,128)S(1)}, u32[]{:S(2)}, u32[]{:S(2)}) async-start(f32[32,1,2]{2,1,0:T(1,128)} %broadcast_in_dim.9), calls=%async_computation.2 | async-start | bytes 32768 | tf_op jit(solution)/shard_map/all_to_all | solution.py:58
  150.8 5.8 %all-to-all-done.2 = f32[32,1,2]{2,1,0:T(1,128)S(1)} async-done(((f32[32,1,2]{2,1,0:T(1,128)}), f32[32,1,2]{2,1,0:T(1,128)S(1)}, u32[]{:S(2)}, u32[]{:S(2)}) %all-to-all-start.2) | async-done | bytes 288 | tf_op jit(solution)/shard_map/all_to_all | solution.py:58
  161.5 2.7 %collective-permute-start.10 = (bf16[2,2,128,640]{3,2,1,0:T(8,128)(2,1)S(1)}, bf16[2,2,128,640]{3,2,1,0:T(8,128)(2,1)}, u32[]{:S(2)}, u32[]{:S(2)}) collective-permute-start(bf16[2,2,128,640]{3,2,1,0:T(8,128)(2,1)S(1)} %get-tuple-element.300), channel_id=1, source_target_pairs={{0,1},{1,2},{2,3},{3,4},{4,5},{5,6},{6,7},{7,8},{8,9},{9,10},{10,1... | collective-permute-start | bytes 1966088 | tf_op jit(solution)/shard_map/ppermute | solution.py:25
  164.2 2.6 %collective-permute-start.11 = (bf16[2,2,128,640]{3,2,1,0:T(8,128)(2,1)S(1)}, bf16[2,2,128,640]{3,2,1,0:T(8,128)(2,1)}, u32[]{:S(2)}, u32[]{:S(2)}) collective-permute-start(bf16[2,2,128,640]{3,2,1,0:T(8,128)(2,1)S(1)} %get-tuple-element.300), channel_id=1, source_target_pairs={{1,0},{2,1},{3,2},{4,3},{5,4},{6,5},{7,6},{8,7},{9,8},{10,9},{11,1... | collective-permute-start | bytes 1966088 | tf_op jit(solution)/shard_map/ppermute | solution.py:27
  167.1 12.6 %all_to_all.32 = f32[32,1,2]{2,1,0:T(1,128)S(1)} all-to-all(f32[32,1,2]{2,1,0:T(1,128)S(1)} %broadcast_in_dim.10), channel_id=1, replica_groups=mesh['freq'=4,'rcv'=32] {'rcv'}, dimensions={0} | all-to-all | bytes 512 | tf_op jit(solution)/shard_map/all_to_all | solution.py:58
  180.5 2.7 %pad_maximum_fusion.1.x_ref = bf16[2,2,128,1920]{3,2,1,0:T(8,128)(2,1)} fusion(bf16[2,2,128,640]{3,2,1,0:T(8,128)(2,1)} %collective-permute-done.11, bf16[2,2,128,640]{3,2,1,0:T(8,128)(2,1)S(1)} %get-tuple-element.300, bf16[2,2,128,640]{3,2,1,0:T(8,128)(2,1)} %collective-permute-done.10), kind=kLoop, calls=%fused_computation.4 | loop fusion | flops 5898240 | bytes 3932160 | tf_op jit(solution)/shard_map/concatenate | solution.py:23
  183.2 11.0 %shard_map.124 = (f32[2,1,128,640]{3,2,1,0:T(8,128)}, f32[2,1,128,640]{3,2,1,0:T(8,128)}, f32[2,1,128,640]{3,2,1,0:T(8,128)}, f32[2,1,128,640]{3,2,1,0:T(8,128)}, f32[1,8,128]{2,1,0:T(8,128)}) custom-call(s32[110]{0:T(128)} %reshape.767.cols_ref, s32[10]{0:T(128)} %reshape.768.counts_ref, f32[4]{0:T(128)} %reshape.770.coef_ref, ...), custom_call_target="tpu_custom_call" | custom-call | flops 1845493760 | bytes 14745600 | tf_op jit(solution)/shard_map/pallas_call | solution.py:275
  195.4 2.7 %collective-permute-start.12 = (f32[2,1,128,640]{3,2,1,0:T(8,128)}, f32[2,1,128,640]{3,2,1,0:T(8,128)S(1)}, u32[]{:S(2)}, u32[]{:S(2)}) collective-permute-start(f32[2,1,128,640]{3,2,1,0:T(8,128)} %get-tuple-element.289), channel_id=1, source_target_pairs={{0,1},{1,2},{2,3},{3,4},{4,5},{5,6},{6,7},{7,8},{8,9},{9,10},{10,1... | collective-permute-start | bytes 1966088 | tf_op jit(solution)/shard_map/ppermute | solution.py:37
  200.2 11.0 %shard_map.125 = (f32[2,1,128,640]{3,2,1,0:T(8,128)}, f32[2,1,128,640]{3,2,1,0:T(8,128)}, f32[2,1,128,640]{3,2,1,0:T(8,128)}, f32[2,1,128,640]{3,2,1,0:T(8,128)}, f32[1,8,128]{2,1,0:T(8,128)}) custom-call(s32[110]{0:T(128)} %reshape.767.cols_ref, s32[10]{0:T(128)} %reshape.768.counts_ref, f32[4]{0:T(128)} %reshape.770.coef_ref, ...), custom_call_target="tpu_custom_call" | custom-call | flops 1845493760 | bytes 14745600 | tf_op jit(solution)/shard_map/pallas_call | solution.py:275
  214.3 6.9 %all-to-all-start.4 = ((f32[32,1,2]{2,1,0:T(1,128)}), f32[32,1,2]{2,1,0:T(1,128)S(1)}, u32[]{:S(2)}, u32[]{:S(2)}) async-start(f32[32,1,2]{2,1,0:T(1,128)} %broadcast_in_dim.11), calls=%async_computation.4 | async-start | bytes 32768 | tf_op jit(solution)/shard_map/all_to_all | solution.py:58
  221.2 3.5 %collective-permute-start.14 = (f32[2,1,128,640]{3,2,1,0:T(8,128)}, f32[2,1,128,640]{3,2,1,0:T(8,128)}, u32[]{:S(2)}, u32[]{:S(2)}) collective-permute-start(f32[2,1,128,640]{3,2,1,0:T(8,128)} %get-tuple-element.292), channel_id=1, source_target_pairs={{0,1},{1,2},{2,3},{3,4},{4,5},{5,6},{6,7},{7,8},{8,9},{9,10},{10,1... | collective-permute-start | bytes 1966088 | tf_op jit(solution)/shard_map/ppermute | solution.py:37
  228.4 4.2 %collective-permute-done.14 = f32[2,1,128,640]{3,2,1,0:T(8,128)} collective-permute-done((f32[2,1,128,640]{3,2,1,0:T(8,128)}, f32[2,1,128,640]{3,2,1,0:T(8,128)}, u32[]{:S(2)}, u32[]{:S(2)}) %collective-permute-start.14) | collective-permute-done | bytes 655392 | tf_op jit(solution)/shard_map/ppermute | solution.py:37
  232.6 4.4 %collective-permute-done.15 = f32[2,1,128,640]{3,2,1,0:T(8,128)} collective-permute-done((f32[2,1,128,640]{3,2,1,0:T(8,128)}, f32[2,1,128,640]{3,2,1,0:T(8,128)}, u32[]{:S(2)}, u32[]{:S(2)}) %collective-permute-start.15) | collective-permute-done | bytes 655392 | tf_op jit(solution)/shard_map/ppermute | solution.py:37
  239.1 2.1 fusion.7
  (103 shorter events, 45.8 us)
Async XLA Ops:
  6.7 13.0 %copy-start.15 = (s32[2,5]{1,0:T(2,128)S(1)}, s32[2,5]{1,0:T(2,128)}, u32[]{:S(2)}) copy-start(s32[2,5]{1,0:T(2,128)} %param.55) | copy-start | bytes 124
  6.7 13.7 %copy-start.14 = (s32[2,5,11]{2,0,1:T(2,128)S(1)}, s32[2,5,11]{2,0,1:T(2,128)}, u32[]{:S(2)}) copy-start(s32[2,5,11]{2,0,1:T(2,128)} %param.54) | copy-start | bytes 1324
  8.3 26.4 %all-to-all-start = ((bf16[2,2,1,128,640]{4,1,0,2,3:T(2,128)(2,1)}), bf16[2,2,1,128,640]{4,1,0,2,3:T(2,128)(2,1)S(1)}, u32[]{:S(2)}, u32[]{:S(2)}) async-start(bf16[2,2,1,128,640]{4,1,0,2,3:T(2,128)(2,1)} %copy.22), calls=%async_computation | async-start | bytes 1310720 | tf_op jit(solution)/shard_map/all_to_all | solution.py:372
  43.2 18.3 %collective-permute-start = (f32[2,1,128,640]{3,2,1,0:T(8,128)}, f32[2,1,128,640]{3,2,1,0:T(8,128)S(1)}, u32[]{:S(2)}, u32[]{:S(2)}) collective-permute-start(f32[2,1,128,640]{3,2,1,0:T(8,128)} %get-tuple-element.269), channel_id=1, source_target_pairs={{0,1},{1,2},{2,3},{3,4},{4,5},{5,6},{6,7},{7,8},{8,9},{9,10},{10,1... | collective-permute-start | bytes 1966088 | tf_op jit(solution)/shard_map/ppermute | solution.py:37
  46.2 15.3 %copy-start.13 = (f32[2,1,128,640]{3,2,1,0:T(8,128)S(1)}, f32[2,1,128,640]{3,2,1,0:T(8,128)}, u32[]{:S(2)}) copy-start(f32[2,1,128,640]{3,2,1,0:T(8,128)} %get-tuple-element.268) | copy-start | bytes 1966084
  46.2 15.3 %collective-permute-start.1 = (f32[2,1,128,640]{3,2,1,0:T(8,128)}, f32[2,1,128,640]{3,2,1,0:T(8,128)S(1)}, u32[]{:S(2)}, u32[]{:S(2)}) collective-permute-start(f32[2,1,128,640]{3,2,1,0:T(8,128)} %get-tuple-element.270), channel_id=1, source_target_pairs={{1,0},{2,1},{3,2},{4,3},{5,4},{6,5},{7,6},{8,7},{9,8},{10,9},{11,1... | collective-permute-start | bytes 1966088 | tf_op jit(solution)/shard_map/ppermute | solution.py:37
  55.9 11.5 %collective-permute-start.2 = (f32[2,1,128,640]{3,2,1,0:T(8,128)}, f32[2,1,128,640]{3,2,1,0:T(8,128)S(1)}, u32[]{:S(2)}, u32[]{:S(2)}) collective-permute-start(f32[2,1,128,640]{3,2,1,0:T(8,128)} %get-tuple-element.272), channel_id=1, source_target_pairs={{0,1},{1,2},{2,3},{3,4},{4,5},{5,6},{6,7},{7,8},{8,9},{9,10},{10,1... | collective-permute-start | bytes 1966088 | tf_op jit(solution)/shard_map/ppermute | solution.py:37
  59.5 12.1 %collective-permute-start.3 = (f32[2,1,128,640]{3,2,1,0:T(8,128)}, f32[2,1,128,640]{3,2,1,0:T(8,128)S(1)}, u32[]{:S(2)}, u32[]{:S(2)}) collective-permute-start(f32[2,1,128,640]{3,2,1,0:T(8,128)} %get-tuple-element.273), channel_id=1, source_target_pairs={{1,0},{2,1},{3,2},{4,3},{5,4},{6,5},{7,6},{8,7},{9,8},{10,9},{11,1... | collective-permute-start | bytes 1966088 | tf_op jit(solution)/shard_map/ppermute | solution.py:37
  61.5 10.2 %copy-start.12 = (f32[2,1,128,640]{3,2,1,0:T(8,128)S(1)}, f32[2,1,128,640]{3,2,1,0:T(8,128)}, u32[]{:S(2)}) copy-start(f32[2,1,128,640]{3,2,1,0:T(8,128)} %get-tuple-element.271) | copy-start | bytes 1966084
  72.1 20.5 %copy-start = (f32[2,2,128,640]{3,2,1,0:T(8,128)}, f32[2,2,128,640]{3,2,1,0:T(8,128)S(1)}, u32[]{:S(2)}) copy-start(f32[2,2,128,640]{3,2,1,0:T(8,128)S(1)} %get-tuple-element.305.q_ref) | copy-start | bytes 3932164
  73.2 17.4 %all-to-all-start.1 = ((f32[32,2,2]{2,1,0:T(2,128)}), f32[32,2,2]{2,1,0:T(2,128)S(1)}, u32[]{:S(2)}, u32[]{:S(2)}) async-start(f32[32,2,2]{2,1,0:T(2,128)} %broadcast_in_dim.8), calls=%async_computation.1 | async-start | bytes 65536 | tf_op jit(solution)/shard_map/all_to_all | solution.py:58
  83.3 11.1 %collective-permute-start.4 = (bf16[2,2,128,640]{3,2,1,0:T(8,128)(2,1)S(1)}, bf16[2,2,128,640]{3,2,1,0:T(8,128)(2,1)S(1)}, u32[]{:S(2)}, u32[]{:S(2)}) collective-permute-start(bf16[2,2,128,640]{3,2,1,0:T(8,128)(2,1)S(1)} %get-tuple-element.304), channel_id=1, source_target_pairs={{0,1},{1,2},{2,3},{3,4},{4,5},{5,6},{6,7},{7,8},{8,9},{9,10},{10,1... | collective-permute-start | bytes 1966088 | tf_op jit(solution)/shard_map/ppermute | solution.py:25
  86.8 12.0 %collective-permute-start.5 = (bf16[2,2,128,640]{3,2,1,0:T(8,128)(2,1)S(1)}, bf16[2,2,128,640]{3,2,1,0:T(8,128)(2,1)}, u32[]{:S(2)}, u32[]{:S(2)}) collective-permute-start(bf16[2,2,128,640]{3,2,1,0:T(8,128)(2,1)S(1)} %get-tuple-element.304), channel_id=1, source_target_pairs={{1,0},{2,1},{3,2},{4,3},{5,4},{6,5},{7,6},{8,7},{9,8},{10,9},{11,1... | collective-permute-start | bytes 1966088 | tf_op jit(solution)/shard_map/ppermute | solution.py:27
  112.3 44.4 %collective-permute-start.6 = (f32[2,1,128,640]{3,2,1,0:T(8,128)}, f32[2,1,128,640]{3,2,1,0:T(8,128)S(1)}, u32[]{:S(2)}, u32[]{:S(2)}) collective-permute-start(f32[2,1,128,640]{3,2,1,0:T(8,128)} %get-tuple-element.279), channel_id=1, source_target_pairs={{0,1},{1,2},{2,3},{3,4},{4,5},{5,6},{6,7},{7,8},{8,9},{9,10},{10,1... | collective-permute-start | bytes 1966088 | tf_op jit(solution)/shard_map/ppermute | solution.py:37
  114.2 42.5 %collective-permute-start.7 = (f32[2,1,128,640]{3,2,1,0:T(8,128)}, f32[2,1,128,640]{3,2,1,0:T(8,128)S(1)}, u32[]{:S(2)}, u32[]{:S(2)}) collective-permute-start(f32[2,1,128,640]{3,2,1,0:T(8,128)} %get-tuple-element.280), channel_id=1, source_target_pairs={{1,0},{2,1},{3,2},{4,3},{5,4},{6,5},{7,6},{8,7},{9,8},{10,9},{11,1... | collective-permute-start | bytes 1966088 | tf_op jit(solution)/shard_map/ppermute | solution.py:37
  127.6 29.3 %collective-permute-start.8 = (f32[2,1,128,640]{3,2,1,0:T(8,128)}, f32[2,1,128,640]{3,2,1,0:T(8,128)}, u32[]{:S(2)}, u32[]{:S(2)}) collective-permute-start(f32[2,1,128,640]{3,2,1,0:T(8,128)} %get-tuple-element.282), channel_id=1, source_target_pairs={{0,1},{1,2},{2,3},{3,4},{4,5},{5,6},{6,7},{7,8},{8,9},{9,10},{10,1... | collective-permute-start | bytes 1966088 | tf_op jit(solution)/shard_map/ppermute | solution.py:37
  130.7 26.2 %collective-permute-start.9 = (f32[2,1,128,640]{3,2,1,0:T(8,128)}, f32[2,1,128,640]{3,2,1,0:T(8,128)}, u32[]{:S(2)}, u32[]{:S(2)}) collective-permute-start(f32[2,1,128,640]{3,2,1,0:T(8,128)} %get-tuple-element.283), channel_id=1, source_target_pairs={{1,0},{2,1},{3,2},{4,3},{5,4},{6,5},{7,6},{8,7},{9,8},{10,9},{11,1... | collective-permute-start | bytes 1966088 | tf_op jit(solution)/shard_map/ppermute | solution.py:37
  135.2 21.6 %copy-start.10 = (f32[2,1,128,640]{3,2,1,0:T(8,128)S(1)}, f32[2,1,128,640]{3,2,1,0:T(8,128)}, u32[]{:S(2)}) copy-start(f32[2,1,128,640]{3,2,1,0:T(8,128)} %get-tuple-element.278) | copy-start | bytes 1966084
  138.4 18.3 %all-to-all-start.2 = ((f32[32,1,2]{2,1,0:T(1,128)}), f32[32,1,2]{2,1,0:T(1,128)S(1)}, u32[]{:S(2)}, u32[]{:S(2)}) async-start(f32[32,1,2]{2,1,0:T(1,128)} %broadcast_in_dim.9), calls=%async_computation.2 | async-start | bytes 32768 | tf_op jit(solution)/shard_map/all_to_all | solution.py:58
  150.8 6.1 %copy-start.4 = (f32[2,2,128,640]{3,2,1,0:T(8,128)}, f32[2,2,128,640]{3,2,1,0:T(8,128)S(1)}, u32[]{:S(2)}) copy-start(f32[2,2,128,640]{3,2,1,0:T(8,128)S(1)} %constant_dynamic-update-slice_fusion) | copy-start | bytes 3932164
  157.8 2.1 copy-start.5
  161.5 21.7 %copy-start.2 = (f32[2,2,128,640]{3,2,1,0:T(8,128)}, f32[2,2,128,640]{3,2,1,0:T(8,128)S(1)}, u32[]{:S(2)}) copy-start(f32[2,2,128,640]{3,2,1,0:T(8,128)S(1)} %get-tuple-element.301.q_ref) | copy-start | bytes 3932164
  161.5 19.0 %collective-permute-start.10 = (bf16[2,2,128,640]{3,2,1,0:T(8,128)(2,1)S(1)}, bf16[2,2,128,640]{3,2,1,0:T(8,128)(2,1)}, u32[]{:S(2)}, u32[]{:S(2)}) collective-permute-start(bf16[2,2,128,640]{3,2,1,0:T(8,128)(2,1)S(1)} %get-tuple-element.300), channel_id=1, source_target_pairs={{0,1},{1,2},{2,3},{3,4},{4,5},{5,6},{6,7},{7,8},{8,9},{9,10},{10,1... | collective-permute-start | bytes 1966088 | tf_op jit(solution)/shard_map/ppermute | solution.py:25
  164.2 16.3 %collective-permute-start.11 = (bf16[2,2,128,640]{3,2,1,0:T(8,128)(2,1)S(1)}, bf16[2,2,128,640]{3,2,1,0:T(8,128)(2,1)}, u32[]{:S(2)}, u32[]{:S(2)}) collective-permute-start(bf16[2,2,128,640]{3,2,1,0:T(8,128)(2,1)S(1)} %get-tuple-element.300), channel_id=1, source_target_pairs={{1,0},{2,1},{3,2},{4,3},{5,4},{6,5},{7,6},{8,7},{9,8},{10,9},{11,1... | collective-permute-start | bytes 1966088 | tf_op jit(solution)/shard_map/ppermute | solution.py:27
  195.4 32.9 %collective-permute-start.12 = (f32[2,1,128,640]{3,2,1,0:T(8,128)}, f32[2,1,128,640]{3,2,1,0:T(8,128)S(1)}, u32[]{:S(2)}, u32[]{:S(2)}) collective-permute-start(f32[2,1,128,640]{3,2,1,0:T(8,128)} %get-tuple-element.289), channel_id=1, source_target_pairs={{0,1},{1,2},{2,3},{3,4},{4,5},{5,6},{6,7},{7,8},{8,9},{9,10},{10,1... | collective-permute-start | bytes 1966088 | tf_op jit(solution)/shard_map/ppermute | solution.py:37
  198.1 30.1 %copy-start.8 = (f32[2,1,128,640]{3,2,1,0:T(8,128)S(1)}, f32[2,1,128,640]{3,2,1,0:T(8,128)}, u32[]{:S(2)}) copy-start(f32[2,1,128,640]{3,2,1,0:T(8,128)} %get-tuple-element.288) | copy-start | bytes 1966084
  198.1 30.1 %collective-permute-start.13 = (f32[2,1,128,640]{3,2,1,0:T(8,128)}, f32[2,1,128,640]{3,2,1,0:T(8,128)S(1)}, u32[]{:S(2)}, u32[]{:S(2)}) collective-permute-start(f32[2,1,128,640]{3,2,1,0:T(8,128)} %get-tuple-element.290), channel_id=1, source_target_pairs={{1,0},{2,1},{3,2},{4,3},{5,4},{6,5},{7,6},{8,7},{9,8},{10,9},{11,1... | collective-permute-start | bytes 1966088 | tf_op jit(solution)/shard_map/ppermute | solution.py:37
  214.3 13.8 %all-to-all-start.4 = ((f32[32,1,2]{2,1,0:T(1,128)}), f32[32,1,2]{2,1,0:T(1,128)S(1)}, u32[]{:S(2)}, u32[]{:S(2)}) async-start(f32[32,1,2]{2,1,0:T(1,128)} %broadcast_in_dim.11), calls=%async_computation.4 | async-start | bytes 32768 | tf_op jit(solution)/shard_map/all_to_all | solution.py:58
  221.2 11.4 %collective-permute-start.14 = (f32[2,1,128,640]{3,2,1,0:T(8,128)}, f32[2,1,128,640]{3,2,1,0:T(8,128)}, u32[]{:S(2)}, u32[]{:S(2)}) collective-permute-start(f32[2,1,128,640]{3,2,1,0:T(8,128)} %get-tuple-element.292), channel_id=1, source_target_pairs={{0,1},{1,2},{2,3},{3,4},{4,5},{5,6},{6,7},{7,8},{8,9},{9,10},{10,1... | collective-permute-start | bytes 1966088 | tf_op jit(solution)/shard_map/ppermute | solution.py:37
  224.8 12.2 %collective-permute-start.15 = (f32[2,1,128,640]{3,2,1,0:T(8,128)}, f32[2,1,128,640]{3,2,1,0:T(8,128)}, u32[]{:S(2)}, u32[]{:S(2)}) collective-permute-start(f32[2,1,128,640]{3,2,1,0:T(8,128)} %get-tuple-element.293), channel_id=1, source_target_pairs={{1,0},{2,1},{3,2},{4,3},{5,4},{6,5},{7,6},{8,7},{9,8},{10,9},{11,1... | collective-permute-start | bytes 1966088 | tf_op jit(solution)/shard_map/ppermute | solution.py:37
  228.3 8.7 %copy-start.9 = (f32[2,1,128,640]{3,2,1,0:T(8,128)S(1)}, f32[2,1,128,640]{3,2,1,0:T(8,128)}, u32[]{:S(2)}) copy-start(f32[2,1,128,640]{3,2,1,0:T(8,128)} %get-tuple-element.291) | copy-start | bytes 1966084
  237.0 2.1 copy-start.7
  (4 other events, 6.4 us)

commit v14 on v10

--- a/solution.py
+++ b/solution.py
@@ -184,6 +184,7 @@
     lower_ref,
     middle_ref,
     upper_ref,
+    squares_ref,
     picked_ref,
     acc_ref,
 ):
@@ -198,6 +199,7 @@
     @pl.when(row == 0)
     def _():
         acc_ref[...] = jnp.zeros(acc_ref.shape, acc_ref.dtype)
+        squares_ref[...] = jnp.zeros(squares_ref.shape, squares_ref.dtype)
 
     rim_blocks = below_ref.shape[-1] // block
     own_blocks = own_ref.shape[-1] // block
@@ -226,6 +228,8 @@
     for part in range(2):
         lanes = slice(part * block, (part + 1) * block)
         p_ref[part] = (q_ref[part] + product[:, lanes]) / scale - shift * u_ref[part]
+    total = jnp.sum(p_ref[0] * p_ref[0] + p_ref[1] * p_ref[1], axis=(0, 1), keepdims=True)
+    squares_ref[...] += jnp.broadcast_to(total, squares_ref.shape)
     field = jnp.concatenate(
         [p_ref[0].astype(jnp.bfloat16), p_ref[1].astype(jnp.bfloat16)], axis=1
     )
@@ -267,7 +271,13 @@
             own,
             pl.BlockSpec((None, None, depth, width), lambda f, r, c, n: (f, r, 0, 0)),
         ],
-        out_specs=[own, part_spec(rim), part_spec(own_rows), part_spec(rim)],
+        out_specs=[
+            own,
+            part_spec(rim),
+            part_spec(own_rows),
+            part_spec(rim),
+            pl.BlockSpec((None, 8, 128), lambda f, r, c, n: (f, 0, 0)),
+        ],
         scratch_shapes=[
             pltpu.VMEM((sources, width), jnp.bfloat16),
             pltpu.VMEM((2, sources, span), jnp.float32),
@@ -281,6 +291,7 @@
             part_shape(rim),
             part_shape(own_rows),
             part_shape(rim),
+            jax.ShapeDtypeStruct((local_freqs, 8, 128), jnp.float32),
         ],
         compiler_params=pltpu.CompilerParams(dimension_semantics=("arbitrary", "arbitrary")),
         cost_estimate=pl.CostEstimate(
@@ -394,10 +405,11 @@
         coefs = jnp.stack(
             [jnp.broadcast_to(scale, shift.shape).reshape(-1), shift.reshape(-1)], axis=1
         ).reshape(-1)
-        residual, *parts = apply_both(
+        residual, lower, middle, upper, partial = apply_both(
             below, rounded, above, raw, left, coefs, stacked, columns, counts
         )
-        return residual, residual + exchange(*parts)
+        total = rcv_sum(partial[:, 0, 0])[None, :, None, None]
+        return residual, residual + exchange(lower, middle, upper), total
 
     def forward(field):
         extended = with_halo(field.astype(jnp.bfloat16), (("rcv", 3),), rim_rows)
@@ -417,8 +429,10 @@
     rhobar = alpha_norm
     for iteration in range(ITERS):
         last = iteration == ITERS - 1
-        residual_left, lifted = forward_adjoint(right_raw, right_scale, left_vector, alpha_norm)
-        beta_norm = jnp.sqrt(squares(residual_left) + EPSILON)
+        residual_left, lifted, left_squares = forward_adjoint(
+            right_raw, right_scale, left_vector, alpha_norm
+        )
+        beta_norm = jnp.sqrt(left_squares + EPSILON)
         left_vector = residual_left / beta_norm
         residual_right = lifted / beta_norm - beta_norm * right_vector
         rho_value = jnp.sqrt(rhobar * rhobar + beta_norm * beta_norm)

time: 226 us -> 225 us (level)
  other arithmetic: 16.1 us -> 12.9 us
    reduce_sum x3 -> x1, other arithmetic: 3.43 us -> 0.27 us  [squares(): return rcv_sum(jnp.sum(field * field, axis=(0, 2, 3)))[None, :, None, None]]
  transfers between devices with their start and end apart: 13 -> 13, of which waited for: 7 -> 7; matrix products, arithmetic and copies ran while one was open for 4% -> 3% of each run, Pallas kernels for 5% -> 5%
where the time goes in v14:
time: 225 us; the launch traced here: 224 us
  Pallas kernels  66.8 us (30%)
  starting transfers between devices  58.3 us (26%)
  waiting for transfers between devices  35.6 us (16%)
  blocking collectives  34.3 us (15%)
  other arithmetic  12.9 us (6%)
  local copies, waits for them, and re-layouts  9.69 us (4%)
  matrix products  5.45 us (2%)
    pallas_call x2, Pallas kernels, apply_both(): pl.pallas_call(_both_kernel, grid_spec=grid_spec, out_shape=[jax.ShapeDty...  42.3 us
    all_to_all x2, blocking collectives, rcv_sum(): gathered = lax.all_to_all(spread, 'rcv', 0, 0, tiled=False)  34.3 us
    ppermute x10, starting transfers between devices, from_behind(): lax.ppermute(value, axis, [(source, source + steps) for source in range(f...  27.2 us
    ppermute x10, waiting for transfers between devices, from_behind(): lax.ppermute(value, axis, [(source, source + steps) for source in range(f...  21 us
    all_to_all x2, starting transfers between devices, rcv_sum(): gathered = lax.all_to_all(spread, 'rcv', 0, 0, tiled=False)  19.6 us
    pallas_call x1, Pallas kernels, apply_adjoint(): pl.pallas_call(_adjoint_kernel, grid_spec=grid_spec, out_shape=[part_shap...  12.9 us
    all_to_all x2, waiting for transfers between devices, rcv_sum(): gathered = lax.all_to_all(spread, 'rcv', 0, 0, tiled=False)  12.6 us
    pallas_call x1, Pallas kernels, stack_blocks(): pl.pallas_call(_stack_kernel, grid_spec=grid_spec, out_shape=jax.ShapeDty...  11.6 us
  transfers between devices with their start and end apart: 13, of which 7 were waited for; matrix products, arithmetic and copies ran while one was open for 3% of the time, Pallas kernels for 5%

profile of v14, /device:TPU:1, one launch (start us, length us, event | category | flops | bytes accessed | tf_op | source)
XLA Modules:
  0.0 224.0 jit_solution(16550239216509271192)
XLA Ops:
  0.8 5.5 %fusion = bf16[2,2,1,4,20480]{4,3,1,0,2:T(4,128)(2,1)S(1)} fusion(bf16[1,256,20480]{2,1,0:T(8,128)(2,1)} %param.28, bf16[256,1,4,2]{0,2,3,1:T(4,128)(2,1)S(1)} %get-tuple-element.172, bf16[256,1,4,2]{0,2,3,1:T(4,128)(2,1)S(1)} %get-tuple-element.171), kind=kOutput, calls=%fused_computation.1 | convolution fusion | flops 168116224 | bytes 11149312 | tf_op jit(solution)/shard_map/snr,ncgf->cfsgr/dot_general | solution.py:374
  6.8 1.5 copy.22
  8.3 11.5 %all-to-all-start = ((bf16[2,2,1,128,640]{4,1,0,2,3:T(2,128)(2,1)}), bf16[2,2,1,128,640]{4,1,0,2,3:T(2,128)(2,1)S(1)}, u32[]{:S(2)}, u32[]{:S(2)}) async-start(bf16[2,2,1,128,640]{4,1,0,2,3:T(2,128)(2,1)} %copy.22), calls=%async_computation | async-start | bytes 1310720 | tf_op jit(solution)/shard_map/all_to_all | solution.py:380
  21.0 11.6 %shard_map.89.m_ref = bf16[2,5,256,2816]{3,2,1,0:T(8,128)(2,1)} custom-call(s32[10]{0:T(128)} %reshape.550.counts_ref, bf16[2,5,11,2,128,128]{5,4,3,2,1,0:T(8,128)(2,1)} %a_ref.1), custom_call_target="tpu_custom_call" | custom-call | tf_op jit(solution)/shard_map/pallas_call | solution.py:104
  32.6 2.0 all-to-all-done
  35.6 12.9 %shard_map.90 = (f32[2,2,128,640]{3,2,1,0:T(8,128)}, f32[2,2,128,640]{3,2,1,0:T(8,128)}, f32[2,2,128,640]{3,2,1,0:T(8,128)}) custom-call(s32[110]{0:T(128)} %reshape.549.cols_ref, s32[10]{0:T(128)} %reshape.550.counts_ref, bf16[2,2,128,640]{3,2,1,0:T(8,128)(2,1)} %bitcast.53, bf16[2,5,256,2816]{3,2,1,0:T(8,128)(2,1)} %shard_map.89.m_ref), custom_call_target="tpu_custom_call" | custom-call | flops 1845493760 | bytes 19005440 | tf_op jit(solution)/shard_map/pallas_call | solution.py:351
  48.5 3.0 %collective-permute-start = (f32[2,2,128,640]{3,2,1,0:T(8,128)}, f32[2,2,128,640]{3,2,1,0:T(8,128)S(1)}, u32[]{:S(2)}, u32[]{:S(2)}) collective-permute-start(f32[2,2,128,640]{3,2,1,0:T(8,128)} %get-tuple-element.136), channel_id=1, source_target_pairs={{0,1},{1,2},{2,3},{3,4},{4,5},{5,6},{6,7},{7,8},{8,9},{9,10},{10,1... | collective-permute-start | bytes 3932168 | tf_op jit(solution)/shard_map/ppermute | solution.py:36
  51.5 1.9 collective-permute-start.1
  53.4 12.9 %collective-permute-done = f32[2,2,128,640]{3,2,1,0:T(8,128)S(1)} collective-permute-done((f32[2,2,128,640]{3,2,1,0:T(8,128)}, f32[2,2,128,640]{3,2,1,0:T(8,128)S(1)}, u32[]{:S(2)}, u32[]{:S(2)}) %collective-permute-start) | collective-permute-done | bytes 1310752 | tf_op jit(solution)/shard_map/ppermute | solution.py:36
  66.3 4.3 %collective-permute-done.1 = f32[2,2,128,640]{3,2,1,0:T(8,128)S(1)} collective-permute-done((f32[2,2,128,640]{3,2,1,0:T(8,128)}, f32[2,2,128,640]{3,2,1,0:T(8,128)S(1)}, u32[]{:S(2)}, u32[]{:S(2)}) %collective-permute-start.1) | collective-permute-done | bytes 1310752 | tf_op jit(solution)/shard_map/ppermute | solution.py:36
  70.6 2.0 fusion.17
  73.8 8.0 %all-to-all-start.1 = ((f32[32,2,2]{2,1,0:T(2,128)}), f32[32,2,2]{2,1,0:T(2,128)S(1)}, u32[]{:S(2)}, u32[]{:S(2)}) async-start(f32[32,2,2]{2,1,0:T(2,128)} %broadcast_in_dim.12), calls=%async_computation.1 | async-start | bytes 65536 | tf_op jit(solution)/shard_map/all_to_all | solution.py:57
  81.8 2.1 collective-permute-start.3
  84.0 3.4 %collective-permute-start.2 = (bf16[2,2,128,640]{3,2,1,0:T(8,128)(2,1)S(1)}, bf16[2,2,128,640]{3,2,1,0:T(8,128)(2,1)}, u32[]{:S(2)}, u32[]{:S(2)}) collective-permute-start(bf16[2,2,128,640]{3,2,1,0:T(8,128)(2,1)S(1)} %get-tuple-element.158.own_ref), channel_id=1, source_target_pairs={{0,1},{1,2},{2,3},{3,4},{4,5},{5,6},{6,7},{7,8},{8,9},{9,10},{10,1... | collective-permute-start | bytes 1966088 | tf_op jit(solution)/shard_map/ppermute | solution.py:36
  87.4 1.7 all-to-all-done.1
  89.9 1.2 convert_divide_fusion.u_ref
  91.1 2.9 %collective-permute-done.3.above_ref = bf16[2,2,128,640]{3,2,1,0:T(8,128)(2,1)} collective-permute-done((bf16[2,2,128,640]{3,2,1,0:T(8,128)(2,1)S(1)}, bf16[2,2,128,640]{3,2,1,0:T(8,128)(2,1)}, u32[]{:S(2)}, u32[]{:S(2)}) %collective-permute-start.3) | collective-permute-done | bytes 655392 | tf_op jit(solution)/shard_map/ppermute | solution.py:36
  94.9 21.2 %shard_map.91 = (f32[2,2,128,640]{3,2,1,0:T(8,128)}, f32[2,2,128,640]{3,2,1,0:T(8,128)}, f32[2,2,128,640]{3,2,1,0:T(8,128)}, f32[2,2,128,640]{3,2,1,0:T(8,128)}, f32[2,8,128]{2,1,0:T(8,128)}) custom-call(s32[110]{0:T(128)} %reshape.549.cols_ref, s32[10]{0:T(128)} %reshape.550.counts_ref, f32[4]{0:T(128)} %reshape.551.coef_ref, ...), custom_call_target="tpu_custom_call" | custom-call | flops 3690987520 | bytes 29491200 | tf_op jit(solution)/shard_map/pallas_call | solution.py:286
  116.1 4.5 %collective-permute-start.4 = (f32[2,2,128,640]{3,2,1,0:T(8,128)}, f32[2,2,128,640]{3,2,1,0:T(8,128)S(1)}, u32[]{:S(2)}, u32[]{:S(2)}) collective-permute-start(f32[2,2,128,640]{3,2,1,0:T(8,128)} %get-tuple-element.141), channel_id=1, source_target_pairs={{0,1},{1,2},{2,3},{3,4},{4,5},{5,6},{6,7},{7,8},{8,9},{9,10},{10,1... | collective-permute-start | bytes 3932168 | tf_op jit(solution)/shard_map/ppermute | solution.py:36
  120.6 1.9 collective-permute-start.5
  123.9 11.6 %all-to-all-start.2 = ((f32[32,1,2]{2,1,0:T(1,128)}), f32[32,1,2]{2,1,0:T(1,128)S(1)}, u32[]{:S(2)}, u32[]{:S(2)}) async-start(f32[32,1,2]{2,1,0:T(1,128)} %broadcast_in_dim.14), calls=%async_computation.2 | async-start | bytes 32768 | tf_op jit(solution)/shard_map/all_to_all | solution.py:57
  135.6 10.9 %all-to-all-done.2 = f32[32,1,2]{2,1,0:T(1,128)S(1)} async-done(((f32[32,1,2]{2,1,0:T(1,128)}), f32[32,1,2]{2,1,0:T(1,128)S(1)}, u32[]{:S(2)}, u32[]{:S(2)}) %all-to-all-start.2) | async-done | bytes 288 | tf_op jit(solution)/shard_map/all_to_all | solution.py:57
  146.5 1.0 copy-done.5
  147.6 4.0 %fusion.16 = (bf16[2,2,128,640]{3,2,1,0:T(8,128)(2,1)S(1)}, f32[2,2,128,640]{3,2,1,0:T(8,128)S(1)}, f32[2,2,128,640]{3,2,1,0:T(8,128)}) fusion(f32[2,2,128,640]{3,2,1,0:T(8,128)S(1)} %copy-done.1, f32[2]{0:T(128)S(1)} %get-tuple-element.156, f32[2]{0:T(128)S(1)} %add_sqrt_fusion.4, f32[2,2,128,640]{3,2,1,0:T(8,128)} %get-tuple-element.139, ...), kind=kLoop, calls=%fused_computation.58 | loop fusion | flops 2949120 | bytes 9830416 | tf_op jit(solution)/shard_map/convert_element_type | solution.py:402
  151.6 2.6 %collective-permute-start.7 = (bf16[2,2,128,640]{3,2,1,0:T(8,128)(2,1)S(1)}, bf16[2,2,128,640]{3,2,1,0:T(8,128)(2,1)}, u32[]{:S(2)}, u32[]{:S(2)}) collective-permute-start(bf16[2,2,128,640]{3,2,1,0:T(8,128)(2,1)S(1)} %get-tuple-element.154.own_ref), channel_id=1, source_target_pairs={{1,0},{2,1},{3,2},{4,3},{5,4},{6,5},{7,6},{8,7},{9,8},{10,9},{11,1... | collective-permute-start | bytes 1966088 | tf_op jit(solution)/shard_map/ppermute | solution.py:36
  154.1 3.1 %collective-permute-start.6 = (bf16[2,2,128,640]{3,2,1,0:T(8,128)(2,1)S(1)}, bf16[2,2,128,640]{3,2,1,0:T(8,128)(2,1)}, u32[]{:S(2)}, u32[]{:S(2)}) collective-permute-start(bf16[2,2,128,640]{3,2,1,0:T(8,128)(2,1)S(1)} %get-tuple-element.154.own_ref), channel_id=1, source_target_pairs={{0,1},{1,2},{2,3},{3,4},{4,5},{5,6},{6,7},{7,8},{8,9},{9,10},{10,1... | collective-permute-start | bytes 1966088 | tf_op jit(solution)/shard_map/ppermute | solution.py:36
  157.5 15.6 %all_to_all.32 = f32[32,1,2]{2,1,0:T(1,128)S(1)} all-to-all(f32[32,1,2]{2,1,0:T(1,128)S(1)} %broadcast_in_dim.15), channel_id=1, replica_groups=mesh['freq'=4,'rcv'=32] {'rcv'}, dimensions={0} | all-to-all | bytes 512 | tf_op jit(solution)/shard_map/all_to_all | solution.py:57
  173.8 21.2 %shard_map.92 = (f32[2,2,128,640]{3,2,1,0:T(8,128)}, f32[2,2,128,640]{3,2,1,0:T(8,128)}, f32[2,2,128,640]{3,2,1,0:T(8,128)}, f32[2,2,128,640]{3,2,1,0:T(8,128)}, f32[2,8,128]{2,1,0:T(8,128)}) custom-call(s32[110]{0:T(128)} %reshape.549.cols_ref, s32[10]{0:T(128)} %reshape.550.counts_ref, f32[4]{0:T(128)} %reshape.552.coef_ref, ...), custom_call_target="tpu_custom_call" | custom-call | flops 3690987520 | bytes 29491200 | tf_op jit(solution)/shard_map/pallas_call | solution.py:286
  195.0 2.8 %collective-permute-start.8 = (f32[2,2,128,640]{3,2,1,0:T(8,128)}, f32[2,2,128,640]{3,2,1,0:T(8,128)S(1)}, u32[]{:S(2)}, u32[]{:S(2)}) collective-permute-start(f32[2,2,128,640]{3,2,1,0:T(8,128)} %get-tuple-element.146), channel_id=1, source_target_pairs={{0,1},{1,2},{2,3},{3,4},{4,5},{5,6},{6,7},{7,8},{8,9},{9,10},{10,1... | collective-permute-start | bytes 3932168 | tf_op jit(solution)/shard_map/ppermute | solution.py:36
  197.7 1.9 collective-permute-start.9
  200.5 18.7 %all_to_all.33 = f32[32,1,2]{2,1,0:T(1,128)S(1)} all-to-all(f32[32,1,2]{2,1,0:T(1,128)S(1)} %broadcast_in_dim.34), channel_id=1, replica_groups=mesh['freq'=4,'rcv'=32] {'rcv'}, dimensions={0} | all-to-all | bytes 512 | tf_op jit(solution)/shard_map/all_to_all | solution.py:57
  219.3 4.7 %subtract_multiply_fusion = (f32[2,2,128,640]{3,2,1,0:T(8,128)}, f32[2,2,128,640]{3,2,1,0:T(8,128)}) fusion(f32[2,2,128,640]{3,2,1,0:T(8,128)} %get-tuple-element.144, f32[2,2,128,640]{3,2,1,0:T(8,128)} %collective-permute-done.9, f32[2,2,128,640]{3,2,1,0:T(8,128)} %get-tuple-element.145, f32[2,2,128,640]{3,2,1,0:T(8,128)S(1)} %collective-permute-done.8, ...), kind=kLoop, calls=%fused_computation.7 | loop fusion | flops 4587520 | bytes 10485816 | tf_op jit(solution)/shard_map/mul | solution.py:453
  (57 shorter events, 9.2 us)
Async XLA Ops:
  6.7 13.0 %copy-start.7 = (s32[2,5]{1,0:T(2,128)S(1)}, s32[2,5]{1,0:T(2,128)}, u32[]{:S(2)}) copy-start(s32[2,5]{1,0:T(2,128)} %param.31) | copy-start | bytes 124
  6.7 13.6 %copy-start.6 = (s32[2,5,11]{2,0,1:T(2,128)S(1)}, s32[2,5,11]{2,0,1:T(2,128)}, u32[]{:S(2)}) copy-start(s32[2,5,11]{2,0,1:T(2,128)} %param.30) | copy-start | bytes 1324
  8.3 26.4 %all-to-all-start = ((bf16[2,2,1,128,640]{4,1,0,2,3:T(2,128)(2,1)}), bf16[2,2,1,128,640]{4,1,0,2,3:T(2,128)(2,1)S(1)}, u32[]{:S(2)}, u32[]{:S(2)}) async-start(bf16[2,2,1,128,640]{4,1,0,2,3:T(2,128)(2,1)} %copy.22), calls=%async_computation | async-start | bytes 1310720 | tf_op jit(solution)/shard_map/all_to_all | solution.py:380
  48.5 17.9 %collective-permute-start = (f32[2,2,128,640]{3,2,1,0:T(8,128)}, f32[2,2,128,640]{3,2,1,0:T(8,128)S(1)}, u32[]{:S(2)}, u32[]{:S(2)}) collective-permute-start(f32[2,2,128,640]{3,2,1,0:T(8,128)} %get-tuple-element.136), channel_id=1, source_target_pairs={{0,1},{1,2},{2,3},{3,4},{4,5},{5,6},{6,7},{7,8},{8,9},{9,10},{10,1... | collective-permute-start | bytes 3932168 | tf_op jit(solution)/shard_map/ppermute | solution.py:36
  51.5 19.1 %collective-permute-start.1 = (f32[2,2,128,640]{3,2,1,0:T(8,128)}, f32[2,2,128,640]{3,2,1,0:T(8,128)S(1)}, u32[]{:S(2)}, u32[]{:S(2)}) collective-permute-start(f32[2,2,128,640]{3,2,1,0:T(8,128)} %get-tuple-element.137), channel_id=1, source_target_pairs={{1,0},{2,1},{3,2},{4,3},{5,4},{6,5},{7,6},{8,7},{9,8},{10,9},{11,1... | collective-permute-start | bytes 3932168 | tf_op jit(solution)/shard_map/ppermute | solution.py:36
  72.6 18.5 %copy-start = (f32[2,2,128,640]{3,2,1,0:T(8,128)}, f32[2,2,128,640]{3,2,1,0:T(8,128)S(1)}, u32[]{:S(2)}) copy-start(f32[2,2,128,640]{3,2,1,0:T(8,128)S(1)} %get-tuple-element.159.q_ref) | copy-start | bytes 3932164
  72.6 18.5 %copy-start.4 = (bf16[2,2,128,640]{3,2,1,0:T(8,128)(2,1)}, bf16[2,2,128,640]{3,2,1,0:T(8,128)(2,1)S(1)}, u32[]{:S(2)}) copy-start(bf16[2,2,128,640]{3,2,1,0:T(8,128)(2,1)S(1)} %get-tuple-element.158.own_ref) | copy-start | bytes 1966084
  73.8 15.3 %all-to-all-start.1 = ((f32[32,2,2]{2,1,0:T(2,128)}), f32[32,2,2]{2,1,0:T(2,128)S(1)}, u32[]{:S(2)}, u32[]{:S(2)}) async-start(f32[32,2,2]{2,1,0:T(2,128)} %broadcast_in_dim.12), calls=%async_computation.1 | async-start | bytes 65536 | tf_op jit(solution)/shard_map/all_to_all | solution.py:57
  81.8 12.1 %collective-permute-start.3 = (bf16[2,2,128,640]{3,2,1,0:T(8,128)(2,1)S(1)}, bf16[2,2,128,640]{3,2,1,0:T(8,128)(2,1)}, u32[]{:S(2)}, u32[]{:S(2)}) collective-permute-start(bf16[2,2,128,640]{3,2,1,0:T(8,128)(2,1)S(1)} %get-tuple-element.158.own_ref), channel_id=1, source_target_pairs={{1,0},{2,1},{3,2},{4,3},{5,4},{6,5},{7,6},{8,7},{9,8},{10,9},{11,1... | collective-permute-start | bytes 1966088 | tf_op jit(solution)/shard_map/ppermute | solution.py:36
  84.0 10.9 %collective-permute-start.2 = (bf16[2,2,128,640]{3,2,1,0:T(8,128)(2,1)S(1)}, bf16[2,2,128,640]{3,2,1,0:T(8,128)(2,1)}, u32[]{:S(2)}, u32[]{:S(2)}) collective-permute-start(bf16[2,2,128,640]{3,2,1,0:T(8,128)(2,1)S(1)} %get-tuple-element.158.own_ref), channel_id=1, source_target_pairs={{0,1},{1,2},{2,3},{3,4},{4,5},{5,6},{6,7},{7,8},{8,9},{9,10},{10,1... | collective-permute-start | bytes 1966088 | tf_op jit(solution)/shard_map/ppermute | solution.py:36
  94.0 53.6 %copy-start.1 = (f32[2,2,128,640]{3,2,1,0:T(8,128)S(1)}, f32[2,2,128,640]{3,2,1,0:T(8,128)}, u32[]{:S(2)}) copy-start(f32[2,2,128,640]{3,2,1,0:T(8,128)} %copy-done) | copy-start | bytes 3932164
  116.1 30.4 %collective-permute-start.4 = (f32[2,2,128,640]{3,2,1,0:T(8,128)}, f32[2,2,128,640]{3,2,1,0:T(8,128)S(1)}, u32[]{:S(2)}, u32[]{:S(2)}) collective-permute-start(f32[2,2,128,640]{3,2,1,0:T(8,128)} %get-tuple-element.141), channel_id=1, source_target_pairs={{0,1},{1,2},{2,3},{3,4},{4,5},{5,6},{6,7},{7,8},{8,9},{9,10},{10,1... | collective-permute-start | bytes 3932168 | tf_op jit(solution)/shard_map/ppermute | solution.py:36
  120.6 25.9 %collective-permute-start.5 = (f32[2,2,128,640]{3,2,1,0:T(8,128)}, f32[2,2,128,640]{3,2,1,0:T(8,128)}, u32[]{:S(2)}, u32[]{:S(2)}) collective-permute-start(f32[2,2,128,640]{3,2,1,0:T(8,128)} %get-tuple-element.142), channel_id=1, source_target_pairs={{1,0},{2,1},{3,2},{4,3},{5,4},{6,5},{7,6},{8,7},{9,8},{10,9},{11,1... | collective-permute-start | bytes 3932168 | tf_op jit(solution)/shard_map/ppermute | solution.py:36
  123.9 22.5 %all-to-all-start.2 = ((f32[32,1,2]{2,1,0:T(1,128)}), f32[32,1,2]{2,1,0:T(1,128)S(1)}, u32[]{:S(2)}, u32[]{:S(2)}) async-start(f32[32,1,2]{2,1,0:T(1,128)} %broadcast_in_dim.14), calls=%async_computation.2 | async-start | bytes 32768 | tf_op jit(solution)/shard_map/all_to_all | solution.py:57
  146.5 1.1 copy-start.5
  151.6 22.2 %copy-start.2 = (f32[2,2,128,640]{3,2,1,0:T(8,128)}, f32[2,2,128,640]{3,2,1,0:T(8,128)S(1)}, u32[]{:S(2)}) copy-start(f32[2,2,128,640]{3,2,1,0:T(8,128)S(1)} %get-tuple-element.155.q_ref) | copy-start | bytes 3932164
  151.6 22.2 %copy-start.3 = (bf16[2,2,128,640]{3,2,1,0:T(8,128)(2,1)}, bf16[2,2,128,640]{3,2,1,0:T(8,128)(2,1)S(1)}, u32[]{:S(2)}) copy-start(bf16[2,2,128,640]{3,2,1,0:T(8,128)(2,1)S(1)} %get-tuple-element.154.own_ref) | copy-start | bytes 1966084
  151.6 22.2 %collective-permute-start.7 = (bf16[2,2,128,640]{3,2,1,0:T(8,128)(2,1)S(1)}, bf16[2,2,128,640]{3,2,1,0:T(8,128)(2,1)}, u32[]{:S(2)}, u32[]{:S(2)}) collective-permute-start(bf16[2,2,128,640]{3,2,1,0:T(8,128)(2,1)S(1)} %get-tuple-element.154.own_ref), channel_id=1, source_target_pairs={{1,0},{2,1},{3,2},{4,3},{5,4},{6,5},{7,6},{8,7},{9,8},{10,9},{11,1... | collective-permute-start | bytes 1966088 | tf_op jit(solution)/shard_map/ppermute | solution.py:36
  154.1 19.7 %collective-permute-start.6 = (bf16[2,2,128,640]{3,2,1,0:T(8,128)(2,1)S(1)}, bf16[2,2,128,640]{3,2,1,0:T(8,128)(2,1)}, u32[]{:S(2)}, u32[]{:S(2)}) collective-permute-start(bf16[2,2,128,640]{3,2,1,0:T(8,128)(2,1)S(1)} %get-tuple-element.154.own_ref), channel_id=1, source_target_pairs={{0,1},{1,2},{2,3},{3,4},{4,5},{5,6},{6,7},{7,8},{8,9},{9,10},{10,1... | collective-permute-start | bytes 1966088 | tf_op jit(solution)/shard_map/ppermute | solution.py:36
  195.0 24.4 %collective-permute-start.8 = (f32[2,2,128,640]{3,2,1,0:T(8,128)}, f32[2,2,128,640]{3,2,1,0:T(8,128)S(1)}, u32[]{:S(2)}, u32[]{:S(2)}) collective-permute-start(f32[2,2,128,640]{3,2,1,0:T(8,128)} %get-tuple-element.146), channel_id=1, source_target_pairs={{0,1},{1,2},{2,3},{3,4},{4,5},{5,6},{6,7},{7,8},{8,9},{9,10},{10,1... | collective-permute-start | bytes 3932168 | tf_op jit(solution)/shard_map/ppermute | solution.py:36
  197.7 21.6 %collective-permute-start.9 = (f32[2,2,128,640]{3,2,1,0:T(8,128)}, f32[2,2,128,640]{3,2,1,0:T(8,128)}, u32[]{:S(2)}, u32[]{:S(2)}) collective-permute-start(f32[2,2,128,640]{3,2,1,0:T(8,128)} %get-tuple-element.147), channel_id=1, source_target_pairs={{1,0},{2,1},{3,2},{4,3},{5,4},{6,5},{7,6},{8,7},{9,8},{10,9},{11,1... | collective-permute-start | bytes 3932168 | tf_op jit(solution)/shard_map/ppermute | solution.py:36
